TPU v7x, 256 devices: a whole 4x4x8 slice. The times are simulated.
256 devices in a mesh: dp: 8 (over x_lo, y), fsdp: 32 (over z, x_hi, core).
Axes of the slice: x: 4 (x_hi: 2, x_lo: 2; x = x_hi * 2 + x_lo), y: 4, z: 8, core: 2. Of those that a mesh axis runs over, the one named last changes fastest.
Arguments:
- states: bfloat16 [6144, 1024], P('dp'), may hold values from -1200 to 1200
- w_in: bfloat16 [1024, 4096], P(None, 'fsdp'), may hold values from -0.1875 to 0.1875
- w_out: bfloat16 [4096, 1024], P('fsdp'), may hold values from -0.09375 to 0.09375
- precision: float32 [1024], replicated, may hold values from 0.125 to 1
- grad_in: float32 [1024, 4096], P(None, 'fsdp'), may hold values from -75 to 75
- grad_out: float32 [4096, 1024], P('fsdp'), may hold values from -75 to 75
Outputs:
- solution_in: float32 [1024, 4096], P(None, 'fsdp')
- solution_out: float32 [4096, 1024], P('fsdp')
- residual_in: float32 [1024, 4096], P(None, 'fsdp')
- residual_out: float32 [4096, 1024], P('fsdp')
All inputs are finite; a program needn't handle non-finite values.
Results may differ from a plain program's by a relative error of at most 0.025.
Values may be sent and summed in bfloat16 or wider, within the bound.
No kernel may reach another device: no remote copies, remote signals or barrier semaphores. Data moves between devices by JAX's collectives and lax.ppermute only.
A program may use at most 64 MiB of HBM per device.

v0:
```python
import jax
import jax.numpy as jnp
from jax import lax
from jax.sharding import PartitionSpec as P

ITERS = 3


damping = 0.2
norm_eps = 1e-05


def silu_slope(preact):
    gating = jax.nn.sigmoid(preact)
    return gating * (1.0 + preact * (1.0 - gating))


def contract_rows(left_side, right_side):
    return lax.dot_general(
        left_side, right_side, (((0,), (0,)), ((), ())), preferred_element_type=jnp.float32
    )


def local_dot(first_in, first_out, second_in, second_out):
    return jnp.sum(first_in * second_in) + jnp.sum(first_out * second_out)


def global_norm(vector_in, vector_out):
    return lax.psum(local_dot(vector_in, vector_out, vector_in, vector_out), "fsdp")


def fisher_product(direction_in, direction_out, normed, hidden_act, slope_act, w_out, metric):
    tangent_in = direction_in.astype(jnp.bfloat16)
    tangent_out = direction_out.astype(jnp.bfloat16)
    pre_tangent = jnp.dot(normed, tangent_in, preferred_element_type=jnp.float32)
    inner_tangent = (slope_act * pre_tangent).astype(jnp.bfloat16)
    partial_out = jnp.dot(inner_tangent, w_out, preferred_element_type=jnp.float32)
    partial_out = partial_out + jnp.dot(hidden_act, tangent_out, preferred_element_type=jnp.float32)
    out_tangent = lax.psum(partial_out.astype(jnp.bfloat16), "fsdp").astype(jnp.float32)
    cotangent = (out_tangent * metric).astype(jnp.bfloat16)
    back_act = lax.dot_general(
        cotangent, w_out, (((1,), (1,)), ((), ())), preferred_element_type=jnp.float32
    )
    grad_pre = (slope_act * back_act).astype(jnp.bfloat16)
    part_out = contract_rows(hidden_act, cotangent)
    part_in = contract_rows(normed, grad_pre)
    fisher_in, fisher_out = lax.psum((part_in, part_out), "dp")
    fisher_in = fisher_in + damping * direction_in
    fisher_out = fisher_out + damping * direction_out
    quadratic = lax.psum(local_dot(direction_in, direction_out, fisher_in, fisher_out), "fsdp")
    return (fisher_in, fisher_out, quadratic)


def on_device(states, w_in, w_out, precision, grad_in, grad_out):
    row_count = states.shape[0]
    metric = precision / (row_count * lax.axis_size("dp"))
    wide_states = states.astype(jnp.float32)
    mean_square = jnp.mean(wide_states * wide_states, axis=1, keepdims=True)
    normed = (wide_states * lax.rsqrt(mean_square + norm_eps)).astype(jnp.bfloat16)
    preact = jnp.dot(normed, w_in, preferred_element_type=jnp.float32)
    hidden_act = jax.nn.silu(preact).astype(jnp.bfloat16)
    slope_act = silu_slope(preact)
    solution_in = jnp.zeros_like(grad_in)
    solution_out = jnp.zeros_like(grad_out)
    residual_in, residual_out = (grad_in, grad_out)
    direction_in, direction_out = (grad_in, grad_out)
    norm_now = global_norm(residual_in, residual_out)
    for iteration in range(ITERS):
        fisher_in, fisher_out, quadratic = fisher_product(
            direction_in, direction_out, normed, hidden_act, slope_act, w_out, metric
        )
        step_size = norm_now / quadratic
        solution_in = solution_in + step_size * direction_in
        solution_out = solution_out + step_size * direction_out
        residual_in = residual_in - step_size * fisher_in
        residual_out = residual_out - step_size * fisher_out
        if iteration + 1 < ITERS:
            norm_next = global_norm(residual_in, residual_out)
            direction_in = residual_in + norm_next / norm_now * direction_in
            direction_out = residual_out + norm_next / norm_now * direction_out
            norm_now = norm_next
    return (solution_in, solution_out, residual_in, residual_out)


def solution(mesh):
    return jax.shard_map(
        on_device,
        mesh=mesh,
        in_specs=(
            P("dp", None),
            P(None, "fsdp"),
            P("fsdp", None),
            P(),
            P(None, "fsdp"),
            P("fsdp", None),
        ),
        out_specs=(P(None, "fsdp"), P("fsdp", None), P(None, "fsdp"), P("fsdp", None)),
        check_vma=False,
    )
```

profile of v0, /device:TPU:1, one launch (start us, length us, event | category | flops | bytes accessed | tf_op | source)
XLA Modules:
  0.0 1496.2 jit_solution(2094628145754783382)
XLA Ops:
  11.6 4.5 fusion.19
  16.1 3.6 add_convert_fusion.2
  20.3 277.6 %all-reduce.11.cloned.1.call-done = bf16[768,1024]{1,0:T(8,128)(2,1)} async-done(((bf16[768,1024]{1,0:T(8,128)(2,1)}), bf16[768,1024]{1,0:T(8,128)(2,1)}) %all-reduce.11.cloned.1.call-update) | async-done | bytes 1572880 | tf_op jit(solution)/shard_map/psum | solution.py:39
  297.9 2.7 fusion.2
  300.6 4.0 fusion.22
  304.6 75.5 %all-reduce.21.cloned.1.call-done = (f32[1024,128]{1,0:T(8,128)}, f32[128,1024]{1,0:T(8,128)}) async-done(((f32[1024,128]{1,0:T(8,128)}, f32[128,1024]{1,0:T(8,128)}), (f32[1024,128]{1,0:T(8,128)}, f32[128,1024]{1,0:T(8,128)})) %all-reduce.21.cloned.1.call-update) | async-done | bytes 1048592 | tf_op jit(solution)/shard_map/psum | solution.py:47
  386.5 71.5 %all-reduce = (f32[]{:T(128)}, f32[]{:T(128)}) all-reduce(f32[]{:T(128)S(6)} %add.118, f32[]{:T(128)S(6)} %add.126), channel_id=1, replica_groups=mesh['dp'=8,'fsdp'=32] {'fsdp'}, use_global_device_ids=true, to_apply=%region_2.3 | all-reduce | flops 2 | bytes 16 | tf_op jit(solution)/shard_map/psum | solution.py:29
  463.2 65.3 %psum.110 = f32[]{:T(128)} all-reduce(f32[]{:T(128)S(6)} %add.127), channel_id=1, replica_groups=mesh['dp'=8,'fsdp'=32] {'fsdp'}, use_global_device_ids=true, to_apply=%region_12.13 | all-reduce | flops 1 | bytes 8 | tf_op jit(solution)/shard_map/psum | solution.py:29
  532.2 4.4 fusion.18
  536.6 3.7 add_convert_fusion.1
  540.4 272.5 %all-reduce.13.cloned.1.call-done = bf16[768,1024]{1,0:T(8,128)(2,1)} async-done(((bf16[768,1024]{1,0:T(8,128)(2,1)}), bf16[768,1024]{1,0:T(8,128)(2,1)}) %all-reduce.13.cloned.1.call-update) | async-done | bytes 1572880 | tf_op jit(solution)/shard_map/psum | solution.py:39
  812.9 2.8 fusion.4
  815.6 4.0 fusion.21
  819.7 75.5 %all-reduce.19.cloned.1.call-done = (f32[1024,128]{1,0:T(8,128)}, f32[128,1024]{1,0:T(8,128)}) async-done(((f32[1024,128]{1,0:T(8,128)}, f32[128,1024]{1,0:T(8,128)}), (f32[1024,128]{1,0:T(8,128)}, f32[128,1024]{1,0:T(8,128)})) %all-reduce.19.cloned.1.call-update) | async-done | bytes 1048592 | tf_op jit(solution)/shard_map/psum | solution.py:47
  900.1 71.5 %psum.114 = f32[]{:T(128)} all-reduce(f32[]{:T(128)S(6)} %add.133), channel_id=1, replica_groups=mesh['dp'=8,'fsdp'=32] {'fsdp'}, use_global_device_ids=true, to_apply=%region_18.19 | all-reduce | flops 1 | bytes 8 | tf_op jit(solution)/shard_map/psum | solution.py:50
  973.0 3.0 multiply_reduce_fusion.3
  979.0 65.5 %psum.115 = f32[]{:T(128)} all-reduce(f32[]{:T(128)S(6)} %add.135), channel_id=1, replica_groups=mesh['dp'=8,'fsdp'=32] {'fsdp'}, use_global_device_ids=true, to_apply=%region_21.22 | all-reduce | flops 1 | bytes 8 | tf_op jit(solution)/shard_map/psum | solution.py:29
  1045.8 4.6 fusion.17
  1050.3 3.8 add_convert_fusion
  1054.2 272.5 %all-reduce.15.cloned.1.call-done = bf16[768,1024]{1,0:T(8,128)(2,1)} async-done(((bf16[768,1024]{1,0:T(8,128)(2,1)}), bf16[768,1024]{1,0:T(8,128)(2,1)}) %all-reduce.15.cloned.1.call-update) | async-done | bytes 1572880 | tf_op jit(solution)/shard_map/psum | solution.py:39
  1326.7 4.0 fusion.20
  1330.7 2.8 fusion.6
  1333.6 75.6 %all-reduce.17.cloned.1.call-done = (f32[1024,128]{1,0:T(8,128)}, f32[128,1024]{1,0:T(8,128)}) async-done(((f32[1024,128]{1,0:T(8,128)}, f32[128,1024]{1,0:T(8,128)}), (f32[1024,128]{1,0:T(8,128)}, f32[128,1024]{1,0:T(8,128)})) %all-reduce.17.cloned.1.call-update) | async-done | bytes 1048592 | tf_op jit(solution)/shard_map/psum | solution.py:47
  1413.1 71.5 %psum.119 = f32[]{:T(128)} all-reduce(f32[]{:T(128)S(6)} %add.141), channel_id=1, replica_groups=mesh['dp'=8,'fsdp'=32] {'fsdp'}, use_global_device_ids=true, to_apply=%region_27.28 | all-reduce | flops 1 | bytes 8 | tf_op jit(solution)/shard_map/psum | solution.py:50
  (59 shorter events, 25.2 us)
Async XLA Ops:
  7.2 4.4 copy-start
  7.2 2.0 copy-start.1
  7.2 290.7 %all-reduce.11.cloned.1.call-start = ((), (), s32[]{:S(2)}) async-start(), calls=%async_computation | async-start | bytes 3145728 | tf_op jit(solution)/shard_map/psum | solution.py:39
  9.2 2.4 copy-start.2
  11.6 286.3 %copy-start.10 = (bf16[768,128]{1,0:T(8,128)(2,1)}, bf16[768,128]{1,0:T(8,128)(2,1)S(1)}, u32[]{:S(2)}) copy-start(bf16[768,128]{1,0:T(8,128)(2,1)S(1)} %get-tuple-element.24) | copy-start | bytes 589828
  11.6 4.5 copy-start.3
  19.6 0.7 copy-start.14
  19.7 360.5 %all-reduce.21.cloned.1.call-start = ((), (), s32[]{:S(2)}) async-start(), calls=%async_computation.5 | async-start | bytes 2097152 | tf_op jit(solution)/shard_map/psum | solution.py:47
  304.6 508.3 %all-reduce.13.cloned.1.call-start = ((), (), s32[]{:S(2)}) async-start(), calls=%async_computation.1 | async-start | bytes 3145728 | tf_op jit(solution)/shard_map/psum | solution.py:39
  380.2 81.0 %copy-start.6 = (f32[128,1024]{1,0:T(8,128)S(1)}, f32[128,1024]{1,0:T(8,128)}, u32[]{:S(2)}) copy-start(f32[128,1024]{1,0:T(8,128)} %get-tuple-element.15) | copy-start | bytes 1572868
  540.3 354.9 %all-reduce.19.cloned.1.call-start = ((), (), s32[]{:S(2)}) async-start(), calls=%async_computation.4 | async-start | bytes 2097152 | tf_op jit(solution)/shard_map/psum | solution.py:47
  819.7 507.1 %all-reduce.15.cloned.1.call-start = ((), (), s32[]{:S(2)}) async-start(), calls=%async_computation.2 | async-start | bytes 3145728 | tf_op jit(solution)/shard_map/psum | solution.py:39
  973.0 3.0 copy-start.4
  973.0 3.0 copy-start.7
  973.0 3.0 copy-start.12
  1054.2 355.0 %all-reduce.17.cloned.1.call-start = ((), (), s32[]{:S(2)}) async-start(), calls=%async_computation.3 | async-start | bytes 2097152 | tf_op jit(solution)/shard_map/psum | solution.py:47
  1330.7 78.4 %copy-start.8 = (f32[128,1024]{1,0:T(8,128)S(1)}, f32[128,1024]{1,0:T(8,128)}, u32[]{:S(2)}) copy-start(f32[128,1024]{1,0:T(8,128)} %get-tuple-element.17) | copy-start | bytes 1572868
  1333.6 77.5 %copy-start.9 = (f32[1024,128]{1,0:T(8,128)S(1)}, f32[1024,128]{1,0:T(8,128)}, u32[]{:S(2)}) copy-start(f32[1024,128]{1,0:T(8,128)} %get-tuple-element.19) | copy-start | bytes 1572868
  1409.2 1.9 copy-start.13
  1485.8 2.3 copy-start.5
  1485.8 2.3 copy-start.11
Sparse Core Ops, SparseCore 0:
  19.8 278.0 all-reduce.10
  304.7 75.4 all-reduce.20
  540.4 272.3 all-reduce.12
  819.8 75.4 all-reduce.18
  1054.3 272.3 all-reduce.14
  1333.7 75.4 all-reduce.16
where the time goes:
time: 1500 us
  waiting for transfers between devices  1050 us (70%)
  blocking collectives  345 us (23%)
  matrix products  47.2 us (3%)
  between operations  28.6 us (2%)
  other arithmetic  24.8 us (2%)
    psum x3, waiting for transfers between devices, fisher_product(): lax.psum(partial_out.astype(jnp.bfloat16), 'fsdp').astype(jnp.float32)  823 us
    psum x3, waiting for transfers between devices, fisher_product(): fisher_in, fisher_out = lax.psum((part_in, part_out), 'dp')  227 us
    psum x3, blocking collectives, global_norm(): lax.psum(local_dot(vector_in, vector_out, vector_in, vector_out), 'fsdp')  202 us
    psum x2, blocking collectives, fisher_product(): lax.psum(local_dot(direction_in, direction_out, fisher_in, fisher_out), '...  143 us
  transfers between devices with their start and end apart: 6, of which 6 were waited for; matrix products, arithmetic and copies ran while one was open for 0% of the time, Pallas kernels for 0%

commit v1 on v0

--- a/solution.py
+++ b/solution.py
@@ -25,8 +25,54 @@
     return jnp.sum(first_in * second_in) + jnp.sum(first_out * second_out)
 
 
-def global_norm(vector_in, vector_out):
-    return lax.psum(local_dot(vector_in, vector_out, vector_in, vector_out), "fsdp")
+def xor_pairs(size, bit):
+    return [(i, i ^ bit) for i in range(size)]
+
+
+def stages_of(size):
+    count = size.bit_length() - 1
+    assert 1 << count == size
+    return count
+
+
+def scalar_sum(values, axis):
+    size = lax.axis_size(axis)
+    gathered = lax.all_to_all(jnp.broadcast_to(values[None], (size,) + values.shape), axis, 0, 0)
+    return jnp.sum(gathered, axis=0)
+
+
+def doubling_sum(parts, axis):
+    size = lax.axis_size(axis)
+    for stage in range(stages_of(size)):
+        pairs = xor_pairs(size, 1 << stage)
+        parts = tuple(part + lax.ppermute(part, axis, pairs) for part in parts)
+    return parts
+
+
+def halving_reduce(term, axis):
+    size = lax.axis_size(axis)
+    index = lax.axis_index(axis)
+    kept = term.astype(jnp.float32)
+    for stage in range(stages_of(size)):
+        half = kept.shape[0] // 2
+        bit = (index >> stage) & 1
+        send = lax.dynamic_slice_in_dim(kept, (1 - bit) * half, half, 0)
+        keep = lax.dynamic_slice_in_dim(kept, bit * half, half, 0)
+        got = lax.ppermute(send.astype(jnp.bfloat16), axis, xor_pairs(size, 1 << stage))
+        kept = keep + got.astype(jnp.float32)
+    return kept
+
+
+def doubling_gather(chunk, axis):
+    size = lax.axis_size(axis)
+    index = lax.axis_index(axis)
+    for stage in reversed(range(stages_of(size))):
+        bit = (index >> stage) & 1
+        other = lax.ppermute(chunk, axis, xor_pairs(size, 1 << stage))
+        chunk = jnp.where(
+            bit == 0, jnp.concatenate([chunk, other], 0), jnp.concatenate([other, chunk], 0)
+        )
+    return chunk
 
 
 def fisher_product(direction_in, direction_out, normed, hidden_act, slope_act, w_out, metric):
@@ -36,19 +82,23 @@
     inner_tangent = (slope_act * pre_tangent).astype(jnp.bfloat16)
     partial_out = jnp.dot(inner_tangent, w_out, preferred_element_type=jnp.float32)
     partial_out = partial_out + jnp.dot(hidden_act, tangent_out, preferred_element_type=jnp.float32)
-    out_tangent = lax.psum(partial_out.astype(jnp.bfloat16), "fsdp").astype(jnp.float32)
-    cotangent = (out_tangent * metric).astype(jnp.bfloat16)
+    out_chunk = halving_reduce(partial_out.astype(jnp.bfloat16), "fsdp")
+    cotangent = doubling_gather((out_chunk * metric).astype(jnp.bfloat16), "fsdp")
     back_act = lax.dot_general(
         cotangent, w_out, (((1,), (1,)), ((), ())), preferred_element_type=jnp.float32
     )
     grad_pre = (slope_act * back_act).astype(jnp.bfloat16)
     part_out = contract_rows(hidden_act, cotangent)
     part_in = contract_rows(normed, grad_pre)
-    fisher_in, fisher_out = lax.psum((part_in, part_out), "dp")
+    fisher_in, fisher_out = doubling_sum((part_in, part_out), "dp")
     fisher_in = fisher_in + damping * direction_in
     fisher_out = fisher_out + damping * direction_out
-    quadratic = lax.psum(local_dot(direction_in, direction_out, fisher_in, fisher_out), "fsdp")
+    quadratic = scalar_sum(local_dot(direction_in, direction_out, fisher_in, fisher_out)[None], "fsdp")[0]
     return (fisher_in, fisher_out, quadratic)
+
+
+def global_norm(vector_in, vector_out):
+    return scalar_sum(local_dot(vector_in, vector_out, vector_in, vector_out)[None], "fsdp")[0]
 
 
 def on_device(states, w_in, w_out, precision, grad_in, grad_out):

time: 1500 us -> 596 us (0.40)
  waiting for transfers between devices: 1050 us -> 321 us
  blocking collectives: 345 us -> 53.9 us
  starting transfers between devices: 0.25 us -> 98.5 us
  other arithmetic: 24.8 us -> 42.8 us
    psum x6 -> x0, waiting for transfers between devices: 1050 us -> none  [the longest x3 823 us: fisher_product(): lax.psum(partial_out.astype(jnp.bfloat16), 'fsdp').astype(jnp.float32)]
    psum x5 -> x0, blocking collectives: 345 us -> none  [the longest x3 202 us: global_norm(): lax.psum(local_dot(vector_in, vector_out, vector_in, vector_out), 'fsdp')]
    ppermute x0 -> x48, waiting for transfers between devices: none -> 304 us  [the longest x18 147 us: doubling_sum(): parts = tuple((part + lax.ppermute(part, axis, pairs) for part in parts))]
    ppermute x0 -> x48, starting transfers between devices: none -> 83 us  [the longest x15 44.8 us: doubling_gather(): other = lax.ppermute(chunk, axis, xor_pairs(size, 1 << stage))]
    all_to_all x0 -> x4, blocking collectives: none -> 53.9 us  [scalar_sum(): lax.all_to_all(jnp.broadcast_to(values[None], (size,) + values.shape), ax...]
    all_to_all x0 -> x2, waiting for transfers between devices: none -> 16.8 us  [scalar_sum(): lax.all_to_all(jnp.broadcast_to(values[None], (size,) + values.shape), ax...]
    all_to_all x0 -> x2, starting transfers between devices: none -> 15.5 us  [scalar_sum(): lax.all_to_all(jnp.broadcast_to(values[None], (size,) + values.shape), ax...]
  transfers between devices with their start and end apart: 6 -> 50, of which waited for: 6 -> 47; matrix products, arithmetic and copies ran while one was open for 0% -> 2% of each run, Pallas kernels for 0% -> 0%
where the time goes in v1:
time: 596 us; the launch traced here: 587 us
  waiting for transfers between devices  321 us (54%)
  starting transfers between devices  98.5 us (17%)
  blocking collectives  53.9 us (9%)
  other arithmetic  42.8 us (7%)
  matrix products  41.6 us (7%)
  between operations  16.3 us (3%)
  local copies, waits for them, and re-layouts  12.7 us (2%)
    ppermute x18, waiting for transfers between devices, doubling_sum(): parts = tuple((part + lax.ppermute(part, axis, pairs) for part in parts))  147 us
    ppermute x15, waiting for transfers between devices, halving_reduce(): lax.ppermute(send.astype(jnp.bfloat16), axis, xor_pairs(size, 1 << stage))  83.8 us
    ppermute x15, waiting for transfers between devices, doubling_gather(): other = lax.ppermute(chunk, axis, xor_pairs(size, 1 << stage))  73.1 us
    all_to_all x4, blocking collectives, scalar_sum(): lax.all_to_all(jnp.broadcast_to(values[None], (size,) + values.shape), ax...  53.9 us
    ppermute x15, starting transfers between devices, doubling_gather(): other = lax.ppermute(chunk, axis, xor_pairs(size, 1 << stage))  44.8 us
    ppermute x18, starting transfers between devices, doubling_sum(): parts = tuple((part + lax.ppermute(part, axis, pairs) for part in parts))  21.5 us
    dot_general x6, matrix products, contract_rows(): lax.dot_general(left_side, right_side, (((0,), (0,)), ((), ())), preferre...  19.9 us
    all_to_all x2, waiting for transfers between devices, scalar_sum(): lax.all_to_all(jnp.broadcast_to(values[None], (size,) + values.shape), ax...  16.8 us
  transfers between devices with their start and end apart: 50, of which 47 were waited for; matrix products, arithmetic and copies ran while one was open for 2% of the time, Pallas kernels for 0%

profile of v1, /device:TPU:1, one launch (start us, length us, event | category | flops | bytes accessed | tf_op | source)
XLA Modules:
  0.0 587.1 jit_solution(13264282826149554692)
XLA Ops:
  23.1 11.1 %collective-permute-done.1 = bf16[192,1024]{1,0:T(8,128)(2,1)} collective-permute-done((bf16[192,1024]{1,0:T(8,128)(2,1)}, bf16[192,1024]{1,0:T(8,128)(2,1)}, u32[]{:S(2)}, u32[]{:S(2)}) %collective-permute-start.1) | collective-permute-done | bytes 393248 | tf_op jit(solution)/shard_map/ppermute | solution.py:61
  114.4 9.3 %collective-permute-done.10 = f32[1024,128]{1,0:T(8,128)S(1)} collective-permute-done((f32[1024,128]{1,0:T(8,128)}, f32[1024,128]{1,0:T(8,128)S(1)}, u32[]{:S(2)}, u32[]{:S(2)}) %collective-permute-start.10) | collective-permute-done | bytes 524320 | tf_op jit(solution)/shard_map/ppermute | solution.py:48
  138.0 10.6 %collective-permute-done.11 = f32[1024,128]{1,0:T(8,128)S(1)} collective-permute-done((f32[1024,128]{1,0:T(8,128)S(1)}, f32[1024,128]{1,0:T(8,128)S(1)}, u32[]{:S(2)}, u32[]{:S(2)}) %collective-permute-start.11) | collective-permute-done | bytes 524320 | tf_op jit(solution)/shard_map/ppermute | solution.py:48
  150.0 9.9 %collective-permute-done.14 = f32[128,1024]{1,0:T(8,128)S(1)} collective-permute-done((f32[128,1024]{1,0:T(8,128)S(1)}, f32[128,1024]{1,0:T(8,128)S(1)}, u32[]{:S(2)}, u32[]{:S(2)}) %collective-permute-start.14) | collective-permute-done | bytes 524320 | tf_op jit(solution)/shard_map/ppermute | solution.py:48
  162.1 10.2 %collective-permute-done.15 = f32[128,1024]{1,0:T(8,128)S(1)} collective-permute-done((f32[128,1024]{1,0:T(8,128)S(1)}, f32[128,1024]{1,0:T(8,128)S(1)}, u32[]{:S(2)}, u32[]{:S(2)}) %collective-permute-start.15) | collective-permute-done | bytes 524320 | tf_op jit(solution)/shard_map/ppermute | solution.py:48
  175.0 11.4 %all-to-all-start.1 = ((f32[32,1,1]{2,1,0:T(1,128)}), f32[32,1,1]{2,1,0:T(1,128)S(1)}, u32[]{:S(2)}, u32[]{:S(2)}) async-start(f32[32,1,1]{2,1,0:T(1,128)} %broadcast_in_dim.13), calls=%async_computation.1 | async-start | bytes 32768 | tf_op jit(solution)/shard_map/all_to_all | solution.py:40
  201.2 8.7 %all-to-all-done = f32[32,1,1]{2,1,0:T(1,128)S(1)} async-done(((f32[32,1,1]{2,1,0:T(1,128)}), f32[32,1,1]{2,1,0:T(1,128)S(1)}, u32[]{:S(2)}, u32[]{:S(2)}) %all-to-all-start) | async-done | bytes 160 | tf_op jit(solution)/shard_map/all_to_all | solution.py:40
  217.5 12.7 %all_to_all.36 = f32[32,1,1]{2,1,0:T(1,128)S(1)} all-to-all(f32[32,1,1]{2,1,0:T(1,128)S(1)} %broadcast_in_dim.14), channel_id=1, replica_groups=mesh['dp'=8,'fsdp'=32] {'fsdp'}, dimensions={0} | all-to-all | bytes 256 | tf_op jit(solution)/shard_map/all_to_all | solution.py:40
  244.1 11.4 %collective-permute-done.17 = bf16[192,1024]{1,0:T(8,128)(2,1)S(1)} collective-permute-done((bf16[192,1024]{1,0:T(8,128)(2,1)S(1)}, bf16[192,1024]{1,0:T(8,128)(2,1)S(1)}, u32[]{:S(2)}, u32[]{:S(2)}) %collective-permute-start.17) | collective-permute-done | bytes 393248 | tf_op jit(solution)/shard_map/ppermute | solution.py:61
  280.5 8.9 %collective-permute-start.22 = (bf16[48,1024]{1,0:T(8,128)(2,1)S(1)}, bf16[48,1024]{1,0:T(8,128)(2,1)S(1)}, u32[]{:S(2)}, u32[]{:S(2)}) collective-permute-start(bf16[48,1024]{1,0:T(8,128)(2,1)S(1)} %maximum_select_fusion.22), channel_id=1, source_target_pairs={{0,8},{1,9},{2,10},{3,11},{4,12},{5,13},{6,14},{7,15},{8,0},{9,1},... | collective-permute-start | bytes 294920 | tf_op jit(solution)/shard_map/ppermute | solution.py:71
  308.1 9.5 %collective-permute-start.25 = (bf16[384,1024]{1,0:T(8,128)(2,1)S(1)}, bf16[384,1024]{1,0:T(8,128)(2,1)}, u32[]{:S(2)}, u32[]{:S(2)}) collective-permute-start(bf16[384,1024]{1,0:T(8,128)(2,1)S(1)} %maximum_select_fusion.4), channel_id=1, source_target_pairs={{0,1},{1,0},{2,3},{3,2},{4,5},{5,4},{6,7},{7,6},{8,9},{9,8},{10,11... | collective-permute-start | bytes 2359304 | tf_op jit(solution)/shard_map/ppermute | solution.py:71
  328.2 9.2 %collective-permute-done.26 = f32[1024,128]{1,0:T(8,128)S(1)} collective-permute-done((f32[1024,128]{1,0:T(8,128)}, f32[1024,128]{1,0:T(8,128)S(1)}, u32[]{:S(2)}, u32[]{:S(2)}) %collective-permute-start.26) | collective-permute-done | bytes 524320 | tf_op jit(solution)/shard_map/ppermute | solution.py:48
  337.9 10.7 %collective-permute-done.29 = f32[128,1024]{1,0:T(8,128)S(1)} collective-permute-done((f32[128,1024]{1,0:T(8,128)S(1)}, f32[128,1024]{1,0:T(8,128)S(1)}, u32[]{:S(2)}, u32[]{:S(2)}) %collective-permute-start.29) | collective-permute-done | bytes 524320 | tf_op jit(solution)/shard_map/ppermute | solution.py:48
  349.2 10.4 %collective-permute-done.27 = f32[1024,128]{1,0:T(8,128)S(1)} collective-permute-done((f32[1024,128]{1,0:T(8,128)S(1)}, f32[1024,128]{1,0:T(8,128)S(1)}, u32[]{:S(2)}, u32[]{:S(2)}) %collective-permute-start.27) | collective-permute-done | bytes 524320 | tf_op jit(solution)/shard_map/ppermute | solution.py:48
  360.0 10.8 %collective-permute-done.30 = f32[128,1024]{1,0:T(8,128)S(1)} collective-permute-done((f32[128,1024]{1,0:T(8,128)S(1)}, f32[128,1024]{1,0:T(8,128)S(1)}, u32[]{:S(2)}, u32[]{:S(2)}) %collective-permute-start.30) | collective-permute-done | bytes 524320 | tf_op jit(solution)/shard_map/ppermute | solution.py:48
  372.1 11.1 %collective-permute-done.31 = f32[128,1024]{1,0:T(8,128)S(1)} collective-permute-done((f32[128,1024]{1,0:T(8,128)S(1)}, f32[128,1024]{1,0:T(8,128)S(1)}, u32[]{:S(2)}, u32[]{:S(2)}) %collective-permute-start.31) | collective-permute-done | bytes 524320 | tf_op jit(solution)/shard_map/ppermute | solution.py:48
  386.1 14.3 %all_to_all.37 = f32[32,1,1]{2,1,0:T(1,128)S(1)} all-to-all(f32[32,1,1]{2,1,0:T(1,128)S(1)} %broadcast_in_dim.15), channel_id=1, replica_groups=mesh['dp'=8,'fsdp'=32] {'fsdp'}, dimensions={0} | all-to-all | bytes 256 | tf_op jit(solution)/shard_map/all_to_all | solution.py:40
  408.5 12.8 %all_to_all.38 = f32[32,1,1]{2,1,0:T(1,128)S(1)} all-to-all(f32[32,1,1]{2,1,0:T(1,128)S(1)} %broadcast_in_dim.16), channel_id=1, replica_groups=mesh['dp'=8,'fsdp'=32] {'fsdp'}, dimensions={0} | all-to-all | bytes 256 | tf_op jit(solution)/shard_map/all_to_all | solution.py:40
  434.3 11.4 %collective-permute-done.33 = bf16[192,1024]{1,0:T(8,128)(2,1)S(1)} collective-permute-done((bf16[192,1024]{1,0:T(8,128)(2,1)S(1)}, bf16[192,1024]{1,0:T(8,128)(2,1)S(1)}, u32[]{:S(2)}, u32[]{:S(2)}) %collective-permute-start.33) | collective-permute-done | bytes 393248 | tf_op jit(solution)/shard_map/ppermute | solution.py:61
  490.3 8.3 %collective-permute-start.41 = (bf16[384,1024]{1,0:T(8,128)(2,1)S(1)}, bf16[384,1024]{1,0:T(8,128)(2,1)S(1)}, u32[]{:S(2)}, u32[]{:S(2)}) collective-permute-start(bf16[384,1024]{1,0:T(8,128)(2,1)S(1)} %maximum_select_fusion.5), channel_id=1, source_target_pairs={{0,1},{1,0},{2,3},{3,2},{4,5},{5,4},{6,7},{7,6},{8,9},{9,8},{10,11... | collective-permute-start | bytes 2359304 | tf_op jit(solution)/shard_map/ppermute | solution.py:71
  529.4 10.8 %collective-permute-done.46 = f32[128,1024]{1,0:T(8,128)S(1)} collective-permute-done((f32[128,1024]{1,0:T(8,128)S(1)}, f32[128,1024]{1,0:T(8,128)S(1)}, u32[]{:S(2)}, u32[]{:S(2)}) %collective-permute-start.46) | collective-permute-done | bytes 524320 | tf_op jit(solution)/shard_map/ppermute | solution.py:48
  540.7 10.7 %collective-permute-done.43 = f32[1024,128]{1,0:T(8,128)S(1)} collective-permute-done((f32[1024,128]{1,0:T(8,128)S(1)}, f32[1024,128]{1,0:T(8,128)S(1)}, u32[]{:S(2)}, u32[]{:S(2)}) %collective-permute-start.43) | collective-permute-done | bytes 524320 | tf_op jit(solution)/shard_map/ppermute | solution.py:48
  552.7 11.2 %collective-permute-done.44 = f32[1024,128]{1,0:T(8,128)S(1)} collective-permute-done((f32[1024,128]{1,0:T(8,128)S(1)}, f32[1024,128]{1,0:T(8,128)S(1)}, u32[]{:S(2)}, u32[]{:S(2)}) %collective-permute-start.44) | collective-permute-done | bytes 524320 | tf_op jit(solution)/shard_map/ppermute | solution.py:48
  566.7 14.2 %all_to_all.39 = f32[32,1,1]{2,1,0:T(1,128)S(1)} all-to-all(f32[32,1,1]{2,1,0:T(1,128)S(1)} %broadcast_in_dim.17), channel_id=1, replica_groups=mesh['dp'=8,'fsdp'=32] {'fsdp'}, dimensions={0} | all-to-all | bytes 256 | tf_op jit(solution)/shard_map/all_to_all | solution.py:40
  (258 shorter events, 311.4 us)
Async XLA Ops:
  22.1 12.1 %collective-permute-start.1 = (bf16[192,1024]{1,0:T(8,128)(2,1)}, bf16[192,1024]{1,0:T(8,128)(2,1)}, u32[]{:S(2)}, u32[]{:S(2)}) collective-permute-start(bf16[192,1024]{1,0:T(8,128)(2,1)} %dynamic-slice_convert_fusion.5), channel_id=1, source_target_pairs={{0,2},{1,3},{2,0},{3,1},{4,6},{5,7},{6,4},{7,5},{8,10},{9,11},{10,... | collective-permute-start | bytes 1179656 | tf_op jit(solution)/shard_map/ppermute | solution.py:61
  110.1 13.6 %collective-permute-start.10 = (f32[1024,128]{1,0:T(8,128)}, f32[1024,128]{1,0:T(8,128)S(1)}, u32[]{:S(2)}, u32[]{:S(2)}) collective-permute-start(f32[1024,128]{1,0:T(8,128)} %fusion.16), channel_id=1, source_target_pairs={{0,32},{32,0},{64,96},{96,64},{128,160},{160,128},{192,224},{224,1... | collective-permute-start | bytes 1572872 | tf_op jit(solution)/shard_map/ppermute | solution.py:48
  114.2 20.8 %collective-permute-start.13 = (f32[128,1024]{1,0:T(8,128)S(1)}, f32[128,1024]{1,0:T(8,128)S(1)}, u32[]{:S(2)}, u32[]{:S(2)}) collective-permute-start(f32[128,1024]{1,0:T(8,128)S(1)} %fusion.19), channel_id=1, source_target_pairs={{0,32},{32,0},{64,96},{96,64},{128,160},{160,128},{192,224},{224,1... | collective-permute-start | bytes 1572872 | tf_op jit(solution)/shard_map/ppermute | solution.py:48
  123.8 24.9 %collective-permute-start.11 = (f32[1024,128]{1,0:T(8,128)S(1)}, f32[1024,128]{1,0:T(8,128)S(1)}, u32[]{:S(2)}, u32[]{:S(2)}) collective-permute-start(f32[1024,128]{1,0:T(8,128)S(1)} %add.258), channel_id=1, source_target_pairs={{0,64},{32,96},{64,0},{96,32},{128,192},{160,224},{192,128},{224,1... | collective-permute-start | bytes 1572872 | tf_op jit(solution)/shard_map/ppermute | solution.py:48
  135.0 24.9 %collective-permute-start.14 = (f32[128,1024]{1,0:T(8,128)S(1)}, f32[128,1024]{1,0:T(8,128)S(1)}, u32[]{:S(2)}, u32[]{:S(2)}) collective-permute-start(f32[128,1024]{1,0:T(8,128)S(1)} %add.262), channel_id=1, source_target_pairs={{0,64},{32,96},{64,0},{96,32},{128,192},{160,224},{192,128},{224,1... | collective-permute-start | bytes 1572872 | tf_op jit(solution)/shard_map/ppermute | solution.py:48
  148.7 12.6 %collective-permute-start.12 = (f32[1024,128]{1,0:T(8,128)S(1)}, f32[1024,128]{1,0:T(8,128)S(1)}, u32[]{:S(2)}, u32[]{:S(2)}) collective-permute-start(f32[1024,128]{1,0:T(8,128)S(1)} %add.259), channel_id=1, source_target_pairs={{0,128},{32,160},{64,192},{96,224},{128,0},{160,32},{192,64},{224,... | collective-permute-start | bytes 1572872 | tf_op jit(solution)/shard_map/ppermute | solution.py:48
  159.9 12.3 %collective-permute-start.15 = (f32[128,1024]{1,0:T(8,128)S(1)}, f32[128,1024]{1,0:T(8,128)S(1)}, u32[]{:S(2)}, u32[]{:S(2)}) collective-permute-start(f32[128,1024]{1,0:T(8,128)S(1)} %add.263), channel_id=1, source_target_pairs={{0,128},{32,160},{64,192},{96,224},{128,0},{160,32},{192,64},{224,... | collective-permute-start | bytes 1572872 | tf_op jit(solution)/shard_map/ppermute | solution.py:48
  175.0 20.8 %all-to-all-start.1 = ((f32[32,1,1]{2,1,0:T(1,128)}), f32[32,1,1]{2,1,0:T(1,128)S(1)}, u32[]{:S(2)}, u32[]{:S(2)}) async-start(f32[32,1,1]{2,1,0:T(1,128)} %broadcast_in_dim.13), calls=%async_computation.1 | async-start | bytes 32768 | tf_op jit(solution)/shard_map/all_to_all | solution.py:40
  196.4 13.5 %all-to-all-start = ((f32[32,1,1]{2,1,0:T(1,128)}), f32[32,1,1]{2,1,0:T(1,128)S(1)}, u32[]{:S(2)}, u32[]{:S(2)}) async-start(f32[32,1,1]{2,1,0:T(1,128)} %broadcast_in_dim.12), calls=%async_computation | async-start | bytes 32768 | tf_op jit(solution)/shard_map/all_to_all | solution.py:40
  243.6 11.9 %collective-permute-start.17 = (bf16[192,1024]{1,0:T(8,128)(2,1)S(1)}, bf16[192,1024]{1,0:T(8,128)(2,1)S(1)}, u32[]{:S(2)}, u32[]{:S(2)}) collective-permute-start(bf16[192,1024]{1,0:T(8,128)(2,1)S(1)} %dynamic-slice_convert_fusion.4), channel_id=1, source_target_pairs={{0,2},{1,3},{2,0},{3,1},{4,6},{5,7},{6,4},{7,5},{8,10},{9,11},{10,... | collective-permute-start | bytes 1179656 | tf_op jit(solution)/shard_map/ppermute | solution.py:61
  280.5 13.4 %collective-permute-start.22 = (bf16[48,1024]{1,0:T(8,128)(2,1)S(1)}, bf16[48,1024]{1,0:T(8,128)(2,1)S(1)}, u32[]{:S(2)}, u32[]{:S(2)}) collective-permute-start(bf16[48,1024]{1,0:T(8,128)(2,1)S(1)} %maximum_select_fusion.22), channel_id=1, source_target_pairs={{0,8},{1,9},{2,10},{3,11},{4,12},{5,13},{6,14},{7,15},{8,0},{9,1},... | collective-permute-start | bytes 294920 | tf_op jit(solution)/shard_map/ppermute | solution.py:71
  324.1 13.3 %collective-permute-start.26 = (f32[1024,128]{1,0:T(8,128)}, f32[1024,128]{1,0:T(8,128)S(1)}, u32[]{:S(2)}, u32[]{:S(2)}) collective-permute-start(f32[1024,128]{1,0:T(8,128)} %fusion.15), channel_id=1, source_target_pairs={{0,32},{32,0},{64,96},{96,64},{128,160},{160,128},{192,224},{224,1... | collective-permute-start | bytes 1572872 | tf_op jit(solution)/shard_map/ppermute | solution.py:48
  326.7 21.9 %collective-permute-start.29 = (f32[128,1024]{1,0:T(8,128)S(1)}, f32[128,1024]{1,0:T(8,128)S(1)}, u32[]{:S(2)}, u32[]{:S(2)}) collective-permute-start(f32[128,1024]{1,0:T(8,128)S(1)} %fusion.18), channel_id=1, source_target_pairs={{0,32},{32,0},{64,96},{96,64},{128,160},{160,128},{192,224},{224,1... | collective-permute-start | bytes 1572872 | tf_op jit(solution)/shard_map/ppermute | solution.py:48
  337.5 22.1 %collective-permute-start.27 = (f32[1024,128]{1,0:T(8,128)S(1)}, f32[1024,128]{1,0:T(8,128)S(1)}, u32[]{:S(2)}, u32[]{:S(2)}) collective-permute-start(f32[1024,128]{1,0:T(8,128)S(1)} %add.276), channel_id=1, source_target_pairs={{0,64},{32,96},{64,0},{96,32},{128,192},{160,224},{192,128},{224,1... | collective-permute-start | bytes 1572872 | tf_op jit(solution)/shard_map/ppermute | solution.py:48
  348.7 22.1 %collective-permute-start.30 = (f32[128,1024]{1,0:T(8,128)S(1)}, f32[128,1024]{1,0:T(8,128)S(1)}, u32[]{:S(2)}, u32[]{:S(2)}) collective-permute-start(f32[128,1024]{1,0:T(8,128)S(1)} %add.280), channel_id=1, source_target_pairs={{0,64},{32,96},{64,0},{96,32},{128,192},{160,224},{192,128},{224,1... | collective-permute-start | bytes 1572872 | tf_op jit(solution)/shard_map/ppermute | solution.py:48
  359.6 11.6 %collective-permute-start.28 = (f32[1024,128]{1,0:T(8,128)S(1)}, f32[1024,128]{1,0:T(8,128)S(1)}, u32[]{:S(2)}, u32[]{:S(2)}) collective-permute-start(f32[1024,128]{1,0:T(8,128)S(1)} %add.277), channel_id=1, source_target_pairs={{0,128},{32,160},{64,192},{96,224},{128,0},{160,32},{192,64},{224,... | collective-permute-start | bytes 1572872 | tf_op jit(solution)/shard_map/ppermute | solution.py:48
  370.9 12.3 %collective-permute-start.31 = (f32[128,1024]{1,0:T(8,128)S(1)}, f32[128,1024]{1,0:T(8,128)S(1)}, u32[]{:S(2)}, u32[]{:S(2)}) collective-permute-start(f32[128,1024]{1,0:T(8,128)S(1)} %add.281), channel_id=1, source_target_pairs={{0,128},{32,160},{64,192},{96,224},{128,0},{160,32},{192,64},{224,... | collective-permute-start | bytes 1572872 | tf_op jit(solution)/shard_map/ppermute | solution.py:48
  433.8 11.9 %collective-permute-start.33 = (bf16[192,1024]{1,0:T(8,128)(2,1)S(1)}, bf16[192,1024]{1,0:T(8,128)(2,1)S(1)}, u32[]{:S(2)}, u32[]{:S(2)}) collective-permute-start(bf16[192,1024]{1,0:T(8,128)(2,1)S(1)} %dynamic-slice_convert_fusion.3), channel_id=1, source_target_pairs={{0,2},{1,3},{2,0},{3,1},{4,6},{5,7},{6,4},{7,5},{8,10},{9,11},{10,... | collective-permute-start | bytes 1179656 | tf_op jit(solution)/shard_map/ppermute | solution.py:61
  501.9 13.4 %collective-permute-start.45 = (f32[128,1024]{1,0:T(8,128)}, f32[128,1024]{1,0:T(8,128)}, u32[]{:S(2)}, u32[]{:S(2)}) collective-permute-start(f32[128,1024]{1,0:T(8,128)} %fusion.17), channel_id=1, source_target_pairs={{0,32},{32,0},{64,96},{96,64},{128,160},{160,128},{192,224},{224,1... | collective-permute-start | bytes 1572872 | tf_op jit(solution)/shard_map/ppermute | solution.py:48
  506.5 20.0 %collective-permute-start.42 = (f32[1024,128]{1,0:T(8,128)}, f32[1024,128]{1,0:T(8,128)S(1)}, u32[]{:S(2)}, u32[]{:S(2)}) collective-permute-start(f32[1024,128]{1,0:T(8,128)} %fusion.14), channel_id=1, source_target_pairs={{0,32},{32,0},{64,96},{96,64},{128,160},{160,128},{192,224},{224,1... | collective-permute-start | bytes 1572872 | tf_op jit(solution)/shard_map/ppermute | solution.py:48
  516.6 23.5 %collective-permute-start.46 = (f32[128,1024]{1,0:T(8,128)S(1)}, f32[128,1024]{1,0:T(8,128)S(1)}, u32[]{:S(2)}, u32[]{:S(2)}) collective-permute-start(f32[128,1024]{1,0:T(8,128)S(1)} %add.299), channel_id=1, source_target_pairs={{0,64},{32,96},{64,0},{96,32},{128,192},{160,224},{192,128},{224,1... | collective-permute-start | bytes 1572872 | tf_op jit(solution)/shard_map/ppermute | solution.py:48
  526.6 24.8 %collective-permute-start.43 = (f32[1024,128]{1,0:T(8,128)S(1)}, f32[1024,128]{1,0:T(8,128)S(1)}, u32[]{:S(2)}, u32[]{:S(2)}) collective-permute-start(f32[1024,128]{1,0:T(8,128)S(1)} %add.295), channel_id=1, source_target_pairs={{0,64},{32,96},{64,0},{96,32},{128,192},{160,224},{192,128},{224,1... | collective-permute-start | bytes 1572872 | tf_op jit(solution)/shard_map/ppermute | solution.py:48
  540.3 11.6 %collective-permute-start.47 = (f32[128,1024]{1,0:T(8,128)S(1)}, f32[128,1024]{1,0:T(8,128)S(1)}, u32[]{:S(2)}, u32[]{:S(2)}) collective-permute-start(f32[128,1024]{1,0:T(8,128)S(1)} %add.300), channel_id=1, source_target_pairs={{0,128},{32,160},{64,192},{96,224},{128,0},{160,32},{192,64},{224,... | collective-permute-start | bytes 1572872 | tf_op jit(solution)/shard_map/ppermute | solution.py:48
  551.5 12.4 %collective-permute-start.44 = (f32[1024,128]{1,0:T(8,128)S(1)}, f32[1024,128]{1,0:T(8,128)S(1)}, u32[]{:S(2)}, u32[]{:S(2)}) collective-permute-start(f32[1024,128]{1,0:T(8,128)S(1)} %add.296), channel_id=1, source_target_pairs={{0,128},{32,160},{64,192},{96,224},{128,0},{160,32},{192,64},{224,... | collective-permute-start | bytes 1572872 | tf_op jit(solution)/shard_map/ppermute | solution.py:48
  (67 other events, 694.0 us)

commit v2 on v1

--- a/solution.py
+++ b/solution.py
@@ -19,10 +19,6 @@
     return lax.dot_general(
         left_side, right_side, (((0,), (0,)), ((), ())), preferred_element_type=jnp.float32
     )
-
-
-def local_dot(first_in, first_out, second_in, second_out):
-    return jnp.sum(first_in * second_in) + jnp.sum(first_out * second_out)
 
 
 def xor_pairs(size, bit):
@@ -75,34 +71,31 @@
     return chunk
 
 
-def fisher_product(direction_in, direction_out, normed, hidden_act, slope_act, w_out, metric):
-    tangent_in = direction_in.astype(jnp.bfloat16)
-    tangent_out = direction_out.astype(jnp.bfloat16)
+def fisher_product(direction, normed, hidden_act, slope_act, w_out, metric, width):
+    tangent = direction.astype(jnp.bfloat16)
+    tangent_in = tangent[:, :width]
+    tangent_out_t = tangent[:, width:]
     pre_tangent = jnp.dot(normed, tangent_in, preferred_element_type=jnp.float32)
     inner_tangent = (slope_act * pre_tangent).astype(jnp.bfloat16)
     partial_out = jnp.dot(inner_tangent, w_out, preferred_element_type=jnp.float32)
-    partial_out = partial_out + jnp.dot(hidden_act, tangent_out, preferred_element_type=jnp.float32)
+    partial_out = partial_out + lax.dot_general(
+        hidden_act, tangent_out_t, (((1,), (1,)), ((), ())), preferred_element_type=jnp.float32
+    )
     out_chunk = halving_reduce(partial_out.astype(jnp.bfloat16), "fsdp")
     cotangent = doubling_gather((out_chunk * metric).astype(jnp.bfloat16), "fsdp")
     back_act = lax.dot_general(
         cotangent, w_out, (((1,), (1,)), ((), ())), preferred_element_type=jnp.float32
     )
     grad_pre = (slope_act * back_act).astype(jnp.bfloat16)
-    part_out = contract_rows(hidden_act, cotangent)
+    part_out_t = contract_rows(cotangent, hidden_act)
     part_in = contract_rows(normed, grad_pre)
-    fisher_in, fisher_out = doubling_sum((part_in, part_out), "dp")
-    fisher_in = fisher_in + damping * direction_in
-    fisher_out = fisher_out + damping * direction_out
-    quadratic = scalar_sum(local_dot(direction_in, direction_out, fisher_in, fisher_out)[None], "fsdp")[0]
-    return (fisher_in, fisher_out, quadratic)
-
-
-def global_norm(vector_in, vector_out):
-    return scalar_sum(local_dot(vector_in, vector_out, vector_in, vector_out)[None], "fsdp")[0]
+    (fisher,) = doubling_sum((jnp.concatenate([part_in, part_out_t], axis=1),), "dp")
+    return fisher + damping * direction
 
 
 def on_device(states, w_in, w_out, precision, grad_in, grad_out):
     row_count = states.shape[0]
+    width = w_in.shape[1]
     metric = precision / (row_count * lax.axis_size("dp"))
     wide_states = states.astype(jnp.float32)
     mean_square = jnp.mean(wide_states * wide_states, axis=1, keepdims=True)
@@ -110,26 +103,29 @@
     preact = jnp.dot(normed, w_in, preferred_element_type=jnp.float32)
     hidden_act = jax.nn.silu(preact).astype(jnp.bfloat16)
     slope_act = silu_slope(preact)
-    solution_in = jnp.zeros_like(grad_in)
-    solution_out = jnp.zeros_like(grad_out)
-    residual_in, residual_out = (grad_in, grad_out)
-    direction_in, direction_out = (grad_in, grad_out)
-    norm_now = global_norm(residual_in, residual_out)
+    residual = jnp.concatenate([grad_in, grad_out.T], axis=1)
+    solution_now = jnp.zeros_like(residual)
+    direction = residual
+    norm_now = scalar_sum(jnp.sum(residual * residual)[None], "fsdp")[0]
     for iteration in range(ITERS):
-        fisher_in, fisher_out, quadratic = fisher_product(
-            direction_in, direction_out, normed, hidden_act, slope_act, w_out, metric
+        fisher = fisher_product(direction, normed, hidden_act, slope_act, w_out, metric, width)
+        sums = jnp.stack(
+            [jnp.sum(direction * fisher), jnp.sum(residual * fisher), jnp.sum(fisher * fisher)]
         )
+        quadratic, cross, fisher_square = scalar_sum(sums, "fsdp")
         step_size = norm_now / quadratic
-        solution_in = solution_in + step_size * direction_in
-        solution_out = solution_out + step_size * direction_out
-        residual_in = residual_in - step_size * fisher_in
-        residual_out = residual_out - step_size * fisher_out
+        solution_now = solution_now + step_size * direction
+        residual = residual - step_size * fisher
         if iteration + 1 < ITERS:
-            norm_next = global_norm(residual_in, residual_out)
-            direction_in = residual_in + norm_next / norm_now * direction_in
-            direction_out = residual_out + norm_next / norm_now * direction_out
+            norm_next = norm_now - 2.0 * step_size * cross + step_size * step_size * fisher_square
+            direction = residual + norm_next / norm_now * direction
             norm_now = norm_next
-    return (solution_in, solution_out, residual_in, residual_out)
+    return (
+        solution_now[:, :width],
+        solution_now[:, width:].T,
+        residual[:, :width],
+        residual[:, width:].T,
+    )
 
 
 def solution(mesh):

time: 596 us -> 616 us (1.034)
  waiting for transfers between devices: 321 us -> 377 us
  blocking collectives: 53.9 us -> 30.1 us
  between operations: 16.3 us -> 7.56 us
  starting transfers between devices: 98.5 us -> 91.8 us
    ppermute x18 -> x9, waiting for transfers between devices: 147 us -> 201 us  [doubling_sum(): parts = tuple((part + lax.ppermute(part, axis, pairs) for part in parts))]
    all_to_all x4 -> x2, blocking collectives: 53.9 us -> 30.1 us  [scalar_sum(): lax.all_to_all(jnp.broadcast_to(values[None], (size,) + values.shape), ax...]
    convert_element_type x0 -> x3, other arithmetic: none -> 7.62 us  [fisher_product(): tangent = direction.astype(jnp.bfloat16)]
    reduce_sum x10 -> x3, other arithmetic: 13.6 us -> 6.17 us  [on_device(): jnp.sum(direction * fisher)]
    ppermute x18 -> x9, starting transfers between devices: 21.5 us -> 15.6 us  [doubling_sum(): parts = tuple((part + lax.ppermute(part, axis, pairs) for part in parts))]
  transfers between devices with their start and end apart: 50 -> 41, of which waited for: 47 -> 41; matrix products, arithmetic and copies ran while one was open for 2% -> 0% of each run, Pallas kernels for 0% -> 0%
where the time goes in v2:
time: 616 us; the launch traced here: 610 us
  waiting for transfers between devices  377 us (61%)
  starting transfers between devices  91.8 us (15%)
  other arithmetic  45.4 us (7%)
  matrix products  40 us (6%)
  blocking collectives  30.1 us (5%)
  local copies, waits for them, and re-layouts  18.2 us (3%)
  between operations  7.56 us (1%)
    ppermute x9, waiting for transfers between devices, doubling_sum(): parts = tuple((part + lax.ppermute(part, axis, pairs) for part in parts))  201 us
    ppermute x15, waiting for transfers between devices, halving_reduce(): lax.ppermute(send.astype(jnp.bfloat16), axis, xor_pairs(size, 1 << stage))  83.9 us
    ppermute x15, waiting for transfers between devices, doubling_gather(): other = lax.ppermute(chunk, axis, xor_pairs(size, 1 << stage))  75.4 us
    ppermute x15, starting transfers between devices, doubling_gather(): other = lax.ppermute(chunk, axis, xor_pairs(size, 1 << stage))  43.3 us
    all_to_all x2, blocking collectives, scalar_sum(): lax.all_to_all(jnp.broadcast_to(values[None], (size,) + values.shape), ax...  30.1 us
    dot_general x6, matrix products, contract_rows(): lax.dot_general(left_side, right_side, (((0,), (0,)), ((), ())), preferre...  18.7 us
    all_to_all x2, waiting for transfers between devices, scalar_sum(): lax.all_to_all(jnp.broadcast_to(values[None], (size,) + values.shape), ax...  16.8 us
    all_to_all x2, starting transfers between devices, scalar_sum(): lax.all_to_all(jnp.broadcast_to(values[None], (size,) + values.shape), ax...  16.4 us
  transfers between devices with their start and end apart: 41, of which 41 were waited for; matrix products, arithmetic and copies ran while one was open for 0% of the time, Pallas kernels for 0%

profile of v2, /device:TPU:1, one launch (start us, length us, event | category | flops | bytes accessed | tf_op | source)
XLA Modules:
  0.0 610.3 jit_solution(13240441840598590136)
XLA Ops:
  24.7 11.1 %collective-permute-done.1 = bf16[192,1024]{1,0:T(8,128)(2,1)} collective-permute-done((bf16[192,1024]{1,0:T(8,128)(2,1)}, bf16[192,1024]{1,0:T(8,128)(2,1)}, u32[]{:S(2)}, u32[]{:S(2)}) %collective-permute-start.1) | collective-permute-done | bytes 393248 | tf_op jit(solution)/shard_map/ppermute | solution.py:57
  97.5 7.6 %collective-permute-start.9 = (bf16[384,1024]{1,0:T(8,128)(2,1)}, bf16[384,1024]{1,0:T(8,128)(2,1)}, u32[]{:S(2)}, u32[]{:S(2)}) collective-permute-start(bf16[384,1024]{1,0:T(8,128)(2,1)} %maximum_select_fusion.3), channel_id=1, source_target_pairs={{0,1},{1,0},{2,3},{3,2},{4,5},{5,4},{6,7},{7,6},{8,9},{9,8},{10,11... | collective-permute-start | bytes 2359304 | tf_op jit(solution)/shard_map/ppermute | solution.py:67
  117.4 23.0 %collective-permute-done.10 = f32[1024,256]{0,1:T(8,128)S(1)} collective-permute-done((f32[1024,256]{0,1:T(8,128)S(1)}, f32[1024,256]{0,1:T(8,128)S(1)}, u32[]{:S(2)}, u32[]{:S(2)}) %collective-permute-start.10) | collective-permute-done | bytes 1048608 | tf_op jit(solution)/shard_map/ppermute | solution.py:44
  143.6 22.0 %collective-permute-done.11 = f32[1024,256]{0,1:T(8,128)S(1)} collective-permute-done((f32[1024,256]{0,1:T(8,128)S(1)}, f32[1024,256]{0,1:T(8,128)S(1)}, u32[]{:S(2)}, u32[]{:S(2)}) %collective-permute-start.11) | collective-permute-done | bytes 1048608 | tf_op jit(solution)/shard_map/ppermute | solution.py:44
  167.2 21.4 %collective-permute-done.12 = f32[1024,256]{0,1:T(8,128)S(1)} collective-permute-done((f32[1024,256]{0,1:T(8,128)S(1)}, f32[1024,256]{0,1:T(8,128)S(1)}, u32[]{:S(2)}, u32[]{:S(2)}) %collective-permute-start.12) | collective-permute-done | bytes 1048608 | tf_op jit(solution)/shard_map/ppermute | solution.py:44
  191.7 12.3 %all-to-all-start = ((f32[32,1,1]{2,1,0:T(1,128)}), f32[32,1,1]{2,1,0:T(1,128)S(1)}, u32[]{:S(2)}, u32[]{:S(2)}) async-start(f32[32,1,1]{2,1,0:T(1,128)} %broadcast_in_dim.8), calls=%async_computation | async-start | bytes 32768 | tf_op jit(solution)/shard_map/all_to_all | solution.py:36
  205.5 7.9 %all-to-all-done = f32[32,1,1]{2,1,0:T(1,128)S(1)} async-done(((f32[32,1,1]{2,1,0:T(1,128)}), f32[32,1,1]{2,1,0:T(1,128)S(1)}, u32[]{:S(2)}, u32[]{:S(2)}) %all-to-all-start) | async-done | bytes 160 | tf_op jit(solution)/shard_map/all_to_all | solution.py:36
  218.8 8.8 %all-to-all-done.1 = f32[32,1,3]{2,1,0:T(1,128)S(1)} async-done(((f32[32,1,3]{2,1,0:T(1,128)}), f32[32,1,3]{2,1,0:T(1,128)S(1)}, u32[]{:S(2)}, u32[]{:S(2)}) %all-to-all-start.1) | async-done | bytes 416 | tf_op jit(solution)/shard_map/all_to_all | solution.py:36
  245.3 11.4 %collective-permute-done.14 = bf16[192,1024]{1,0:T(8,128)(2,1)S(1)} collective-permute-done((bf16[192,1024]{1,0:T(8,128)(2,1)S(1)}, bf16[192,1024]{1,0:T(8,128)(2,1)S(1)}, u32[]{:S(2)}, u32[]{:S(2)}) %collective-permute-start.14) | collective-permute-done | bytes 393248 | tf_op jit(solution)/shard_map/ppermute | solution.py:57
  292.9 8.1 %collective-permute-done.21 = bf16[192,1024]{1,0:T(8,128)(2,1)S(1)} collective-permute-done((bf16[192,1024]{1,0:T(8,128)(2,1)S(1)}, bf16[192,1024]{1,0:T(8,128)(2,1)S(1)}, u32[]{:S(2)}, u32[]{:S(2)}) %collective-permute-start.21) | collective-permute-done | bytes 393248 | tf_op jit(solution)/shard_map/ppermute | solution.py:67
  301.3 17.2 %collective-permute-start.22 = (bf16[384,1024]{1,0:T(8,128)(2,1)S(1)}, bf16[384,1024]{1,0:T(8,128)(2,1)S(1)}, u32[]{:S(2)}, u32[]{:S(2)}) collective-permute-start(bf16[384,1024]{1,0:T(8,128)(2,1)S(1)} %maximum_select_fusion.4), channel_id=1, source_target_pairs={{0,1},{1,0},{2,3},{3,2},{4,5},{5,4},{6,7},{7,6},{8,9},{9,8},{10,11... | collective-permute-start | bytes 2359304 | tf_op jit(solution)/shard_map/ppermute | solution.py:67
  329.3 23.0 %collective-permute-done.23 = f32[1024,256]{0,1:T(8,128)S(1)} collective-permute-done((f32[1024,256]{0,1:T(8,128)S(1)}, f32[1024,256]{0,1:T(8,128)S(1)}, u32[]{:S(2)}, u32[]{:S(2)}) %collective-permute-start.23) | collective-permute-done | bytes 1048608 | tf_op jit(solution)/shard_map/ppermute | solution.py:44
  355.6 22.1 %collective-permute-done.24 = f32[1024,256]{0,1:T(8,128)S(1)} collective-permute-done((f32[1024,256]{0,1:T(8,128)S(1)}, f32[1024,256]{0,1:T(8,128)S(1)}, u32[]{:S(2)}, u32[]{:S(2)}) %collective-permute-start.24) | collective-permute-done | bytes 1048608 | tf_op jit(solution)/shard_map/ppermute | solution.py:44
  378.2 22.3 %collective-permute-done.25 = f32[1024,256]{0,1:T(8,128)S(1)} collective-permute-done((f32[1024,256]{0,1:T(8,128)S(1)}, f32[1024,256]{0,1:T(8,128)S(1)}, u32[]{:S(2)}, u32[]{:S(2)}) %collective-permute-start.25) | collective-permute-done | bytes 1048608 | tf_op jit(solution)/shard_map/ppermute | solution.py:44
  404.8 15.1 %all_to_all.24 = f32[32,1,3]{2,1,0:T(1,128)S(1)} all-to-all(f32[32,1,3]{2,1,0:T(1,128)S(1)} %broadcast_in_dim.10), channel_id=1, replica_groups=mesh['dp'=8,'fsdp'=32] {'fsdp'}, dimensions={0} | all-to-all | bytes 768 | tf_op jit(solution)/shard_map/all_to_all | solution.py:36
  437.1 11.4 %collective-permute-done.27 = bf16[192,1024]{1,0:T(8,128)(2,1)S(1)} collective-permute-done((bf16[192,1024]{1,0:T(8,128)(2,1)S(1)}, bf16[192,1024]{1,0:T(8,128)(2,1)S(1)}, u32[]{:S(2)}, u32[]{:S(2)}) %collective-permute-start.27) | collective-permute-done | bytes 393248 | tf_op jit(solution)/shard_map/ppermute | solution.py:57
  460.1 6.4 %collective-permute-done.30 = bf16[24,1024]{1,0:T(8,128)(2,1)S(1)} collective-permute-done((bf16[24,1024]{1,0:T(8,128)(2,1)S(1)}, bf16[24,1024]{1,0:T(8,128)(2,1)S(1)}, u32[]{:S(2)}, u32[]{:S(2)}) %collective-permute-start.30) | collective-permute-done | bytes 49184 | tf_op jit(solution)/shard_map/ppermute | solution.py:57
  467.1 6.4 %collective-permute-done.31 = bf16[24,1024]{1,0:T(8,128)(2,1)S(1)} collective-permute-done((bf16[24,1024]{1,0:T(8,128)(2,1)S(1)}, bf16[24,1024]{1,0:T(8,128)(2,1)S(1)}, u32[]{:S(2)}, u32[]{:S(2)}) %collective-permute-start.31) | collective-permute-done | bytes 49184 | tf_op jit(solution)/shard_map/ppermute | solution.py:67
  485.0 8.1 %collective-permute-done.34 = bf16[192,1024]{1,0:T(8,128)(2,1)S(1)} collective-permute-done((bf16[192,1024]{1,0:T(8,128)(2,1)S(1)}, bf16[192,1024]{1,0:T(8,128)(2,1)S(1)}, u32[]{:S(2)}, u32[]{:S(2)}) %collective-permute-start.34) | collective-permute-done | bytes 393248 | tf_op jit(solution)/shard_map/ppermute | solution.py:67
  494.4 8.1 %collective-permute-start.35 = (bf16[384,1024]{1,0:T(8,128)(2,1)S(1)}, bf16[384,1024]{1,0:T(8,128)(2,1)}, u32[]{:S(2)}, u32[]{:S(2)}) collective-permute-start(bf16[384,1024]{1,0:T(8,128)(2,1)S(1)} %maximum_select_fusion.5), channel_id=1, source_target_pairs={{0,1},{1,0},{2,3},{3,2},{4,5},{5,4},{6,7},{7,6},{8,9},{9,8},{10,11... | collective-permute-start | bytes 2359304 | tf_op jit(solution)/shard_map/ppermute | solution.py:67
  512.3 23.0 %collective-permute-done.36 = f32[1024,256]{0,1:T(8,128)S(1)} collective-permute-done((f32[1024,256]{0,1:T(8,128)S(1)}, f32[1024,256]{0,1:T(8,128)S(1)}, u32[]{:S(2)}, u32[]{:S(2)}) %collective-permute-start.36) | collective-permute-done | bytes 1048608 | tf_op jit(solution)/shard_map/ppermute | solution.py:44
  538.6 22.1 %collective-permute-done.37 = f32[1024,256]{0,1:T(8,128)S(1)} collective-permute-done((f32[1024,256]{0,1:T(8,128)S(1)}, f32[1024,256]{0,1:T(8,128)S(1)}, u32[]{:S(2)}, u32[]{:S(2)}) %collective-permute-start.37) | collective-permute-done | bytes 1048608 | tf_op jit(solution)/shard_map/ppermute | solution.py:44
  561.2 22.3 %collective-permute-done.38 = f32[1024,256]{0,1:T(8,128)S(1)} collective-permute-done((f32[1024,256]{0,1:T(8,128)S(1)}, f32[1024,256]{0,1:T(8,128)S(1)}, u32[]{:S(2)}, u32[]{:S(2)}) %collective-permute-start.38) | collective-permute-done | bytes 1048608 | tf_op jit(solution)/shard_map/ppermute | solution.py:44
  587.6 15.1 %all_to_all.25 = f32[32,1,3]{2,1,0:T(1,128)S(1)} all-to-all(f32[32,1,3]{2,1,0:T(1,128)S(1)} %broadcast_in_dim.11), channel_id=1, replica_groups=mesh['dp'=8,'fsdp'=32] {'fsdp'}, dimensions={0} | all-to-all | bytes 768 | tf_op jit(solution)/shard_map/all_to_all | solution.py:36
  (202 shorter events, 246.6 us)
Async XLA Ops:
  23.7 12.1 %collective-permute-start.1 = (bf16[192,1024]{1,0:T(8,128)(2,1)}, bf16[192,1024]{1,0:T(8,128)(2,1)}, u32[]{:S(2)}, u32[]{:S(2)}) collective-permute-start(bf16[192,1024]{1,0:T(8,128)(2,1)} %dynamic-slice_convert_fusion.5), channel_id=1, source_target_pairs={{0,2},{1,3},{2,0},{3,1},{4,6},{5,7},{6,4},{7,5},{8,10},{9,11},{10,... | collective-permute-start | bytes 1179656 | tf_op jit(solution)/shard_map/ppermute | solution.py:57
  54.3 7.0 %collective-permute-start.4 = (bf16[24,1024]{1,0:T(8,128)(2,1)S(1)}, bf16[24,1024]{1,0:T(8,128)(2,1)}, u32[]{:S(2)}, u32[]{:S(2)}) collective-permute-start(bf16[24,1024]{1,0:T(8,128)(2,1)S(1)} %dynamic-slice_convert_fusion.14), channel_id=1, source_target_pairs={{0,16},{1,17},{2,18},{3,19},{4,20},{5,21},{6,22},{7,23},{8,24},{9,... | collective-permute-start | bytes 147464 | tf_op jit(solution)/shard_map/ppermute | solution.py:57
  62.2 7.0 %collective-permute-start.5 = (bf16[24,1024]{1,0:T(8,128)(2,1)S(1)}, bf16[24,1024]{1,0:T(8,128)(2,1)}, u32[]{:S(2)}, u32[]{:S(2)}) collective-permute-start(bf16[24,1024]{1,0:T(8,128)(2,1)S(1)} %multiply_convert_fusion.3), channel_id=1, source_target_pairs={{0,16},{1,17},{2,18},{3,19},{4,20},{5,21},{6,22},{7,23},{8,24},{9,... | collective-permute-start | bytes 147464 | tf_op jit(solution)/shard_map/ppermute | solution.py:67
  86.4 8.4 %collective-permute-start.8 = (bf16[192,1024]{1,0:T(8,128)(2,1)}, bf16[192,1024]{1,0:T(8,128)(2,1)}, u32[]{:S(2)}, u32[]{:S(2)}) collective-permute-start(bf16[192,1024]{1,0:T(8,128)(2,1)} %maximum_select_fusion.6), channel_id=1, source_target_pairs={{0,2},{1,3},{2,0},{3,1},{4,6},{5,7},{6,4},{7,5},{8,10},{9,11},{10,... | collective-permute-start | bytes 1179656 | tf_op jit(solution)/shard_map/ppermute | solution.py:67
  97.5 9.8 %collective-permute-start.9 = (bf16[384,1024]{1,0:T(8,128)(2,1)}, bf16[384,1024]{1,0:T(8,128)(2,1)}, u32[]{:S(2)}, u32[]{:S(2)}) collective-permute-start(bf16[384,1024]{1,0:T(8,128)(2,1)} %maximum_select_fusion.3), channel_id=1, source_target_pairs={{0,1},{1,0},{2,3},{3,2},{4,5},{5,4},{6,7},{7,6},{8,9},{9,8},{10,11... | collective-permute-start | bytes 2359304 | tf_op jit(solution)/shard_map/ppermute | solution.py:67
  115.7 24.7 %collective-permute-start.10 = (f32[1024,256]{0,1:T(8,128)S(1)}, f32[1024,256]{0,1:T(8,128)S(1)}, u32[]{:S(2)}, u32[]{:S(2)}) collective-permute-start(f32[1024,256]{0,1:T(8,128)S(1)} %pad_maximum_fusion.1), channel_id=1, source_target_pairs={{0,32},{32,0},{64,96},{96,64},{128,160},{160,128},{192,224},{224,1... | collective-permute-start | bytes 3145736 | tf_op jit(solution)/shard_map/ppermute | solution.py:44
  140.6 25.1 %collective-permute-start.11 = (f32[1024,256]{0,1:T(8,128)S(1)}, f32[1024,256]{0,1:T(8,128)S(1)}, u32[]{:S(2)}, u32[]{:S(2)}) collective-permute-start(f32[1024,256]{0,1:T(8,128)S(1)} %fusion.40), channel_id=1, source_target_pairs={{0,64},{32,96},{64,0},{96,32},{128,192},{160,224},{192,128},{224,1... | collective-permute-start | bytes 3145736 | tf_op jit(solution)/shard_map/ppermute | solution.py:44
  165.8 22.7 %collective-permute-start.12 = (f32[1024,256]{0,1:T(8,128)S(1)}, f32[1024,256]{0,1:T(8,128)S(1)}, u32[]{:S(2)}, u32[]{:S(2)}) collective-permute-start(f32[1024,256]{0,1:T(8,128)S(1)} %add.198), channel_id=1, source_target_pairs={{0,128},{32,160},{64,192},{96,224},{128,0},{160,32},{192,64},{224,... | collective-permute-start | bytes 3145736 | tf_op jit(solution)/shard_map/ppermute | solution.py:44
  191.7 21.7 %all-to-all-start = ((f32[32,1,1]{2,1,0:T(1,128)}), f32[32,1,1]{2,1,0:T(1,128)S(1)}, u32[]{:S(2)}, u32[]{:S(2)}) async-start(f32[32,1,1]{2,1,0:T(1,128)} %broadcast_in_dim.8), calls=%async_computation | async-start | bytes 32768 | tf_op jit(solution)/shard_map/all_to_all | solution.py:36
  214.0 13.6 %all-to-all-start.1 = ((f32[32,1,3]{2,1,0:T(1,128)}), f32[32,1,3]{2,1,0:T(1,128)S(1)}, u32[]{:S(2)}, u32[]{:S(2)}) async-start(f32[32,1,3]{2,1,0:T(1,128)} %broadcast_in_dim.9), calls=%async_computation.1 | async-start | bytes 32768 | tf_op jit(solution)/shard_map/all_to_all | solution.py:36
  244.8 11.9 %collective-permute-start.14 = (bf16[192,1024]{1,0:T(8,128)(2,1)S(1)}, bf16[192,1024]{1,0:T(8,128)(2,1)S(1)}, u32[]{:S(2)}, u32[]{:S(2)}) collective-permute-start(bf16[192,1024]{1,0:T(8,128)(2,1)S(1)} %dynamic-slice_convert_fusion.4), channel_id=1, source_target_pairs={{0,2},{1,3},{2,0},{3,1},{4,6},{5,7},{6,4},{7,5},{8,10},{9,11},{10,... | collective-permute-start | bytes 1179656 | tf_op jit(solution)/shard_map/ppermute | solution.py:57
  267.8 6.9 %collective-permute-start.17 = (bf16[24,1024]{1,0:T(8,128)(2,1)S(1)}, bf16[24,1024]{1,0:T(8,128)(2,1)S(1)}, u32[]{:S(2)}, u32[]{:S(2)}) collective-permute-start(bf16[24,1024]{1,0:T(8,128)(2,1)S(1)} %dynamic-slice_convert_fusion.13), channel_id=1, source_target_pairs={{0,16},{1,17},{2,18},{3,19},{4,20},{5,21},{6,22},{7,23},{8,24},{9,... | collective-permute-start | bytes 147464 | tf_op jit(solution)/shard_map/ppermute | solution.py:57
  274.8 6.9 %collective-permute-start.18 = (bf16[24,1024]{1,0:T(8,128)(2,1)S(1)}, bf16[24,1024]{1,0:T(8,128)(2,1)S(1)}, u32[]{:S(2)}, u32[]{:S(2)}) collective-permute-start(bf16[24,1024]{1,0:T(8,128)(2,1)S(1)} %multiply_convert_fusion.2), channel_id=1, source_target_pairs={{0,16},{1,17},{2,18},{3,19},{4,20},{5,21},{6,22},{7,23},{8,24},{9,... | collective-permute-start | bytes 147464 | tf_op jit(solution)/shard_map/ppermute | solution.py:67
  292.8 8.2 %collective-permute-start.21 = (bf16[192,1024]{1,0:T(8,128)(2,1)S(1)}, bf16[192,1024]{1,0:T(8,128)(2,1)S(1)}, u32[]{:S(2)}, u32[]{:S(2)}) collective-permute-start(bf16[192,1024]{1,0:T(8,128)(2,1)S(1)} %maximum_select_fusion.7), channel_id=1, source_target_pairs={{0,2},{1,3},{2,0},{3,1},{4,6},{5,7},{6,4},{7,5},{8,10},{9,11},{10,... | collective-permute-start | bytes 1179656 | tf_op jit(solution)/shard_map/ppermute | solution.py:67
  301.3 19.1 %collective-permute-start.22 = (bf16[384,1024]{1,0:T(8,128)(2,1)S(1)}, bf16[384,1024]{1,0:T(8,128)(2,1)S(1)}, u32[]{:S(2)}, u32[]{:S(2)}) collective-permute-start(bf16[384,1024]{1,0:T(8,128)(2,1)S(1)} %maximum_select_fusion.4), channel_id=1, source_target_pairs={{0,1},{1,0},{2,3},{3,2},{4,5},{5,4},{6,7},{7,6},{8,9},{9,8},{10,11... | collective-permute-start | bytes 2359304 | tf_op jit(solution)/shard_map/ppermute | solution.py:67
  327.9 24.4 %collective-permute-start.23 = (f32[1024,256]{0,1:T(8,128)S(1)}, f32[1024,256]{0,1:T(8,128)S(1)}, u32[]{:S(2)}, u32[]{:S(2)}) collective-permute-start(f32[1024,256]{0,1:T(8,128)S(1)} %pad_maximum_fusion.2), channel_id=1, source_target_pairs={{0,32},{32,0},{64,96},{96,64},{128,160},{160,128},{192,224},{224,1... | collective-permute-start | bytes 3145736 | tf_op jit(solution)/shard_map/ppermute | solution.py:44
  352.6 25.1 %collective-permute-start.24 = (f32[1024,256]{0,1:T(8,128)S(1)}, f32[1024,256]{0,1:T(8,128)S(1)}, u32[]{:S(2)}, u32[]{:S(2)}) collective-permute-start(f32[1024,256]{0,1:T(8,128)S(1)} %fusion.39), channel_id=1, source_target_pairs={{0,64},{32,96},{64,0},{96,32},{128,192},{160,224},{192,128},{224,1... | collective-permute-start | bytes 3145736 | tf_op jit(solution)/shard_map/ppermute | solution.py:44
  377.8 22.7 %collective-permute-start.25 = (f32[1024,256]{0,1:T(8,128)S(1)}, f32[1024,256]{0,1:T(8,128)S(1)}, u32[]{:S(2)}, u32[]{:S(2)}) collective-permute-start(f32[1024,256]{0,1:T(8,128)S(1)} %add.210), channel_id=1, source_target_pairs={{0,128},{32,160},{64,192},{96,224},{128,0},{160,32},{192,64},{224,... | collective-permute-start | bytes 3145736 | tf_op jit(solution)/shard_map/ppermute | solution.py:44
  436.6 11.9 %collective-permute-start.27 = (bf16[192,1024]{1,0:T(8,128)(2,1)S(1)}, bf16[192,1024]{1,0:T(8,128)(2,1)S(1)}, u32[]{:S(2)}, u32[]{:S(2)}) collective-permute-start(bf16[192,1024]{1,0:T(8,128)(2,1)S(1)} %dynamic-slice_convert_fusion.3), channel_id=1, source_target_pairs={{0,2},{1,3},{2,0},{3,1},{4,6},{5,7},{6,4},{7,5},{8,10},{9,11},{10,... | collective-permute-start | bytes 1179656 | tf_op jit(solution)/shard_map/ppermute | solution.py:57
  484.9 8.2 %collective-permute-start.34 = (bf16[192,1024]{1,0:T(8,128)(2,1)S(1)}, bf16[192,1024]{1,0:T(8,128)(2,1)S(1)}, u32[]{:S(2)}, u32[]{:S(2)}) collective-permute-start(bf16[192,1024]{1,0:T(8,128)(2,1)S(1)} %maximum_select_fusion.8), channel_id=1, source_target_pairs={{0,2},{1,3},{2,0},{3,1},{4,6},{5,7},{6,4},{7,5},{8,10},{9,11},{10,... | collective-permute-start | bytes 1179656 | tf_op jit(solution)/shard_map/ppermute | solution.py:67
  494.4 10.1 %collective-permute-start.35 = (bf16[384,1024]{1,0:T(8,128)(2,1)S(1)}, bf16[384,1024]{1,0:T(8,128)(2,1)}, u32[]{:S(2)}, u32[]{:S(2)}) collective-permute-start(bf16[384,1024]{1,0:T(8,128)(2,1)S(1)} %maximum_select_fusion.5), channel_id=1, source_target_pairs={{0,1},{1,0},{2,3},{3,2},{4,5},{5,4},{6,7},{7,6},{8,9},{9,8},{10,11... | collective-permute-start | bytes 2359304 | tf_op jit(solution)/shard_map/ppermute | solution.py:67
  511.0 24.4 %collective-permute-start.36 = (f32[1024,256]{0,1:T(8,128)S(1)}, f32[1024,256]{0,1:T(8,128)S(1)}, u32[]{:S(2)}, u32[]{:S(2)}) collective-permute-start(f32[1024,256]{0,1:T(8,128)S(1)} %pad_maximum_fusion.3), channel_id=1, source_target_pairs={{0,32},{32,0},{64,96},{96,64},{128,160},{160,128},{192,224},{224,1... | collective-permute-start | bytes 3145736 | tf_op jit(solution)/shard_map/ppermute | solution.py:44
  535.6 25.1 %collective-permute-start.37 = (f32[1024,256]{0,1:T(8,128)S(1)}, f32[1024,256]{0,1:T(8,128)S(1)}, u32[]{:S(2)}, u32[]{:S(2)}) collective-permute-start(f32[1024,256]{0,1:T(8,128)S(1)} %fusion.38), channel_id=1, source_target_pairs={{0,64},{32,96},{64,0},{96,32},{128,192},{160,224},{192,128},{224,1... | collective-permute-start | bytes 3145736 | tf_op jit(solution)/shard_map/ppermute | solution.py:44
  560.8 22.7 %collective-permute-start.38 = (f32[1024,256]{0,1:T(8,128)S(1)}, f32[1024,256]{0,1:T(8,128)S(1)}, u32[]{:S(2)}, u32[]{:S(2)}) collective-permute-start(f32[1024,256]{0,1:T(8,128)S(1)} %add.223), channel_id=1, source_target_pairs={{0,128},{32,160},{64,192},{96,224},{128,0},{160,32},{192,64},{224,... | collective-permute-start | bytes 3145736 | tf_op jit(solution)/shard_map/ppermute | solution.py:44
  (42 other events, 469.5 us)

commit v3 on v2

--- a/solution.py
+++ b/solution.py
@@ -37,12 +37,23 @@
     return jnp.sum(gathered, axis=0)
 
 
-def doubling_sum(parts, axis):
+def doubling_sum(whole, axis, pieces=4):
     size = lax.axis_size(axis)
-    for stage in range(stages_of(size)):
-        pairs = xor_pairs(size, 1 << stage)
-        parts = tuple(part + lax.ppermute(part, axis, pairs) for part in parts)
-    return parts
+    count = stages_of(size)
+    parts = jnp.split(whole, pieces, axis=0)
+    for stage in range(count):
+        parts = [
+            part + lax.ppermute(part, axis, xor_pairs(size, 1 << ((stage + number) % count)))
+            for number, part in enumerate(parts)
+        ]
+    return jnp.concatenate(parts, axis=0)
+
+
+def split_permute(value, axis, pairs):
+    if value.shape[0] < 192:
+        return lax.ppermute(value, axis, pairs)
+    upper, lower = jnp.split(value, 2, axis=0)
+    return jnp.concatenate([lax.ppermute(upper, axis, pairs), lax.ppermute(lower, axis, pairs)], 0)
 
 
 def halving_reduce(term, axis):
@@ -54,7 +65,7 @@
         bit = (index >> stage) & 1
         send = lax.dynamic_slice_in_dim(kept, (1 - bit) * half, half, 0)
         keep = lax.dynamic_slice_in_dim(kept, bit * half, half, 0)
-        got = lax.ppermute(send.astype(jnp.bfloat16), axis, xor_pairs(size, 1 << stage))
+        got = split_permute(send.astype(jnp.bfloat16), axis, xor_pairs(size, 1 << stage))
         kept = keep + got.astype(jnp.float32)
     return kept
 
@@ -64,7 +75,7 @@
     index = lax.axis_index(axis)
     for stage in reversed(range(stages_of(size))):
         bit = (index >> stage) & 1
-        other = lax.ppermute(chunk, axis, xor_pairs(size, 1 << stage))
+        other = split_permute(chunk, axis, xor_pairs(size, 1 << stage))
         chunk = jnp.where(
             bit == 0, jnp.concatenate([chunk, other], 0), jnp.concatenate([other, chunk], 0)
         )
@@ -89,7 +100,7 @@
     grad_pre = (slope_act * back_act).astype(jnp.bfloat16)
     part_out_t = contract_rows(cotangent, hidden_act)
     part_in = contract_rows(normed, grad_pre)
-    (fisher,) = doubling_sum((jnp.concatenate([part_in, part_out_t], axis=1),), "dp")
+    fisher = doubling_sum(jnp.concatenate([part_in, part_out_t], axis=1), "dp")
     return fisher + damping * direction
 
 

time: 616 us -> 536 us (0.87)
  waiting for transfers between devices: 377 us -> 270 us
  starting transfers between devices: 91.8 us -> 115 us
    ppermute x39 -> x78, waiting for transfers between devices: 361 us -> 254 us  [the longest x36 109 us: doubling_sum(): lax.ppermute(part, axis, xor_pairs(size, 1 << (stage + number) % count))]
    ppermute x39 -> x78, starting transfers between devices: 75.4 us -> 100 us  [the longest x36 34.6 us: doubling_sum(): lax.ppermute(part, axis, xor_pairs(size, 1 << (stage + number) % count))]
  transfers between devices with their start and end apart: 41 -> 80, of which waited for: 41 -> 67; matrix products, arithmetic and copies ran while one was open for 0% -> 1% of each run, Pallas kernels for 0% -> 0%
where the time goes in v3:
time: 536 us; the launch traced here: 527 us
  waiting for transfers between devices  270 us (50%)
  starting transfers between devices  115 us (21%)
  other arithmetic  42.2 us (8%)
  matrix products  40.6 us (8%)
  blocking collectives  28.5 us (5%)
  local copies, waits for them, and re-layouts  22 us (4%)
  between operations  8.21 us (2%)
    ppermute x36, waiting for transfers between devices, doubling_sum(): lax.ppermute(part, axis, xor_pairs(size, 1 << (stage + number) % count))  109 us
    ppermute x18, waiting for transfers between devices, split_permute(): return lax.ppermute(value, axis, pairs)  90.6 us
    ppermute x36, starting transfers between devices, doubling_sum(): lax.ppermute(part, axis, xor_pairs(size, 1 << (stage + number) % count))  34.6 us
    ppermute x12, starting transfers between devices, split_permute(): lax.ppermute(upper, axis, pairs)  34.3 us
    ppermute x12, waiting for transfers between devices, split_permute(): lax.ppermute(upper, axis, pairs)  31.4 us
    all_to_all x2, blocking collectives, scalar_sum(): lax.all_to_all(jnp.broadcast_to(values[None], (size,) + values.shape), ax...  28.5 us
    ppermute x12, waiting for transfers between devices, split_permute(): lax.ppermute(lower, axis, pairs)  22.4 us
    dot_general x6, matrix products, contract_rows(): lax.dot_general(left_side, right_side, (((0,), (0,)), ((), ())), preferre...  18.8 us
  transfers between devices with their start and end apart: 80, of which 67 were waited for; matrix products, arithmetic and copies ran while one was open for 1% of the time, Pallas kernels for 0%

profile of v3, /device:TPU:1, one launch (start us, length us, event | category | flops | bytes accessed | tf_op | source)
XLA Modules:
  0.0 526.6 jit_solution(7195480955124187644)
XLA Ops:
  38.2 5.5 %collective-permute-done.4 = bf16[96,1024]{1,0:T(8,128)(2,1)} collective-permute-done((bf16[96,1024]{1,0:T(8,128)(2,1)}, bf16[96,1024]{1,0:T(8,128)(2,1)}, u32[]{:S(2)}, u32[]{:S(2)}) %collective-permute-start.4) | collective-permute-done | bytes 196640 | tf_op jit(solution)/shard_map/ppermute | solution.py:54
  70.8 5.6 %collective-permute-done.8 = bf16[48,1024]{1,0:T(8,128)(2,1)} collective-permute-done((bf16[48,1024]{1,0:T(8,128)(2,1)}, bf16[48,1024]{1,0:T(8,128)(2,1)}, u32[]{:S(2)}, u32[]{:S(2)}) %collective-permute-start.8) | collective-permute-done | bytes 98336 | tf_op jit(solution)/shard_map/ppermute | solution.py:54
  78.2 5.5 %collective-permute-done.9 = bf16[96,1024]{1,0:T(8,128)(2,1)} collective-permute-done((bf16[96,1024]{1,0:T(8,128)(2,1)}, bf16[96,1024]{1,0:T(8,128)(2,1)}, u32[]{:S(2)}, u32[]{:S(2)}) %collective-permute-start.9) | collective-permute-done | bytes 196640 | tf_op jit(solution)/shard_map/ppermute | solution.py:54
  99.3 7.9 %collective-permute-start.12 = (bf16[192,1024]{1,0:T(8,128)(2,1)}, bf16[192,1024]{1,0:T(8,128)(2,1)}, u32[]{:S(2)}, u32[]{:S(2)}) collective-permute-start(bf16[192,1024]{1,0:T(8,128)(2,1)} %get-tuple-element.60), channel_id=1, source_target_pairs={{0,1},{1,0},{2,3},{3,2},{4,5},{5,4},{6,7},{7,6},{8,9},{9,8},{10,11... | collective-permute-start | bytes 1179656 | tf_op jit(solution)/shard_map/ppermute | solution.py:56
  159.2 8.0 %collective-permute-done.22 = f32[256,256]{0,1:T(8,128)S(1)} collective-permute-done((f32[256,256]{0,1:T(8,128)S(1)}, f32[256,256]{0,1:T(8,128)S(1)}, u32[]{:S(2)}, u32[]{:S(2)}) %collective-permute-start.22) | collective-permute-done | bytes 262176 | tf_op jit(solution)/shard_map/ppermute | solution.py:46
  169.6 9.7 %all-to-all-start = ((f32[32,1,1]{2,1,0:T(1,128)}), f32[32,1,1]{2,1,0:T(1,128)S(1)}, u32[]{:S(2)}, u32[]{:S(2)}) async-start(f32[32,1,1]{2,1,0:T(1,128)} %broadcast_in_dim.8), calls=%async_computation | async-start | bytes 32768 | tf_op jit(solution)/shard_map/all_to_all | solution.py:36
  180.7 7.9 %all-to-all-done = f32[32,1,1]{2,1,0:T(1,128)S(1)} async-done(((f32[32,1,1]{2,1,0:T(1,128)}), f32[32,1,1]{2,1,0:T(1,128)S(1)}, u32[]{:S(2)}, u32[]{:S(2)}) %all-to-all-start) | async-done | bytes 160 | tf_op jit(solution)/shard_map/all_to_all | solution.py:36
  194.5 8.7 %all-to-all-done.1 = f32[32,1,3]{2,1,0:T(1,128)S(1)} async-done(((f32[32,1,3]{2,1,0:T(1,128)}), f32[32,1,3]{2,1,0:T(1,128)S(1)}, u32[]{:S(2)}, u32[]{:S(2)}) %all-to-all-start.1) | async-done | bytes 416 | tf_op jit(solution)/shard_map/all_to_all | solution.py:36
  244.3 6.3 %collective-permute-done.32 = bf16[24,1024]{1,0:T(8,128)(2,1)S(1)} collective-permute-done((bf16[24,1024]{1,0:T(8,128)(2,1)S(1)}, bf16[24,1024]{1,0:T(8,128)(2,1)S(1)}, u32[]{:S(2)}, u32[]{:S(2)}) %collective-permute-start.32) | collective-permute-done | bytes 49184 | tf_op jit(solution)/shard_map/ppermute | solution.py:54
  251.3 6.3 %collective-permute-done.33 = bf16[24,1024]{1,0:T(8,128)(2,1)S(1)} collective-permute-done((bf16[24,1024]{1,0:T(8,128)(2,1)S(1)}, bf16[24,1024]{1,0:T(8,128)(2,1)S(1)}, u32[]{:S(2)}, u32[]{:S(2)}) %collective-permute-start.33) | collective-permute-done | bytes 49184 | tf_op jit(solution)/shard_map/ppermute | solution.py:54
  257.7 5.3 %collective-permute-done.34 = bf16[48,1024]{1,0:T(8,128)(2,1)S(1)} collective-permute-done((bf16[48,1024]{1,0:T(8,128)(2,1)S(1)}, bf16[48,1024]{1,0:T(8,128)(2,1)S(1)}, u32[]{:S(2)}, u32[]{:S(2)}) %collective-permute-start.34) | collective-permute-done | bytes 98336 | tf_op jit(solution)/shard_map/ppermute | solution.py:54
  263.2 5.3 %collective-permute-done.35 = bf16[96,1024]{1,0:T(8,128)(2,1)S(1)} collective-permute-done((bf16[96,1024]{1,0:T(8,128)(2,1)S(1)}, bf16[96,1024]{1,0:T(8,128)(2,1)S(1)}, u32[]{:S(2)}, u32[]{:S(2)}) %collective-permute-start.35) | collective-permute-done | bytes 196640 | tf_op jit(solution)/shard_map/ppermute | solution.py:54
  277.3 8.3 %collective-permute-start.38 = (bf16[192,1024]{1,0:T(8,128)(2,1)S(1)}, bf16[192,1024]{1,0:T(8,128)(2,1)S(1)}, u32[]{:S(2)}, u32[]{:S(2)}) collective-permute-start(bf16[192,1024]{1,0:T(8,128)(2,1)S(1)} %get-tuple-element.56), channel_id=1, source_target_pairs={{0,1},{1,0},{2,3},{3,2},{4,5},{5,4},{6,7},{7,6},{8,9},{9,8},{10,11... | collective-permute-start | bytes 1179656 | tf_op jit(solution)/shard_map/ppermute | solution.py:56
  297.0 5.7 %collective-permute-done.40 = f32[256,256]{0,1:T(8,128)S(1)} collective-permute-done((f32[256,256]{0,1:T(8,128)S(1)}, f32[256,256]{0,1:T(8,128)S(1)}, u32[]{:S(2)}, u32[]{:S(2)}) %collective-permute-start.40) | collective-permute-done | bytes 262176 | tf_op jit(solution)/shard_map/ppermute | solution.py:46
  308.4 5.5 %collective-permute-done.49 = f32[256,256]{0,1:T(8,128)S(1)} collective-permute-done((f32[256,256]{0,1:T(8,128)S(1)}, f32[256,256]{0,1:T(8,128)S(1)}, u32[]{:S(2)}, u32[]{:S(2)}) %collective-permute-start.49) | collective-permute-done | bytes 262176 | tf_op jit(solution)/shard_map/ppermute | solution.py:46
  325.3 5.5 %collective-permute-done.47 = f32[256,256]{0,1:T(8,128)S(1)} collective-permute-done((f32[256,256]{0,1:T(8,128)S(1)}, f32[256,256]{0,1:T(8,128)S(1)}, u32[]{:S(2)}, u32[]{:S(2)}) %collective-permute-start.47) | collective-permute-done | bytes 262176 | tf_op jit(solution)/shard_map/ppermute | solution.py:46
  345.7 14.4 %all_to_all.24 = f32[32,1,3]{2,1,0:T(1,128)S(1)} all-to-all(f32[32,1,3]{2,1,0:T(1,128)S(1)} %broadcast_in_dim.10), channel_id=1, replica_groups=mesh['dp'=8,'fsdp'=32] {'fsdp'}, dimensions={0} | all-to-all | bytes 768 | tf_op jit(solution)/shard_map/all_to_all | solution.py:36
  400.5 6.3 %collective-permute-done.58 = bf16[24,1024]{1,0:T(8,128)(2,1)S(1)} collective-permute-done((bf16[24,1024]{1,0:T(8,128)(2,1)S(1)}, bf16[24,1024]{1,0:T(8,128)(2,1)S(1)}, u32[]{:S(2)}, u32[]{:S(2)}) %collective-permute-start.58) | collective-permute-done | bytes 49184 | tf_op jit(solution)/shard_map/ppermute | solution.py:54
  407.4 6.3 %collective-permute-done.59 = bf16[24,1024]{1,0:T(8,128)(2,1)S(1)} collective-permute-done((bf16[24,1024]{1,0:T(8,128)(2,1)S(1)}, bf16[24,1024]{1,0:T(8,128)(2,1)S(1)}, u32[]{:S(2)}, u32[]{:S(2)}) %collective-permute-start.59) | collective-permute-done | bytes 49184 | tf_op jit(solution)/shard_map/ppermute | solution.py:54
  413.9 5.3 %collective-permute-done.60 = bf16[48,1024]{1,0:T(8,128)(2,1)S(1)} collective-permute-done((bf16[48,1024]{1,0:T(8,128)(2,1)S(1)}, bf16[48,1024]{1,0:T(8,128)(2,1)S(1)}, u32[]{:S(2)}, u32[]{:S(2)}) %collective-permute-start.60) | collective-permute-done | bytes 98336 | tf_op jit(solution)/shard_map/ppermute | solution.py:54
  419.4 5.4 %collective-permute-done.61 = bf16[96,1024]{1,0:T(8,128)(2,1)S(1)} collective-permute-done((bf16[96,1024]{1,0:T(8,128)(2,1)S(1)}, bf16[96,1024]{1,0:T(8,128)(2,1)S(1)}, u32[]{:S(2)}, u32[]{:S(2)}) %collective-permute-start.61) | collective-permute-done | bytes 196640 | tf_op jit(solution)/shard_map/ppermute | solution.py:54
  434.4 8.3 %collective-permute-start.64 = (bf16[192,1024]{1,0:T(8,128)(2,1)S(1)}, bf16[192,1024]{1,0:T(8,128)(2,1)S(1)}, u32[]{:S(2)}, u32[]{:S(2)}) collective-permute-start(bf16[192,1024]{1,0:T(8,128)(2,1)S(1)} %get-tuple-element.52), channel_id=1, source_target_pairs={{0,1},{1,0},{2,3},{3,2},{4,5},{5,4},{6,7},{7,6},{8,9},{9,8},{10,11... | collective-permute-start | bytes 1179656 | tf_op jit(solution)/shard_map/ppermute | solution.py:56
  492.6 8.0 %collective-permute-done.74 = f32[256,256]{0,1:T(8,128)S(1)} collective-permute-done((f32[256,256]{0,1:T(8,128)S(1)}, f32[256,256]{0,1:T(8,128)S(1)}, u32[]{:S(2)}, u32[]{:S(2)}) %collective-permute-start.74) | collective-permute-done | bytes 262176 | tf_op jit(solution)/shard_map/ppermute | solution.py:46
  504.6 14.1 %all_to_all.25 = f32[32,1,3]{2,1,0:T(1,128)S(1)} all-to-all(f32[32,1,3]{2,1,0:T(1,128)S(1)} %broadcast_in_dim.11), channel_id=1, replica_groups=mesh['dp'=8,'fsdp'=32] {'fsdp'}, dimensions={0} | all-to-all | bytes 768 | tf_op jit(solution)/shard_map/all_to_all | solution.py:36
  (340 shorter events, 342.9 us)
Async XLA Ops:
  119.2 14.3 %collective-permute-start.17 = (f32[256,256]{0,1:T(8,128)S(1)}, f32[256,256]{0,1:T(8,128)S(1)}, u32[]{:S(2)}, u32[]{:S(2)}) collective-permute-start(f32[256,256]{0,1:T(8,128)S(1)} %get-tuple-element.49), channel_id=1, source_target_pairs={{0,64},{32,96},{64,0},{96,32},{128,192},{160,224},{192,128},{224,1... | collective-permute-start | bytes 786440 | tf_op jit(solution)/shard_map/ppermute | solution.py:46
  121.8 14.8 %collective-permute-start.23 = (f32[256,256]{0,1:T(8,128)S(1)}, f32[256,256]{0,1:T(8,128)S(1)}, u32[]{:S(2)}, u32[]{:S(2)}) collective-permute-start(f32[256,256]{0,1:T(8,128)S(1)} %get-tuple-element.50), channel_id=1, source_target_pairs={{0,32},{32,0},{64,96},{96,64},{128,160},{160,128},{192,224},{224,1... | collective-permute-start | bytes 786440 | tf_op jit(solution)/shard_map/ppermute | solution.py:46
  121.8 17.9 %collective-permute-start.20 = (f32[256,256]{0,1:T(8,128)S(1)}, f32[256,256]{0,1:T(8,128)S(1)}, u32[]{:S(2)}, u32[]{:S(2)}) collective-permute-start(f32[256,256]{0,1:T(8,128)S(1)} %get-tuple-element.51), channel_id=1, source_target_pairs={{0,128},{32,160},{64,192},{96,224},{128,0},{160,32},{192,64},{224,... | collective-permute-start | bytes 786440 | tf_op jit(solution)/shard_map/ppermute | solution.py:46
  125.4 19.3 %collective-permute-start.15 = (f32[256,256]{0,1:T(8,128)S(1)}, f32[256,256]{0,1:T(8,128)S(1)}, u32[]{:S(2)}, u32[]{:S(2)}) collective-permute-start(f32[256,256]{0,1:T(8,128)S(1)} %add.278), channel_id=1, source_target_pairs={{0,64},{32,96},{64,0},{96,32},{128,192},{160,224},{192,128},{224,1... | collective-permute-start | bytes 786440 | tf_op jit(solution)/shard_map/ppermute | solution.py:46
  136.7 13.7 %collective-permute-start.24 = (f32[256,256]{0,1:T(8,128)S(1)}, f32[256,256]{0,1:T(8,128)S(1)}, u32[]{:S(2)}, u32[]{:S(2)}) collective-permute-start(f32[256,256]{0,1:T(8,128)S(1)} %add.287), channel_id=1, source_target_pairs={{0,64},{32,96},{64,0},{96,32},{128,192},{160,224},{192,128},{224,1... | collective-permute-start | bytes 786440 | tf_op jit(solution)/shard_map/ppermute | solution.py:46
  139.7 13.8 %collective-permute-start.21 = (f32[256,256]{0,1:T(8,128)S(1)}, f32[256,256]{0,1:T(8,128)S(1)}, u32[]{:S(2)}, u32[]{:S(2)}) collective-permute-start(f32[256,256]{0,1:T(8,128)S(1)} %add.284), channel_id=1, source_target_pairs={{0,32},{32,0},{64,96},{96,64},{128,160},{160,128},{192,224},{224,1... | collective-permute-start | bytes 786440 | tf_op jit(solution)/shard_map/ppermute | solution.py:46
  145.2 13.9 %collective-permute-start.19 = (f32[256,256]{0,1:T(8,128)S(1)}, f32[256,256]{0,1:T(8,128)S(1)}, u32[]{:S(2)}, u32[]{:S(2)}) collective-permute-start(f32[256,256]{0,1:T(8,128)S(1)} %add.282), channel_id=1, source_target_pairs={{0,32},{32,0},{64,96},{96,64},{128,160},{160,128},{192,224},{224,1... | collective-permute-start | bytes 786440 | tf_op jit(solution)/shard_map/ppermute | solution.py:46
  153.5 13.7 %collective-permute-start.22 = (f32[256,256]{0,1:T(8,128)S(1)}, f32[256,256]{0,1:T(8,128)S(1)}, u32[]{:S(2)}, u32[]{:S(2)}) collective-permute-start(f32[256,256]{0,1:T(8,128)S(1)} %add.285), channel_id=1, source_target_pairs={{0,64},{32,96},{64,0},{96,32},{128,192},{160,224},{192,128},{224,1... | collective-permute-start | bytes 786440 | tf_op jit(solution)/shard_map/ppermute | solution.py:46
  169.6 19.1 %all-to-all-start = ((f32[32,1,1]{2,1,0:T(1,128)}), f32[32,1,1]{2,1,0:T(1,128)S(1)}, u32[]{:S(2)}, u32[]{:S(2)}) async-start(f32[32,1,1]{2,1,0:T(1,128)} %broadcast_in_dim.8), calls=%async_computation | async-start | bytes 32768 | tf_op jit(solution)/shard_map/all_to_all | solution.py:36
  189.3 14.0 %all-to-all-start.1 = ((f32[32,1,3]{2,1,0:T(1,128)}), f32[32,1,3]{2,1,0:T(1,128)S(1)}, u32[]{:S(2)}, u32[]{:S(2)}) async-start(f32[32,1,3]{2,1,0:T(1,128)} %broadcast_in_dim.9), calls=%async_computation.1 | async-start | bytes 32768 | tf_op jit(solution)/shard_map/all_to_all | solution.py:36
  295.2 12.7 %collective-permute-start.43 = (f32[256,256]{0,1:T(8,128)S(1)}, f32[256,256]{0,1:T(8,128)S(1)}, u32[]{:S(2)}, u32[]{:S(2)}) collective-permute-start(f32[256,256]{0,1:T(8,128)S(1)} %get-tuple-element.45), channel_id=1, source_target_pairs={{0,64},{32,96},{64,0},{96,32},{128,192},{160,224},{192,128},{224,1... | collective-permute-start | bytes 786440 | tf_op jit(solution)/shard_map/ppermute | solution.py:46
  296.3 17.6 %collective-permute-start.49 = (f32[256,256]{0,1:T(8,128)S(1)}, f32[256,256]{0,1:T(8,128)S(1)}, u32[]{:S(2)}, u32[]{:S(2)}) collective-permute-start(f32[256,256]{0,1:T(8,128)S(1)} %get-tuple-element.46), channel_id=1, source_target_pairs={{0,32},{32,0},{64,96},{96,64},{128,160},{160,128},{192,224},{224,1... | collective-permute-start | bytes 786440 | tf_op jit(solution)/shard_map/ppermute | solution.py:46
  296.7 17.7 %collective-permute-start.46 = (f32[256,256]{0,1:T(8,128)S(1)}, f32[256,256]{0,1:T(8,128)S(1)}, u32[]{:S(2)}, u32[]{:S(2)}) collective-permute-start(f32[256,256]{0,1:T(8,128)S(1)} %get-tuple-element.47), channel_id=1, source_target_pairs={{0,128},{32,160},{64,192},{96,224},{128,0},{160,32},{192,64},{224,... | collective-permute-start | bytes 786440 | tf_op jit(solution)/shard_map/ppermute | solution.py:46
  302.8 16.5 %collective-permute-start.41 = (f32[256,256]{0,1:T(8,128)S(1)}, f32[256,256]{0,1:T(8,128)S(1)}, u32[]{:S(2)}, u32[]{:S(2)}) collective-permute-start(f32[256,256]{0,1:T(8,128)S(1)} %add.299), channel_id=1, source_target_pairs={{0,64},{32,96},{64,0},{96,32},{128,192},{160,224},{192,128},{224,1... | collective-permute-start | bytes 786440 | tf_op jit(solution)/shard_map/ppermute | solution.py:46
  314.5 16.3 %collective-permute-start.47 = (f32[256,256]{0,1:T(8,128)S(1)}, f32[256,256]{0,1:T(8,128)S(1)}, u32[]{:S(2)}, u32[]{:S(2)}) collective-permute-start(f32[256,256]{0,1:T(8,128)S(1)} %add.305), channel_id=1, source_target_pairs={{0,32},{32,0},{64,96},{96,64},{128,160},{160,128},{192,224},{224,1... | collective-permute-start | bytes 786440 | tf_op jit(solution)/shard_map/ppermute | solution.py:46
  319.7 16.7 %collective-permute-start.45 = (f32[256,256]{0,1:T(8,128)S(1)}, f32[256,256]{0,1:T(8,128)S(1)}, u32[]{:S(2)}, u32[]{:S(2)}) collective-permute-start(f32[256,256]{0,1:T(8,128)S(1)} %add.303), channel_id=1, source_target_pairs={{0,32},{32,0},{64,96},{96,64},{128,160},{160,128},{192,224},{224,1... | collective-permute-start | bytes 786440 | tf_op jit(solution)/shard_map/ppermute | solution.py:46
  451.4 15.5 %collective-permute-start.69 = (f32[256,256]{0,1:T(8,128)S(1)}, f32[256,256]{0,1:T(8,128)S(1)}, u32[]{:S(2)}, u32[]{:S(2)}) collective-permute-start(f32[256,256]{0,1:T(8,128)S(1)} %get-tuple-element.41), channel_id=1, source_target_pairs={{0,64},{32,96},{64,0},{96,32},{128,192},{160,224},{192,128},{224,1... | collective-permute-start | bytes 786440 | tf_op jit(solution)/shard_map/ppermute | solution.py:46
  455.3 14.8 %collective-permute-start.75 = (f32[256,256]{0,1:T(8,128)S(1)}, f32[256,256]{0,1:T(8,128)S(1)}, u32[]{:S(2)}, u32[]{:S(2)}) collective-permute-start(f32[256,256]{0,1:T(8,128)S(1)} %get-tuple-element.42), channel_id=1, source_target_pairs={{0,32},{32,0},{64,96},{96,64},{128,160},{160,128},{192,224},{224,1... | collective-permute-start | bytes 786440 | tf_op jit(solution)/shard_map/ppermute | solution.py:46
  455.3 17.7 %collective-permute-start.72 = (f32[256,256]{0,1:T(8,128)S(1)}, f32[256,256]{0,1:T(8,128)S(1)}, u32[]{:S(2)}, u32[]{:S(2)}) collective-permute-start(f32[256,256]{0,1:T(8,128)S(1)} %get-tuple-element.43), channel_id=1, source_target_pairs={{0,128},{32,160},{64,192},{96,224},{128,0},{160,32},{192,64},{224,... | collective-permute-start | bytes 786440 | tf_op jit(solution)/shard_map/ppermute | solution.py:46
  458.9 19.3 %collective-permute-start.67 = (f32[256,256]{0,1:T(8,128)S(1)}, f32[256,256]{0,1:T(8,128)S(1)}, u32[]{:S(2)}, u32[]{:S(2)}) collective-permute-start(f32[256,256]{0,1:T(8,128)S(1)} %add.321), channel_id=1, source_target_pairs={{0,64},{32,96},{64,0},{96,32},{128,192},{160,224},{192,128},{224,1... | collective-permute-start | bytes 786440 | tf_op jit(solution)/shard_map/ppermute | solution.py:46
  470.1 13.7 %collective-permute-start.76 = (f32[256,256]{0,1:T(8,128)S(1)}, f32[256,256]{0,1:T(8,128)S(1)}, u32[]{:S(2)}, u32[]{:S(2)}) collective-permute-start(f32[256,256]{0,1:T(8,128)S(1)} %add.330), channel_id=1, source_target_pairs={{0,64},{32,96},{64,0},{96,32},{128,192},{160,224},{192,128},{224,1... | collective-permute-start | bytes 786440 | tf_op jit(solution)/shard_map/ppermute | solution.py:46
  473.0 13.9 %collective-permute-start.73 = (f32[256,256]{0,1:T(8,128)S(1)}, f32[256,256]{0,1:T(8,128)S(1)}, u32[]{:S(2)}, u32[]{:S(2)}) collective-permute-start(f32[256,256]{0,1:T(8,128)S(1)} %add.327), channel_id=1, source_target_pairs={{0,32},{32,0},{64,96},{96,64},{128,160},{160,128},{192,224},{224,1... | collective-permute-start | bytes 786440 | tf_op jit(solution)/shard_map/ppermute | solution.py:46
  478.6 13.9 %collective-permute-start.71 = (f32[256,256]{0,1:T(8,128)S(1)}, f32[256,256]{0,1:T(8,128)S(1)}, u32[]{:S(2)}, u32[]{:S(2)}) collective-permute-start(f32[256,256]{0,1:T(8,128)S(1)} %add.325), channel_id=1, source_target_pairs={{0,32},{32,0},{64,96},{96,64},{128,160},{160,128},{192,224},{224,1... | collective-permute-start | bytes 786440 | tf_op jit(solution)/shard_map/ppermute | solution.py:46
  487.0 13.6 %collective-permute-start.74 = (f32[256,256]{0,1:T(8,128)S(1)}, f32[256,256]{0,1:T(8,128)S(1)}, u32[]{:S(2)}, u32[]{:S(2)}) collective-permute-start(f32[256,256]{0,1:T(8,128)S(1)} %add.328), channel_id=1, source_target_pairs={{0,64},{32,96},{64,0},{96,32},{128,192},{160,224},{192,128},{224,1... | collective-permute-start | bytes 786440 | tf_op jit(solution)/shard_map/ppermute | solution.py:46
  (90 other events, 807.3 us)

commit v4 on v2

--- a/solution.py
+++ b/solution.py
@@ -37,37 +37,44 @@
     return jnp.sum(gathered, axis=0)
 
 
-def doubling_sum(parts, axis):
-    size = lax.axis_size(axis)
-    for stage in range(stages_of(size)):
-        pairs = xor_pairs(size, 1 << stage)
-        parts = tuple(part + lax.ppermute(part, axis, pairs) for part in parts)
-    return parts
+def digit_groups(size, first_bits):
+    count = stages_of(size)
+    groups = [(0, min(first_bits, count))]
+    if count > first_bits:
+        groups.append((first_bits, count - first_bits))
+    return groups
 
 
-def halving_reduce(term, axis):
+def spread_reduce(value, axis, groups, send_type):
     size = lax.axis_size(axis)
     index = lax.axis_index(axis)
-    kept = term.astype(jnp.float32)
-    for stage in range(stages_of(size)):
-        half = kept.shape[0] // 2
-        bit = (index >> stage) & 1
-        send = lax.dynamic_slice_in_dim(kept, (1 - bit) * half, half, 0)
-        keep = lax.dynamic_slice_in_dim(kept, bit * half, half, 0)
-        got = lax.ppermute(send.astype(jnp.bfloat16), axis, xor_pairs(size, 1 << stage))
-        kept = keep + got.astype(jnp.float32)
+    kept = value.astype(jnp.float32)
+    for low, bits in groups:
+        width = 1 << bits
+        digit = (index >> low) & (width - 1)
+        rows = kept.shape[0] // width
+        total = lax.dynamic_slice_in_dim(kept, digit * rows, rows, 0)
+        for offset in range(1, width):
+            send = lax.dynamic_slice_in_dim(kept, (digit ^ offset) * rows, rows, 0)
+            got = lax.ppermute(send.astype(send_type), axis, xor_pairs(size, offset << low))
+            total = total + got.astype(jnp.float32)
+        kept = total
     return kept
 
 
-def doubling_gather(chunk, axis):
+def spread_gather(chunk, axis, groups):
     size = lax.axis_size(axis)
     index = lax.axis_index(axis)
-    for stage in reversed(range(stages_of(size))):
-        bit = (index >> stage) & 1
-        other = lax.ppermute(chunk, axis, xor_pairs(size, 1 << stage))
-        chunk = jnp.where(
-            bit == 0, jnp.concatenate([chunk, other], 0), jnp.concatenate([other, chunk], 0)
-        )
+    for low, bits in reversed(groups):
+        width = 1 << bits
+        digit = (index >> low) & (width - 1)
+        rows = chunk.shape[0]
+        whole = jnp.zeros((rows * width,) + chunk.shape[1:], chunk.dtype)
+        whole = lax.dynamic_update_slice_in_dim(whole, chunk, digit * rows, 0)
+        for offset in range(1, width):
+            got = lax.ppermute(chunk, axis, xor_pairs(size, offset << low))
+            whole = lax.dynamic_update_slice_in_dim(whole, got, (digit ^ offset) * rows, 0)
+        chunk = whole
     return chunk
 
 
@@ -81,15 +88,18 @@
     partial_out = partial_out + lax.dot_general(
         hidden_act, tangent_out_t, (((1,), (1,)), ((), ())), preferred_element_type=jnp.float32
     )
-    out_chunk = halving_reduce(partial_out.astype(jnp.bfloat16), "fsdp")
-    cotangent = doubling_gather((out_chunk * metric).astype(jnp.bfloat16), "fsdp")
+    fsdp_groups = digit_groups(lax.axis_size("fsdp"), 2)
+    out_chunk = spread_reduce(partial_out.astype(jnp.bfloat16), "fsdp", fsdp_groups, jnp.bfloat16)
+    cotangent = spread_gather((out_chunk * metric).astype(jnp.bfloat16), "fsdp", fsdp_groups)
     back_act = lax.dot_general(
         cotangent, w_out, (((1,), (1,)), ((), ())), preferred_element_type=jnp.float32
     )
     grad_pre = (slope_act * back_act).astype(jnp.bfloat16)
     part_out_t = contract_rows(cotangent, hidden_act)
     part_in = contract_rows(normed, grad_pre)
-    (fisher,) = doubling_sum((jnp.concatenate([part_in, part_out_t], axis=1),), "dp")
+    dp_groups = digit_groups(lax.axis_size("dp"), 3)
+    fisher_chunk = spread_reduce(jnp.concatenate([part_in, part_out_t], axis=1), "dp", dp_groups, jnp.float32)
+    fisher = spread_gather(fisher_chunk, "dp", dp_groups)
     return fisher + damping * direction
 
 

time: 616 us -> 524 us (0.85)
  the two profiles are of different devices: /device:TPU:1 before, /device:TPU:25 now
where the time goes in v4:
time: 524 us; the launch traced here: 514 us
  starting transfers between devices  188 us (36%)
  waiting for transfers between devices  185 us (35%)
  blocking collectives  45.4 us (9%)
  matrix products  36.8 us (7%)
  other arithmetic  29.2 us (6%)
  local copies, waits for them, and re-layouts  21.2 us (4%)
  between operations  8.17 us (2%)
    ppermute x51, starting transfers between devices, spread_gather(): got = lax.ppermute(chunk, axis, xor_pairs(size, offset << low))  94.5 us
    ppermute x51, waiting for transfers between devices, spread_reduce(): lax.ppermute(send.astype(send_type), axis, xor_pairs(size, offset << low))  85 us
    ppermute x51, waiting for transfers between devices, spread_gather(): got = lax.ppermute(chunk, axis, xor_pairs(size, offset << low))  83.3 us
    ppermute x51, starting transfers between devices, spread_reduce(): lax.ppermute(send.astype(send_type), axis, xor_pairs(size, offset << low))  77 us
    all_to_all x2, blocking collectives, scalar_sum(): lax.all_to_all(jnp.broadcast_to(values[None], (size,) + values.shape), ax...  45.4 us
    all_to_all x2, starting transfers between devices, scalar_sum(): lax.all_to_all(jnp.broadcast_to(values[None], (size,) + values.shape), ax...  16.8 us
    all_to_all x2, waiting for transfers between devices, scalar_sum(): lax.all_to_all(jnp.broadcast_to(values[None], (size,) + values.shape), ax...  16.7 us
    dot_general x3, matrix products, fisher_product(): jnp.dot(inner_tangent, w_out, preferred_element_type=jnp.float32)  13.4 us
  transfers between devices with their start and end apart: 104, of which 45 were waited for; matrix products, arithmetic and copies ran while one was open for 1% of the time, Pallas kernels for 0%

profile of v4, /device:TPU:25, one launch (start us, length us, event | category | flops | bytes accessed | tf_op | source)
XLA Modules:
  0.0 514.1 jit_solution(8370891555633488986)
XLA Ops:
  21.3 9.3 %collective-permute-done.1 = bf16[192,1024]{1,0:T(8,128)(2,1)} collective-permute-done((bf16[192,1024]{1,0:T(8,128)(2,1)}, bf16[192,1024]{1,0:T(8,128)(2,1)}, u32[]{:S(2)}, u32[]{:S(2)}) %collective-permute-start.1) | collective-permute-done | bytes 393248 | tf_op jit(solution)/shard_map/ppermute | solution.py:59
  30.6 8.6 %collective-permute-done.2 = bf16[192,1024]{1,0:T(8,128)(2,1)} collective-permute-done((bf16[192,1024]{1,0:T(8,128)(2,1)S(1)}, bf16[192,1024]{1,0:T(8,128)(2,1)}, u32[]{:S(2)}, u32[]{:S(2)}) %collective-permute-start.2) | collective-permute-done | bytes 393248 | tf_op jit(solution)/shard_map/ppermute | solution.py:59
  46.6 5.8 %collective-permute-start.6 = (bf16[24,1024]{1,0:T(8,128)(2,1)S(1)}, bf16[24,1024]{1,0:T(8,128)(2,1)S(1)}, u32[]{:S(2)}, u32[]{:S(2)}) collective-permute-start(bf16[24,1024]{1,0:T(8,128)(2,1)S(1)} %get-tuple-element.95), channel_id=1, source_target_pairs={{0,16},{1,17},{2,18},{3,19},{4,20},{5,21},{6,22},{7,23},{8,24},{9,... | collective-permute-start | bytes 147464 | tf_op jit(solution)/shard_map/ppermute | solution.py:59
  87.3 7.7 %collective-permute-done.18 = bf16[192,1024]{1,0:T(8,128)(2,1)} collective-permute-done((bf16[192,1024]{1,0:T(8,128)(2,1)S(1)}, bf16[192,1024]{1,0:T(8,128)(2,1)}, u32[]{:S(2)}, u32[]{:S(2)}) %collective-permute-start.18) | collective-permute-done | bytes 393248 | tf_op jit(solution)/shard_map/ppermute | solution.py:75
  96.0 7.7 %collective-permute-done.19 = bf16[192,1024]{1,0:T(8,128)(2,1)} collective-permute-done((bf16[192,1024]{1,0:T(8,128)(2,1)S(1)}, bf16[192,1024]{1,0:T(8,128)(2,1)}, u32[]{:S(2)}, u32[]{:S(2)}) %collective-permute-start.19) | collective-permute-done | bytes 393248 | tf_op jit(solution)/shard_map/ppermute | solution.py:75
  132.8 4.8 collective-permute-start.32
  137.6 9.0 %collective-permute-start.33 = (f32[128,256]{0,1:T(8,128)S(1)}, f32[128,256]{0,1:T(8,128)S(1)}, u32[]{:S(2)}, u32[]{:S(2)}) collective-permute-start(f32[128,256]{0,1:T(8,128)S(1)} %get-tuple-element.41), channel_id=1, source_target_pairs={{0,224},{32,192},{64,160},{96,128},{128,96},{160,64},{192,32},{224... | collective-permute-start | bytes 393224 | tf_op jit(solution)/shard_map/ppermute | solution.py:75
  146.8 5.8 %collective-permute-done.33 = f32[128,256]{0,1:T(8,128)S(1)} collective-permute-done((f32[128,256]{0,1:T(8,128)S(1)}, f32[128,256]{0,1:T(8,128)S(1)}, u32[]{:S(2)}, u32[]{:S(2)}) %collective-permute-start.33) | collective-permute-done | bytes 131104 | tf_op jit(solution)/shard_map/ppermute | solution.py:75
  154.8 12.7 %all-to-all-start = ((f32[32,1,1]{2,1,0:T(1,128)}), f32[32,1,1]{2,1,0:T(1,128)S(1)}, u32[]{:S(2)}, u32[]{:S(2)}) async-start(f32[32,1,1]{2,1,0:T(1,128)} %broadcast_in_dim.8), calls=%async_computation | async-start | bytes 32768 | tf_op jit(solution)/shard_map/all_to_all | solution.py:36
  168.9 7.9 %all-to-all-done = f32[32,1,1]{2,1,0:T(1,128)S(1)} async-done(((f32[32,1,1]{2,1,0:T(1,128)}), f32[32,1,1]{2,1,0:T(1,128)S(1)}, u32[]{:S(2)}, u32[]{:S(2)}) %all-to-all-start) | async-done | bytes 160 | tf_op jit(solution)/shard_map/all_to_all | solution.py:36
  182.2 8.8 %all-to-all-done.1 = f32[32,1,3]{2,1,0:T(1,128)S(1)} async-done(((f32[32,1,3]{2,1,0:T(1,128)}), f32[32,1,3]{2,1,0:T(1,128)S(1)}, u32[]{:S(2)}, u32[]{:S(2)}) %all-to-all-start.1) | async-done | bytes 416 | tf_op jit(solution)/shard_map/all_to_all | solution.py:36
  208.9 8.8 %collective-permute-done.35 = bf16[192,1024]{1,0:T(8,128)(2,1)S(1)} collective-permute-done((bf16[192,1024]{1,0:T(8,128)(2,1)S(1)}, bf16[192,1024]{1,0:T(8,128)(2,1)S(1)}, u32[]{:S(2)}, u32[]{:S(2)}) %collective-permute-start.35) | collective-permute-done | bytes 393248 | tf_op jit(solution)/shard_map/ppermute | solution.py:59
  217.7 8.7 %collective-permute-done.36 = bf16[192,1024]{1,0:T(8,128)(2,1)S(1)} collective-permute-done((bf16[192,1024]{1,0:T(8,128)(2,1)S(1)}, bf16[192,1024]{1,0:T(8,128)(2,1)S(1)}, u32[]{:S(2)}, u32[]{:S(2)}) %collective-permute-start.36) | collective-permute-done | bytes 393248 | tf_op jit(solution)/shard_map/ppermute | solution.py:59
  250.2 4.6 collective-permute-start.49
  266.9 8.5 %collective-permute-done.52 = bf16[192,1024]{1,0:T(8,128)(2,1)S(1)} collective-permute-done((bf16[192,1024]{1,0:T(8,128)(2,1)S(1)}, bf16[192,1024]{1,0:T(8,128)(2,1)S(1)}, u32[]{:S(2)}, u32[]{:S(2)}) %collective-permute-start.52) | collective-permute-done | bytes 393248 | tf_op jit(solution)/shard_map/ppermute | solution.py:75
  275.5 8.7 %collective-permute-done.53 = bf16[192,1024]{1,0:T(8,128)(2,1)S(1)} collective-permute-done((bf16[192,1024]{1,0:T(8,128)(2,1)S(1)}, bf16[192,1024]{1,0:T(8,128)(2,1)S(1)}, u32[]{:S(2)}, u32[]{:S(2)}) %collective-permute-start.53) | collective-permute-done | bytes 393248 | tf_op jit(solution)/shard_map/ppermute | solution.py:75
  327.3 22.4 %all_to_all.24 = f32[32,1,3]{2,1,0:T(1,128)S(1)} all-to-all(f32[32,1,3]{2,1,0:T(1,128)S(1)} %broadcast_in_dim.10), channel_id=1, replica_groups=mesh['dp'=8,'fsdp'=32] {'fsdp'}, dimensions={0} | all-to-all | bytes 768 | tf_op jit(solution)/shard_map/all_to_all | solution.py:36
  367.1 8.8 %collective-permute-done.69 = bf16[192,1024]{1,0:T(8,128)(2,1)S(1)} collective-permute-done((bf16[192,1024]{1,0:T(8,128)(2,1)S(1)}, bf16[192,1024]{1,0:T(8,128)(2,1)S(1)}, u32[]{:S(2)}, u32[]{:S(2)}) %collective-permute-start.69) | collective-permute-done | bytes 393248 | tf_op jit(solution)/shard_map/ppermute | solution.py:59
  375.9 8.7 %collective-permute-done.70 = bf16[192,1024]{1,0:T(8,128)(2,1)S(1)} collective-permute-done((bf16[192,1024]{1,0:T(8,128)(2,1)S(1)}, bf16[192,1024]{1,0:T(8,128)(2,1)S(1)}, u32[]{:S(2)}, u32[]{:S(2)}) %collective-permute-start.70) | collective-permute-done | bytes 393248 | tf_op jit(solution)/shard_map/ppermute | solution.py:59
  408.2 4.7 collective-permute-start.83
  424.4 8.5 %collective-permute-done.86 = bf16[192,1024]{1,0:T(8,128)(2,1)S(1)} collective-permute-done((bf16[192,1024]{1,0:T(8,128)(2,1)S(1)}, bf16[192,1024]{1,0:T(8,128)(2,1)S(1)}, u32[]{:S(2)}, u32[]{:S(2)}) %collective-permute-start.86) | collective-permute-done | bytes 393248 | tf_op jit(solution)/shard_map/ppermute | solution.py:75
  433.0 8.7 %collective-permute-done.87 = bf16[192,1024]{1,0:T(8,128)(2,1)S(1)} collective-permute-done((bf16[192,1024]{1,0:T(8,128)(2,1)S(1)}, bf16[192,1024]{1,0:T(8,128)(2,1)S(1)}, u32[]{:S(2)}, u32[]{:S(2)}) %collective-permute-start.87) | collective-permute-done | bytes 393248 | tf_op jit(solution)/shard_map/ppermute | solution.py:75
  469.7 4.7 collective-permute-start.100
  485.1 23.0 %all_to_all.25 = f32[32,1,3]{2,1,0:T(1,128)S(1)} all-to-all(f32[32,1,3]{2,1,0:T(1,128)S(1)} %broadcast_in_dim.11), channel_id=1, replica_groups=mesh['dp'=8,'fsdp'=32] {'fsdp'}, dimensions={0} | all-to-all | bytes 768 | tf_op jit(solution)/shard_map/all_to_all | solution.py:36
  (364 shorter events, 289.0 us)
Async XLA Ops:
  18.1 12.5 %collective-permute-start.1 = (bf16[192,1024]{1,0:T(8,128)(2,1)}, bf16[192,1024]{1,0:T(8,128)(2,1)}, u32[]{:S(2)}, u32[]{:S(2)}) collective-permute-start(bf16[192,1024]{1,0:T(8,128)(2,1)} %get-tuple-element.52), channel_id=1, source_target_pairs={{0,2},{1,3},{2,0},{3,1},{4,6},{5,7},{6,4},{7,5},{8,10},{9,11},{10,... | collective-permute-start | bytes 1179656 | tf_op jit(solution)/shard_map/ppermute | solution.py:59
  20.9 18.3 %collective-permute-start.2 = (bf16[192,1024]{1,0:T(8,128)(2,1)S(1)}, bf16[192,1024]{1,0:T(8,128)(2,1)}, u32[]{:S(2)}, u32[]{:S(2)}) collective-permute-start(bf16[192,1024]{1,0:T(8,128)(2,1)S(1)} %get-tuple-element.51), channel_id=1, source_target_pairs={{0,3},{1,2},{2,1},{3,0},{4,7},{5,6},{6,5},{7,4},{8,11},{9,10},{10,... | collective-permute-start | bytes 1179656 | tf_op jit(solution)/shard_map/ppermute | solution.py:59
  43.6 12.9 %collective-permute-start.4 = (bf16[24,1024]{1,0:T(8,128)(2,1)S(1)}, bf16[24,1024]{1,0:T(8,128)(2,1)S(1)}, u32[]{:S(2)}, u32[]{:S(2)}) collective-permute-start(bf16[24,1024]{1,0:T(8,128)(2,1)S(1)} %get-tuple-element.97), channel_id=1, source_target_pairs={{0,8},{1,9},{2,10},{3,11},{4,12},{5,13},{6,14},{7,15},{8,0},{9,1},... | collective-permute-start | bytes 147464 | tf_op jit(solution)/shard_map/ppermute | solution.py:59
  63.5 11.3 %collective-permute-start.11 = (bf16[24,1024]{1,0:T(8,128)(2,1)S(1)}, bf16[24,1024]{1,0:T(8,128)(2,1)S(1)}, u32[]{:S(2)}, u32[]{:S(2)}) collective-permute-start(bf16[24,1024]{1,0:T(8,128)(2,1)S(1)} %get-tuple-element.43), channel_id=1, source_target_pairs={{0,8},{1,9},{2,10},{3,11},{4,12},{5,13},{6,14},{7,15},{8,0},{9,1},... | collective-permute-start | bytes 147464 | tf_op jit(solution)/shard_map/ppermute | solution.py:75
  82.7 12.2 %collective-permute-start.18 = (bf16[192,1024]{1,0:T(8,128)(2,1)S(1)}, bf16[192,1024]{1,0:T(8,128)(2,1)}, u32[]{:S(2)}, u32[]{:S(2)}) collective-permute-start(bf16[192,1024]{1,0:T(8,128)(2,1)S(1)} %constant_dynamic-update-slice_fusion.52), channel_id=1, source_target_pairs={{0,2},{1,3},{2,0},{3,1},{4,6},{5,7},{6,4},{7,5},{8,10},{9,11},{10,... | collective-permute-start | bytes 1179656 | tf_op jit(solution)/shard_map/ppermute | solution.py:75
  85.5 18.1 %collective-permute-start.19 = (bf16[192,1024]{1,0:T(8,128)(2,1)S(1)}, bf16[192,1024]{1,0:T(8,128)(2,1)}, u32[]{:S(2)}, u32[]{:S(2)}) collective-permute-start(bf16[192,1024]{1,0:T(8,128)(2,1)S(1)} %constant_dynamic-update-slice_fusion.52), channel_id=1, source_target_pairs={{0,3},{1,2},{2,1},{3,0},{4,7},{5,6},{6,5},{7,4},{8,11},{9,10},{10,... | collective-permute-start | bytes 1179656 | tf_op jit(solution)/shard_map/ppermute | solution.py:75
  131.6 15.0 %collective-permute-start.29 = (f32[128,256]{0,1:T(8,128)S(1)}, f32[128,256]{0,1:T(8,128)S(1)}, u32[]{:S(2)}, u32[]{:S(2)}) collective-permute-start(f32[128,256]{0,1:T(8,128)S(1)} %get-tuple-element.41), channel_id=1, source_target_pairs={{0,96},{32,64},{64,32},{96,0},{128,224},{160,192},{192,160},{224,1... | collective-permute-start | bytes 393224 | tf_op jit(solution)/shard_map/ppermute | solution.py:75
  131.6 15.1 %collective-permute-start.30 = (f32[128,256]{0,1:T(8,128)S(1)}, f32[128,256]{0,1:T(8,128)S(1)}, u32[]{:S(2)}, u32[]{:S(2)}) collective-permute-start(f32[128,256]{0,1:T(8,128)S(1)} %get-tuple-element.41), channel_id=1, source_target_pairs={{0,128},{32,160},{64,192},{96,224},{128,0},{160,32},{192,64},{224,... | collective-permute-start | bytes 393224 | tf_op jit(solution)/shard_map/ppermute | solution.py:75
  132.8 13.9 %collective-permute-start.31 = (f32[128,256]{0,1:T(8,128)S(1)}, f32[128,256]{0,1:T(8,128)S(1)}, u32[]{:S(2)}, u32[]{:S(2)}) collective-permute-start(f32[128,256]{0,1:T(8,128)S(1)} %get-tuple-element.41), channel_id=1, source_target_pairs={{0,160},{32,128},{64,224},{96,192},{128,32},{160,0},{192,96},{224,... | collective-permute-start | bytes 393224 | tf_op jit(solution)/shard_map/ppermute | solution.py:75
  132.8 13.9 %collective-permute-start.32 = (f32[128,256]{0,1:T(8,128)S(1)}, f32[128,256]{0,1:T(8,128)S(1)}, u32[]{:S(2)}, u32[]{:S(2)}) collective-permute-start(f32[128,256]{0,1:T(8,128)S(1)} %get-tuple-element.41), channel_id=1, source_target_pairs={{0,192},{32,224},{64,128},{96,160},{128,64},{160,96},{192,0},{224,... | collective-permute-start | bytes 393224 | tf_op jit(solution)/shard_map/ppermute | solution.py:75
  137.6 14.9 %collective-permute-start.33 = (f32[128,256]{0,1:T(8,128)S(1)}, f32[128,256]{0,1:T(8,128)S(1)}, u32[]{:S(2)}, u32[]{:S(2)}) collective-permute-start(f32[128,256]{0,1:T(8,128)S(1)} %get-tuple-element.41), channel_id=1, source_target_pairs={{0,224},{32,192},{64,160},{96,128},{128,96},{160,64},{192,32},{224... | collective-permute-start | bytes 393224 | tf_op jit(solution)/shard_map/ppermute | solution.py:75
  154.8 22.1 %all-to-all-start = ((f32[32,1,1]{2,1,0:T(1,128)}), f32[32,1,1]{2,1,0:T(1,128)S(1)}, u32[]{:S(2)}, u32[]{:S(2)}) async-start(f32[32,1,1]{2,1,0:T(1,128)} %broadcast_in_dim.8), calls=%async_computation | async-start | bytes 32768 | tf_op jit(solution)/shard_map/all_to_all | solution.py:36
  177.4 13.5 %all-to-all-start.1 = ((f32[32,1,3]{2,1,0:T(1,128)}), f32[32,1,3]{2,1,0:T(1,128)S(1)}, u32[]{:S(2)}, u32[]{:S(2)}) async-start(f32[32,1,3]{2,1,0:T(1,128)} %broadcast_in_dim.9), calls=%async_computation.1 | async-start | bytes 32768 | tf_op jit(solution)/shard_map/all_to_all | solution.py:36
  205.6 12.1 %collective-permute-start.35 = (bf16[192,1024]{1,0:T(8,128)(2,1)S(1)}, bf16[192,1024]{1,0:T(8,128)(2,1)S(1)}, u32[]{:S(2)}, u32[]{:S(2)}) collective-permute-start(bf16[192,1024]{1,0:T(8,128)(2,1)S(1)} %get-tuple-element.49), channel_id=1, source_target_pairs={{0,2},{1,3},{2,0},{3,1},{4,6},{5,7},{6,4},{7,5},{8,10},{9,11},{10,... | collective-permute-start | bytes 1179656 | tf_op jit(solution)/shard_map/ppermute | solution.py:59
  206.1 20.3 %collective-permute-start.36 = (bf16[192,1024]{1,0:T(8,128)(2,1)S(1)}, bf16[192,1024]{1,0:T(8,128)(2,1)S(1)}, u32[]{:S(2)}, u32[]{:S(2)}) collective-permute-start(bf16[192,1024]{1,0:T(8,128)(2,1)S(1)} %get-tuple-element.48), channel_id=1, source_target_pairs={{0,3},{1,2},{2,1},{3,0},{4,7},{5,6},{6,5},{7,4},{8,11},{9,10},{10,... | collective-permute-start | bytes 1179656 | tf_op jit(solution)/shard_map/ppermute | solution.py:59
  242.6 12.3 %collective-permute-start.45 = (bf16[24,1024]{1,0:T(8,128)(2,1)S(1)}, bf16[24,1024]{1,0:T(8,128)(2,1)S(1)}, u32[]{:S(2)}, u32[]{:S(2)}) collective-permute-start(bf16[24,1024]{1,0:T(8,128)(2,1)S(1)} %get-tuple-element.39), channel_id=1, source_target_pairs={{0,8},{1,9},{2,10},{3,11},{4,12},{5,13},{6,14},{7,15},{8,0},{9,1},... | collective-permute-start | bytes 147464 | tf_op jit(solution)/shard_map/ppermute | solution.py:75
  263.4 12.1 %collective-permute-start.52 = (bf16[192,1024]{1,0:T(8,128)(2,1)S(1)}, bf16[192,1024]{1,0:T(8,128)(2,1)S(1)}, u32[]{:S(2)}, u32[]{:S(2)}) collective-permute-start(bf16[192,1024]{1,0:T(8,128)(2,1)S(1)} %constant_dynamic-update-slice_fusion.32), channel_id=1, source_target_pairs={{0,2},{1,3},{2,0},{3,1},{4,6},{5,7},{6,4},{7,5},{8,10},{9,11},{10,... | collective-permute-start | bytes 1179656 | tf_op jit(solution)/shard_map/ppermute | solution.py:75
  263.4 20.8 %collective-permute-start.53 = (bf16[192,1024]{1,0:T(8,128)(2,1)S(1)}, bf16[192,1024]{1,0:T(8,128)(2,1)S(1)}, u32[]{:S(2)}, u32[]{:S(2)}) collective-permute-start(bf16[192,1024]{1,0:T(8,128)(2,1)S(1)} %constant_dynamic-update-slice_fusion.32), channel_id=1, source_target_pairs={{0,3},{1,2},{2,1},{3,0},{4,7},{5,6},{6,5},{7,4},{8,11},{9,10},{10,... | collective-permute-start | bytes 1179656 | tf_op jit(solution)/shard_map/ppermute | solution.py:75
  363.8 12.1 %collective-permute-start.69 = (bf16[192,1024]{1,0:T(8,128)(2,1)S(1)}, bf16[192,1024]{1,0:T(8,128)(2,1)S(1)}, u32[]{:S(2)}, u32[]{:S(2)}) collective-permute-start(bf16[192,1024]{1,0:T(8,128)(2,1)S(1)} %get-tuple-element.46), channel_id=1, source_target_pairs={{0,2},{1,3},{2,0},{3,1},{4,6},{5,7},{6,4},{7,5},{8,10},{9,11},{10,... | collective-permute-start | bytes 1179656 | tf_op jit(solution)/shard_map/ppermute | solution.py:59
  364.3 20.3 %collective-permute-start.70 = (bf16[192,1024]{1,0:T(8,128)(2,1)S(1)}, bf16[192,1024]{1,0:T(8,128)(2,1)S(1)}, u32[]{:S(2)}, u32[]{:S(2)}) collective-permute-start(bf16[192,1024]{1,0:T(8,128)(2,1)S(1)} %get-tuple-element.45), channel_id=1, source_target_pairs={{0,3},{1,2},{2,1},{3,0},{4,7},{5,6},{6,5},{7,4},{8,11},{9,10},{10,... | collective-permute-start | bytes 1179656 | tf_op jit(solution)/shard_map/ppermute | solution.py:59
  385.7 10.9 %collective-permute-start.73 = (bf16[24,1024]{1,0:T(8,128)(2,1)S(1)}, bf16[24,1024]{1,0:T(8,128)(2,1)S(1)}, u32[]{:S(2)}, u32[]{:S(2)}) collective-permute-start(bf16[24,1024]{1,0:T(8,128)(2,1)S(1)} %get-tuple-element.82), channel_id=1, source_target_pairs={{0,12},{1,13},{2,14},{3,15},{4,8},{5,9},{6,10},{7,11},{8,4},{9,5},... | collective-permute-start | bytes 147464 | tf_op jit(solution)/shard_map/ppermute | solution.py:59
  400.8 12.1 %collective-permute-start.79 = (bf16[24,1024]{1,0:T(8,128)(2,1)S(1)}, bf16[24,1024]{1,0:T(8,128)(2,1)S(1)}, u32[]{:S(2)}, u32[]{:S(2)}) collective-permute-start(bf16[24,1024]{1,0:T(8,128)(2,1)S(1)} %get-tuple-element.32), channel_id=1, source_target_pairs={{0,8},{1,9},{2,10},{3,11},{4,12},{5,13},{6,14},{7,15},{8,0},{9,1},... | collective-permute-start | bytes 147464 | tf_op jit(solution)/shard_map/ppermute | solution.py:75
  420.9 12.1 %collective-permute-start.86 = (bf16[192,1024]{1,0:T(8,128)(2,1)S(1)}, bf16[192,1024]{1,0:T(8,128)(2,1)S(1)}, u32[]{:S(2)}, u32[]{:S(2)}) collective-permute-start(bf16[192,1024]{1,0:T(8,128)(2,1)S(1)} %constant_dynamic-update-slice_fusion.12), channel_id=1, source_target_pairs={{0,2},{1,3},{2,0},{3,1},{4,6},{5,7},{6,4},{7,5},{8,10},{9,11},{10,... | collective-permute-start | bytes 1179656 | tf_op jit(solution)/shard_map/ppermute | solution.py:75
  421.2 20.4 %collective-permute-start.87 = (bf16[192,1024]{1,0:T(8,128)(2,1)S(1)}, bf16[192,1024]{1,0:T(8,128)(2,1)S(1)}, u32[]{:S(2)}, u32[]{:S(2)}) collective-permute-start(bf16[192,1024]{1,0:T(8,128)(2,1)S(1)} %constant_dynamic-update-slice_fusion.12), channel_id=1, source_target_pairs={{0,3},{1,2},{2,1},{3,0},{4,7},{5,6},{6,5},{7,4},{8,11},{9,10},{10,... | collective-permute-start | bytes 1179656 | tf_op jit(solution)/shard_map/ppermute | solution.py:75
  (107 other events, 923.2 us)

commit v5 on v4

--- a/solution.py
+++ b/solution.py
@@ -114,22 +114,29 @@
     hidden_act = jax.nn.silu(preact).astype(jnp.bfloat16)
     slope_act = silu_slope(preact)
     residual = jnp.concatenate([grad_in, grad_out.T], axis=1)
-    solution_now = jnp.zeros_like(residual)
-    direction = residual
-    norm_now = scalar_sum(jnp.sum(residual * residual)[None], "fsdp")[0]
-    for iteration in range(ITERS):
+
+    def iterate(_, carry):
+        solution_now, residual, direction = carry
         fisher = fisher_product(direction, normed, hidden_act, slope_act, w_out, metric, width)
         sums = jnp.stack(
-            [jnp.sum(direction * fisher), jnp.sum(residual * fisher), jnp.sum(fisher * fisher)]
+            [
+                jnp.sum(direction * fisher),
+                jnp.sum(residual * fisher),
+                jnp.sum(fisher * fisher),
+                jnp.sum(residual * residual),
+            ]
         )
-        quadratic, cross, fisher_square = scalar_sum(sums, "fsdp")
+        quadratic, cross, fisher_square, norm_now = scalar_sum(sums, "fsdp")
         step_size = norm_now / quadratic
         solution_now = solution_now + step_size * direction
-        residual = residual - step_size * fisher
-        if iteration + 1 < ITERS:
-            norm_next = norm_now - 2.0 * step_size * cross + step_size * step_size * fisher_square
-            direction = residual + norm_next / norm_now * direction
-            norm_now = norm_next
+        residual_next = residual - step_size * fisher
+        norm_next = norm_now - 2.0 * step_size * cross + step_size * step_size * fisher_square
+        direction = residual_next + norm_next / norm_now * direction
+        return (solution_now, residual_next, direction)
+
+    solution_now, residual, _ = lax.fori_loop(
+        0, ITERS, iterate, (jnp.zeros_like(residual), residual, residual)
+    )
     return (
         solution_now[:, :width],
         solution_now[:, width:].T,

time: 524 us -> 506 us (0.966)
  the two profiles are of different devices: /device:TPU:25 before, /device:TPU:1 now
where the time goes in v5:
time: 506 us; the launch traced here: 505 us
  waiting for transfers between devices  190 us (38%)
  starting transfers between devices  183 us (36%)
  other arithmetic  42.8 us (8%)
  matrix products  39.2 us (8%)
  local copies, waits for them, and re-layouts  36.1 us (7%)
  loops' own time  12.9 us (3%)
    ppermute x51, waiting for transfers between devices, spread_reduce(): lax.ppermute(send.astype(send_type), axis, xor_pairs(size, offset << low))  88.8 us
    ppermute x51, starting transfers between devices, spread_gather(): got = lax.ppermute(chunk, axis, xor_pairs(size, offset << low))  78.7 us
    ppermute x51, starting transfers between devices, spread_reduce(): lax.ppermute(send.astype(send_type), axis, xor_pairs(size, offset << low))  77.8 us
    ppermute x51, waiting for transfers between devices, spread_gather(): got = lax.ppermute(chunk, axis, xor_pairs(size, offset << low))  73.6 us
    all_to_all x3, waiting for transfers between devices, scalar_sum(): lax.all_to_all(jnp.broadcast_to(values[None], (size,) + values.shape), ax...  27.9 us
    all_to_all x3, starting transfers between devices, scalar_sum(): lax.all_to_all(jnp.broadcast_to(values[None], (size,) + values.shape), ax...  26.4 us
    dot_general x6, matrix products, contract_rows(): lax.dot_general(left_side, right_side, (((0,), (0,)), ((), ())), preferre...  15.9 us
    dot_general x3, matrix products, fisher_product(): jnp.dot(inner_tangent, w_out, preferred_element_type=jnp.float32)  14.4 us
  transfers between devices with their start and end apart: 105, of which 51 were waited for; matrix products, arithmetic and copies ran while one was open for 3% of the time, Pallas kernels for 0%

profile of v5, /device:TPU:1, one launch (start us, length us, event | category | flops | bytes accessed | tf_op | source)
XLA Modules:
  0.0 504.9 jit_solution(13539296342557133002)
XLA Ops:
  7.4 493.0 %while.15 = (s32[]{:T(128)}, f32[1024,256]{0,1:T(8,128)}, f32[1024,256]{0,1:T(8,128)S(1)}, f32[1024,256]{0,1:T(8,128)S(1)}, bf16[768,1024]{1,0:T(8,128)(2,1)}, /...) while((s32[]{:T(128)}, f32[1024,256]{0,1:T(8,128)}, ...), condition=%wide.region_7.8_spmd.clone, body=%wide.region_1.7_spmd.clone.sunk | while | flops 1218019456 | bytes 95085584 | solution.py:137
  7.5 4.8 fusion.63
  22.8 7.0 %collective-permute-done = bf16[192,1024]{1,0:T(8,128)(2,1)} collective-permute-done((bf16[192,1024]{1,0:T(8,128)(2,1)S(1)}, bf16[192,1024]{1,0:T(8,128)(2,1)}, u32[]{:S(2)}, u32[]{:S(2)}) %collective-permute-start) | collective-permute-done | bytes 393248 | tf_op jit(solution)/shard_map/while/body/eval_jaxpr/ppermute | solution.py:59
  29.8 9.3 %collective-permute-done.1 = bf16[192,1024]{1,0:T(8,128)(2,1)} collective-permute-done((bf16[192,1024]{1,0:T(8,128)(2,1)S(1)}, bf16[192,1024]{1,0:T(8,128)(2,1)}, u32[]{:S(2)}, u32[]{:S(2)}) %collective-permute-start.1) | collective-permute-done | bytes 393248 | tf_op jit(solution)/shard_map/while/body/eval_jaxpr/ppermute | solution.py:59
  40.9 5.8 %collective-permute-start.3 = (bf16[24,1024]{1,0:T(8,128)(2,1)S(1)}, bf16[24,1024]{1,0:T(8,128)(2,1)}, u32[]{:S(2)}, u32[]{:S(2)}) collective-permute-start(bf16[24,1024]{1,0:T(8,128)(2,1)S(1)} %get-tuple-element.282), channel_id=1, source_target_pairs={{0,28},{1,29},{2,30},{3,31},{4,24},{5,25},{6,26},{7,27},{8,20},{9,... | collective-permute-start | bytes 147464 | tf_op jit(solution)/shard_map/while/body/eval_jaxpr/ppermute | solution.py:59
  89.5 4.9 collective-permute-done.18
  95.2 7.9 %collective-permute-done.19 = bf16[192,1024]{1,0:T(8,128)(2,1)S(1)} collective-permute-done((bf16[192,1024]{1,0:T(8,128)(2,1)S(1)}, bf16[192,1024]{1,0:T(8,128)(2,1)S(1)}, u32[]{:S(2)}, u32[]{:S(2)}) %collective-permute-start.19) | collective-permute-done | bytes 393248 | tf_op jit(solution)/shard_map/while/body/eval_jaxpr/ppermute | solution.py:75
  149.9 9.8 %all-to-all-start = ((f32[32,1,4]{2,1,0:T(1,128)}), f32[32,1,4]{2,1,0:T(1,128)S(1)}, u32[]{:S(2)}, u32[]{:S(2)}) async-start(f32[32,1,4]{2,1,0:T(1,128)} %broadcast_in_dim.4), calls=%async_computation | async-start | bytes 32768 | tf_op jit(solution)/shard_map/while/body/eval_jaxpr/all_to_all | solution.py:36
  159.7 9.3 %all-to-all-done = f32[32,1,4]{2,1,0:T(1,128)S(1)} async-done(((f32[32,1,4]{2,1,0:T(1,128)}), f32[32,1,4]{2,1,0:T(1,128)S(1)}, u32[]{:S(2)}, u32[]{:S(2)}) %all-to-all-start) | async-done | bytes 544 | tf_op jit(solution)/shard_map/while/body/eval_jaxpr/all_to_all | solution.py:36
  176.7 4.8 fusion.63
  189.7 9.5 %collective-permute-done = bf16[192,1024]{1,0:T(8,128)(2,1)} collective-permute-done((bf16[192,1024]{1,0:T(8,128)(2,1)S(1)}, bf16[192,1024]{1,0:T(8,128)(2,1)}, u32[]{:S(2)}, u32[]{:S(2)}) %collective-permute-start) | collective-permute-done | bytes 393248 | tf_op jit(solution)/shard_map/while/body/eval_jaxpr/ppermute | solution.py:59
  199.2 8.4 %collective-permute-done.1 = bf16[192,1024]{1,0:T(8,128)(2,1)} collective-permute-done((bf16[192,1024]{1,0:T(8,128)(2,1)S(1)}, bf16[192,1024]{1,0:T(8,128)(2,1)}, u32[]{:S(2)}, u32[]{:S(2)}) %collective-permute-start.1) | collective-permute-done | bytes 393248 | tf_op jit(solution)/shard_map/while/body/eval_jaxpr/ppermute | solution.py:59
  253.0 4.9 collective-permute-done.18
  258.7 7.9 %collective-permute-done.19 = bf16[192,1024]{1,0:T(8,128)(2,1)S(1)} collective-permute-done((bf16[192,1024]{1,0:T(8,128)(2,1)S(1)}, bf16[192,1024]{1,0:T(8,128)(2,1)S(1)}, u32[]{:S(2)}, u32[]{:S(2)}) %collective-permute-start.19) | collective-permute-done | bytes 393248 | tf_op jit(solution)/shard_map/while/body/eval_jaxpr/ppermute | solution.py:75
  304.1 4.7 collective-permute-done.33
  313.3 7.4 %all-to-all-start = ((f32[32,1,4]{2,1,0:T(1,128)}), f32[32,1,4]{2,1,0:T(1,128)S(1)}, u32[]{:S(2)}, u32[]{:S(2)}) async-start(f32[32,1,4]{2,1,0:T(1,128)} %broadcast_in_dim.4), calls=%async_computation | async-start | bytes 32768 | tf_op jit(solution)/shard_map/while/body/eval_jaxpr/all_to_all | solution.py:36
  320.6 9.3 %all-to-all-done = f32[32,1,4]{2,1,0:T(1,128)S(1)} async-done(((f32[32,1,4]{2,1,0:T(1,128)}), f32[32,1,4]{2,1,0:T(1,128)S(1)}, u32[]{:S(2)}, u32[]{:S(2)}) %all-to-all-start) | async-done | bytes 544 | tf_op jit(solution)/shard_map/while/body/eval_jaxpr/all_to_all | solution.py:36
  338.9 4.8 fusion.63
  351.8 9.5 %collective-permute-done = bf16[192,1024]{1,0:T(8,128)(2,1)} collective-permute-done((bf16[192,1024]{1,0:T(8,128)(2,1)S(1)}, bf16[192,1024]{1,0:T(8,128)(2,1)}, u32[]{:S(2)}, u32[]{:S(2)}) %collective-permute-start) | collective-permute-done | bytes 393248 | tf_op jit(solution)/shard_map/while/body/eval_jaxpr/ppermute | solution.py:59
  361.4 8.4 %collective-permute-done.1 = bf16[192,1024]{1,0:T(8,128)(2,1)} collective-permute-done((bf16[192,1024]{1,0:T(8,128)(2,1)S(1)}, bf16[192,1024]{1,0:T(8,128)(2,1)}, u32[]{:S(2)}, u32[]{:S(2)}) %collective-permute-start.1) | collective-permute-done | bytes 393248 | tf_op jit(solution)/shard_map/while/body/eval_jaxpr/ppermute | solution.py:59
  415.2 4.9 collective-permute-done.18
  420.9 7.9 %collective-permute-done.19 = bf16[192,1024]{1,0:T(8,128)(2,1)S(1)} collective-permute-done((bf16[192,1024]{1,0:T(8,128)(2,1)S(1)}, bf16[192,1024]{1,0:T(8,128)(2,1)S(1)}, u32[]{:S(2)}, u32[]{:S(2)}) %collective-permute-start.19) | collective-permute-done | bytes 393248 | tf_op jit(solution)/shard_map/while/body/eval_jaxpr/ppermute | solution.py:75
  472.9 9.3 %all-to-all-start = ((f32[32,1,4]{2,1,0:T(1,128)}), f32[32,1,4]{2,1,0:T(1,128)S(1)}, u32[]{:S(2)}, u32[]{:S(2)}) async-start(f32[32,1,4]{2,1,0:T(1,128)} %broadcast_in_dim.4), calls=%async_computation | async-start | bytes 32768 | tf_op jit(solution)/shard_map/while/body/eval_jaxpr/all_to_all | solution.py:36
  482.2 9.3 %all-to-all-done = f32[32,1,4]{2,1,0:T(1,128)S(1)} async-done(((f32[32,1,4]{2,1,0:T(1,128)}), f32[32,1,4]{2,1,0:T(1,128)S(1)}, u32[]{:S(2)}, u32[]{:S(2)}) %all-to-all-start) | async-done | bytes 544 | tf_op jit(solution)/shard_map/while/body/eval_jaxpr/all_to_all | solution.py:36
  (393 shorter events, 321.5 us)
Async XLA Ops:
  16.7 13.1 %collective-permute-start = (bf16[192,1024]{1,0:T(8,128)(2,1)S(1)}, bf16[192,1024]{1,0:T(8,128)(2,1)}, u32[]{:S(2)}, u32[]{:S(2)}) collective-permute-start(bf16[192,1024]{1,0:T(8,128)(2,1)S(1)} %get-tuple-element.279), channel_id=1, source_target_pairs={{0,3},{1,2},{2,1},{3,0},{4,7},{5,6},{6,5},{7,4},{8,11},{9,10},{10,... | collective-permute-start | bytes 1179656 | tf_op jit(solution)/shard_map/while/body/eval_jaxpr/ppermute | solution.py:59
  20.9 18.2 %collective-permute-start.1 = (bf16[192,1024]{1,0:T(8,128)(2,1)S(1)}, bf16[192,1024]{1,0:T(8,128)(2,1)}, u32[]{:S(2)}, u32[]{:S(2)}) collective-permute-start(bf16[192,1024]{1,0:T(8,128)(2,1)S(1)} %get-tuple-element.280), channel_id=1, source_target_pairs={{0,2},{1,3},{2,0},{3,1},{4,6},{5,7},{6,4},{7,5},{8,10},{9,11},{10,... | collective-permute-start | bytes 1179656 | tf_op jit(solution)/shard_map/while/body/eval_jaxpr/ppermute | solution.py:59
  22.8 16.3 %collective-permute-start.2 = (bf16[192,1024]{1,0:T(8,128)(2,1)S(1)}, bf16[192,1024]{1,0:T(8,128)(2,1)}, u32[]{:S(2)}, u32[]{:S(2)}) collective-permute-start(bf16[192,1024]{1,0:T(8,128)(2,1)S(1)} %get-tuple-element.281), channel_id=1, source_target_pairs={{0,1},{1,0},{2,3},{3,2},{4,5},{5,4},{6,7},{7,6},{8,9},{9,8},{10,11... | collective-permute-start | bytes 1179656 | tf_op jit(solution)/shard_map/while/body/eval_jaxpr/ppermute | solution.py:59
  40.9 13.3 %collective-permute-start.3 = (bf16[24,1024]{1,0:T(8,128)(2,1)S(1)}, bf16[24,1024]{1,0:T(8,128)(2,1)}, u32[]{:S(2)}, u32[]{:S(2)}) collective-permute-start(bf16[24,1024]{1,0:T(8,128)(2,1)S(1)} %get-tuple-element.282), channel_id=1, source_target_pairs={{0,28},{1,29},{2,30},{3,31},{4,24},{5,25},{6,26},{7,27},{8,20},{9,... | collective-permute-start | bytes 147464 | tf_op jit(solution)/shard_map/while/body/eval_jaxpr/ppermute | solution.py:59
  63.3 11.1 %collective-permute-start.11 = (bf16[24,1024]{1,0:T(8,128)(2,1)S(1)}, bf16[24,1024]{1,0:T(8,128)(2,1)S(1)}, u32[]{:S(2)}, u32[]{:S(2)}) collective-permute-start(bf16[24,1024]{1,0:T(8,128)(2,1)S(1)} %get-tuple-element.290), channel_id=1, source_target_pairs={{0,8},{1,9},{2,10},{3,11},{4,12},{5,13},{6,14},{7,15},{8,0},{9,1},... | collective-permute-start | bytes 147464 | tf_op jit(solution)/shard_map/while/body/eval_jaxpr/ppermute | solution.py:75
  82.3 12.1 %collective-permute-start.18 = (bf16[192,1024]{1,0:T(8,128)(2,1)S(1)}, bf16[192,1024]{1,0:T(8,128)(2,1)S(1)}, u32[]{:S(2)}, u32[]{:S(2)}) collective-permute-start(bf16[192,1024]{1,0:T(8,128)(2,1)S(1)} %constant_dynamic-update-slice_fusion.47), channel_id=1, source_target_pairs={{0,2},{1,3},{2,0},{3,1},{4,6},{5,7},{6,4},{7,5},{8,10},{9,11},{10,... | collective-permute-start | bytes 1179656 | tf_op jit(solution)/shard_map/while/body/eval_jaxpr/ppermute | solution.py:75
  85.0 18.1 %collective-permute-start.19 = (bf16[192,1024]{1,0:T(8,128)(2,1)S(1)}, bf16[192,1024]{1,0:T(8,128)(2,1)S(1)}, u32[]{:S(2)}, u32[]{:S(2)}) collective-permute-start(bf16[192,1024]{1,0:T(8,128)(2,1)S(1)} %constant_dynamic-update-slice_fusion.47), channel_id=1, source_target_pairs={{0,3},{1,2},{2,1},{3,0},{4,7},{5,6},{6,5},{7,4},{8,11},{9,10},{10,... | collective-permute-start | bytes 1179656 | tf_op jit(solution)/shard_map/while/body/eval_jaxpr/ppermute | solution.py:75
  149.9 19.1 %all-to-all-start = ((f32[32,1,4]{2,1,0:T(1,128)}), f32[32,1,4]{2,1,0:T(1,128)S(1)}, u32[]{:S(2)}, u32[]{:S(2)}) async-start(f32[32,1,4]{2,1,0:T(1,128)} %broadcast_in_dim.4), calls=%async_computation | async-start | bytes 32768 | tf_op jit(solution)/shard_map/while/body/eval_jaxpr/all_to_all | solution.py:36
  185.9 13.3 %collective-permute-start = (bf16[192,1024]{1,0:T(8,128)(2,1)S(1)}, bf16[192,1024]{1,0:T(8,128)(2,1)}, u32[]{:S(2)}, u32[]{:S(2)}) collective-permute-start(bf16[192,1024]{1,0:T(8,128)(2,1)S(1)} %get-tuple-element.279), channel_id=1, source_target_pairs={{0,3},{1,2},{2,1},{3,0},{4,7},{5,6},{6,5},{7,4},{8,11},{9,10},{10,... | collective-permute-start | bytes 1179656 | tf_op jit(solution)/shard_map/while/body/eval_jaxpr/ppermute | solution.py:59
  186.9 20.7 %collective-permute-start.1 = (bf16[192,1024]{1,0:T(8,128)(2,1)S(1)}, bf16[192,1024]{1,0:T(8,128)(2,1)}, u32[]{:S(2)}, u32[]{:S(2)}) collective-permute-start(bf16[192,1024]{1,0:T(8,128)(2,1)S(1)} %get-tuple-element.280), channel_id=1, source_target_pairs={{0,2},{1,3},{2,0},{3,1},{4,6},{5,7},{6,4},{7,5},{8,10},{9,11},{10,... | collective-permute-start | bytes 1179656 | tf_op jit(solution)/shard_map/while/body/eval_jaxpr/ppermute | solution.py:59
  189.5 18.1 %collective-permute-start.2 = (bf16[192,1024]{1,0:T(8,128)(2,1)S(1)}, bf16[192,1024]{1,0:T(8,128)(2,1)}, u32[]{:S(2)}, u32[]{:S(2)}) collective-permute-start(bf16[192,1024]{1,0:T(8,128)(2,1)S(1)} %get-tuple-element.281), channel_id=1, source_target_pairs={{0,1},{1,0},{2,3},{3,2},{4,5},{5,4},{6,7},{7,6},{8,9},{9,8},{10,11... | collective-permute-start | bytes 1179656 | tf_op jit(solution)/shard_map/while/body/eval_jaxpr/ppermute | solution.py:59
  209.8 10.2 %collective-permute-start.4 = (bf16[24,1024]{1,0:T(8,128)(2,1)S(1)}, bf16[24,1024]{1,0:T(8,128)(2,1)}, u32[]{:S(2)}, u32[]{:S(2)}) collective-permute-start(bf16[24,1024]{1,0:T(8,128)(2,1)S(1)} %get-tuple-element.283), channel_id=1, source_target_pairs={{0,24},{1,25},{2,26},{3,27},{4,28},{5,29},{6,30},{7,31},{8,16},{9,... | collective-permute-start | bytes 147464 | tf_op jit(solution)/shard_map/while/body/eval_jaxpr/ppermute | solution.py:59
  245.8 12.1 %collective-permute-start.18 = (bf16[192,1024]{1,0:T(8,128)(2,1)S(1)}, bf16[192,1024]{1,0:T(8,128)(2,1)S(1)}, u32[]{:S(2)}, u32[]{:S(2)}) collective-permute-start(bf16[192,1024]{1,0:T(8,128)(2,1)S(1)} %constant_dynamic-update-slice_fusion.47), channel_id=1, source_target_pairs={{0,2},{1,3},{2,0},{3,1},{4,6},{5,7},{6,4},{7,5},{8,10},{9,11},{10,... | collective-permute-start | bytes 1179656 | tf_op jit(solution)/shard_map/while/body/eval_jaxpr/ppermute | solution.py:75
  246.3 20.3 %collective-permute-start.19 = (bf16[192,1024]{1,0:T(8,128)(2,1)S(1)}, bf16[192,1024]{1,0:T(8,128)(2,1)S(1)}, u32[]{:S(2)}, u32[]{:S(2)}) collective-permute-start(bf16[192,1024]{1,0:T(8,128)(2,1)S(1)} %constant_dynamic-update-slice_fusion.47), channel_id=1, source_target_pairs={{0,3},{1,2},{2,1},{3,0},{4,7},{5,6},{6,5},{7,4},{8,11},{9,10},{10,... | collective-permute-start | bytes 1179656 | tf_op jit(solution)/shard_map/while/body/eval_jaxpr/ppermute | solution.py:75
  299.0 9.9 %collective-permute-start.33 = (f32[128,256]{0,1:T(8,128)S(1)}, f32[128,256]{0,1:T(8,128)S(1)}, u32[]{:S(2)}, u32[]{:S(2)}) collective-permute-start(f32[128,256]{0,1:T(8,128)S(1)} %get-tuple-element.298), channel_id=1, source_target_pairs={{0,224},{32,192},{64,160},{96,128},{128,96},{160,64},{192,32},{224... | collective-permute-start | bytes 393224 | tf_op jit(solution)/shard_map/while/body/eval_jaxpr/ppermute | solution.py:75
  313.3 16.7 %all-to-all-start = ((f32[32,1,4]{2,1,0:T(1,128)}), f32[32,1,4]{2,1,0:T(1,128)S(1)}, u32[]{:S(2)}, u32[]{:S(2)}) async-start(f32[32,1,4]{2,1,0:T(1,128)} %broadcast_in_dim.4), calls=%async_computation | async-start | bytes 32768 | tf_op jit(solution)/shard_map/while/body/eval_jaxpr/all_to_all | solution.py:36
  348.1 13.3 %collective-permute-start = (bf16[192,1024]{1,0:T(8,128)(2,1)S(1)}, bf16[192,1024]{1,0:T(8,128)(2,1)}, u32[]{:S(2)}, u32[]{:S(2)}) collective-permute-start(bf16[192,1024]{1,0:T(8,128)(2,1)S(1)} %get-tuple-element.279), channel_id=1, source_target_pairs={{0,3},{1,2},{2,1},{3,0},{4,7},{5,6},{6,5},{7,4},{8,11},{9,10},{10,... | collective-permute-start | bytes 1179656 | tf_op jit(solution)/shard_map/while/body/eval_jaxpr/ppermute | solution.py:59
  349.1 20.7 %collective-permute-start.1 = (bf16[192,1024]{1,0:T(8,128)(2,1)S(1)}, bf16[192,1024]{1,0:T(8,128)(2,1)}, u32[]{:S(2)}, u32[]{:S(2)}) collective-permute-start(bf16[192,1024]{1,0:T(8,128)(2,1)S(1)} %get-tuple-element.280), channel_id=1, source_target_pairs={{0,2},{1,3},{2,0},{3,1},{4,6},{5,7},{6,4},{7,5},{8,10},{9,11},{10,... | collective-permute-start | bytes 1179656 | tf_op jit(solution)/shard_map/while/body/eval_jaxpr/ppermute | solution.py:59
  351.7 18.1 %collective-permute-start.2 = (bf16[192,1024]{1,0:T(8,128)(2,1)S(1)}, bf16[192,1024]{1,0:T(8,128)(2,1)}, u32[]{:S(2)}, u32[]{:S(2)}) collective-permute-start(bf16[192,1024]{1,0:T(8,128)(2,1)S(1)} %get-tuple-element.281), channel_id=1, source_target_pairs={{0,1},{1,0},{2,3},{3,2},{4,5},{5,4},{6,7},{7,6},{8,9},{9,8},{10,11... | collective-permute-start | bytes 1179656 | tf_op jit(solution)/shard_map/while/body/eval_jaxpr/ppermute | solution.py:59
  372.0 10.2 %collective-permute-start.4 = (bf16[24,1024]{1,0:T(8,128)(2,1)S(1)}, bf16[24,1024]{1,0:T(8,128)(2,1)}, u32[]{:S(2)}, u32[]{:S(2)}) collective-permute-start(bf16[24,1024]{1,0:T(8,128)(2,1)S(1)} %get-tuple-element.283), channel_id=1, source_target_pairs={{0,24},{1,25},{2,26},{3,27},{4,28},{5,29},{6,30},{7,31},{8,16},{9,... | collective-permute-start | bytes 147464 | tf_op jit(solution)/shard_map/while/body/eval_jaxpr/ppermute | solution.py:59
  391.9 9.9 %collective-permute-start.12 = (bf16[24,1024]{1,0:T(8,128)(2,1)S(1)}, bf16[24,1024]{1,0:T(8,128)(2,1)S(1)}, u32[]{:S(2)}, u32[]{:S(2)}) collective-permute-start(bf16[24,1024]{1,0:T(8,128)(2,1)S(1)} %get-tuple-element.290), channel_id=1, source_target_pairs={{0,12},{1,13},{2,14},{3,15},{4,8},{5,9},{6,10},{7,11},{8,4},{9,5},... | collective-permute-start | bytes 147464 | tf_op jit(solution)/shard_map/while/body/eval_jaxpr/ppermute | solution.py:75
  408.0 12.1 %collective-permute-start.18 = (bf16[192,1024]{1,0:T(8,128)(2,1)S(1)}, bf16[192,1024]{1,0:T(8,128)(2,1)S(1)}, u32[]{:S(2)}, u32[]{:S(2)}) collective-permute-start(bf16[192,1024]{1,0:T(8,128)(2,1)S(1)} %constant_dynamic-update-slice_fusion.47), channel_id=1, source_target_pairs={{0,2},{1,3},{2,0},{3,1},{4,6},{5,7},{6,4},{7,5},{8,10},{9,11},{10,... | collective-permute-start | bytes 1179656 | tf_op jit(solution)/shard_map/while/body/eval_jaxpr/ppermute | solution.py:75
  408.5 20.3 %collective-permute-start.19 = (bf16[192,1024]{1,0:T(8,128)(2,1)S(1)}, bf16[192,1024]{1,0:T(8,128)(2,1)S(1)}, u32[]{:S(2)}, u32[]{:S(2)}) collective-permute-start(bf16[192,1024]{1,0:T(8,128)(2,1)S(1)} %constant_dynamic-update-slice_fusion.47), channel_id=1, source_target_pairs={{0,3},{1,2},{2,1},{3,0},{4,7},{5,6},{6,5},{7,4},{8,11},{9,10},{10,... | collective-permute-start | bytes 1179656 | tf_op jit(solution)/shard_map/while/body/eval_jaxpr/ppermute | solution.py:75
  472.9 18.6 %all-to-all-start = ((f32[32,1,4]{2,1,0:T(1,128)}), f32[32,1,4]{2,1,0:T(1,128)S(1)}, u32[]{:S(2)}, u32[]{:S(2)}) async-start(f32[32,1,4]{2,1,0:T(1,128)} %broadcast_in_dim.4), calls=%async_computation | async-start | bytes 32768 | tf_op jit(solution)/shard_map/while/body/eval_jaxpr/all_to_all | solution.py:36
  (117 other events, 782.1 us)

commit v6 on v5

--- a/solution.py
+++ b/solution.py
@@ -32,7 +32,10 @@
 
 
 def scalar_sum(values, axis):
-    size = lax.axis_size(axis)
+    names = axis if isinstance(axis, tuple) else (axis,)
+    size = 1
+    for name in names:
+        size *= lax.axis_size(name)
     gathered = lax.all_to_all(jnp.broadcast_to(values[None], (size,) + values.shape), axis, 0, 0)
     return jnp.sum(gathered, axis=0)
 
@@ -78,7 +81,7 @@
     return chunk
 
 
-def fisher_product(direction, normed, hidden_act, slope_act, w_out, metric, width):
+def fisher_product(direction, residual, normed, hidden_act, slope_act, w_out, metric, width):
     tangent = direction.astype(jnp.bfloat16)
     tangent_in = tangent[:, :width]
     tangent_out_t = tangent[:, width:]
@@ -98,9 +101,22 @@
     part_out_t = contract_rows(cotangent, hidden_act)
     part_in = contract_rows(normed, grad_pre)
     dp_groups = digit_groups(lax.axis_size("dp"), 3)
-    fisher_chunk = spread_reduce(jnp.concatenate([part_in, part_out_t], axis=1), "dp", dp_groups, jnp.float32)
+    reduced = spread_reduce(jnp.concatenate([part_in, part_out_t], axis=1), "dp", dp_groups, jnp.float32)
+    rows = reduced.shape[0]
+    start = lax.axis_index("dp") * rows
+    direction_chunk = lax.dynamic_slice_in_dim(direction, start, rows, 0)
+    residual_chunk = lax.dynamic_slice_in_dim(residual, start, rows, 0)
+    fisher_chunk = reduced + damping * direction_chunk
+    sums = jnp.stack(
+        [
+            jnp.sum(direction_chunk * fisher_chunk),
+            jnp.sum(residual_chunk * fisher_chunk),
+            jnp.sum(fisher_chunk * fisher_chunk),
+            jnp.sum(residual_chunk * residual_chunk),
+        ]
+    )
     fisher = spread_gather(fisher_chunk, "dp", dp_groups)
-    return fisher + damping * direction
+    return fisher, scalar_sum(sums, ("dp", "fsdp"))
 
 
 def on_device(states, w_in, w_out, precision, grad_in, grad_out):
@@ -117,16 +133,10 @@
 
     def iterate(_, carry):
         solution_now, residual, direction = carry
-        fisher = fisher_product(direction, normed, hidden_act, slope_act, w_out, metric, width)
-        sums = jnp.stack(
-            [
-                jnp.sum(direction * fisher),
-                jnp.sum(residual * fisher),
-                jnp.sum(fisher * fisher),
-                jnp.sum(residual * residual),
-            ]
+        fisher, sums = fisher_product(
+            direction, residual, normed, hidden_act, slope_act, w_out, metric, width
         )
-        quadratic, cross, fisher_square, norm_now = scalar_sum(sums, "fsdp")
+        quadratic, cross, fisher_square, norm_now = sums
         step_size = norm_now / quadratic
         solution_now = solution_now + step_size * direction
         residual_next = residual - step_size * fisher

time: 506 us -> 490 us (0.968)
  waiting for transfers between devices: 190 us -> 172 us
  matrix products: 39.2 us -> 25.3 us
  starting transfers between devices: 183 us -> 194 us
  local copies, waits for them, and re-layouts: 36.1 us -> 42.6 us
    dynamic_update_slice x51, local copies, waits for them, and re-layouts: 10.4 us -> 20.4 us  [spread_gather(): lax.dynamic_update_slice_in_dim(whole, got, (digit ^ offset) * rows, 0)]
    all_to_all x3, starting transfers between devices: 26.4 us -> 35.9 us  [scalar_sum(): lax.all_to_all(jnp.broadcast_to(values[None], (size,) + values.shape), ax...]
    ppermute x51, waiting for transfers between devices: 73.6 us -> 64.2 us  [spread_gather(): got = lax.ppermute(chunk, axis, xor_pairs(size, offset << low))]
    all_to_all x3, waiting for transfers between devices: 27.9 us -> 20.5 us  [scalar_sum(): lax.all_to_all(jnp.broadcast_to(values[None], (size,) + values.shape), ax...]
    dot_general x6, matrix products: 15.9 us -> 9.14 us  [contract_rows(): lax.dot_general(left_side, right_side, (((0,), (0,)), ((), ())), preferre...]
  transfers between devices with their start and end apart: 105 -> 105, of which waited for: 51 -> 47; matrix products, arithmetic and copies ran while one was open for 3% -> 8% of each run, Pallas kernels for 0% -> 0%
where the time goes in v6:
time: 490 us; the launch traced here: 488 us
  starting transfers between devices  194 us (40%)
  waiting for transfers between devices  172 us (35%)
  local copies, waits for them, and re-layouts  42.6 us (9%)
  other arithmetic  39.5 us (8%)
  matrix products  25.3 us (5%)
  loops' own time  13 us (3%)
    ppermute x51, waiting for transfers between devices, spread_reduce(): lax.ppermute(send.astype(send_type), axis, xor_pairs(size, offset << low))  87.8 us
    ppermute x51, starting transfers between devices, spread_reduce(): lax.ppermute(send.astype(send_type), axis, xor_pairs(size, offset << low))  79.5 us
    ppermute x51, starting transfers between devices, spread_gather(): got = lax.ppermute(chunk, axis, xor_pairs(size, offset << low))  79 us
    ppermute x51, waiting for transfers between devices, spread_gather(): got = lax.ppermute(chunk, axis, xor_pairs(size, offset << low))  64.2 us
    all_to_all x3, starting transfers between devices, scalar_sum(): lax.all_to_all(jnp.broadcast_to(values[None], (size,) + values.shape), ax...  35.9 us
    all_to_all x3, waiting for transfers between devices, scalar_sum(): lax.all_to_all(jnp.broadcast_to(values[None], (size,) + values.shape), ax...  20.5 us
    dynamic_update_slice x51, local copies, waits for them, and re-layouts, spread_gather(): lax.dynamic_update_slice_in_dim(whole, got, (digit ^ offset) * rows, 0)  20.4 us
    another operation x1, loops' own time, on_device(): lax.fori_loop(0, ITERS, iterate, (jnp.zeros_like(residual), residual, res...  13 us
  transfers between devices with their start and end apart: 105, of which 47 were waited for; matrix products, arithmetic and copies ran while one was open for 8% of the time, Pallas kernels for 0%

profile of v6, /device:TPU:1, one launch (start us, length us, event | category | flops | bytes accessed | tf_op | source)
XLA Modules:
  0.0 488.0 jit_solution(5540876309888979861)
XLA Ops:
  7.3 474.8 %while.15 = (s32[]{:T(128)}, f32[1024,256]{0,1:T(8,128)}, f32[1024,256]{0,1:T(8,128)}, f32[1024,256]{0,1:T(8,128)S(1)}, bf16[768,1024]{1,0:T(8,128)(2,1)}, /*ind...) while((s32[]{:T(128)}, f32[1024,256]{0,1:T(8,128)}, ...), condition=%wide.region_7.8_spmd.clone, body=%wide.region_1.7_spmd.clone.sunk | while | flops 1215202304 | bytes 101289504 | solution.py:147
  15.2 4.2 collective-permute-start
  21.4 7.0 %collective-permute-done = bf16[192,1024]{1,0:T(8,128)(2,1)S(1)} collective-permute-done((bf16[192,1024]{1,0:T(8,128)(2,1)S(1)}, bf16[192,1024]{1,0:T(8,128)(2,1)S(1)}, u32[]{:S(2)}, u32[]{:S(2)}) %collective-permute-start) | collective-permute-done | bytes 393248 | tf_op jit(solution)/shard_map/while/body/eval_jaxpr/ppermute | solution.py:62
  28.3 9.2 %collective-permute-done.1 = bf16[192,1024]{1,0:T(8,128)(2,1)S(1)} collective-permute-done((bf16[192,1024]{1,0:T(8,128)(2,1)S(1)}, bf16[192,1024]{1,0:T(8,128)(2,1)S(1)}, u32[]{:S(2)}, u32[]{:S(2)}) %collective-permute-start.1) | collective-permute-done | bytes 393248 | tf_op jit(solution)/shard_map/while/body/eval_jaxpr/ppermute | solution.py:62
  38.9 5.8 %collective-permute-start.3 = (bf16[24,1024]{1,0:T(8,128)(2,1)S(1)}, bf16[24,1024]{1,0:T(8,128)(2,1)S(1)}, u32[]{:S(2)}, u32[]{:S(2)}) collective-permute-start(bf16[24,1024]{1,0:T(8,128)(2,1)S(1)} %get-tuple-element.228), channel_id=1, source_target_pairs={{0,28},{1,29},{2,30},{3,31},{4,24},{5,25},{6,26},{7,27},{8,20},{9,... | collective-permute-start | bytes 147464 | tf_op jit(solution)/shard_map/while/body/eval_jaxpr/ppermute | solution.py:62
  67.3 4.0 collective-permute-start.15
  83.9 7.6 %collective-permute-done.18 = bf16[192,1024]{1,0:T(8,128)(2,1)} collective-permute-done((bf16[192,1024]{1,0:T(8,128)(2,1)S(1)}, bf16[192,1024]{1,0:T(8,128)(2,1)}, u32[]{:S(2)}, u32[]{:S(2)}) %collective-permute-start.18) | collective-permute-done | bytes 393248 | tf_op jit(solution)/shard_map/while/body/eval_jaxpr/ppermute | solution.py:78
  92.5 7.6 %collective-permute-done.19 = bf16[192,1024]{1,0:T(8,128)(2,1)S(1)} collective-permute-done((bf16[192,1024]{1,0:T(8,128)(2,1)S(1)}, bf16[192,1024]{1,0:T(8,128)(2,1)S(1)}, u32[]{:S(2)}, u32[]{:S(2)}) %collective-permute-start.19) | collective-permute-done | bytes 393248 | tf_op jit(solution)/shard_map/while/body/eval_jaxpr/ppermute | solution.py:78
  126.8 11.7 %all-to-all-start = ((f32[256,1,4]{2,1,0:T(1,128)}), f32[256,1,4]{2,1,0:T(1,128)}, u32[]{:S(2)}, u32[]{:S(2)}) async-start(f32[256,1,4]{2,1,0:T(1,128)} %broadcast_in_dim.4), calls=%async_computation | async-start | bytes 262144 | tf_op jit(solution)/shard_map/while/body/eval_jaxpr/all_to_all | solution.py:39
  143.5 6.8 %all-to-all-done = f32[256,1,4]{2,1,0:T(1,128)} async-done(((f32[256,1,4]{2,1,0:T(1,128)}), f32[256,1,4]{2,1,0:T(1,128)}, u32[]{:S(2)}, u32[]{:S(2)}) %all-to-all-start) | async-done | bytes 4128 | tf_op jit(solution)/shard_map/while/body/eval_jaxpr/all_to_all | solution.py:39
  182.7 7.5 %collective-permute-done = bf16[192,1024]{1,0:T(8,128)(2,1)S(1)} collective-permute-done((bf16[192,1024]{1,0:T(8,128)(2,1)S(1)}, bf16[192,1024]{1,0:T(8,128)(2,1)S(1)}, u32[]{:S(2)}, u32[]{:S(2)}) %collective-permute-start) | collective-permute-done | bytes 393248 | tf_op jit(solution)/shard_map/while/body/eval_jaxpr/ppermute | solution.py:62
  190.3 9.2 %collective-permute-done.1 = bf16[192,1024]{1,0:T(8,128)(2,1)S(1)} collective-permute-done((bf16[192,1024]{1,0:T(8,128)(2,1)S(1)}, bf16[192,1024]{1,0:T(8,128)(2,1)S(1)}, u32[]{:S(2)}, u32[]{:S(2)}) %collective-permute-start.1) | collective-permute-done | bytes 393248 | tf_op jit(solution)/shard_map/while/body/eval_jaxpr/ppermute | solution.py:62
  214.1 4.4 collective-permute-done.8
  241.3 7.6 %collective-permute-done.18 = bf16[192,1024]{1,0:T(8,128)(2,1)} collective-permute-done((bf16[192,1024]{1,0:T(8,128)(2,1)S(1)}, bf16[192,1024]{1,0:T(8,128)(2,1)}, u32[]{:S(2)}, u32[]{:S(2)}) %collective-permute-start.18) | collective-permute-done | bytes 393248 | tf_op jit(solution)/shard_map/while/body/eval_jaxpr/ppermute | solution.py:78
  249.9 7.6 %collective-permute-done.19 = bf16[192,1024]{1,0:T(8,128)(2,1)S(1)} collective-permute-done((bf16[192,1024]{1,0:T(8,128)(2,1)S(1)}, bf16[192,1024]{1,0:T(8,128)(2,1)S(1)}, u32[]{:S(2)}, u32[]{:S(2)}) %collective-permute-start.19) | collective-permute-done | bytes 393248 | tf_op jit(solution)/shard_map/while/body/eval_jaxpr/ppermute | solution.py:78
  282.4 12.1 %all-to-all-start = ((f32[256,1,4]{2,1,0:T(1,128)}), f32[256,1,4]{2,1,0:T(1,128)}, u32[]{:S(2)}, u32[]{:S(2)}) async-start(f32[256,1,4]{2,1,0:T(1,128)} %broadcast_in_dim.4), calls=%async_computation | async-start | bytes 262144 | tf_op jit(solution)/shard_map/while/body/eval_jaxpr/all_to_all | solution.py:39
  299.5 6.8 %all-to-all-done = f32[256,1,4]{2,1,0:T(1,128)} async-done(((f32[256,1,4]{2,1,0:T(1,128)}), f32[256,1,4]{2,1,0:T(1,128)}, u32[]{:S(2)}, u32[]{:S(2)}) %all-to-all-start) | async-done | bytes 4128 | tf_op jit(solution)/shard_map/while/body/eval_jaxpr/all_to_all | solution.py:39
  338.7 7.6 %collective-permute-done = bf16[192,1024]{1,0:T(8,128)(2,1)S(1)} collective-permute-done((bf16[192,1024]{1,0:T(8,128)(2,1)S(1)}, bf16[192,1024]{1,0:T(8,128)(2,1)S(1)}, u32[]{:S(2)}, u32[]{:S(2)}) %collective-permute-start) | collective-permute-done | bytes 393248 | tf_op jit(solution)/shard_map/while/body/eval_jaxpr/ppermute | solution.py:62
  346.3 9.2 %collective-permute-done.1 = bf16[192,1024]{1,0:T(8,128)(2,1)S(1)} collective-permute-done((bf16[192,1024]{1,0:T(8,128)(2,1)S(1)}, bf16[192,1024]{1,0:T(8,128)(2,1)S(1)}, u32[]{:S(2)}, u32[]{:S(2)}) %collective-permute-start.1) | collective-permute-done | bytes 393248 | tf_op jit(solution)/shard_map/while/body/eval_jaxpr/ppermute | solution.py:62
  370.1 4.4 collective-permute-done.8
  397.3 7.6 %collective-permute-done.18 = bf16[192,1024]{1,0:T(8,128)(2,1)} collective-permute-done((bf16[192,1024]{1,0:T(8,128)(2,1)S(1)}, bf16[192,1024]{1,0:T(8,128)(2,1)}, u32[]{:S(2)}, u32[]{:S(2)}) %collective-permute-start.18) | collective-permute-done | bytes 393248 | tf_op jit(solution)/shard_map/while/body/eval_jaxpr/ppermute | solution.py:78
  405.9 7.6 %collective-permute-done.19 = bf16[192,1024]{1,0:T(8,128)(2,1)S(1)} collective-permute-done((bf16[192,1024]{1,0:T(8,128)(2,1)S(1)}, bf16[192,1024]{1,0:T(8,128)(2,1)S(1)}, u32[]{:S(2)}, u32[]{:S(2)}) %collective-permute-start.19) | collective-permute-done | bytes 393248 | tf_op jit(solution)/shard_map/while/body/eval_jaxpr/ppermute | solution.py:78
  438.4 12.1 %all-to-all-start = ((f32[256,1,4]{2,1,0:T(1,128)}), f32[256,1,4]{2,1,0:T(1,128)}, u32[]{:S(2)}, u32[]{:S(2)}) async-start(f32[256,1,4]{2,1,0:T(1,128)} %broadcast_in_dim.4), calls=%async_computation | async-start | bytes 262144 | tf_op jit(solution)/shard_map/while/body/eval_jaxpr/all_to_all | solution.py:39
  455.5 6.8 %all-to-all-done = f32[256,1,4]{2,1,0:T(1,128)} async-done(((f32[256,1,4]{2,1,0:T(1,128)}), f32[256,1,4]{2,1,0:T(1,128)}, u32[]{:S(2)}, u32[]{:S(2)}) %all-to-all-start) | async-done | bytes 4128 | tf_op jit(solution)/shard_map/while/body/eval_jaxpr/all_to_all | solution.py:39
  (380 shorter events, 300.0 us)
Async XLA Ops:
  19.4 18.1 %collective-permute-start.1 = (bf16[192,1024]{1,0:T(8,128)(2,1)S(1)}, bf16[192,1024]{1,0:T(8,128)(2,1)S(1)}, u32[]{:S(2)}, u32[]{:S(2)}) collective-permute-start(bf16[192,1024]{1,0:T(8,128)(2,1)S(1)} %get-tuple-element.226), channel_id=1, source_target_pairs={{0,2},{1,3},{2,0},{3,1},{4,6},{5,7},{6,4},{7,5},{8,10},{9,11},{10,... | collective-permute-start | bytes 1179656 | tf_op jit(solution)/shard_map/while/body/eval_jaxpr/ppermute | solution.py:62
  82.0 18.1 %collective-permute-start.19 = (bf16[192,1024]{1,0:T(8,128)(2,1)S(1)}, bf16[192,1024]{1,0:T(8,128)(2,1)S(1)}, u32[]{:S(2)}, u32[]{:S(2)}) collective-permute-start(bf16[192,1024]{1,0:T(8,128)(2,1)S(1)} %constant_dynamic-update-slice_fusion.47), channel_id=1, source_target_pairs={{0,3},{1,2},{2,1},{3,0},{4,7},{5,6},{6,5},{7,4},{8,11},{9,10},{10,... | collective-permute-start | bytes 1179656 | tf_op jit(solution)/shard_map/while/body/eval_jaxpr/ppermute | solution.py:78
  121.0 35.2 %collective-permute-start.27 = (f32[128,256]{0,1:T(8,128)S(1)}, f32[128,256]{0,1:T(8,128)}, u32[]{:S(2)}, u32[]{:S(2)}) collective-permute-start(f32[128,256]{0,1:T(8,128)S(1)} %get-tuple-element.243), channel_id=1, source_target_pairs={{0,32},{32,0},{64,96},{96,64},{128,160},{160,128},{192,224},{224,1... | collective-permute-start | bytes 393224 | tf_op jit(solution)/shard_map/while/body/eval_jaxpr/ppermute | solution.py:78
  126.8 23.5 %all-to-all-start = ((f32[256,1,4]{2,1,0:T(1,128)}), f32[256,1,4]{2,1,0:T(1,128)}, u32[]{:S(2)}, u32[]{:S(2)}) async-start(f32[256,1,4]{2,1,0:T(1,128)} %broadcast_in_dim.4), calls=%async_computation | async-start | bytes 262144 | tf_op jit(solution)/shard_map/while/body/eval_jaxpr/all_to_all | solution.py:39
  138.5 19.7 %collective-permute-start.28 = (f32[128,256]{0,1:T(8,128)S(1)}, f32[128,256]{0,1:T(8,128)}, u32[]{:S(2)}, u32[]{:S(2)}) collective-permute-start(f32[128,256]{0,1:T(8,128)S(1)} %get-tuple-element.243), channel_id=1, source_target_pairs={{0,64},{32,96},{64,0},{96,32},{128,192},{160,224},{192,128},{224,1... | collective-permute-start | bytes 393224 | tf_op jit(solution)/shard_map/while/body/eval_jaxpr/ppermute | solution.py:78
  141.5 20.5 %collective-permute-start.29 = (f32[128,256]{0,1:T(8,128)S(1)}, f32[128,256]{0,1:T(8,128)}, u32[]{:S(2)}, u32[]{:S(2)}) collective-permute-start(f32[128,256]{0,1:T(8,128)S(1)} %get-tuple-element.243), channel_id=1, source_target_pairs={{0,96},{32,64},{64,32},{96,0},{128,224},{160,192},{192,160},{224,1... | collective-permute-start | bytes 393224 | tf_op jit(solution)/shard_map/while/body/eval_jaxpr/ppermute | solution.py:78
  142.3 20.5 %collective-permute-start.30 = (f32[128,256]{0,1:T(8,128)S(1)}, f32[128,256]{0,1:T(8,128)}, u32[]{:S(2)}, u32[]{:S(2)}) collective-permute-start(f32[128,256]{0,1:T(8,128)S(1)} %get-tuple-element.243), channel_id=1, source_target_pairs={{0,128},{32,160},{64,192},{96,224},{128,0},{160,32},{192,64},{224,... | collective-permute-start | bytes 393224 | tf_op jit(solution)/shard_map/while/body/eval_jaxpr/ppermute | solution.py:78
  143.5 20.3 %collective-permute-start.31 = (f32[128,256]{0,1:T(8,128)S(1)}, f32[128,256]{0,1:T(8,128)}, u32[]{:S(2)}, u32[]{:S(2)}) collective-permute-start(f32[128,256]{0,1:T(8,128)S(1)} %get-tuple-element.243), channel_id=1, source_target_pairs={{0,160},{32,128},{64,224},{96,192},{128,32},{160,0},{192,96},{224,... | collective-permute-start | bytes 393224 | tf_op jit(solution)/shard_map/while/body/eval_jaxpr/ppermute | solution.py:78
  180.8 18.7 %collective-permute-start.1 = (bf16[192,1024]{1,0:T(8,128)(2,1)S(1)}, bf16[192,1024]{1,0:T(8,128)(2,1)S(1)}, u32[]{:S(2)}, u32[]{:S(2)}) collective-permute-start(bf16[192,1024]{1,0:T(8,128)(2,1)S(1)} %get-tuple-element.226), channel_id=1, source_target_pairs={{0,2},{1,3},{2,0},{3,1},{4,6},{5,7},{6,4},{7,5},{8,10},{9,11},{10,... | collective-permute-start | bytes 1179656 | tf_op jit(solution)/shard_map/while/body/eval_jaxpr/ppermute | solution.py:62
  238.3 19.2 %collective-permute-start.19 = (bf16[192,1024]{1,0:T(8,128)(2,1)S(1)}, bf16[192,1024]{1,0:T(8,128)(2,1)S(1)}, u32[]{:S(2)}, u32[]{:S(2)}) collective-permute-start(bf16[192,1024]{1,0:T(8,128)(2,1)S(1)} %constant_dynamic-update-slice_fusion.47), channel_id=1, source_target_pairs={{0,3},{1,2},{2,1},{3,0},{4,7},{5,6},{6,5},{7,4},{8,11},{9,10},{10,... | collective-permute-start | bytes 1179656 | tf_op jit(solution)/shard_map/while/body/eval_jaxpr/ppermute | solution.py:78
  276.6 35.5 %collective-permute-start.27 = (f32[128,256]{0,1:T(8,128)S(1)}, f32[128,256]{0,1:T(8,128)}, u32[]{:S(2)}, u32[]{:S(2)}) collective-permute-start(f32[128,256]{0,1:T(8,128)S(1)} %get-tuple-element.243), channel_id=1, source_target_pairs={{0,32},{32,0},{64,96},{96,64},{128,160},{160,128},{192,224},{224,1... | collective-permute-start | bytes 393224 | tf_op jit(solution)/shard_map/while/body/eval_jaxpr/ppermute | solution.py:78
  282.4 24.0 %all-to-all-start = ((f32[256,1,4]{2,1,0:T(1,128)}), f32[256,1,4]{2,1,0:T(1,128)}, u32[]{:S(2)}, u32[]{:S(2)}) async-start(f32[256,1,4]{2,1,0:T(1,128)} %broadcast_in_dim.4), calls=%async_computation | async-start | bytes 262144 | tf_op jit(solution)/shard_map/while/body/eval_jaxpr/all_to_all | solution.py:39
  294.5 19.7 %collective-permute-start.28 = (f32[128,256]{0,1:T(8,128)S(1)}, f32[128,256]{0,1:T(8,128)}, u32[]{:S(2)}, u32[]{:S(2)}) collective-permute-start(f32[128,256]{0,1:T(8,128)S(1)} %get-tuple-element.243), channel_id=1, source_target_pairs={{0,64},{32,96},{64,0},{96,32},{128,192},{160,224},{192,128},{224,1... | collective-permute-start | bytes 393224 | tf_op jit(solution)/shard_map/while/body/eval_jaxpr/ppermute | solution.py:78
  297.5 20.5 %collective-permute-start.29 = (f32[128,256]{0,1:T(8,128)S(1)}, f32[128,256]{0,1:T(8,128)}, u32[]{:S(2)}, u32[]{:S(2)}) collective-permute-start(f32[128,256]{0,1:T(8,128)S(1)} %get-tuple-element.243), channel_id=1, source_target_pairs={{0,96},{32,64},{64,32},{96,0},{128,224},{160,192},{192,160},{224,1... | collective-permute-start | bytes 393224 | tf_op jit(solution)/shard_map/while/body/eval_jaxpr/ppermute | solution.py:78
  298.3 20.5 %collective-permute-start.30 = (f32[128,256]{0,1:T(8,128)S(1)}, f32[128,256]{0,1:T(8,128)}, u32[]{:S(2)}, u32[]{:S(2)}) collective-permute-start(f32[128,256]{0,1:T(8,128)S(1)} %get-tuple-element.243), channel_id=1, source_target_pairs={{0,128},{32,160},{64,192},{96,224},{128,0},{160,32},{192,64},{224,... | collective-permute-start | bytes 393224 | tf_op jit(solution)/shard_map/while/body/eval_jaxpr/ppermute | solution.py:78
  299.5 20.3 %collective-permute-start.31 = (f32[128,256]{0,1:T(8,128)S(1)}, f32[128,256]{0,1:T(8,128)}, u32[]{:S(2)}, u32[]{:S(2)}) collective-permute-start(f32[128,256]{0,1:T(8,128)S(1)} %get-tuple-element.243), channel_id=1, source_target_pairs={{0,160},{32,128},{64,224},{96,192},{128,32},{160,0},{192,96},{224,... | collective-permute-start | bytes 393224 | tf_op jit(solution)/shard_map/while/body/eval_jaxpr/ppermute | solution.py:78
  336.8 18.7 %collective-permute-start.1 = (bf16[192,1024]{1,0:T(8,128)(2,1)S(1)}, bf16[192,1024]{1,0:T(8,128)(2,1)S(1)}, u32[]{:S(2)}, u32[]{:S(2)}) collective-permute-start(bf16[192,1024]{1,0:T(8,128)(2,1)S(1)} %get-tuple-element.226), channel_id=1, source_target_pairs={{0,2},{1,3},{2,0},{3,1},{4,6},{5,7},{6,4},{7,5},{8,10},{9,11},{10,... | collective-permute-start | bytes 1179656 | tf_op jit(solution)/shard_map/while/body/eval_jaxpr/ppermute | solution.py:62
  394.3 19.2 %collective-permute-start.19 = (bf16[192,1024]{1,0:T(8,128)(2,1)S(1)}, bf16[192,1024]{1,0:T(8,128)(2,1)S(1)}, u32[]{:S(2)}, u32[]{:S(2)}) collective-permute-start(bf16[192,1024]{1,0:T(8,128)(2,1)S(1)} %constant_dynamic-update-slice_fusion.47), channel_id=1, source_target_pairs={{0,3},{1,2},{2,1},{3,0},{4,7},{5,6},{6,5},{7,4},{8,11},{9,10},{10,... | collective-permute-start | bytes 1179656 | tf_op jit(solution)/shard_map/while/body/eval_jaxpr/ppermute | solution.py:78
  432.6 35.6 %collective-permute-start.27 = (f32[128,256]{0,1:T(8,128)S(1)}, f32[128,256]{0,1:T(8,128)}, u32[]{:S(2)}, u32[]{:S(2)}) collective-permute-start(f32[128,256]{0,1:T(8,128)S(1)} %get-tuple-element.243), channel_id=1, source_target_pairs={{0,32},{32,0},{64,96},{96,64},{128,160},{160,128},{192,224},{224,1... | collective-permute-start | bytes 393224 | tf_op jit(solution)/shard_map/while/body/eval_jaxpr/ppermute | solution.py:78
  438.4 24.0 %all-to-all-start = ((f32[256,1,4]{2,1,0:T(1,128)}), f32[256,1,4]{2,1,0:T(1,128)}, u32[]{:S(2)}, u32[]{:S(2)}) async-start(f32[256,1,4]{2,1,0:T(1,128)} %broadcast_in_dim.4), calls=%async_computation | async-start | bytes 262144 | tf_op jit(solution)/shard_map/while/body/eval_jaxpr/all_to_all | solution.py:39
  450.5 19.7 %collective-permute-start.28 = (f32[128,256]{0,1:T(8,128)S(1)}, f32[128,256]{0,1:T(8,128)}, u32[]{:S(2)}, u32[]{:S(2)}) collective-permute-start(f32[128,256]{0,1:T(8,128)S(1)} %get-tuple-element.243), channel_id=1, source_target_pairs={{0,64},{32,96},{64,0},{96,32},{128,192},{160,224},{192,128},{224,1... | collective-permute-start | bytes 393224 | tf_op jit(solution)/shard_map/while/body/eval_jaxpr/ppermute | solution.py:78
  453.5 20.5 %collective-permute-start.29 = (f32[128,256]{0,1:T(8,128)S(1)}, f32[128,256]{0,1:T(8,128)}, u32[]{:S(2)}, u32[]{:S(2)}) collective-permute-start(f32[128,256]{0,1:T(8,128)S(1)} %get-tuple-element.243), channel_id=1, source_target_pairs={{0,96},{32,64},{64,32},{96,0},{128,224},{160,192},{192,160},{224,1... | collective-permute-start | bytes 393224 | tf_op jit(solution)/shard_map/while/body/eval_jaxpr/ppermute | solution.py:78
  454.3 20.5 %collective-permute-start.30 = (f32[128,256]{0,1:T(8,128)S(1)}, f32[128,256]{0,1:T(8,128)}, u32[]{:S(2)}, u32[]{:S(2)}) collective-permute-start(f32[128,256]{0,1:T(8,128)S(1)} %get-tuple-element.243), channel_id=1, source_target_pairs={{0,128},{32,160},{64,192},{96,224},{128,0},{160,32},{192,64},{224,... | collective-permute-start | bytes 393224 | tf_op jit(solution)/shard_map/while/body/eval_jaxpr/ppermute | solution.py:78
  455.5 20.3 %collective-permute-start.31 = (f32[128,256]{0,1:T(8,128)S(1)}, f32[128,256]{0,1:T(8,128)}, u32[]{:S(2)}, u32[]{:S(2)}) collective-permute-start(f32[128,256]{0,1:T(8,128)S(1)} %get-tuple-element.243), channel_id=1, source_target_pairs={{0,160},{32,128},{64,224},{96,192},{128,32},{160,0},{192,96},{224,... | collective-permute-start | bytes 393224 | tf_op jit(solution)/shard_map/while/body/eval_jaxpr/ppermute | solution.py:78
  (112 other events, 1089.9 us)

commit v7 on v6

--- a/solution.py
+++ b/solution.py
@@ -85,14 +85,34 @@
     tangent = direction.astype(jnp.bfloat16)
     tangent_in = tangent[:, :width]
     tangent_out_t = tangent[:, width:]
-    pre_tangent = jnp.dot(normed, tangent_in, preferred_element_type=jnp.float32)
-    inner_tangent = (slope_act * pre_tangent).astype(jnp.bfloat16)
-    partial_out = jnp.dot(inner_tangent, w_out, preferred_element_type=jnp.float32)
-    partial_out = partial_out + lax.dot_general(
-        hidden_act, tangent_out_t, (((1,), (1,)), ((), ())), preferred_element_type=jnp.float32
-    )
-    fsdp_groups = digit_groups(lax.axis_size("fsdp"), 2)
-    out_chunk = spread_reduce(partial_out.astype(jnp.bfloat16), "fsdp", fsdp_groups, jnp.bfloat16)
+
+    def block_term(start, rows):
+        normed_rows = lax.dynamic_slice_in_dim(normed, start, rows, 0)
+        slope_rows = lax.dynamic_slice_in_dim(slope_act, start, rows, 0)
+        hidden_rows = lax.dynamic_slice_in_dim(hidden_act, start, rows, 0)
+        pre_tangent = jnp.dot(normed_rows, tangent_in, preferred_element_type=jnp.float32)
+        inner_tangent = (slope_rows * pre_tangent).astype(jnp.bfloat16)
+        term = jnp.dot(inner_tangent, w_out, preferred_element_type=jnp.float32)
+        term = term + lax.dot_general(
+            hidden_rows, tangent_out_t, (((1,), (1,)), ((), ())), preferred_element_type=jnp.float32
+        )
+        return term.astype(jnp.bfloat16)
+
+    fsdp_size = lax.axis_size("fsdp")
+    fsdp_groups = digit_groups(fsdp_size, 2)
+    (low, bits), later_groups = fsdp_groups[0], fsdp_groups[1:]
+    group = 1 << bits
+    digit = (lax.axis_index("fsdp") >> low) & (group - 1)
+    rows = normed.shape[0] // group
+    received = []
+    for offset in range(1, group):
+        send = block_term((digit ^ offset) * rows, rows)
+        received.append(lax.ppermute(send, "fsdp", xor_pairs(fsdp_size, offset << low)))
+    out_chunk = block_term(digit * rows, rows).astype(jnp.float32)
+    for got in received:
+        out_chunk = out_chunk + got.astype(jnp.float32)
+    if later_groups:
+        out_chunk = spread_reduce(out_chunk, "fsdp", later_groups, jnp.bfloat16)
     cotangent = spread_gather((out_chunk * metric).astype(jnp.bfloat16), "fsdp", fsdp_groups)
     back_act = lax.dot_general(
         cotangent, w_out, (((1,), (1,)), ((), ())), preferred_element_type=jnp.float32

time: 490 us -> 492 us (level)
  matrix products: 25.3 us -> 55.5 us
  waiting for transfers between devices: 172 us -> 153 us
  starting transfers between devices: 194 us -> 188 us
    ppermute x51 -> x42, waiting for transfers between devices: 87.8 us -> 37.5 us  [spread_reduce(): lax.ppermute(send.astype(send_type), axis, xor_pairs(size, offset << low))]
    dot_general x6 -> x24, matrix products: 14.8 us -> 43.1 us  [the longest x12 24.6 us: block_term(): lax.dot_general(hidden_rows, tangent_out_t, (((1,), (1,)), ((), ())), pre...]
    ppermute x0 -> x9, waiting for transfers between devices: none -> 23.8 us  [fisher_product(): lax.ppermute(send, 'fsdp', xor_pairs(fsdp_size, offset << low))]
    ppermute x0 -> x9, starting transfers between devices: none -> 15.4 us  [fisher_product(): lax.ppermute(send, 'fsdp', xor_pairs(fsdp_size, offset << low))]
    ppermute x51 -> x42, starting transfers between devices: 79.5 us -> 64.1 us  [spread_reduce(): lax.ppermute(send.astype(send_type), axis, xor_pairs(size, offset << low))]
    while x51 -> x27, local copies, waits for them, and re-layouts: 8.84 us -> 3.43 us
  transfers between devices with their start and end apart: 105 -> 105, of which waited for: 47 -> 44; matrix products, arithmetic and copies ran while one was open for 8% -> 13% of each run, Pallas kernels for 0% -> 0%
where the time goes in v7:
time: 492 us; the launch traced here: 491 us
  starting transfers between devices  188 us (38%)
  waiting for transfers between devices  153 us (31%)
  matrix products  55.5 us (11%)
  other arithmetic  42.4 us (9%)
  local copies, waits for them, and re-layouts  38.1 us (8%)
  loops' own time  12.5 us (3%)
    ppermute x51, starting transfers between devices, spread_gather(): got = lax.ppermute(chunk, axis, xor_pairs(size, offset << low))  77.5 us
    ppermute x51, waiting for transfers between devices, spread_gather(): got = lax.ppermute(chunk, axis, xor_pairs(size, offset << low))  68.6 us
    ppermute x42, starting transfers between devices, spread_reduce(): lax.ppermute(send.astype(send_type), axis, xor_pairs(size, offset << low))  64.1 us
    ppermute x42, waiting for transfers between devices, spread_reduce(): lax.ppermute(send.astype(send_type), axis, xor_pairs(size, offset << low))  37.5 us
    all_to_all x3, starting transfers between devices, scalar_sum(): lax.all_to_all(jnp.broadcast_to(values[None], (size,) + values.shape), ax...  31.2 us
    dot_general x12, matrix products, block_term(): lax.dot_general(hidden_rows, tangent_out_t, (((1,), (1,)), ((), ())), pre...  24.6 us
    ppermute x9, waiting for transfers between devices, fisher_product(): lax.ppermute(send, 'fsdp', xor_pairs(fsdp_size, offset << low))  23.8 us
    all_to_all x3, waiting for transfers between devices, scalar_sum(): lax.all_to_all(jnp.broadcast_to(values[None], (size,) + values.shape), ax...  23.1 us
  transfers between devices with their start and end apart: 105, of which 44 were waited for; matrix products, arithmetic and copies ran while one was open for 13% of the time, Pallas kernels for 0%

profile of v7, /device:TPU:1, one launch (start us, length us, event | category | flops | bytes accessed | tf_op | source)
XLA Modules:
  0.0 490.5 jit_solution(5194984121422890710)
XLA Ops:
  8.7 475.9 %while.15 = (s32[]{:T(128)}, f32[1024,256]{0,1:T(8,128)}, f32[1024,256]{0,1:T(8,128)}, f32[1024,256]{0,1:T(8,128)}, f32[768,128]{1,0:T(8,128)S(1)}, /*index=5*/b...) while((s32[]{:T(128)}, f32[1024,256]{0,1:T(8,128)}, ...), condition=%wide.region_7.8_spmd.clone, body=%wide.region_1.7_spmd.clone.sunk | while | flops 1214612480 | bytes 79928656 | solution.py:167
  14.3 4.1 collective-permute-start
  29.3 7.6 %collective-permute-done.1 = bf16[192,1024]{1,0:T(8,128)(2,1)} collective-permute-done((bf16[192,1024]{1,0:T(8,128)(2,1)}, bf16[192,1024]{1,0:T(8,128)(2,1)}, u32[]{:S(2)}, u32[]{:S(2)}) %collective-permute-start.1) | collective-permute-done | bytes 393248 | tf_op jit(solution)/shard_map/while/body/eval_jaxpr/ppermute | solution.py:110
  38.8 5.8 %collective-permute-start.3 = (bf16[24,1024]{1,0:T(8,128)(2,1)S(1)}, bf16[24,1024]{1,0:T(8,128)(2,1)S(1)}, u32[]{:S(2)}, u32[]{:S(2)}) collective-permute-start(bf16[24,1024]{1,0:T(8,128)(2,1)S(1)} %get-tuple-element.219), channel_id=1, source_target_pairs={{0,28},{1,29},{2,30},{3,31},{4,24},{5,25},{6,26},{7,27},{8,20},{9,... | collective-permute-start | bytes 147464 | tf_op jit(solution)/shard_map/while/body/eval_jaxpr/ppermute | solution.py:62
  67.1 4.0 collective-permute-start.15
  83.6 7.7 %collective-permute-done.18 = bf16[192,1024]{1,0:T(8,128)(2,1)} collective-permute-done((bf16[192,1024]{1,0:T(8,128)(2,1)S(1)}, bf16[192,1024]{1,0:T(8,128)(2,1)}, u32[]{:S(2)}, u32[]{:S(2)}) %collective-permute-start.18) | collective-permute-done | bytes 393248 | tf_op jit(solution)/shard_map/while/body/eval_jaxpr/ppermute | solution.py:78
  92.3 7.6 %collective-permute-done.19 = bf16[192,1024]{1,0:T(8,128)(2,1)S(1)} collective-permute-done((bf16[192,1024]{1,0:T(8,128)(2,1)S(1)}, bf16[192,1024]{1,0:T(8,128)(2,1)S(1)}, u32[]{:S(2)}, u32[]{:S(2)}) %collective-permute-start.19) | collective-permute-done | bytes 393248 | tf_op jit(solution)/shard_map/while/body/eval_jaxpr/ppermute | solution.py:78
  129.1 10.7 %all-to-all-start = ((f32[256,1,4]{2,1,0:T(1,128)}), f32[256,1,4]{2,1,0:T(1,128)S(1)}, u32[]{:S(2)}, u32[]{:S(2)}) async-start(f32[256,1,4]{2,1,0:T(1,128)} %broadcast_in_dim.4), calls=%async_computation | async-start | bytes 262144 | tf_op jit(solution)/shard_map/while/body/eval_jaxpr/all_to_all | solution.py:39
  144.8 7.7 %all-to-all-done = f32[256,1,4]{2,1,0:T(1,128)S(1)} async-done(((f32[256,1,4]{2,1,0:T(1,128)}), f32[256,1,4]{2,1,0:T(1,128)S(1)}, u32[]{:S(2)}, u32[]{:S(2)}) %all-to-all-start) | async-done | bytes 4128 | tf_op jit(solution)/shard_map/while/body/eval_jaxpr/all_to_all | solution.py:39
  167.5 4.1 multiply_add_fusion.2
  190.8 8.1 %collective-permute-done.1 = bf16[192,1024]{1,0:T(8,128)(2,1)} collective-permute-done((bf16[192,1024]{1,0:T(8,128)(2,1)}, bf16[192,1024]{1,0:T(8,128)(2,1)}, u32[]{:S(2)}, u32[]{:S(2)}) %collective-permute-start.1) | collective-permute-done | bytes 393248 | tf_op jit(solution)/shard_map/while/body/eval_jaxpr/ppermute | solution.py:110
  214.0 4.1 collective-permute-done.8
  241.1 7.7 %collective-permute-done.18 = bf16[192,1024]{1,0:T(8,128)(2,1)} collective-permute-done((bf16[192,1024]{1,0:T(8,128)(2,1)S(1)}, bf16[192,1024]{1,0:T(8,128)(2,1)}, u32[]{:S(2)}, u32[]{:S(2)}) %collective-permute-start.18) | collective-permute-done | bytes 393248 | tf_op jit(solution)/shard_map/while/body/eval_jaxpr/ppermute | solution.py:78
  249.7 7.6 %collective-permute-done.19 = bf16[192,1024]{1,0:T(8,128)(2,1)S(1)} collective-permute-done((bf16[192,1024]{1,0:T(8,128)(2,1)S(1)}, bf16[192,1024]{1,0:T(8,128)(2,1)S(1)}, u32[]{:S(2)}, u32[]{:S(2)}) %collective-permute-start.19) | collective-permute-done | bytes 393248 | tf_op jit(solution)/shard_map/while/body/eval_jaxpr/ppermute | solution.py:78
  285.7 10.2 %all-to-all-start = ((f32[256,1,4]{2,1,0:T(1,128)}), f32[256,1,4]{2,1,0:T(1,128)S(1)}, u32[]{:S(2)}, u32[]{:S(2)}) async-start(f32[256,1,4]{2,1,0:T(1,128)} %broadcast_in_dim.4), calls=%async_computation | async-start | bytes 262144 | tf_op jit(solution)/shard_map/while/body/eval_jaxpr/all_to_all | solution.py:39
  301.0 7.7 %all-to-all-done = f32[256,1,4]{2,1,0:T(1,128)S(1)} async-done(((f32[256,1,4]{2,1,0:T(1,128)}), f32[256,1,4]{2,1,0:T(1,128)S(1)}, u32[]{:S(2)}, u32[]{:S(2)}) %all-to-all-start) | async-done | bytes 4128 | tf_op jit(solution)/shard_map/while/body/eval_jaxpr/all_to_all | solution.py:39
  323.6 4.4 multiply_add_fusion.2
  347.3 8.1 %collective-permute-done.1 = bf16[192,1024]{1,0:T(8,128)(2,1)} collective-permute-done((bf16[192,1024]{1,0:T(8,128)(2,1)}, bf16[192,1024]{1,0:T(8,128)(2,1)}, u32[]{:S(2)}, u32[]{:S(2)}) %collective-permute-start.1) | collective-permute-done | bytes 393248 | tf_op jit(solution)/shard_map/while/body/eval_jaxpr/ppermute | solution.py:110
  370.5 4.0 collective-permute-done.8
  397.5 7.7 %collective-permute-done.18 = bf16[192,1024]{1,0:T(8,128)(2,1)} collective-permute-done((bf16[192,1024]{1,0:T(8,128)(2,1)S(1)}, bf16[192,1024]{1,0:T(8,128)(2,1)}, u32[]{:S(2)}, u32[]{:S(2)}) %collective-permute-start.18) | collective-permute-done | bytes 393248 | tf_op jit(solution)/shard_map/while/body/eval_jaxpr/ppermute | solution.py:78
  406.2 7.6 %collective-permute-done.19 = bf16[192,1024]{1,0:T(8,128)(2,1)S(1)} collective-permute-done((bf16[192,1024]{1,0:T(8,128)(2,1)S(1)}, bf16[192,1024]{1,0:T(8,128)(2,1)S(1)}, u32[]{:S(2)}, u32[]{:S(2)}) %collective-permute-start.19) | collective-permute-done | bytes 393248 | tf_op jit(solution)/shard_map/while/body/eval_jaxpr/ppermute | solution.py:78
  442.2 10.2 %all-to-all-start = ((f32[256,1,4]{2,1,0:T(1,128)}), f32[256,1,4]{2,1,0:T(1,128)S(1)}, u32[]{:S(2)}, u32[]{:S(2)}) async-start(f32[256,1,4]{2,1,0:T(1,128)} %broadcast_in_dim.4), calls=%async_computation | async-start | bytes 262144 | tf_op jit(solution)/shard_map/while/body/eval_jaxpr/all_to_all | solution.py:39
  457.5 7.7 %all-to-all-done = f32[256,1,4]{2,1,0:T(1,128)S(1)} async-done(((f32[256,1,4]{2,1,0:T(1,128)}), f32[256,1,4]{2,1,0:T(1,128)S(1)}, u32[]{:S(2)}, u32[]{:S(2)}) %all-to-all-start) | async-done | bytes 4128 | tf_op jit(solution)/shard_map/while/body/eval_jaxpr/all_to_all | solution.py:39
  480.1 4.4 multiply_add_fusion.2
  (366 shorter events, 318.4 us)
Async XLA Ops:
  14.3 14.9 %collective-permute-start = (bf16[192,1024]{1,0:T(8,128)(2,1)}, bf16[192,1024]{1,0:T(8,128)(2,1)}, u32[]{:S(2)}, u32[]{:S(2)}) collective-permute-start(bf16[192,1024]{1,0:T(8,128)(2,1)} %fusion.150), channel_id=1, source_target_pairs={{0,3},{1,2},{2,1},{3,0},{4,7},{5,6},{6,5},{7,4},{8,11},{9,10},{10,... | collective-permute-start | bytes 1179656 | tf_op jit(solution)/shard_map/while/body/eval_jaxpr/ppermute | solution.py:110
  81.8 18.1 %collective-permute-start.19 = (bf16[192,1024]{1,0:T(8,128)(2,1)S(1)}, bf16[192,1024]{1,0:T(8,128)(2,1)S(1)}, u32[]{:S(2)}, u32[]{:S(2)}) collective-permute-start(bf16[192,1024]{1,0:T(8,128)(2,1)S(1)} %constant_dynamic-update-slice_fusion.47), channel_id=1, source_target_pairs={{0,3},{1,2},{2,1},{3,0},{4,7},{5,6},{6,5},{7,4},{8,11},{9,10},{10,... | collective-permute-start | bytes 1179656 | tf_op jit(solution)/shard_map/while/body/eval_jaxpr/ppermute | solution.py:78
  123.2 34.1 %collective-permute-start.27 = (f32[128,256]{0,1:T(8,128)S(1)}, f32[128,256]{0,1:T(8,128)S(1)}, u32[]{:S(2)}, u32[]{:S(2)}) collective-permute-start(f32[128,256]{0,1:T(8,128)S(1)} %get-tuple-element.234), channel_id=1, source_target_pairs={{0,32},{32,0},{64,96},{96,64},{128,160},{160,128},{192,224},{224,1... | collective-permute-start | bytes 393224 | tf_op jit(solution)/shard_map/while/body/eval_jaxpr/ppermute | solution.py:78
  129.1 23.4 %all-to-all-start = ((f32[256,1,4]{2,1,0:T(1,128)}), f32[256,1,4]{2,1,0:T(1,128)S(1)}, u32[]{:S(2)}, u32[]{:S(2)}) async-start(f32[256,1,4]{2,1,0:T(1,128)} %broadcast_in_dim.4), calls=%async_computation | async-start | bytes 262144 | tf_op jit(solution)/shard_map/while/body/eval_jaxpr/all_to_all | solution.py:39
  139.8 19.4 %collective-permute-start.28 = (f32[128,256]{0,1:T(8,128)S(1)}, f32[128,256]{0,1:T(8,128)S(1)}, u32[]{:S(2)}, u32[]{:S(2)}) collective-permute-start(f32[128,256]{0,1:T(8,128)S(1)} %get-tuple-element.234), channel_id=1, source_target_pairs={{0,64},{32,96},{64,0},{96,32},{128,192},{160,224},{192,128},{224,1... | collective-permute-start | bytes 393224 | tf_op jit(solution)/shard_map/while/body/eval_jaxpr/ppermute | solution.py:78
  142.7 19.7 %collective-permute-start.29 = (f32[128,256]{0,1:T(8,128)S(1)}, f32[128,256]{0,1:T(8,128)S(1)}, u32[]{:S(2)}, u32[]{:S(2)}) collective-permute-start(f32[128,256]{0,1:T(8,128)S(1)} %get-tuple-element.234), channel_id=1, source_target_pairs={{0,96},{32,64},{64,32},{96,0},{128,224},{160,192},{192,160},{224,1... | collective-permute-start | bytes 393224 | tf_op jit(solution)/shard_map/while/body/eval_jaxpr/ppermute | solution.py:78
  143.6 19.4 %collective-permute-start.30 = (f32[128,256]{0,1:T(8,128)S(1)}, f32[128,256]{0,1:T(8,128)S(1)}, u32[]{:S(2)}, u32[]{:S(2)}) collective-permute-start(f32[128,256]{0,1:T(8,128)S(1)} %get-tuple-element.234), channel_id=1, source_target_pairs={{0,128},{32,160},{64,192},{96,224},{128,0},{160,32},{192,64},{224,... | collective-permute-start | bytes 393224 | tf_op jit(solution)/shard_map/while/body/eval_jaxpr/ppermute | solution.py:78
  144.8 19.0 %collective-permute-start.31 = (f32[128,256]{0,1:T(8,128)S(1)}, f32[128,256]{0,1:T(8,128)S(1)}, u32[]{:S(2)}, u32[]{:S(2)}) collective-permute-start(f32[128,256]{0,1:T(8,128)S(1)} %get-tuple-element.234), channel_id=1, source_target_pairs={{0,160},{32,128},{64,224},{96,192},{128,32},{160,0},{192,96},{224,... | collective-permute-start | bytes 393224 | tf_op jit(solution)/shard_map/while/body/eval_jaxpr/ppermute | solution.py:78
  183.8 15.1 %collective-permute-start.1 = (bf16[192,1024]{1,0:T(8,128)(2,1)}, bf16[192,1024]{1,0:T(8,128)(2,1)}, u32[]{:S(2)}, u32[]{:S(2)}) collective-permute-start(bf16[192,1024]{1,0:T(8,128)(2,1)} %fusion.152), channel_id=1, source_target_pairs={{0,2},{1,3},{2,0},{3,1},{4,6},{5,7},{6,4},{7,5},{8,10},{9,11},{10,... | collective-permute-start | bytes 1179656 | tf_op jit(solution)/shard_map/while/body/eval_jaxpr/ppermute | solution.py:110
  238.2 19.1 %collective-permute-start.19 = (bf16[192,1024]{1,0:T(8,128)(2,1)S(1)}, bf16[192,1024]{1,0:T(8,128)(2,1)S(1)}, u32[]{:S(2)}, u32[]{:S(2)}) collective-permute-start(bf16[192,1024]{1,0:T(8,128)(2,1)S(1)} %constant_dynamic-update-slice_fusion.47), channel_id=1, source_target_pairs={{0,3},{1,2},{2,1},{3,0},{4,7},{5,6},{6,5},{7,4},{8,11},{9,10},{10,... | collective-permute-start | bytes 1179656 | tf_op jit(solution)/shard_map/while/body/eval_jaxpr/ppermute | solution.py:78
  279.1 34.4 %collective-permute-start.27 = (f32[128,256]{0,1:T(8,128)S(1)}, f32[128,256]{0,1:T(8,128)S(1)}, u32[]{:S(2)}, u32[]{:S(2)}) collective-permute-start(f32[128,256]{0,1:T(8,128)S(1)} %get-tuple-element.234), channel_id=1, source_target_pairs={{0,32},{32,0},{64,96},{96,64},{128,160},{160,128},{192,224},{224,1... | collective-permute-start | bytes 393224 | tf_op jit(solution)/shard_map/while/body/eval_jaxpr/ppermute | solution.py:78
  285.7 23.0 %all-to-all-start = ((f32[256,1,4]{2,1,0:T(1,128)}), f32[256,1,4]{2,1,0:T(1,128)S(1)}, u32[]{:S(2)}, u32[]{:S(2)}) async-start(f32[256,1,4]{2,1,0:T(1,128)} %broadcast_in_dim.4), calls=%async_computation | async-start | bytes 262144 | tf_op jit(solution)/shard_map/while/body/eval_jaxpr/all_to_all | solution.py:39
  295.9 19.4 %collective-permute-start.28 = (f32[128,256]{0,1:T(8,128)S(1)}, f32[128,256]{0,1:T(8,128)S(1)}, u32[]{:S(2)}, u32[]{:S(2)}) collective-permute-start(f32[128,256]{0,1:T(8,128)S(1)} %get-tuple-element.234), channel_id=1, source_target_pairs={{0,64},{32,96},{64,0},{96,32},{128,192},{160,224},{192,128},{224,1... | collective-permute-start | bytes 393224 | tf_op jit(solution)/shard_map/while/body/eval_jaxpr/ppermute | solution.py:78
  298.9 19.7 %collective-permute-start.29 = (f32[128,256]{0,1:T(8,128)S(1)}, f32[128,256]{0,1:T(8,128)S(1)}, u32[]{:S(2)}, u32[]{:S(2)}) collective-permute-start(f32[128,256]{0,1:T(8,128)S(1)} %get-tuple-element.234), channel_id=1, source_target_pairs={{0,96},{32,64},{64,32},{96,0},{128,224},{160,192},{192,160},{224,1... | collective-permute-start | bytes 393224 | tf_op jit(solution)/shard_map/while/body/eval_jaxpr/ppermute | solution.py:78
  299.8 19.4 %collective-permute-start.30 = (f32[128,256]{0,1:T(8,128)S(1)}, f32[128,256]{0,1:T(8,128)S(1)}, u32[]{:S(2)}, u32[]{:S(2)}) collective-permute-start(f32[128,256]{0,1:T(8,128)S(1)} %get-tuple-element.234), channel_id=1, source_target_pairs={{0,128},{32,160},{64,192},{96,224},{128,0},{160,32},{192,64},{224,... | collective-permute-start | bytes 393224 | tf_op jit(solution)/shard_map/while/body/eval_jaxpr/ppermute | solution.py:78
  301.0 19.0 %collective-permute-start.31 = (f32[128,256]{0,1:T(8,128)S(1)}, f32[128,256]{0,1:T(8,128)S(1)}, u32[]{:S(2)}, u32[]{:S(2)}) collective-permute-start(f32[128,256]{0,1:T(8,128)S(1)} %get-tuple-element.234), channel_id=1, source_target_pairs={{0,160},{32,128},{64,224},{96,192},{128,32},{160,0},{192,96},{224,... | collective-permute-start | bytes 393224 | tf_op jit(solution)/shard_map/while/body/eval_jaxpr/ppermute | solution.py:78
  340.3 15.1 %collective-permute-start.1 = (bf16[192,1024]{1,0:T(8,128)(2,1)}, bf16[192,1024]{1,0:T(8,128)(2,1)}, u32[]{:S(2)}, u32[]{:S(2)}) collective-permute-start(bf16[192,1024]{1,0:T(8,128)(2,1)} %fusion.152), channel_id=1, source_target_pairs={{0,2},{1,3},{2,0},{3,1},{4,6},{5,7},{6,4},{7,5},{8,10},{9,11},{10,... | collective-permute-start | bytes 1179656 | tf_op jit(solution)/shard_map/while/body/eval_jaxpr/ppermute | solution.py:110
  394.7 19.1 %collective-permute-start.19 = (bf16[192,1024]{1,0:T(8,128)(2,1)S(1)}, bf16[192,1024]{1,0:T(8,128)(2,1)S(1)}, u32[]{:S(2)}, u32[]{:S(2)}) collective-permute-start(bf16[192,1024]{1,0:T(8,128)(2,1)S(1)} %constant_dynamic-update-slice_fusion.47), channel_id=1, source_target_pairs={{0,3},{1,2},{2,1},{3,0},{4,7},{5,6},{6,5},{7,4},{8,11},{9,10},{10,... | collective-permute-start | bytes 1179656 | tf_op jit(solution)/shard_map/while/body/eval_jaxpr/ppermute | solution.py:78
  435.5 34.5 %collective-permute-start.27 = (f32[128,256]{0,1:T(8,128)S(1)}, f32[128,256]{0,1:T(8,128)S(1)}, u32[]{:S(2)}, u32[]{:S(2)}) collective-permute-start(f32[128,256]{0,1:T(8,128)S(1)} %get-tuple-element.234), channel_id=1, source_target_pairs={{0,32},{32,0},{64,96},{96,64},{128,160},{160,128},{192,224},{224,1... | collective-permute-start | bytes 393224 | tf_op jit(solution)/shard_map/while/body/eval_jaxpr/ppermute | solution.py:78
  442.2 23.0 %all-to-all-start = ((f32[256,1,4]{2,1,0:T(1,128)}), f32[256,1,4]{2,1,0:T(1,128)S(1)}, u32[]{:S(2)}, u32[]{:S(2)}) async-start(f32[256,1,4]{2,1,0:T(1,128)} %broadcast_in_dim.4), calls=%async_computation | async-start | bytes 262144 | tf_op jit(solution)/shard_map/while/body/eval_jaxpr/all_to_all | solution.py:39
  452.4 19.4 %collective-permute-start.28 = (f32[128,256]{0,1:T(8,128)S(1)}, f32[128,256]{0,1:T(8,128)S(1)}, u32[]{:S(2)}, u32[]{:S(2)}) collective-permute-start(f32[128,256]{0,1:T(8,128)S(1)} %get-tuple-element.234), channel_id=1, source_target_pairs={{0,64},{32,96},{64,0},{96,32},{128,192},{160,224},{192,128},{224,1... | collective-permute-start | bytes 393224 | tf_op jit(solution)/shard_map/while/body/eval_jaxpr/ppermute | solution.py:78
  455.4 19.7 %collective-permute-start.29 = (f32[128,256]{0,1:T(8,128)S(1)}, f32[128,256]{0,1:T(8,128)S(1)}, u32[]{:S(2)}, u32[]{:S(2)}) collective-permute-start(f32[128,256]{0,1:T(8,128)S(1)} %get-tuple-element.234), channel_id=1, source_target_pairs={{0,96},{32,64},{64,32},{96,0},{128,224},{160,192},{192,160},{224,1... | collective-permute-start | bytes 393224 | tf_op jit(solution)/shard_map/while/body/eval_jaxpr/ppermute | solution.py:78
  456.3 19.4 %collective-permute-start.30 = (f32[128,256]{0,1:T(8,128)S(1)}, f32[128,256]{0,1:T(8,128)S(1)}, u32[]{:S(2)}, u32[]{:S(2)}) collective-permute-start(f32[128,256]{0,1:T(8,128)S(1)} %get-tuple-element.234), channel_id=1, source_target_pairs={{0,128},{32,160},{64,192},{96,224},{128,0},{160,32},{192,64},{224,... | collective-permute-start | bytes 393224 | tf_op jit(solution)/shard_map/while/body/eval_jaxpr/ppermute | solution.py:78
  457.4 19.0 %collective-permute-start.31 = (f32[128,256]{0,1:T(8,128)S(1)}, f32[128,256]{0,1:T(8,128)S(1)}, u32[]{:S(2)}, u32[]{:S(2)}) collective-permute-start(f32[128,256]{0,1:T(8,128)S(1)} %get-tuple-element.234), channel_id=1, source_target_pairs={{0,160},{32,128},{64,224},{96,192},{128,32},{160,0},{192,96},{224,... | collective-permute-start | bytes 393224 | tf_op jit(solution)/shard_map/while/body/eval_jaxpr/ppermute | solution.py:78
  (99 other events, 841.4 us)

commit v8 on v6

--- a/solution.py
+++ b/solution.py
@@ -81,6 +81,48 @@
     return chunk
 
 
+def xor_arrange(value, axis, groups):
+    if not groups:
+        return value
+    (low, bits), rest = groups[0], groups[1:]
+    width = 1 << bits
+    digit = (lax.axis_index(axis) >> low) & (width - 1)
+    rows = value.shape[0] // width
+    return jnp.concatenate(
+        [
+            xor_arrange(lax.dynamic_slice_in_dim(value, (digit ^ p) * rows, rows, 0), axis, rest)
+            for p in range(width)
+        ],
+        axis=0,
+    )
+
+
+def arranged_reduce(value, axis, groups, send_type):
+    size = lax.axis_size(axis)
+    kept = value.astype(jnp.float32)
+    for low, bits in groups:
+        width = 1 << bits
+        rows = kept.shape[0] // width
+        total = kept[:rows]
+        for offset in range(1, width):
+            send = kept[offset * rows : (offset + 1) * rows]
+            got = lax.ppermute(send.astype(send_type), axis, xor_pairs(size, offset << low))
+            total = total + got.astype(jnp.float32)
+        kept = total
+    return kept
+
+
+def arranged_gather(chunk, axis, groups):
+    size = lax.axis_size(axis)
+    for low, bits in reversed(groups):
+        width = 1 << bits
+        pieces = [chunk] + [
+            lax.ppermute(chunk, axis, xor_pairs(size, offset << low)) for offset in range(1, width)
+        ]
+        chunk = jnp.concatenate(pieces, axis=0)
+    return chunk
+
+
 def fisher_product(direction, residual, normed, hidden_act, slope_act, w_out, metric, width):
     tangent = direction.astype(jnp.bfloat16)
     tangent_in = tangent[:, :width]
@@ -92,8 +134,8 @@
         hidden_act, tangent_out_t, (((1,), (1,)), ((), ())), preferred_element_type=jnp.float32
     )
     fsdp_groups = digit_groups(lax.axis_size("fsdp"), 2)
-    out_chunk = spread_reduce(partial_out.astype(jnp.bfloat16), "fsdp", fsdp_groups, jnp.bfloat16)
-    cotangent = spread_gather((out_chunk * metric).astype(jnp.bfloat16), "fsdp", fsdp_groups)
+    out_chunk = arranged_reduce(partial_out.astype(jnp.bfloat16), "fsdp", fsdp_groups, jnp.bfloat16)
+    cotangent = arranged_gather((out_chunk * metric).astype(jnp.bfloat16), "fsdp", fsdp_groups)
     back_act = lax.dot_general(
         cotangent, w_out, (((1,), (1,)), ((), ())), preferred_element_type=jnp.float32
     )
@@ -129,6 +171,10 @@
     preact = jnp.dot(normed, w_in, preferred_element_type=jnp.float32)
     hidden_act = jax.nn.silu(preact).astype(jnp.bfloat16)
     slope_act = silu_slope(preact)
+    fsdp_groups = digit_groups(lax.axis_size("fsdp"), 2)
+    normed, hidden_act, slope_act = (
+        xor_arrange(value, "fsdp", fsdp_groups) for value in (normed, hidden_act, slope_act)
+    )
     residual = jnp.concatenate([grad_in, grad_out.T], axis=1)
 
     def iterate(_, carry):

time: 490 us -> 556 us (1.13)
  local copies, waits for them, and re-layouts: 42.6 us -> 123 us
  other arithmetic: 39.5 us -> 33.2 us
    ppermute x0 -> x60, waiting for transfers between devices: none -> 124 us  [the longest x30 65.8 us: arranged_reduce(): lax.ppermute(send.astype(send_type), axis, xor_pairs(size, offset << low))]
    ppermute x0 -> x60, starting transfers between devices: none -> 105 us  [the longest x30 54.2 us: arranged_reduce(): lax.ppermute(send.astype(send_type), axis, xor_pairs(size, offset << low))]
    ppermute x51 -> x21, waiting for transfers between devices: 64.2 us -> 0.06 us  [spread_gather(): got = lax.ppermute(chunk, axis, xor_pairs(size, offset << low))]
    ppermute x51 -> x21, waiting for transfers between devices: 87.8 us -> 25.3 us  [spread_reduce(): lax.ppermute(send.astype(send_type), axis, xor_pairs(size, offset << low))]
    unnamed x16 -> x115, local copies, waits for them, and re-layouts: 1.81 us -> 62.2 us
    ppermute x51 -> x21, starting transfers between devices: 79.5 us -> 22 us  [spread_reduce(): lax.ppermute(send.astype(send_type), axis, xor_pairs(size, offset << low))]
    ppermute x51 -> x21, starting transfers between devices: 79 us -> 26.7 us  [spread_gather(): got = lax.ppermute(chunk, axis, xor_pairs(size, offset << low))]
    while x51 -> x84, local copies, waits for them, and re-layouts: 8.84 us -> 19.8 us
  transfers between devices with their start and end apart: 105 -> 105, of which waited for: 47 -> 39; matrix products, arithmetic and copies ran while one was open for 8% -> 10% of each run, Pallas kernels for 0% -> 0%
where the time goes in v8:
time: 556 us; the launch traced here: 553 us
  starting transfers between devices  189 us (34%)
  waiting for transfers between devices  170 us (31%)
  local copies, waits for them, and re-layouts  123 us (22%)
  other arithmetic  33.2 us (6%)
  matrix products  24.9 us (4%)
  loops' own time  12.4 us (2%)
    ppermute x30, waiting for transfers between devices, arranged_reduce(): lax.ppermute(send.astype(send_type), axis, xor_pairs(size, offset << low))  65.8 us
    unnamed x115, local copies, waits for them, and re-layouts  62.2 us
    ppermute x30, waiting for transfers between devices, arranged_gather(): lax.ppermute(chunk, axis, xor_pairs(size, offset << low))  57.9 us
    ppermute x30, starting transfers between devices, arranged_reduce(): lax.ppermute(send.astype(send_type), axis, xor_pairs(size, offset << low))  54.2 us
    ppermute x30, starting transfers between devices, arranged_gather(): lax.ppermute(chunk, axis, xor_pairs(size, offset << low))  50.3 us
    all_to_all x3, starting transfers between devices, scalar_sum(): lax.all_to_all(jnp.broadcast_to(values[None], (size,) + values.shape), ax...  36 us
    dynamic_update_slice x21, local copies, waits for them, and re-layouts, spread_gather(): lax.dynamic_update_slice_in_dim(whole, got, (digit ^ offset) * rows, 0)  27.9 us
    ppermute x21, starting transfers between devices, spread_gather(): got = lax.ppermute(chunk, axis, xor_pairs(size, offset << low))  26.7 us
  transfers between devices with their start and end apart: 105, of which 39 were waited for; matrix products, arithmetic and copies ran while one was open for 10% of the time, Pallas kernels for 0%

profile of v8, /device:TPU:1, one launch (start us, length us, event | category | flops | bytes accessed | tf_op | source)
XLA Modules:
  0.0 553.4 jit_solution(3637496465703388876)
XLA Ops:
  67.8 480.8 %while.15 = (s32[]{:T(128)}, f32[1024,256]{0,1:T(8,128)}, f32[1024,256]{0,1:T(8,128)}, f32[1024,256]{0,1:T(8,128)S(1)}, bf16[768,1024]{1,0:T(8,128)(2,1)}, /*ind...) while((s32[]{:T(128)}, f32[1024,256]{0,1:T(8,128)}, ...), condition=%wide.region_7.8_spmd.clone, body=%wide.region_1.7_spmd.clone.sunk | while | flops 1214809088 | bytes 95832728 | solution.py:193
  74.1 4.2 collective-permute-start
  80.3 7.0 %collective-permute-done = bf16[192,1024]{1,0:T(8,128)(2,1)S(1)} collective-permute-done((bf16[192,1024]{1,0:T(8,128)(2,1)S(1)}, bf16[192,1024]{1,0:T(8,128)(2,1)S(1)}, u32[]{:S(2)}, u32[]{:S(2)}) %collective-permute-start) | collective-permute-done | bytes 393248 | tf_op jit(solution)/shard_map/while/body/eval_jaxpr/ppermute | solution.py:109
  87.3 9.2 %collective-permute-done.1 = bf16[192,1024]{1,0:T(8,128)(2,1)S(1)} collective-permute-done((bf16[192,1024]{1,0:T(8,128)(2,1)S(1)}, bf16[192,1024]{1,0:T(8,128)(2,1)S(1)}, u32[]{:S(2)}, u32[]{:S(2)}) %collective-permute-start.1) | collective-permute-done | bytes 393248 | tf_op jit(solution)/shard_map/while/body/eval_jaxpr/ppermute | solution.py:109
  96.7 5.8 %collective-permute-start.3 = (bf16[24,1024]{1,0:T(8,128)(2,1)S(1)}, bf16[24,1024]{1,0:T(8,128)(2,1)S(1)}, u32[]{:S(2)}, u32[]{:S(2)}) collective-permute-start(bf16[24,1024]{1,0:T(8,128)(2,1)S(1)} %get-tuple-element.261), channel_id=1, source_target_pairs={{0,28},{1,29},{2,30},{3,31},{4,24},{5,25},{6,26},{7,27},{8,20},{9,... | collective-permute-start | bytes 147464 | tf_op jit(solution)/shard_map/while/body/eval_jaxpr/ppermute | solution.py:109
  113.8 4.0 collective-permute-done.8
  125.6 4.0 collective-permute-start.15
  141.7 9.2 %collective-permute-done.18 = bf16[192,1024]{1,0:T(8,128)(2,1)S(1)} collective-permute-done((bf16[192,1024]{1,0:T(8,128)(2,1)}, bf16[192,1024]{1,0:T(8,128)(2,1)S(1)}, u32[]{:S(2)}, u32[]{:S(2)}) %collective-permute-start.18) | collective-permute-done | bytes 393248 | tf_op jit(solution)/shard_map/while/body/eval_jaxpr/ppermute | solution.py:120
  150.9 8.6 %collective-permute-done.19 = bf16[192,1024]{1,0:T(8,128)(2,1)S(1)} collective-permute-done((bf16[192,1024]{1,0:T(8,128)(2,1)}, bf16[192,1024]{1,0:T(8,128)(2,1)S(1)}, u32[]{:S(2)}, u32[]{:S(2)}) %collective-permute-start.19) | collective-permute-done | bytes 393248 | tf_op jit(solution)/shard_map/while/body/eval_jaxpr/ppermute | solution.py:120
  163.6 3.8 collective-permute-start.21
  186.6 12.1 %all-to-all-start = ((f32[256,1,4]{2,1,0:T(1,128)}), f32[256,1,4]{2,1,0:T(1,128)}, u32[]{:S(2)}, u32[]{:S(2)}) async-start(f32[256,1,4]{2,1,0:T(1,128)} %broadcast_in_dim.4), calls=%async_computation | async-start | bytes 262144 | tf_op jit(solution)/shard_map/while/body/eval_jaxpr/all_to_all | solution.py:39
  203.8 7.0 %all-to-all-done = f32[256,1,4]{2,1,0:T(1,128)} async-done(((f32[256,1,4]{2,1,0:T(1,128)}), f32[256,1,4]{2,1,0:T(1,128)}, u32[]{:S(2)}, u32[]{:S(2)}) %all-to-all-start) | async-done | bytes 4128 | tf_op jit(solution)/shard_map/while/body/eval_jaxpr/all_to_all | solution.py:39
  244.0 7.4 %collective-permute-done = bf16[192,1024]{1,0:T(8,128)(2,1)S(1)} collective-permute-done((bf16[192,1024]{1,0:T(8,128)(2,1)S(1)}, bf16[192,1024]{1,0:T(8,128)(2,1)S(1)}, u32[]{:S(2)}, u32[]{:S(2)}) %collective-permute-start) | collective-permute-done | bytes 393248 | tf_op jit(solution)/shard_map/while/body/eval_jaxpr/ppermute | solution.py:109
  251.4 9.3 %collective-permute-done.1 = bf16[192,1024]{1,0:T(8,128)(2,1)S(1)} collective-permute-done((bf16[192,1024]{1,0:T(8,128)(2,1)S(1)}, bf16[192,1024]{1,0:T(8,128)(2,1)S(1)}, u32[]{:S(2)}, u32[]{:S(2)}) %collective-permute-start.1) | collective-permute-done | bytes 393248 | tf_op jit(solution)/shard_map/while/body/eval_jaxpr/ppermute | solution.py:109
  301.0 9.2 %collective-permute-done.18 = bf16[192,1024]{1,0:T(8,128)(2,1)S(1)} collective-permute-done((bf16[192,1024]{1,0:T(8,128)(2,1)}, bf16[192,1024]{1,0:T(8,128)(2,1)S(1)}, u32[]{:S(2)}, u32[]{:S(2)}) %collective-permute-start.18) | collective-permute-done | bytes 393248 | tf_op jit(solution)/shard_map/while/body/eval_jaxpr/ppermute | solution.py:120
  310.2 8.6 %collective-permute-done.19 = bf16[192,1024]{1,0:T(8,128)(2,1)S(1)} collective-permute-done((bf16[192,1024]{1,0:T(8,128)(2,1)}, bf16[192,1024]{1,0:T(8,128)(2,1)S(1)}, u32[]{:S(2)}, u32[]{:S(2)}) %collective-permute-start.19) | collective-permute-done | bytes 393248 | tf_op jit(solution)/shard_map/while/body/eval_jaxpr/ppermute | solution.py:120
  344.6 11.9 %all-to-all-start = ((f32[256,1,4]{2,1,0:T(1,128)}), f32[256,1,4]{2,1,0:T(1,128)}, u32[]{:S(2)}, u32[]{:S(2)}) async-start(f32[256,1,4]{2,1,0:T(1,128)} %broadcast_in_dim.4), calls=%async_computation | async-start | bytes 262144 | tf_op jit(solution)/shard_map/while/body/eval_jaxpr/all_to_all | solution.py:39
  361.6 7.0 %all-to-all-done = f32[256,1,4]{2,1,0:T(1,128)} async-done(((f32[256,1,4]{2,1,0:T(1,128)}), f32[256,1,4]{2,1,0:T(1,128)}, u32[]{:S(2)}, u32[]{:S(2)}) %all-to-all-start) | async-done | bytes 4128 | tf_op jit(solution)/shard_map/while/body/eval_jaxpr/all_to_all | solution.py:39
  401.8 7.4 %collective-permute-done = bf16[192,1024]{1,0:T(8,128)(2,1)S(1)} collective-permute-done((bf16[192,1024]{1,0:T(8,128)(2,1)S(1)}, bf16[192,1024]{1,0:T(8,128)(2,1)S(1)}, u32[]{:S(2)}, u32[]{:S(2)}) %collective-permute-start) | collective-permute-done | bytes 393248 | tf_op jit(solution)/shard_map/while/body/eval_jaxpr/ppermute | solution.py:109
  409.2 9.3 %collective-permute-done.1 = bf16[192,1024]{1,0:T(8,128)(2,1)S(1)} collective-permute-done((bf16[192,1024]{1,0:T(8,128)(2,1)S(1)}, bf16[192,1024]{1,0:T(8,128)(2,1)S(1)}, u32[]{:S(2)}, u32[]{:S(2)}) %collective-permute-start.1) | collective-permute-done | bytes 393248 | tf_op jit(solution)/shard_map/while/body/eval_jaxpr/ppermute | solution.py:109
  458.8 9.2 %collective-permute-done.18 = bf16[192,1024]{1,0:T(8,128)(2,1)S(1)} collective-permute-done((bf16[192,1024]{1,0:T(8,128)(2,1)}, bf16[192,1024]{1,0:T(8,128)(2,1)S(1)}, u32[]{:S(2)}, u32[]{:S(2)}) %collective-permute-start.18) | collective-permute-done | bytes 393248 | tf_op jit(solution)/shard_map/while/body/eval_jaxpr/ppermute | solution.py:120
  468.1 8.6 %collective-permute-done.19 = bf16[192,1024]{1,0:T(8,128)(2,1)S(1)} collective-permute-done((bf16[192,1024]{1,0:T(8,128)(2,1)}, bf16[192,1024]{1,0:T(8,128)(2,1)S(1)}, u32[]{:S(2)}, u32[]{:S(2)}) %collective-permute-start.19) | collective-permute-done | bytes 393248 | tf_op jit(solution)/shard_map/while/body/eval_jaxpr/ppermute | solution.py:120
  502.5 11.9 %all-to-all-start = ((f32[256,1,4]{2,1,0:T(1,128)}), f32[256,1,4]{2,1,0:T(1,128)}, u32[]{:S(2)}, u32[]{:S(2)}) async-start(f32[256,1,4]{2,1,0:T(1,128)} %broadcast_in_dim.4), calls=%async_computation | async-start | bytes 262144 | tf_op jit(solution)/shard_map/while/body/eval_jaxpr/all_to_all | solution.py:39
  519.4 7.0 %all-to-all-done = f32[256,1,4]{2,1,0:T(1,128)} async-done(((f32[256,1,4]{2,1,0:T(1,128)}), f32[256,1,4]{2,1,0:T(1,128)}, u32[]{:S(2)}, u32[]{:S(2)}) %all-to-all-start) | async-done | bytes 4128 | tf_op jit(solution)/shard_map/while/body/eval_jaxpr/all_to_all | solution.py:39
  (482 shorter events, 358.5 us)
Async XLA Ops:
  78.3 18.1 %collective-permute-start.1 = (bf16[192,1024]{1,0:T(8,128)(2,1)S(1)}, bf16[192,1024]{1,0:T(8,128)(2,1)S(1)}, u32[]{:S(2)}, u32[]{:S(2)}) collective-permute-start(bf16[192,1024]{1,0:T(8,128)(2,1)S(1)} %get-tuple-element.258), channel_id=1, source_target_pairs={{0,2},{1,3},{2,0},{3,1},{4,6},{5,7},{6,4},{7,5},{8,10},{9,11},{10,... | collective-permute-start | bytes 1179656 | tf_op jit(solution)/shard_map/while/body/eval_jaxpr/ppermute | solution.py:109
  141.2 18.3 %collective-permute-start.19 = (bf16[192,1024]{1,0:T(8,128)(2,1)}, bf16[192,1024]{1,0:T(8,128)(2,1)S(1)}, u32[]{:S(2)}, u32[]{:S(2)}) collective-permute-start(bf16[192,1024]{1,0:T(8,128)(2,1)} %get-tuple-element.284), channel_id=1, source_target_pairs={{0,3},{1,2},{2,1},{3,0},{4,7},{5,6},{6,5},{7,4},{8,11},{9,10},{10,... | collective-permute-start | bytes 1179656 | tf_op jit(solution)/shard_map/while/body/eval_jaxpr/ppermute | solution.py:120
  181.1 35.4 %collective-permute-start.27 = (f32[128,256]{0,1:T(8,128)S(1)}, f32[128,256]{0,1:T(8,128)}, u32[]{:S(2)}, u32[]{:S(2)}) collective-permute-start(f32[128,256]{0,1:T(8,128)S(1)} %get-tuple-element.291), channel_id=1, source_target_pairs={{0,32},{32,0},{64,96},{96,64},{128,160},{160,128},{192,224},{224,1... | collective-permute-start | bytes 393224 | tf_op jit(solution)/shard_map/while/body/eval_jaxpr/ppermute | solution.py:78
  186.6 24.1 %all-to-all-start = ((f32[256,1,4]{2,1,0:T(1,128)}), f32[256,1,4]{2,1,0:T(1,128)}, u32[]{:S(2)}, u32[]{:S(2)}) async-start(f32[256,1,4]{2,1,0:T(1,128)} %broadcast_in_dim.4), calls=%async_computation | async-start | bytes 262144 | tf_op jit(solution)/shard_map/while/body/eval_jaxpr/all_to_all | solution.py:39
  198.7 20.4 %collective-permute-start.28 = (f32[128,256]{0,1:T(8,128)S(1)}, f32[128,256]{0,1:T(8,128)}, u32[]{:S(2)}, u32[]{:S(2)}) collective-permute-start(f32[128,256]{0,1:T(8,128)S(1)} %get-tuple-element.291), channel_id=1, source_target_pairs={{0,64},{32,96},{64,0},{96,32},{128,192},{160,224},{192,128},{224,1... | collective-permute-start | bytes 393224 | tf_op jit(solution)/shard_map/while/body/eval_jaxpr/ppermute | solution.py:78
  201.7 21.7 %collective-permute-start.29 = (f32[128,256]{0,1:T(8,128)S(1)}, f32[128,256]{0,1:T(8,128)}, u32[]{:S(2)}, u32[]{:S(2)}) collective-permute-start(f32[128,256]{0,1:T(8,128)S(1)} %get-tuple-element.291), channel_id=1, source_target_pairs={{0,96},{32,64},{64,32},{96,0},{128,224},{160,192},{192,160},{224,1... | collective-permute-start | bytes 393224 | tf_op jit(solution)/shard_map/while/body/eval_jaxpr/ppermute | solution.py:78
  202.6 22.4 %collective-permute-start.30 = (f32[128,256]{0,1:T(8,128)S(1)}, f32[128,256]{0,1:T(8,128)}, u32[]{:S(2)}, u32[]{:S(2)}) collective-permute-start(f32[128,256]{0,1:T(8,128)S(1)} %get-tuple-element.291), channel_id=1, source_target_pairs={{0,128},{32,160},{64,192},{96,224},{128,0},{160,32},{192,64},{224,... | collective-permute-start | bytes 393224 | tf_op jit(solution)/shard_map/while/body/eval_jaxpr/ppermute | solution.py:78
  203.8 22.8 %collective-permute-start.31 = (f32[128,256]{0,1:T(8,128)S(1)}, f32[128,256]{0,1:T(8,128)}, u32[]{:S(2)}, u32[]{:S(2)}) collective-permute-start(f32[128,256]{0,1:T(8,128)S(1)} %get-tuple-element.291), channel_id=1, source_target_pairs={{0,160},{32,128},{64,224},{96,192},{128,32},{160,0},{192,96},{224,... | collective-permute-start | bytes 393224 | tf_op jit(solution)/shard_map/while/body/eval_jaxpr/ppermute | solution.py:78
  241.7 18.9 %collective-permute-start.1 = (bf16[192,1024]{1,0:T(8,128)(2,1)S(1)}, bf16[192,1024]{1,0:T(8,128)(2,1)S(1)}, u32[]{:S(2)}, u32[]{:S(2)}) collective-permute-start(bf16[192,1024]{1,0:T(8,128)(2,1)S(1)} %get-tuple-element.258), channel_id=1, source_target_pairs={{0,2},{1,3},{2,0},{3,1},{4,6},{5,7},{6,4},{7,5},{8,10},{9,11},{10,... | collective-permute-start | bytes 1179656 | tf_op jit(solution)/shard_map/while/body/eval_jaxpr/ppermute | solution.py:109
  299.6 19.2 %collective-permute-start.19 = (bf16[192,1024]{1,0:T(8,128)(2,1)}, bf16[192,1024]{1,0:T(8,128)(2,1)S(1)}, u32[]{:S(2)}, u32[]{:S(2)}) collective-permute-start(bf16[192,1024]{1,0:T(8,128)(2,1)} %get-tuple-element.284), channel_id=1, source_target_pairs={{0,3},{1,2},{2,1},{3,0},{4,7},{5,6},{6,5},{7,4},{8,11},{9,10},{10,... | collective-permute-start | bytes 1179656 | tf_op jit(solution)/shard_map/while/body/eval_jaxpr/ppermute | solution.py:120
  339.6 34.7 %collective-permute-start.27 = (f32[128,256]{0,1:T(8,128)S(1)}, f32[128,256]{0,1:T(8,128)}, u32[]{:S(2)}, u32[]{:S(2)}) collective-permute-start(f32[128,256]{0,1:T(8,128)S(1)} %get-tuple-element.291), channel_id=1, source_target_pairs={{0,32},{32,0},{64,96},{96,64},{128,160},{160,128},{192,224},{224,1... | collective-permute-start | bytes 393224 | tf_op jit(solution)/shard_map/while/body/eval_jaxpr/ppermute | solution.py:78
  344.6 23.9 %all-to-all-start = ((f32[256,1,4]{2,1,0:T(1,128)}), f32[256,1,4]{2,1,0:T(1,128)}, u32[]{:S(2)}, u32[]{:S(2)}) async-start(f32[256,1,4]{2,1,0:T(1,128)} %broadcast_in_dim.4), calls=%async_computation | async-start | bytes 262144 | tf_op jit(solution)/shard_map/while/body/eval_jaxpr/all_to_all | solution.py:39
  356.6 20.4 %collective-permute-start.28 = (f32[128,256]{0,1:T(8,128)S(1)}, f32[128,256]{0,1:T(8,128)}, u32[]{:S(2)}, u32[]{:S(2)}) collective-permute-start(f32[128,256]{0,1:T(8,128)S(1)} %get-tuple-element.291), channel_id=1, source_target_pairs={{0,64},{32,96},{64,0},{96,32},{128,192},{160,224},{192,128},{224,1... | collective-permute-start | bytes 393224 | tf_op jit(solution)/shard_map/while/body/eval_jaxpr/ppermute | solution.py:78
  359.5 21.7 %collective-permute-start.29 = (f32[128,256]{0,1:T(8,128)S(1)}, f32[128,256]{0,1:T(8,128)}, u32[]{:S(2)}, u32[]{:S(2)}) collective-permute-start(f32[128,256]{0,1:T(8,128)S(1)} %get-tuple-element.291), channel_id=1, source_target_pairs={{0,96},{32,64},{64,32},{96,0},{128,224},{160,192},{192,160},{224,1... | collective-permute-start | bytes 393224 | tf_op jit(solution)/shard_map/while/body/eval_jaxpr/ppermute | solution.py:78
  360.4 22.4 %collective-permute-start.30 = (f32[128,256]{0,1:T(8,128)S(1)}, f32[128,256]{0,1:T(8,128)}, u32[]{:S(2)}, u32[]{:S(2)}) collective-permute-start(f32[128,256]{0,1:T(8,128)S(1)} %get-tuple-element.291), channel_id=1, source_target_pairs={{0,128},{32,160},{64,192},{96,224},{128,0},{160,32},{192,64},{224,... | collective-permute-start | bytes 393224 | tf_op jit(solution)/shard_map/while/body/eval_jaxpr/ppermute | solution.py:78
  361.6 22.8 %collective-permute-start.31 = (f32[128,256]{0,1:T(8,128)S(1)}, f32[128,256]{0,1:T(8,128)}, u32[]{:S(2)}, u32[]{:S(2)}) collective-permute-start(f32[128,256]{0,1:T(8,128)S(1)} %get-tuple-element.291), channel_id=1, source_target_pairs={{0,160},{32,128},{64,224},{96,192},{128,32},{160,0},{192,96},{224,... | collective-permute-start | bytes 393224 | tf_op jit(solution)/shard_map/while/body/eval_jaxpr/ppermute | solution.py:78
  399.5 18.9 %collective-permute-start.1 = (bf16[192,1024]{1,0:T(8,128)(2,1)S(1)}, bf16[192,1024]{1,0:T(8,128)(2,1)S(1)}, u32[]{:S(2)}, u32[]{:S(2)}) collective-permute-start(bf16[192,1024]{1,0:T(8,128)(2,1)S(1)} %get-tuple-element.258), channel_id=1, source_target_pairs={{0,2},{1,3},{2,0},{3,1},{4,6},{5,7},{6,4},{7,5},{8,10},{9,11},{10,... | collective-permute-start | bytes 1179656 | tf_op jit(solution)/shard_map/while/body/eval_jaxpr/ppermute | solution.py:109
  457.4 19.2 %collective-permute-start.19 = (bf16[192,1024]{1,0:T(8,128)(2,1)}, bf16[192,1024]{1,0:T(8,128)(2,1)S(1)}, u32[]{:S(2)}, u32[]{:S(2)}) collective-permute-start(bf16[192,1024]{1,0:T(8,128)(2,1)} %get-tuple-element.284), channel_id=1, source_target_pairs={{0,3},{1,2},{2,1},{3,0},{4,7},{5,6},{6,5},{7,4},{8,11},{9,10},{10,... | collective-permute-start | bytes 1179656 | tf_op jit(solution)/shard_map/while/body/eval_jaxpr/ppermute | solution.py:120
  497.4 34.7 %collective-permute-start.27 = (f32[128,256]{0,1:T(8,128)S(1)}, f32[128,256]{0,1:T(8,128)}, u32[]{:S(2)}, u32[]{:S(2)}) collective-permute-start(f32[128,256]{0,1:T(8,128)S(1)} %get-tuple-element.291), channel_id=1, source_target_pairs={{0,32},{32,0},{64,96},{96,64},{128,160},{160,128},{192,224},{224,1... | collective-permute-start | bytes 393224 | tf_op jit(solution)/shard_map/while/body/eval_jaxpr/ppermute | solution.py:78
  502.5 23.9 %all-to-all-start = ((f32[256,1,4]{2,1,0:T(1,128)}), f32[256,1,4]{2,1,0:T(1,128)}, u32[]{:S(2)}, u32[]{:S(2)}) async-start(f32[256,1,4]{2,1,0:T(1,128)} %broadcast_in_dim.4), calls=%async_computation | async-start | bytes 262144 | tf_op jit(solution)/shard_map/while/body/eval_jaxpr/all_to_all | solution.py:39
  514.4 20.4 %collective-permute-start.28 = (f32[128,256]{0,1:T(8,128)S(1)}, f32[128,256]{0,1:T(8,128)}, u32[]{:S(2)}, u32[]{:S(2)}) collective-permute-start(f32[128,256]{0,1:T(8,128)S(1)} %get-tuple-element.291), channel_id=1, source_target_pairs={{0,64},{32,96},{64,0},{96,32},{128,192},{160,224},{192,128},{224,1... | collective-permute-start | bytes 393224 | tf_op jit(solution)/shard_map/while/body/eval_jaxpr/ppermute | solution.py:78
  517.4 21.7 %collective-permute-start.29 = (f32[128,256]{0,1:T(8,128)S(1)}, f32[128,256]{0,1:T(8,128)}, u32[]{:S(2)}, u32[]{:S(2)}) collective-permute-start(f32[128,256]{0,1:T(8,128)S(1)} %get-tuple-element.291), channel_id=1, source_target_pairs={{0,96},{32,64},{64,32},{96,0},{128,224},{160,192},{192,160},{224,1... | collective-permute-start | bytes 393224 | tf_op jit(solution)/shard_map/while/body/eval_jaxpr/ppermute | solution.py:78
  518.3 22.4 %collective-permute-start.30 = (f32[128,256]{0,1:T(8,128)S(1)}, f32[128,256]{0,1:T(8,128)}, u32[]{:S(2)}, u32[]{:S(2)}) collective-permute-start(f32[128,256]{0,1:T(8,128)S(1)} %get-tuple-element.291), channel_id=1, source_target_pairs={{0,128},{32,160},{64,192},{96,224},{128,0},{160,32},{192,64},{224,... | collective-permute-start | bytes 393224 | tf_op jit(solution)/shard_map/while/body/eval_jaxpr/ppermute | solution.py:78
  519.4 22.8 %collective-permute-start.31 = (f32[128,256]{0,1:T(8,128)S(1)}, f32[128,256]{0,1:T(8,128)}, u32[]{:S(2)}, u32[]{:S(2)}) collective-permute-start(f32[128,256]{0,1:T(8,128)S(1)} %get-tuple-element.291), channel_id=1, source_target_pairs={{0,160},{32,128},{64,224},{96,192},{128,32},{160,0},{192,96},{224,... | collective-permute-start | bytes 393224 | tf_op jit(solution)/shard_map/while/body/eval_jaxpr/ppermute | solution.py:78
  (118 other events, 1228.7 us)

commit v9 on v6

--- a/solution.py
+++ b/solution.py
@@ -40,11 +40,16 @@
     return jnp.sum(gathered, axis=0)
 
 
-def digit_groups(size, first_bits):
+def digit_groups(size, widths):
     count = stages_of(size)
-    groups = [(0, min(first_bits, count))]
-    if count > first_bits:
-        groups.append((first_bits, count - first_bits))
+    groups, low = [], 0
+    for bits in widths:
+        if low >= count:
+            break
+        groups.append((low, min(bits, count - low)))
+        low += groups[-1][1]
+    if low < count:
+        groups.append((low, count - low))
     return groups
 
 
@@ -91,7 +96,7 @@
     partial_out = partial_out + lax.dot_general(
         hidden_act, tangent_out_t, (((1,), (1,)), ((), ())), preferred_element_type=jnp.float32
     )
-    fsdp_groups = digit_groups(lax.axis_size("fsdp"), 2)
+    fsdp_groups = digit_groups(lax.axis_size("fsdp"), (1, 1))
     out_chunk = spread_reduce(partial_out.astype(jnp.bfloat16), "fsdp", fsdp_groups, jnp.bfloat16)
     cotangent = spread_gather((out_chunk * metric).astype(jnp.bfloat16), "fsdp", fsdp_groups)
     back_act = lax.dot_general(
@@ -100,7 +105,7 @@
     grad_pre = (slope_act * back_act).astype(jnp.bfloat16)
     part_out_t = contract_rows(cotangent, hidden_act)
     part_in = contract_rows(normed, grad_pre)
-    dp_groups = digit_groups(lax.axis_size("dp"), 3)
+    dp_groups = digit_groups(lax.axis_size("dp"), (3,))
     reduced = spread_reduce(jnp.concatenate([part_in, part_out_t], axis=1), "dp", dp_groups, jnp.float32)
     rows = reduced.shape[0]
     start = lax.axis_index("dp") * rows

time: 490 us -> 455 us (0.929)
  waiting for transfers between devices: 172 us -> 145 us
  starting transfers between devices: 194 us -> 189 us
    ppermute x51 -> x48, waiting for transfers between devices: 64.2 us -> 46.5 us  [spread_gather(): got = lax.ppermute(chunk, axis, xor_pairs(size, offset << low))]
    ppermute x51 -> x48, waiting for transfers between devices: 87.8 us -> 77.2 us  [spread_reduce(): lax.ppermute(send.astype(send_type), axis, xor_pairs(size, offset << low))]
    ppermute x51 -> x48, starting transfers between devices: 79.5 us -> 70.4 us  [spread_reduce(): lax.ppermute(send.astype(send_type), axis, xor_pairs(size, offset << low))]
    dynamic_update_slice x51 -> x48, local copies, waits for them, and re-layouts: 20.4 us -> 17.7 us  [spread_gather(): lax.dynamic_update_slice_in_dim(whole, got, (digit ^ offset) * rows, 0)]
    ppermute x51 -> x48, starting transfers between devices: 79 us -> 80.2 us  [spread_gather(): got = lax.ppermute(chunk, axis, xor_pairs(size, offset << low))]
  transfers between devices with their start and end apart: 105 -> 99, of which waited for: 47 -> 47; matrix products, arithmetic and copies ran while one was open for 8% -> 8% of each run, Pallas kernels for 0% -> 0%
where the time goes in v9:
time: 455 us; the launch traced here: 454 us
  starting transfers between devices  189 us (42%)
  waiting for transfers between devices  145 us (32%)
  other arithmetic  41.1 us (9%)
  local copies, waits for them, and re-layouts  40.2 us (9%)
  matrix products  25.3 us (6%)
  loops' own time  12.9 us (3%)
    ppermute x48, starting transfers between devices, spread_gather(): got = lax.ppermute(chunk, axis, xor_pairs(size, offset << low))  80.2 us
    ppermute x48, waiting for transfers between devices, spread_reduce(): lax.ppermute(send.astype(send_type), axis, xor_pairs(size, offset << low))  77.2 us
    ppermute x48, starting transfers between devices, spread_reduce(): lax.ppermute(send.astype(send_type), axis, xor_pairs(size, offset << low))  70.4 us
    ppermute x48, waiting for transfers between devices, spread_gather(): got = lax.ppermute(chunk, axis, xor_pairs(size, offset << low))  46.5 us
    all_to_all x3, starting transfers between devices, scalar_sum(): lax.all_to_all(jnp.broadcast_to(values[None], (size,) + values.shape), ax...  38.3 us
    all_to_all x3, waiting for transfers between devices, scalar_sum(): lax.all_to_all(jnp.broadcast_to(values[None], (size,) + values.shape), ax...  20.9 us
    dynamic_update_slice x48, local copies, waits for them, and re-layouts, spread_gather(): lax.dynamic_update_slice_in_dim(whole, got, (digit ^ offset) * rows, 0)  17.7 us
    another operation x1, loops' own time, on_device(): lax.fori_loop(0, ITERS, iterate, (jnp.zeros_like(residual), residual, res...  12.9 us
  transfers between devices with their start and end apart: 99, of which 47 were waited for; matrix products, arithmetic and copies ran while one was open for 8% of the time, Pallas kernels for 0%

profile of v9, /device:TPU:1, one launch (start us, length us, event | category | flops | bytes accessed | tf_op | source)
XLA Modules:
  0.0 453.8 jit_solution(14976467968549822884)
XLA Ops:
  7.3 440.6 %while.15 = (s32[]{:T(128)}, f32[1024,256]{0,1:T(8,128)}, f32[1024,256]{0,1:T(8,128)}, f32[1024,256]{0,1:T(8,128)S(1)}, bf16[768,1024]{1,0:T(8,128)(2,1)}, /*ind...) while((s32[]{:T(128)}, f32[1024,256]{0,1:T(8,128)}, ...), condition=%wide.region_7.8_spmd.clone, body=%wide.region_1.7_spmd.clone.sunk | while | flops 1215202304 | bytes 106794472 | solution.py:152
  23.2 10.8 %collective-permute-done.1 = bf16[192,1024]{1,0:T(8,128)(2,1)S(1)} collective-permute-done((bf16[192,1024]{1,0:T(8,128)(2,1)S(1)}, bf16[192,1024]{1,0:T(8,128)(2,1)S(1)}, u32[]{:S(2)}, u32[]{:S(2)}) %collective-permute-start.1) | collective-permute-done | bytes 393248 | tf_op jit(solution)/shard_map/while/body/eval_jaxpr/ppermute | solution.py:67
  34.1 4.0 collective-permute-start.2
  38.6 3.5 collective-permute-start.4
  56.2 4.7 %collective-permute-start.12 = (bf16[24,1024]{1,0:T(8,128)(2,1)S(1)}, bf16[24,1024]{1,0:T(8,128)(2,1)S(1)}, u32[]{:S(2)}, u32[]{:S(2)}) collective-permute-start(bf16[24,1024]{1,0:T(8,128)(2,1)S(1)} %get-tuple-element.227), channel_id=1, source_target_pairs={{0,16},{1,17},{2,18},{3,19},{4,20},{5,21},{6,22},{7,23},{8,24},{9,... | collective-permute-start | bytes 147464 | tf_op jit(solution)/shard_map/while/body/eval_jaxpr/ppermute | solution.py:83
  61.0 4.0 collective-permute-start.14
  73.8 7.0 %collective-permute-done.16 = bf16[192,1024]{1,0:T(8,128)(2,1)S(1)} collective-permute-done((bf16[192,1024]{1,0:T(8,128)(2,1)S(1)}, bf16[192,1024]{1,0:T(8,128)(2,1)S(1)}, u32[]{:S(2)}, u32[]{:S(2)}) %collective-permute-start.16) | collective-permute-done | bytes 393248 | tf_op jit(solution)/shard_map/while/body/eval_jaxpr/ppermute | solution.py:83
  90.5 3.9 collective-permute-start.19
  113.8 12.2 %all-to-all-start = ((f32[256,1,4]{2,1,0:T(1,128)}), f32[256,1,4]{2,1,0:T(1,128)}, u32[]{:S(2)}, u32[]{:S(2)}) async-start(f32[256,1,4]{2,1,0:T(1,128)} %broadcast_in_dim.4), calls=%async_computation | async-start | bytes 262144 | tf_op jit(solution)/shard_map/while/body/eval_jaxpr/all_to_all | solution.py:39
  131.1 7.0 %all-to-all-done = f32[256,1,4]{2,1,0:T(1,128)} async-done(((f32[256,1,4]{2,1,0:T(1,128)}), f32[256,1,4]{2,1,0:T(1,128)}, u32[]{:S(2)}, u32[]{:S(2)}) %all-to-all-start) | async-done | bytes 4128 | tf_op jit(solution)/shard_map/while/body/eval_jaxpr/all_to_all | solution.py:39
  172.2 10.7 %collective-permute-done.1 = bf16[192,1024]{1,0:T(8,128)(2,1)S(1)} collective-permute-done((bf16[192,1024]{1,0:T(8,128)(2,1)S(1)}, bf16[192,1024]{1,0:T(8,128)(2,1)S(1)}, u32[]{:S(2)}, u32[]{:S(2)}) %collective-permute-start.1) | collective-permute-done | bytes 393248 | tf_op jit(solution)/shard_map/while/body/eval_jaxpr/ppermute | solution.py:67
  183.6 3.5 collective-permute-start.3
  187.4 3.9 collective-permute-start.5
  196.6 4.3 collective-permute-done.7
  219.9 7.5 %collective-permute-done.16 = bf16[192,1024]{1,0:T(8,128)(2,1)S(1)} collective-permute-done((bf16[192,1024]{1,0:T(8,128)(2,1)S(1)}, bf16[192,1024]{1,0:T(8,128)(2,1)S(1)}, u32[]{:S(2)}, u32[]{:S(2)}) %collective-permute-start.16) | collective-permute-done | bytes 393248 | tf_op jit(solution)/shard_map/while/body/eval_jaxpr/ppermute | solution.py:83
  258.0 13.0 %all-to-all-start = ((f32[256,1,4]{2,1,0:T(1,128)}), f32[256,1,4]{2,1,0:T(1,128)}, u32[]{:S(2)}, u32[]{:S(2)}) async-start(f32[256,1,4]{2,1,0:T(1,128)} %broadcast_in_dim.4), calls=%async_computation | async-start | bytes 262144 | tf_op jit(solution)/shard_map/while/body/eval_jaxpr/all_to_all | solution.py:39
  276.1 7.0 %all-to-all-done = f32[256,1,4]{2,1,0:T(1,128)} async-done(((f32[256,1,4]{2,1,0:T(1,128)}), f32[256,1,4]{2,1,0:T(1,128)}, u32[]{:S(2)}, u32[]{:S(2)}) %all-to-all-start) | async-done | bytes 4128 | tf_op jit(solution)/shard_map/while/body/eval_jaxpr/all_to_all | solution.py:39
  317.3 10.7 %collective-permute-done.1 = bf16[192,1024]{1,0:T(8,128)(2,1)S(1)} collective-permute-done((bf16[192,1024]{1,0:T(8,128)(2,1)S(1)}, bf16[192,1024]{1,0:T(8,128)(2,1)S(1)}, u32[]{:S(2)}, u32[]{:S(2)}) %collective-permute-start.1) | collective-permute-done | bytes 393248 | tf_op jit(solution)/shard_map/while/body/eval_jaxpr/ppermute | solution.py:67
  328.6 3.5 collective-permute-start.3
  332.4 3.9 collective-permute-start.5
  341.6 4.3 collective-permute-done.7
  364.9 7.5 %collective-permute-done.16 = bf16[192,1024]{1,0:T(8,128)(2,1)S(1)} collective-permute-done((bf16[192,1024]{1,0:T(8,128)(2,1)S(1)}, bf16[192,1024]{1,0:T(8,128)(2,1)S(1)}, u32[]{:S(2)}, u32[]{:S(2)}) %collective-permute-start.16) | collective-permute-done | bytes 393248 | tf_op jit(solution)/shard_map/while/body/eval_jaxpr/ppermute | solution.py:83
  403.0 13.0 %all-to-all-start = ((f32[256,1,4]{2,1,0:T(1,128)}), f32[256,1,4]{2,1,0:T(1,128)}, u32[]{:S(2)}, u32[]{:S(2)}) async-start(f32[256,1,4]{2,1,0:T(1,128)} %broadcast_in_dim.4), calls=%async_computation | async-start | bytes 262144 | tf_op jit(solution)/shard_map/while/body/eval_jaxpr/all_to_all | solution.py:39
  421.0 7.0 %all-to-all-done = f32[256,1,4]{2,1,0:T(1,128)} async-done(((f32[256,1,4]{2,1,0:T(1,128)}), f32[256,1,4]{2,1,0:T(1,128)}, u32[]{:S(2)}, u32[]{:S(2)}) %all-to-all-start) | async-done | bytes 4128 | tf_op jit(solution)/shard_map/while/body/eval_jaxpr/all_to_all | solution.py:39
  (377 shorter events, 283.4 us)
Async XLA Ops:
  22.0 11.9 %collective-permute-start.1 = (bf16[192,1024]{1,0:T(8,128)(2,1)S(1)}, bf16[192,1024]{1,0:T(8,128)(2,1)S(1)}, u32[]{:S(2)}, u32[]{:S(2)}) collective-permute-start(bf16[192,1024]{1,0:T(8,128)(2,1)S(1)} %dynamic-slice_convert_fusion.13), channel_id=1, source_target_pairs={{0,2},{1,3},{2,0},{3,1},{4,6},{5,7},{6,4},{7,5},{8,10},{9,11},{10,... | collective-permute-start | bytes 1179656 | tf_op jit(solution)/shard_map/while/body/eval_jaxpr/ppermute | solution.py:67
  34.1 11.4 %collective-permute-start.2 = (bf16[24,1024]{1,0:T(8,128)(2,1)S(1)}, bf16[24,1024]{1,0:T(8,128)(2,1)S(1)}, u32[]{:S(2)}, u32[]{:S(2)}) collective-permute-start(bf16[24,1024]{1,0:T(8,128)(2,1)S(1)} %get-tuple-element.219), channel_id=1, source_target_pairs={{0,28},{1,29},{2,30},{3,31},{4,24},{5,25},{6,26},{7,27},{8,20},{9,... | collective-permute-start | bytes 147464 | tf_op jit(solution)/shard_map/while/body/eval_jaxpr/ppermute | solution.py:67
  52.7 12.3 %collective-permute-start.10 = (bf16[24,1024]{1,0:T(8,128)(2,1)S(1)}, bf16[24,1024]{1,0:T(8,128)(2,1)S(1)}, u32[]{:S(2)}, u32[]{:S(2)}) collective-permute-start(bf16[24,1024]{1,0:T(8,128)(2,1)S(1)} %get-tuple-element.227), channel_id=1, source_target_pairs={{0,8},{1,9},{2,10},{3,11},{4,12},{5,13},{6,14},{7,15},{8,0},{9,1},... | collective-permute-start | bytes 147464 | tf_op jit(solution)/shard_map/while/body/eval_jaxpr/ppermute | solution.py:83
  54.5 10.6 %collective-permute-start.11 = (bf16[24,1024]{1,0:T(8,128)(2,1)S(1)}, bf16[24,1024]{1,0:T(8,128)(2,1)S(1)}, u32[]{:S(2)}, u32[]{:S(2)}) collective-permute-start(bf16[24,1024]{1,0:T(8,128)(2,1)S(1)} %get-tuple-element.227), channel_id=1, source_target_pairs={{0,12},{1,13},{2,14},{3,15},{4,8},{5,9},{6,10},{7,11},{8,4},{9,5},... | collective-permute-start | bytes 147464 | tf_op jit(solution)/shard_map/while/body/eval_jaxpr/ppermute | solution.py:83
  107.9 35.9 %collective-permute-start.25 = (f32[128,256]{0,1:T(8,128)S(1)}, f32[128,256]{0,1:T(8,128)}, u32[]{:S(2)}, u32[]{:S(2)}) collective-permute-start(f32[128,256]{0,1:T(8,128)S(1)} %get-tuple-element.234), channel_id=1, source_target_pairs={{0,32},{32,0},{64,96},{96,64},{128,160},{160,128},{192,224},{224,1... | collective-permute-start | bytes 393224 | tf_op jit(solution)/shard_map/while/body/eval_jaxpr/ppermute | solution.py:83
  113.8 24.3 %all-to-all-start = ((f32[256,1,4]{2,1,0:T(1,128)}), f32[256,1,4]{2,1,0:T(1,128)}, u32[]{:S(2)}, u32[]{:S(2)}) async-start(f32[256,1,4]{2,1,0:T(1,128)} %broadcast_in_dim.4), calls=%async_computation | async-start | bytes 262144 | tf_op jit(solution)/shard_map/while/body/eval_jaxpr/all_to_all | solution.py:39
  126.0 19.8 %collective-permute-start.26 = (f32[128,256]{0,1:T(8,128)S(1)}, f32[128,256]{0,1:T(8,128)}, u32[]{:S(2)}, u32[]{:S(2)}) collective-permute-start(f32[128,256]{0,1:T(8,128)S(1)} %get-tuple-element.234), channel_id=1, source_target_pairs={{0,64},{32,96},{64,0},{96,32},{128,192},{160,224},{192,128},{224,1... | collective-permute-start | bytes 393224 | tf_op jit(solution)/shard_map/while/body/eval_jaxpr/ppermute | solution.py:83
  129.0 20.3 %collective-permute-start.27 = (f32[128,256]{0,1:T(8,128)S(1)}, f32[128,256]{0,1:T(8,128)}, u32[]{:S(2)}, u32[]{:S(2)}) collective-permute-start(f32[128,256]{0,1:T(8,128)S(1)} %get-tuple-element.234), channel_id=1, source_target_pairs={{0,96},{32,64},{64,32},{96,0},{128,224},{160,192},{192,160},{224,1... | collective-permute-start | bytes 393224 | tf_op jit(solution)/shard_map/while/body/eval_jaxpr/ppermute | solution.py:83
  129.9 20.3 %collective-permute-start.28 = (f32[128,256]{0,1:T(8,128)S(1)}, f32[128,256]{0,1:T(8,128)}, u32[]{:S(2)}, u32[]{:S(2)}) collective-permute-start(f32[128,256]{0,1:T(8,128)S(1)} %get-tuple-element.234), channel_id=1, source_target_pairs={{0,128},{32,160},{64,192},{96,224},{128,0},{160,32},{192,64},{224,... | collective-permute-start | bytes 393224 | tf_op jit(solution)/shard_map/while/body/eval_jaxpr/ppermute | solution.py:83
  131.1 20.1 %collective-permute-start.29 = (f32[128,256]{0,1:T(8,128)S(1)}, f32[128,256]{0,1:T(8,128)}, u32[]{:S(2)}, u32[]{:S(2)}) collective-permute-start(f32[128,256]{0,1:T(8,128)S(1)} %get-tuple-element.234), channel_id=1, source_target_pairs={{0,160},{32,128},{64,224},{96,192},{128,32},{160,0},{192,96},{224,... | collective-permute-start | bytes 393224 | tf_op jit(solution)/shard_map/while/body/eval_jaxpr/ppermute | solution.py:83
  171.1 11.9 %collective-permute-start.1 = (bf16[192,1024]{1,0:T(8,128)(2,1)S(1)}, bf16[192,1024]{1,0:T(8,128)(2,1)S(1)}, u32[]{:S(2)}, u32[]{:S(2)}) collective-permute-start(bf16[192,1024]{1,0:T(8,128)(2,1)S(1)} %dynamic-slice_convert_fusion.13), channel_id=1, source_target_pairs={{0,2},{1,3},{2,0},{3,1},{4,6},{5,7},{6,4},{7,5},{8,10},{9,11},{10,... | collective-permute-start | bytes 1179656 | tf_op jit(solution)/shard_map/while/body/eval_jaxpr/ppermute | solution.py:67
  252.8 36.0 %collective-permute-start.25 = (f32[128,256]{0,1:T(8,128)S(1)}, f32[128,256]{0,1:T(8,128)}, u32[]{:S(2)}, u32[]{:S(2)}) collective-permute-start(f32[128,256]{0,1:T(8,128)S(1)} %get-tuple-element.234), channel_id=1, source_target_pairs={{0,32},{32,0},{64,96},{96,64},{128,160},{160,128},{192,224},{224,1... | collective-permute-start | bytes 393224 | tf_op jit(solution)/shard_map/while/body/eval_jaxpr/ppermute | solution.py:83
  258.0 25.0 %all-to-all-start = ((f32[256,1,4]{2,1,0:T(1,128)}), f32[256,1,4]{2,1,0:T(1,128)}, u32[]{:S(2)}, u32[]{:S(2)}) async-start(f32[256,1,4]{2,1,0:T(1,128)} %broadcast_in_dim.4), calls=%async_computation | async-start | bytes 262144 | tf_op jit(solution)/shard_map/while/body/eval_jaxpr/all_to_all | solution.py:39
  271.1 19.8 %collective-permute-start.26 = (f32[128,256]{0,1:T(8,128)S(1)}, f32[128,256]{0,1:T(8,128)}, u32[]{:S(2)}, u32[]{:S(2)}) collective-permute-start(f32[128,256]{0,1:T(8,128)S(1)} %get-tuple-element.234), channel_id=1, source_target_pairs={{0,64},{32,96},{64,0},{96,32},{128,192},{160,224},{192,128},{224,1... | collective-permute-start | bytes 393224 | tf_op jit(solution)/shard_map/while/body/eval_jaxpr/ppermute | solution.py:83
  274.0 20.3 %collective-permute-start.27 = (f32[128,256]{0,1:T(8,128)S(1)}, f32[128,256]{0,1:T(8,128)}, u32[]{:S(2)}, u32[]{:S(2)}) collective-permute-start(f32[128,256]{0,1:T(8,128)S(1)} %get-tuple-element.234), channel_id=1, source_target_pairs={{0,96},{32,64},{64,32},{96,0},{128,224},{160,192},{192,160},{224,1... | collective-permute-start | bytes 393224 | tf_op jit(solution)/shard_map/while/body/eval_jaxpr/ppermute | solution.py:83
  274.9 20.3 %collective-permute-start.28 = (f32[128,256]{0,1:T(8,128)S(1)}, f32[128,256]{0,1:T(8,128)}, u32[]{:S(2)}, u32[]{:S(2)}) collective-permute-start(f32[128,256]{0,1:T(8,128)S(1)} %get-tuple-element.234), channel_id=1, source_target_pairs={{0,128},{32,160},{64,192},{96,224},{128,0},{160,32},{192,64},{224,... | collective-permute-start | bytes 393224 | tf_op jit(solution)/shard_map/while/body/eval_jaxpr/ppermute | solution.py:83
  276.1 20.1 %collective-permute-start.29 = (f32[128,256]{0,1:T(8,128)S(1)}, f32[128,256]{0,1:T(8,128)}, u32[]{:S(2)}, u32[]{:S(2)}) collective-permute-start(f32[128,256]{0,1:T(8,128)S(1)} %get-tuple-element.234), channel_id=1, source_target_pairs={{0,160},{32,128},{64,224},{96,192},{128,32},{160,0},{192,96},{224,... | collective-permute-start | bytes 393224 | tf_op jit(solution)/shard_map/while/body/eval_jaxpr/ppermute | solution.py:83
  316.1 11.9 %collective-permute-start.1 = (bf16[192,1024]{1,0:T(8,128)(2,1)S(1)}, bf16[192,1024]{1,0:T(8,128)(2,1)S(1)}, u32[]{:S(2)}, u32[]{:S(2)}) collective-permute-start(bf16[192,1024]{1,0:T(8,128)(2,1)S(1)} %dynamic-slice_convert_fusion.13), channel_id=1, source_target_pairs={{0,2},{1,3},{2,0},{3,1},{4,6},{5,7},{6,4},{7,5},{8,10},{9,11},{10,... | collective-permute-start | bytes 1179656 | tf_op jit(solution)/shard_map/while/body/eval_jaxpr/ppermute | solution.py:67
  397.7 36.0 %collective-permute-start.25 = (f32[128,256]{0,1:T(8,128)S(1)}, f32[128,256]{0,1:T(8,128)}, u32[]{:S(2)}, u32[]{:S(2)}) collective-permute-start(f32[128,256]{0,1:T(8,128)S(1)} %get-tuple-element.234), channel_id=1, source_target_pairs={{0,32},{32,0},{64,96},{96,64},{128,160},{160,128},{192,224},{224,1... | collective-permute-start | bytes 393224 | tf_op jit(solution)/shard_map/while/body/eval_jaxpr/ppermute | solution.py:83
  403.0 25.0 %all-to-all-start = ((f32[256,1,4]{2,1,0:T(1,128)}), f32[256,1,4]{2,1,0:T(1,128)}, u32[]{:S(2)}, u32[]{:S(2)}) async-start(f32[256,1,4]{2,1,0:T(1,128)} %broadcast_in_dim.4), calls=%async_computation | async-start | bytes 262144 | tf_op jit(solution)/shard_map/while/body/eval_jaxpr/all_to_all | solution.py:39
  416.0 19.8 %collective-permute-start.26 = (f32[128,256]{0,1:T(8,128)S(1)}, f32[128,256]{0,1:T(8,128)}, u32[]{:S(2)}, u32[]{:S(2)}) collective-permute-start(f32[128,256]{0,1:T(8,128)S(1)} %get-tuple-element.234), channel_id=1, source_target_pairs={{0,64},{32,96},{64,0},{96,32},{128,192},{160,224},{192,128},{224,1... | collective-permute-start | bytes 393224 | tf_op jit(solution)/shard_map/while/body/eval_jaxpr/ppermute | solution.py:83
  419.0 20.3 %collective-permute-start.27 = (f32[128,256]{0,1:T(8,128)S(1)}, f32[128,256]{0,1:T(8,128)}, u32[]{:S(2)}, u32[]{:S(2)}) collective-permute-start(f32[128,256]{0,1:T(8,128)S(1)} %get-tuple-element.234), channel_id=1, source_target_pairs={{0,96},{32,64},{64,32},{96,0},{128,224},{160,192},{192,160},{224,1... | collective-permute-start | bytes 393224 | tf_op jit(solution)/shard_map/while/body/eval_jaxpr/ppermute | solution.py:83
  419.8 20.3 %collective-permute-start.28 = (f32[128,256]{0,1:T(8,128)S(1)}, f32[128,256]{0,1:T(8,128)}, u32[]{:S(2)}, u32[]{:S(2)}) collective-permute-start(f32[128,256]{0,1:T(8,128)S(1)} %get-tuple-element.234), channel_id=1, source_target_pairs={{0,128},{32,160},{64,192},{96,224},{128,0},{160,32},{192,64},{224,... | collective-permute-start | bytes 393224 | tf_op jit(solution)/shard_map/while/body/eval_jaxpr/ppermute | solution.py:83
  421.0 20.1 %collective-permute-start.29 = (f32[128,256]{0,1:T(8,128)S(1)}, f32[128,256]{0,1:T(8,128)}, u32[]{:S(2)}, u32[]{:S(2)}) collective-permute-start(f32[128,256]{0,1:T(8,128)S(1)} %get-tuple-element.234), channel_id=1, source_target_pairs={{0,160},{32,128},{64,224},{96,192},{128,32},{160,0},{192,96},{224,... | collective-permute-start | bytes 393224 | tf_op jit(solution)/shard_map/while/body/eval_jaxpr/ppermute | solution.py:83
  (106 other events, 890.8 us)

commit v10 on v9

--- a/solution.py
+++ b/solution.py
@@ -53,6 +53,14 @@
     return groups
 
 
+def chunk_position(axis, groups):
+    index = lax.axis_index(axis)
+    position = 0
+    for low, bits in groups:
+        position = position * (1 << bits) + ((index >> low) & ((1 << bits) - 1))
+    return position
+
+
 def spread_reduce(value, axis, groups, send_type):
     size = lax.axis_size(axis)
     index = lax.axis_index(axis)
@@ -105,10 +113,10 @@
     grad_pre = (slope_act * back_act).astype(jnp.bfloat16)
     part_out_t = contract_rows(cotangent, hidden_act)
     part_in = contract_rows(normed, grad_pre)
-    dp_groups = digit_groups(lax.axis_size("dp"), (3,))
+    dp_groups = digit_groups(lax.axis_size("dp"), (2, 1))
     reduced = spread_reduce(jnp.concatenate([part_in, part_out_t], axis=1), "dp", dp_groups, jnp.float32)
     rows = reduced.shape[0]
-    start = lax.axis_index("dp") * rows
+    start = chunk_position("dp", dp_groups) * rows
     direction_chunk = lax.dynamic_slice_in_dim(direction, start, rows, 0)
     residual_chunk = lax.dynamic_slice_in_dim(residual, start, rows, 0)
     fisher_chunk = reduced + damping * direction_chunk

time: 455 us -> 475 us (1.044)
  waiting for transfers between devices: 145 us -> 198 us
  starting transfers between devices: 189 us -> 158 us
    ppermute x48 -> x39, waiting for transfers between devices: 77.2 us -> 99.3 us  [spread_reduce(): lax.ppermute(send.astype(send_type), axis, xor_pairs(size, offset << low))]
    all_to_all x3, waiting for transfers between devices: 20.9 us -> 38.2 us  [scalar_sum(): lax.all_to_all(jnp.broadcast_to(values[None], (size,) + values.shape), ax...]
    ppermute x48 -> x39, starting transfers between devices: 80.2 us -> 65.3 us  [spread_gather(): got = lax.ppermute(chunk, axis, xor_pairs(size, offset << low))]
    ppermute x48 -> x39, waiting for transfers between devices: 46.5 us -> 61 us  [spread_gather(): got = lax.ppermute(chunk, axis, xor_pairs(size, offset << low))]
    ppermute x48 -> x39, starting transfers between devices: 70.4 us -> 57.9 us  [spread_reduce(): lax.ppermute(send.astype(send_type), axis, xor_pairs(size, offset << low))]
    dynamic_update_slice x48 -> x39, local copies, waits for them, and re-layouts: 17.7 us -> 6.36 us  [spread_gather(): lax.dynamic_update_slice_in_dim(whole, got, (digit ^ offset) * rows, 0)]
    dynamic_update_slice x6 -> x9, local copies, waits for them, and re-layouts: 0.31 us -> 6.31 us  [spread_gather(): whole = lax.dynamic_update_slice_in_dim(whole, chunk, digit * rows, 0)]
  transfers between devices with their start and end apart: 99 -> 81, of which waited for: 47 -> 47; matrix products, arithmetic and copies ran while one was open for 8% -> 6% of each run, Pallas kernels for 0% -> 0%
where the time goes in v10:
time: 475 us; the launch traced here: 474 us
  waiting for transfers between devices  198 us (42%)
  starting transfers between devices  158 us (33%)
  local copies, waits for them, and re-layouts  37.6 us (8%)
  other arithmetic  37.1 us (8%)
  matrix products  29.5 us (6%)
  loops' own time  12.3 us (3%)
    ppermute x39, waiting for transfers between devices, spread_reduce(): lax.ppermute(send.astype(send_type), axis, xor_pairs(size, offset << low))  99.3 us
    ppermute x39, starting transfers between devices, spread_gather(): got = lax.ppermute(chunk, axis, xor_pairs(size, offset << low))  65.3 us
    ppermute x39, waiting for transfers between devices, spread_gather(): got = lax.ppermute(chunk, axis, xor_pairs(size, offset << low))  61 us
    ppermute x39, starting transfers between devices, spread_reduce(): lax.ppermute(send.astype(send_type), axis, xor_pairs(size, offset << low))  57.9 us
    all_to_all x3, waiting for transfers between devices, scalar_sum(): lax.all_to_all(jnp.broadcast_to(values[None], (size,) + values.shape), ax...  38.2 us
    all_to_all x3, starting transfers between devices, scalar_sum(): lax.all_to_all(jnp.broadcast_to(values[None], (size,) + values.shape), ax...  35.2 us
    dot_general x6, matrix products, contract_rows(): lax.dot_general(left_side, right_side, (((0,), (0,)), ((), ())), preferre...  13.4 us
    another operation x1, loops' own time, on_device(): lax.fori_loop(0, ITERS, iterate, (jnp.zeros_like(residual), residual, res...  12.3 us
  transfers between devices with their start and end apart: 81, of which 47 were waited for; matrix products, arithmetic and copies ran while one was open for 6% of the time, Pallas kernels for 0%

profile of v10, /device:TPU:1, one launch (start us, length us, event | category | flops | bytes accessed | tf_op | source)
XLA Modules:
  0.0 474.1 jit_solution(18188340656606564525)
XLA Ops:
  7.2 461.0 %while.15 = (s32[]{:T(128)}, f32[1024,256]{0,1:T(8,128)}, f32[1024,256]{0,1:T(8,128)}, f32[1024,256]{0,1:T(8,128)S(1)}, bf16[768,1024]{1,0:T(8,128)(2,1)}, /*ind...) while((s32[]{:T(128)}, f32[1024,256]{0,1:T(8,128)}, ...), condition=%wide.region_7.8_spmd.clone, body=%wide.region_1.7_spmd.clone.sunk | while | flops 1215202304 | bytes 112036928 | solution.py:160
  23.1 10.8 %collective-permute-done.1 = bf16[192,1024]{1,0:T(8,128)(2,1)S(1)} collective-permute-done((bf16[192,1024]{1,0:T(8,128)(2,1)S(1)}, bf16[192,1024]{1,0:T(8,128)(2,1)S(1)}, u32[]{:S(2)}, u32[]{:S(2)}) %collective-permute-start.1) | collective-permute-done | bytes 393248 | tf_op jit(solution)/shard_map/while/body/eval_jaxpr/ppermute | solution.py:75
  34.1 4.0 collective-permute-start.2
  56.2 4.7 %collective-permute-start.12 = (bf16[24,1024]{1,0:T(8,128)(2,1)S(1)}, bf16[24,1024]{1,0:T(8,128)(2,1)S(1)}, u32[]{:S(2)}, u32[]{:S(2)}) collective-permute-start(bf16[24,1024]{1,0:T(8,128)(2,1)S(1)} %get-tuple-element.221), channel_id=1, source_target_pairs={{0,16},{1,17},{2,18},{3,19},{4,20},{5,21},{6,22},{7,23},{8,24},{9,... | collective-permute-start | bytes 147464 | tf_op jit(solution)/shard_map/while/body/eval_jaxpr/ppermute | solution.py:91
  60.9 4.0 collective-permute-start.14
  75.4 5.3 %collective-permute-done.16 = bf16[192,1024]{1,0:T(8,128)(2,1)S(1)} collective-permute-done((bf16[192,1024]{1,0:T(8,128)(2,1)S(1)}, bf16[192,1024]{1,0:T(8,128)(2,1)S(1)}, u32[]{:S(2)}, u32[]{:S(2)}) %collective-permute-start.16) | collective-permute-done | bytes 393248 | tf_op jit(solution)/shard_map/while/body/eval_jaxpr/ppermute | solution.py:91
  96.8 11.3 %collective-permute-done.18 = f32[256,256]{0,1:T(8,128)S(1)} collective-permute-done((f32[256,256]{0,1:T(8,128)}, f32[256,256]{0,1:T(8,128)S(1)}, u32[]{:S(2)}, u32[]{:S(2)}) %collective-permute-start.18) | collective-permute-done | bytes 262176 | tf_op jit(solution)/shard_map/while/body/eval_jaxpr/ppermute | solution.py:75
  121.1 13.7 %all-to-all-start = ((f32[256,1,4]{2,1,0:T(1,128)}), f32[256,1,4]{2,1,0:T(1,128)S(1)}, u32[]{:S(2)}, u32[]{:S(2)}) async-start(f32[256,1,4]{2,1,0:T(1,128)} %broadcast_in_dim.4), calls=%async_computation | async-start | bytes 262144 | tf_op jit(solution)/shard_map/while/body/eval_jaxpr/all_to_all | solution.py:39
  134.8 12.7 %all-to-all-done = f32[256,1,4]{2,1,0:T(1,128)S(1)} async-done(((f32[256,1,4]{2,1,0:T(1,128)}), f32[256,1,4]{2,1,0:T(1,128)S(1)}, u32[]{:S(2)}, u32[]{:S(2)}) %all-to-all-start) | async-done | bytes 4128 | tf_op jit(solution)/shard_map/while/body/eval_jaxpr/all_to_all | solution.py:39
  156.3 6.0 %collective-permute-done.25 = f32[256,256]{0,1:T(8,128)S(1)} collective-permute-done((f32[256,256]{0,1:T(8,128)S(1)}, f32[256,256]{0,1:T(8,128)S(1)}, u32[]{:S(2)}, u32[]{:S(2)}) %collective-permute-start.25) | collective-permute-done | bytes 262176 | tf_op jit(solution)/shard_map/while/body/eval_jaxpr/ppermute | solution.py:91
  180.4 10.9 %collective-permute-done.1 = bf16[192,1024]{1,0:T(8,128)(2,1)S(1)} collective-permute-done((bf16[192,1024]{1,0:T(8,128)(2,1)S(1)}, bf16[192,1024]{1,0:T(8,128)(2,1)S(1)}, u32[]{:S(2)}, u32[]{:S(2)}) %collective-permute-start.1) | collective-permute-done | bytes 393248 | tf_op jit(solution)/shard_map/while/body/eval_jaxpr/ppermute | solution.py:75
  195.7 3.9 collective-permute-start.5
  227.4 6.9 %collective-permute-done.16 = bf16[192,1024]{1,0:T(8,128)(2,1)S(1)} collective-permute-done((bf16[192,1024]{1,0:T(8,128)(2,1)S(1)}, bf16[192,1024]{1,0:T(8,128)(2,1)S(1)}, u32[]{:S(2)}, u32[]{:S(2)}) %collective-permute-start.16) | collective-permute-done | bytes 393248 | tf_op jit(solution)/shard_map/while/body/eval_jaxpr/ppermute | solution.py:91
  250.7 11.3 %collective-permute-done.18 = f32[256,256]{0,1:T(8,128)S(1)} collective-permute-done((f32[256,256]{0,1:T(8,128)}, f32[256,256]{0,1:T(8,128)S(1)}, u32[]{:S(2)}, u32[]{:S(2)}) %collective-permute-start.18) | collective-permute-done | bytes 262176 | tf_op jit(solution)/shard_map/while/body/eval_jaxpr/ppermute | solution.py:75
  274.9 10.8 %all-to-all-start = ((f32[256,1,4]{2,1,0:T(1,128)}), f32[256,1,4]{2,1,0:T(1,128)S(1)}, u32[]{:S(2)}, u32[]{:S(2)}) async-start(f32[256,1,4]{2,1,0:T(1,128)} %broadcast_in_dim.4), calls=%async_computation | async-start | bytes 262144 | tf_op jit(solution)/shard_map/while/body/eval_jaxpr/all_to_all | solution.py:39
  285.7 12.7 %all-to-all-done = f32[256,1,4]{2,1,0:T(1,128)S(1)} async-done(((f32[256,1,4]{2,1,0:T(1,128)}), f32[256,1,4]{2,1,0:T(1,128)S(1)}, u32[]{:S(2)}, u32[]{:S(2)}) %all-to-all-start) | async-done | bytes 4128 | tf_op jit(solution)/shard_map/while/body/eval_jaxpr/all_to_all | solution.py:39
  307.2 6.0 %collective-permute-done.25 = f32[256,256]{0,1:T(8,128)S(1)} collective-permute-done((f32[256,256]{0,1:T(8,128)S(1)}, f32[256,256]{0,1:T(8,128)S(1)}, u32[]{:S(2)}, u32[]{:S(2)}) %collective-permute-start.25) | collective-permute-done | bytes 262176 | tf_op jit(solution)/shard_map/while/body/eval_jaxpr/ppermute | solution.py:91
  331.3 10.9 %collective-permute-done.1 = bf16[192,1024]{1,0:T(8,128)(2,1)S(1)} collective-permute-done((bf16[192,1024]{1,0:T(8,128)(2,1)S(1)}, bf16[192,1024]{1,0:T(8,128)(2,1)S(1)}, u32[]{:S(2)}, u32[]{:S(2)}) %collective-permute-start.1) | collective-permute-done | bytes 393248 | tf_op jit(solution)/shard_map/while/body/eval_jaxpr/ppermute | solution.py:75
  346.6 3.9 collective-permute-start.5
  378.3 6.9 %collective-permute-done.16 = bf16[192,1024]{1,0:T(8,128)(2,1)S(1)} collective-permute-done((bf16[192,1024]{1,0:T(8,128)(2,1)S(1)}, bf16[192,1024]{1,0:T(8,128)(2,1)S(1)}, u32[]{:S(2)}, u32[]{:S(2)}) %collective-permute-start.16) | collective-permute-done | bytes 393248 | tf_op jit(solution)/shard_map/while/body/eval_jaxpr/ppermute | solution.py:91
  401.6 11.3 %collective-permute-done.18 = f32[256,256]{0,1:T(8,128)S(1)} collective-permute-done((f32[256,256]{0,1:T(8,128)}, f32[256,256]{0,1:T(8,128)S(1)}, u32[]{:S(2)}, u32[]{:S(2)}) %collective-permute-start.18) | collective-permute-done | bytes 262176 | tf_op jit(solution)/shard_map/while/body/eval_jaxpr/ppermute | solution.py:75
  425.8 10.8 %all-to-all-start = ((f32[256,1,4]{2,1,0:T(1,128)}), f32[256,1,4]{2,1,0:T(1,128)S(1)}, u32[]{:S(2)}, u32[]{:S(2)}) async-start(f32[256,1,4]{2,1,0:T(1,128)} %broadcast_in_dim.4), calls=%async_computation | async-start | bytes 262144 | tf_op jit(solution)/shard_map/while/body/eval_jaxpr/all_to_all | solution.py:39
  436.6 12.7 %all-to-all-done = f32[256,1,4]{2,1,0:T(1,128)S(1)} async-done(((f32[256,1,4]{2,1,0:T(1,128)}), f32[256,1,4]{2,1,0:T(1,128)S(1)}, u32[]{:S(2)}, u32[]{:S(2)}) %all-to-all-start) | async-done | bytes 4128 | tf_op jit(solution)/shard_map/while/body/eval_jaxpr/all_to_all | solution.py:39
  458.1 6.0 %collective-permute-done.25 = f32[256,256]{0,1:T(8,128)S(1)} collective-permute-done((f32[256,256]{0,1:T(8,128)S(1)}, f32[256,256]{0,1:T(8,128)S(1)}, u32[]{:S(2)}, u32[]{:S(2)}) %collective-permute-start.25) | collective-permute-done | bytes 262176 | tf_op jit(solution)/shard_map/while/body/eval_jaxpr/ppermute | solution.py:91
  (335 shorter events, 263.7 us)
Async XLA Ops:
  22.0 11.9 %collective-permute-start.1 = (bf16[192,1024]{1,0:T(8,128)(2,1)S(1)}, bf16[192,1024]{1,0:T(8,128)(2,1)S(1)}, u32[]{:S(2)}, u32[]{:S(2)}) collective-permute-start(bf16[192,1024]{1,0:T(8,128)(2,1)S(1)} %dynamic-slice_convert_fusion.13), channel_id=1, source_target_pairs={{0,2},{1,3},{2,0},{3,1},{4,6},{5,7},{6,4},{7,5},{8,10},{9,11},{10,... | collective-permute-start | bytes 1179656 | tf_op jit(solution)/shard_map/while/body/eval_jaxpr/ppermute | solution.py:75
  34.1 11.4 %collective-permute-start.2 = (bf16[24,1024]{1,0:T(8,128)(2,1)S(1)}, bf16[24,1024]{1,0:T(8,128)(2,1)S(1)}, u32[]{:S(2)}, u32[]{:S(2)}) collective-permute-start(bf16[24,1024]{1,0:T(8,128)(2,1)S(1)} %get-tuple-element.213), channel_id=1, source_target_pairs={{0,28},{1,29},{2,30},{3,31},{4,24},{5,25},{6,26},{7,27},{8,20},{9,... | collective-permute-start | bytes 147464 | tf_op jit(solution)/shard_map/while/body/eval_jaxpr/ppermute | solution.py:75
  52.7 12.3 %collective-permute-start.10 = (bf16[24,1024]{1,0:T(8,128)(2,1)S(1)}, bf16[24,1024]{1,0:T(8,128)(2,1)S(1)}, u32[]{:S(2)}, u32[]{:S(2)}) collective-permute-start(bf16[24,1024]{1,0:T(8,128)(2,1)S(1)} %get-tuple-element.221), channel_id=1, source_target_pairs={{0,8},{1,9},{2,10},{3,11},{4,12},{5,13},{6,14},{7,15},{8,0},{9,1},... | collective-permute-start | bytes 147464 | tf_op jit(solution)/shard_map/while/body/eval_jaxpr/ppermute | solution.py:91
  54.5 10.6 %collective-permute-start.11 = (bf16[24,1024]{1,0:T(8,128)(2,1)S(1)}, bf16[24,1024]{1,0:T(8,128)(2,1)S(1)}, u32[]{:S(2)}, u32[]{:S(2)}) collective-permute-start(bf16[24,1024]{1,0:T(8,128)(2,1)S(1)} %get-tuple-element.221), channel_id=1, source_target_pairs={{0,12},{1,13},{2,14},{3,15},{4,8},{5,9},{6,10},{7,11},{8,4},{9,5},... | collective-permute-start | bytes 147464 | tf_op jit(solution)/shard_map/while/body/eval_jaxpr/ppermute | solution.py:91
  93.5 14.7 %collective-permute-start.18 = (f32[256,256]{0,1:T(8,128)}, f32[256,256]{0,1:T(8,128)S(1)}, u32[]{:S(2)}, u32[]{:S(2)}) collective-permute-start(f32[256,256]{0,1:T(8,128)} %get-tuple-element.222), channel_id=1, source_target_pairs={{0,96},{32,64},{64,32},{96,0},{128,224},{160,192},{192,160},{224,1... | collective-permute-start | bytes 786440 | tf_op jit(solution)/shard_map/while/body/eval_jaxpr/ppermute | solution.py:75
  96.2 11.9 %collective-permute-start.19 = (f32[256,256]{0,1:T(8,128)}, f32[256,256]{0,1:T(8,128)S(1)}, u32[]{:S(2)}, u32[]{:S(2)}) collective-permute-start(f32[256,256]{0,1:T(8,128)} %get-tuple-element.223), channel_id=1, source_target_pairs={{0,64},{32,96},{64,0},{96,32},{128,192},{160,224},{192,128},{224,1... | collective-permute-start | bytes 786440 | tf_op jit(solution)/shard_map/while/body/eval_jaxpr/ppermute | solution.py:75
  96.6 12.0 %collective-permute-start.20 = (f32[256,256]{0,1:T(8,128)S(1)}, f32[256,256]{0,1:T(8,128)S(1)}, u32[]{:S(2)}, u32[]{:S(2)}) collective-permute-start(f32[256,256]{0,1:T(8,128)S(1)} %get-tuple-element.224), channel_id=1, source_target_pairs={{0,32},{32,0},{64,96},{96,64},{128,160},{160,128},{192,224},{224,1... | collective-permute-start | bytes 786440 | tf_op jit(solution)/shard_map/while/body/eval_jaxpr/ppermute | solution.py:75
  116.5 38.6 %collective-permute-start.23 = (f32[256,256]{0,1:T(8,128)S(1)}, f32[256,256]{0,1:T(8,128)S(1)}, u32[]{:S(2)}, u32[]{:S(2)}) collective-permute-start(f32[256,256]{0,1:T(8,128)S(1)} %constant_dynamic-update-slice_fusion.49), channel_id=1, source_target_pairs={{0,32},{32,0},{64,96},{96,64},{128,160},{160,128},{192,224},{224,1... | collective-permute-start | bytes 786440 | tf_op jit(solution)/shard_map/while/body/eval_jaxpr/ppermute | solution.py:91
  121.1 26.4 %all-to-all-start = ((f32[256,1,4]{2,1,0:T(1,128)}), f32[256,1,4]{2,1,0:T(1,128)S(1)}, u32[]{:S(2)}, u32[]{:S(2)}) async-start(f32[256,1,4]{2,1,0:T(1,128)} %broadcast_in_dim.4), calls=%async_computation | async-start | bytes 262144 | tf_op jit(solution)/shard_map/while/body/eval_jaxpr/all_to_all | solution.py:39
  179.4 11.9 %collective-permute-start.1 = (bf16[192,1024]{1,0:T(8,128)(2,1)S(1)}, bf16[192,1024]{1,0:T(8,128)(2,1)S(1)}, u32[]{:S(2)}, u32[]{:S(2)}) collective-permute-start(bf16[192,1024]{1,0:T(8,128)(2,1)S(1)} %dynamic-slice_convert_fusion.13), channel_id=1, source_target_pairs={{0,2},{1,3},{2,0},{3,1},{4,6},{5,7},{6,4},{7,5},{8,10},{9,11},{10,... | collective-permute-start | bytes 1179656 | tf_op jit(solution)/shard_map/while/body/eval_jaxpr/ppermute | solution.py:75
  192.0 10.6 %collective-permute-start.3 = (bf16[24,1024]{1,0:T(8,128)(2,1)S(1)}, bf16[24,1024]{1,0:T(8,128)(2,1)S(1)}, u32[]{:S(2)}, u32[]{:S(2)}) collective-permute-start(bf16[24,1024]{1,0:T(8,128)(2,1)S(1)} %get-tuple-element.214), channel_id=1, source_target_pairs={{0,24},{1,25},{2,26},{3,27},{4,28},{5,29},{6,30},{7,31},{8,16},{9,... | collective-permute-start | bytes 147464 | tf_op jit(solution)/shard_map/while/body/eval_jaxpr/ppermute | solution.py:75
  247.4 14.5 %collective-permute-start.18 = (f32[256,256]{0,1:T(8,128)}, f32[256,256]{0,1:T(8,128)S(1)}, u32[]{:S(2)}, u32[]{:S(2)}) collective-permute-start(f32[256,256]{0,1:T(8,128)} %get-tuple-element.222), channel_id=1, source_target_pairs={{0,96},{32,64},{64,32},{96,0},{128,224},{160,192},{192,160},{224,1... | collective-permute-start | bytes 786440 | tf_op jit(solution)/shard_map/while/body/eval_jaxpr/ppermute | solution.py:75
  249.6 12.4 %collective-permute-start.19 = (f32[256,256]{0,1:T(8,128)}, f32[256,256]{0,1:T(8,128)S(1)}, u32[]{:S(2)}, u32[]{:S(2)}) collective-permute-start(f32[256,256]{0,1:T(8,128)} %get-tuple-element.223), channel_id=1, source_target_pairs={{0,64},{32,96},{64,0},{96,32},{128,192},{160,224},{192,128},{224,1... | collective-permute-start | bytes 786440 | tf_op jit(solution)/shard_map/while/body/eval_jaxpr/ppermute | solution.py:75
  250.4 11.9 %collective-permute-start.20 = (f32[256,256]{0,1:T(8,128)S(1)}, f32[256,256]{0,1:T(8,128)S(1)}, u32[]{:S(2)}, u32[]{:S(2)}) collective-permute-start(f32[256,256]{0,1:T(8,128)S(1)} %get-tuple-element.224), channel_id=1, source_target_pairs={{0,32},{32,0},{64,96},{96,64},{128,160},{160,128},{192,224},{224,1... | collective-permute-start | bytes 786440 | tf_op jit(solution)/shard_map/while/body/eval_jaxpr/ppermute | solution.py:75
  270.3 35.7 %collective-permute-start.23 = (f32[256,256]{0,1:T(8,128)S(1)}, f32[256,256]{0,1:T(8,128)S(1)}, u32[]{:S(2)}, u32[]{:S(2)}) collective-permute-start(f32[256,256]{0,1:T(8,128)S(1)} %constant_dynamic-update-slice_fusion.49), channel_id=1, source_target_pairs={{0,32},{32,0},{64,96},{96,64},{128,160},{160,128},{192,224},{224,1... | collective-permute-start | bytes 786440 | tf_op jit(solution)/shard_map/while/body/eval_jaxpr/ppermute | solution.py:91
  274.9 23.5 %all-to-all-start = ((f32[256,1,4]{2,1,0:T(1,128)}), f32[256,1,4]{2,1,0:T(1,128)S(1)}, u32[]{:S(2)}, u32[]{:S(2)}) async-start(f32[256,1,4]{2,1,0:T(1,128)} %broadcast_in_dim.4), calls=%async_computation | async-start | bytes 262144 | tf_op jit(solution)/shard_map/while/body/eval_jaxpr/all_to_all | solution.py:39
  330.3 11.9 %collective-permute-start.1 = (bf16[192,1024]{1,0:T(8,128)(2,1)S(1)}, bf16[192,1024]{1,0:T(8,128)(2,1)S(1)}, u32[]{:S(2)}, u32[]{:S(2)}) collective-permute-start(bf16[192,1024]{1,0:T(8,128)(2,1)S(1)} %dynamic-slice_convert_fusion.13), channel_id=1, source_target_pairs={{0,2},{1,3},{2,0},{3,1},{4,6},{5,7},{6,4},{7,5},{8,10},{9,11},{10,... | collective-permute-start | bytes 1179656 | tf_op jit(solution)/shard_map/while/body/eval_jaxpr/ppermute | solution.py:75
  342.9 10.6 %collective-permute-start.3 = (bf16[24,1024]{1,0:T(8,128)(2,1)S(1)}, bf16[24,1024]{1,0:T(8,128)(2,1)S(1)}, u32[]{:S(2)}, u32[]{:S(2)}) collective-permute-start(bf16[24,1024]{1,0:T(8,128)(2,1)S(1)} %get-tuple-element.214), channel_id=1, source_target_pairs={{0,24},{1,25},{2,26},{3,27},{4,28},{5,29},{6,30},{7,31},{8,16},{9,... | collective-permute-start | bytes 147464 | tf_op jit(solution)/shard_map/while/body/eval_jaxpr/ppermute | solution.py:75
  361.4 10.2 %collective-permute-start.11 = (bf16[24,1024]{1,0:T(8,128)(2,1)S(1)}, bf16[24,1024]{1,0:T(8,128)(2,1)S(1)}, u32[]{:S(2)}, u32[]{:S(2)}) collective-permute-start(bf16[24,1024]{1,0:T(8,128)(2,1)S(1)} %get-tuple-element.221), channel_id=1, source_target_pairs={{0,12},{1,13},{2,14},{3,15},{4,8},{5,9},{6,10},{7,11},{8,4},{9,5},... | collective-permute-start | bytes 147464 | tf_op jit(solution)/shard_map/while/body/eval_jaxpr/ppermute | solution.py:91
  398.3 14.5 %collective-permute-start.18 = (f32[256,256]{0,1:T(8,128)}, f32[256,256]{0,1:T(8,128)S(1)}, u32[]{:S(2)}, u32[]{:S(2)}) collective-permute-start(f32[256,256]{0,1:T(8,128)} %get-tuple-element.222), channel_id=1, source_target_pairs={{0,96},{32,64},{64,32},{96,0},{128,224},{160,192},{192,160},{224,1... | collective-permute-start | bytes 786440 | tf_op jit(solution)/shard_map/while/body/eval_jaxpr/ppermute | solution.py:75
  400.5 12.4 %collective-permute-start.19 = (f32[256,256]{0,1:T(8,128)}, f32[256,256]{0,1:T(8,128)S(1)}, u32[]{:S(2)}, u32[]{:S(2)}) collective-permute-start(f32[256,256]{0,1:T(8,128)} %get-tuple-element.223), channel_id=1, source_target_pairs={{0,64},{32,96},{64,0},{96,32},{128,192},{160,224},{192,128},{224,1... | collective-permute-start | bytes 786440 | tf_op jit(solution)/shard_map/while/body/eval_jaxpr/ppermute | solution.py:75
  401.3 11.9 %collective-permute-start.20 = (f32[256,256]{0,1:T(8,128)S(1)}, f32[256,256]{0,1:T(8,128)S(1)}, u32[]{:S(2)}, u32[]{:S(2)}) collective-permute-start(f32[256,256]{0,1:T(8,128)S(1)} %get-tuple-element.224), channel_id=1, source_target_pairs={{0,32},{32,0},{64,96},{96,64},{128,160},{160,128},{192,224},{224,1... | collective-permute-start | bytes 786440 | tf_op jit(solution)/shard_map/while/body/eval_jaxpr/ppermute | solution.py:75
  421.3 35.7 %collective-permute-start.23 = (f32[256,256]{0,1:T(8,128)S(1)}, f32[256,256]{0,1:T(8,128)S(1)}, u32[]{:S(2)}, u32[]{:S(2)}) collective-permute-start(f32[256,256]{0,1:T(8,128)S(1)} %constant_dynamic-update-slice_fusion.49), channel_id=1, source_target_pairs={{0,32},{32,0},{64,96},{96,64},{128,160},{160,128},{192,224},{224,1... | collective-permute-start | bytes 786440 | tf_op jit(solution)/shard_map/while/body/eval_jaxpr/ppermute | solution.py:91
  425.8 23.5 %all-to-all-start = ((f32[256,1,4]{2,1,0:T(1,128)}), f32[256,1,4]{2,1,0:T(1,128)S(1)}, u32[]{:S(2)}, u32[]{:S(2)}) async-start(f32[256,1,4]{2,1,0:T(1,128)} %broadcast_in_dim.4), calls=%async_computation | async-start | bytes 262144 | tf_op jit(solution)/shard_map/while/body/eval_jaxpr/all_to_all | solution.py:39
  (85 other events, 519.7 us)

commit v11 on v9

--- a/solution.py
+++ b/solution.py
@@ -96,7 +96,7 @@
     partial_out = partial_out + lax.dot_general(
         hidden_act, tangent_out_t, (((1,), (1,)), ((), ())), preferred_element_type=jnp.float32
     )
-    fsdp_groups = digit_groups(lax.axis_size("fsdp"), (1, 1))
+    fsdp_groups = digit_groups(lax.axis_size("fsdp"), (1, 1, 2))
     out_chunk = spread_reduce(partial_out.astype(jnp.bfloat16), "fsdp", fsdp_groups, jnp.bfloat16)
     cotangent = spread_gather((out_chunk * metric).astype(jnp.bfloat16), "fsdp", fsdp_groups)
     back_act = lax.dot_general(

time: 455 us -> 454 us (level)
  starting transfers between devices: 189 us -> 168 us
  waiting for transfers between devices: 145 us -> 165 us
    ppermute x48 -> x39, waiting for transfers between devices: 77.2 us -> 91.3 us  [spread_reduce(): lax.ppermute(send.astype(send_type), axis, xor_pairs(size, offset << low))]
    ppermute x48 -> x39, starting transfers between devices: 70.4 us -> 56.4 us  [spread_reduce(): lax.ppermute(send.astype(send_type), axis, xor_pairs(size, offset << low))]
    ppermute x48 -> x39, starting transfers between devices: 80.2 us -> 71.7 us  [spread_gather(): got = lax.ppermute(chunk, axis, xor_pairs(size, offset << low))]
    ppermute x48 -> x39, waiting for transfers between devices: 46.5 us -> 52.8 us  [spread_gather(): got = lax.ppermute(chunk, axis, xor_pairs(size, offset << low))]
    dynamic_update_slice x48 -> x39, local copies, waits for them, and re-layouts: 17.7 us -> 17.6 us  [spread_gather(): lax.dynamic_update_slice_in_dim(whole, got, (digit ^ offset) * rows, 0)]
  transfers between devices with their start and end apart: 99 -> 81, of which waited for: 47 -> 55; matrix products, arithmetic and copies ran while one was open for 8% -> 8% of each run, Pallas kernels for 0% -> 0%
where the time goes in v11:
time: 454 us; the launch traced here: 453 us
  starting transfers between devices  168 us (37%)
  waiting for transfers between devices  165 us (36%)
  other arithmetic  41.1 us (9%)
  local copies, waits for them, and re-layouts  40.3 us (9%)
  matrix products  25.3 us (6%)
  loops' own time  12.3 us (3%)
    ppermute x39, waiting for transfers between devices, spread_reduce(): lax.ppermute(send.astype(send_type), axis, xor_pairs(size, offset << low))  91.3 us
    ppermute x39, starting transfers between devices, spread_gather(): got = lax.ppermute(chunk, axis, xor_pairs(size, offset << low))  71.7 us
    ppermute x39, starting transfers between devices, spread_reduce(): lax.ppermute(send.astype(send_type), axis, xor_pairs(size, offset << low))  56.4 us
    ppermute x39, waiting for transfers between devices, spread_gather(): got = lax.ppermute(chunk, axis, xor_pairs(size, offset << low))  52.8 us
    all_to_all x3, starting transfers between devices, scalar_sum(): lax.all_to_all(jnp.broadcast_to(values[None], (size,) + values.shape), ax...  39.8 us
    all_to_all x3, waiting for transfers between devices, scalar_sum(): lax.all_to_all(jnp.broadcast_to(values[None], (size,) + values.shape), ax...  20.9 us
    dynamic_update_slice x39, local copies, waits for them, and re-layouts, spread_gather(): lax.dynamic_update_slice_in_dim(whole, got, (digit ^ offset) * rows, 0)  17.6 us
    another operation x1, loops' own time, on_device(): lax.fori_loop(0, ITERS, iterate, (jnp.zeros_like(residual), residual, res...  12.3 us
  transfers between devices with their start and end apart: 81, of which 55 were waited for; matrix products, arithmetic and copies ran while one was open for 8% of the time, Pallas kernels for 0%

profile of v11, /device:TPU:1, one launch (start us, length us, event | category | flops | bytes accessed | tf_op | source)
XLA Modules:
  0.0 452.6 jit_solution(12841815455291284044)
XLA Ops:
  7.2 439.4 %while.15 = (s32[]{:T(128)}, f32[1024,256]{0,1:T(8,128)}, f32[1024,256]{0,1:T(8,128)}, f32[1024,256]{0,1:T(8,128)S(1)}, bf16[768,1024]{1,0:T(8,128)(2,1)}, /*ind...) while((s32[]{:T(128)}, f32[1024,256]{0,1:T(8,128)}, ...), condition=%wide.region_7.8_spmd.clone, body=%wide.region_1.7_spmd.clone.sunk | while | flops 1215202304 | bytes 107482256 | solution.py:152
  23.1 10.8 %collective-permute-done.1 = bf16[192,1024]{1,0:T(8,128)(2,1)S(1)} collective-permute-done((bf16[192,1024]{1,0:T(8,128)(2,1)S(1)}, bf16[192,1024]{1,0:T(8,128)(2,1)S(1)}, u32[]{:S(2)}, u32[]{:S(2)}) %collective-permute-start.1) | collective-permute-done | bytes 393248 | tf_op jit(solution)/shard_map/while/body/eval_jaxpr/ppermute | solution.py:67
  39.6 5.5 %collective-permute-done.3 = bf16[48,1024]{1,0:T(8,128)(2,1)S(1)} collective-permute-done((bf16[48,1024]{1,0:T(8,128)(2,1)S(1)}, bf16[48,1024]{1,0:T(8,128)(2,1)S(1)}, u32[]{:S(2)}, u32[]{:S(2)}) %collective-permute-start.3) | collective-permute-done | bytes 98336 | tf_op jit(solution)/shard_map/while/body/eval_jaxpr/ppermute | solution.py:67
  45.2 5.2 %collective-permute-start.5 = (bf16[24,1024]{1,0:T(8,128)(2,1)S(1)}, bf16[24,1024]{1,0:T(8,128)(2,1)S(1)}, u32[]{:S(2)}, u32[]{:S(2)}) collective-permute-start(bf16[24,1024]{1,0:T(8,128)(2,1)S(1)} %dynamic-slice_convert_fusion.13), channel_id=1, source_target_pairs={{0,16},{1,17},{2,18},{3,19},{4,20},{5,21},{6,22},{7,23},{8,24},{9,... | collective-permute-start | bytes 147464 | tf_op jit(solution)/shard_map/while/body/eval_jaxpr/ppermute | solution.py:67
  52.2 5.2 %collective-permute-start.6 = (bf16[24,1024]{1,0:T(8,128)(2,1)S(1)}, bf16[24,1024]{1,0:T(8,128)(2,1)S(1)}, u32[]{:S(2)}, u32[]{:S(2)}) collective-permute-start(bf16[24,1024]{1,0:T(8,128)(2,1)S(1)} %get-tuple-element.215), channel_id=1, source_target_pairs={{0,16},{1,17},{2,18},{3,19},{4,20},{5,21},{6,22},{7,23},{8,24},{9,... | collective-permute-start | bytes 147464 | tf_op jit(solution)/shard_map/while/body/eval_jaxpr/ppermute | solution.py:83
  70.0 5.9 %collective-permute-done.10 = bf16[192,1024]{1,0:T(8,128)(2,1)S(1)} collective-permute-done((bf16[192,1024]{1,0:T(8,128)(2,1)S(1)}, bf16[192,1024]{1,0:T(8,128)(2,1)S(1)}, u32[]{:S(2)}, u32[]{:S(2)}) %collective-permute-start.10) | collective-permute-done | bytes 393248 | tf_op jit(solution)/shard_map/while/body/eval_jaxpr/ppermute | solution.py:83
  75.9 6.1 %collective-permute-start.11 = (bf16[384,1024]{1,0:T(8,128)(2,1)S(1)}, bf16[384,1024]{1,0:T(8,128)(2,1)}, u32[]{:S(2)}, u32[]{:S(2)}) collective-permute-start(bf16[384,1024]{1,0:T(8,128)(2,1)S(1)} %constant_dynamic-update-slice_fusion.43), channel_id=1, source_target_pairs={{0,1},{1,0},{2,3},{3,2},{4,5},{5,4},{6,7},{7,6},{8,9},{9,8},{10,11... | collective-permute-start | bytes 2359304 | tf_op jit(solution)/shard_map/while/body/eval_jaxpr/ppermute | solution.py:83
  111.7 14.4 %all-to-all-start = ((f32[256,1,4]{2,1,0:T(1,128)}), f32[256,1,4]{2,1,0:T(1,128)}, u32[]{:S(2)}, u32[]{:S(2)}) async-start(f32[256,1,4]{2,1,0:T(1,128)} %broadcast_in_dim.4), calls=%async_computation | async-start | bytes 262144 | tf_op jit(solution)/shard_map/while/body/eval_jaxpr/all_to_all | solution.py:39
  131.2 7.0 %all-to-all-done = f32[256,1,4]{2,1,0:T(1,128)} async-done(((f32[256,1,4]{2,1,0:T(1,128)}), f32[256,1,4]{2,1,0:T(1,128)}, u32[]{:S(2)}, u32[]{:S(2)}) %all-to-all-start) | async-done | bytes 4128 | tf_op jit(solution)/shard_map/while/body/eval_jaxpr/all_to_all | solution.py:39
  172.0 10.8 %collective-permute-done.1 = bf16[192,1024]{1,0:T(8,128)(2,1)S(1)} collective-permute-done((bf16[192,1024]{1,0:T(8,128)(2,1)S(1)}, bf16[192,1024]{1,0:T(8,128)(2,1)S(1)}, u32[]{:S(2)}, u32[]{:S(2)}) %collective-permute-start.1) | collective-permute-done | bytes 393248 | tf_op jit(solution)/shard_map/while/body/eval_jaxpr/ppermute | solution.py:67
  188.4 5.1 %collective-permute-done.3 = bf16[48,1024]{1,0:T(8,128)(2,1)S(1)} collective-permute-done((bf16[48,1024]{1,0:T(8,128)(2,1)S(1)}, bf16[48,1024]{1,0:T(8,128)(2,1)S(1)}, u32[]{:S(2)}, u32[]{:S(2)}) %collective-permute-start.3) | collective-permute-done | bytes 98336 | tf_op jit(solution)/shard_map/while/body/eval_jaxpr/ppermute | solution.py:67
  195.6 4.9 %collective-permute-done.5 = bf16[24,1024]{1,0:T(8,128)(2,1)S(1)} collective-permute-done((bf16[24,1024]{1,0:T(8,128)(2,1)S(1)}, bf16[24,1024]{1,0:T(8,128)(2,1)S(1)}, u32[]{:S(2)}, u32[]{:S(2)}) %collective-permute-start.5) | collective-permute-done | bytes 49184 | tf_op jit(solution)/shard_map/while/body/eval_jaxpr/ppermute | solution.py:67
  217.5 6.3 %collective-permute-done.10 = bf16[192,1024]{1,0:T(8,128)(2,1)S(1)} collective-permute-done((bf16[192,1024]{1,0:T(8,128)(2,1)S(1)}, bf16[192,1024]{1,0:T(8,128)(2,1)S(1)}, u32[]{:S(2)}, u32[]{:S(2)}) %collective-permute-start.10) | collective-permute-done | bytes 393248 | tf_op jit(solution)/shard_map/while/body/eval_jaxpr/ppermute | solution.py:83
  223.9 6.1 %collective-permute-start.11 = (bf16[384,1024]{1,0:T(8,128)(2,1)S(1)}, bf16[384,1024]{1,0:T(8,128)(2,1)}, u32[]{:S(2)}, u32[]{:S(2)}) collective-permute-start(bf16[384,1024]{1,0:T(8,128)(2,1)S(1)} %constant_dynamic-update-slice_fusion.43), channel_id=1, source_target_pairs={{0,1},{1,0},{2,3},{3,2},{4,5},{5,4},{6,7},{7,6},{8,9},{9,8},{10,11... | collective-permute-start | bytes 2359304 | tf_op jit(solution)/shard_map/while/body/eval_jaxpr/ppermute | solution.py:83
  258.1 12.6 %all-to-all-start = ((f32[256,1,4]{2,1,0:T(1,128)}), f32[256,1,4]{2,1,0:T(1,128)}, u32[]{:S(2)}, u32[]{:S(2)}) async-start(f32[256,1,4]{2,1,0:T(1,128)} %broadcast_in_dim.4), calls=%async_computation | async-start | bytes 262144 | tf_op jit(solution)/shard_map/while/body/eval_jaxpr/all_to_all | solution.py:39
  275.8 7.0 %all-to-all-done = f32[256,1,4]{2,1,0:T(1,128)} async-done(((f32[256,1,4]{2,1,0:T(1,128)}), f32[256,1,4]{2,1,0:T(1,128)}, u32[]{:S(2)}, u32[]{:S(2)}) %all-to-all-start) | async-done | bytes 4128 | tf_op jit(solution)/shard_map/while/body/eval_jaxpr/all_to_all | solution.py:39
  316.6 10.8 %collective-permute-done.1 = bf16[192,1024]{1,0:T(8,128)(2,1)S(1)} collective-permute-done((bf16[192,1024]{1,0:T(8,128)(2,1)S(1)}, bf16[192,1024]{1,0:T(8,128)(2,1)S(1)}, u32[]{:S(2)}, u32[]{:S(2)}) %collective-permute-start.1) | collective-permute-done | bytes 393248 | tf_op jit(solution)/shard_map/while/body/eval_jaxpr/ppermute | solution.py:67
  333.0 5.1 %collective-permute-done.3 = bf16[48,1024]{1,0:T(8,128)(2,1)S(1)} collective-permute-done((bf16[48,1024]{1,0:T(8,128)(2,1)S(1)}, bf16[48,1024]{1,0:T(8,128)(2,1)S(1)}, u32[]{:S(2)}, u32[]{:S(2)}) %collective-permute-start.3) | collective-permute-done | bytes 98336 | tf_op jit(solution)/shard_map/while/body/eval_jaxpr/ppermute | solution.py:67
  340.2 4.9 %collective-permute-done.5 = bf16[24,1024]{1,0:T(8,128)(2,1)S(1)} collective-permute-done((bf16[24,1024]{1,0:T(8,128)(2,1)S(1)}, bf16[24,1024]{1,0:T(8,128)(2,1)S(1)}, u32[]{:S(2)}, u32[]{:S(2)}) %collective-permute-start.5) | collective-permute-done | bytes 49184 | tf_op jit(solution)/shard_map/while/body/eval_jaxpr/ppermute | solution.py:67
  347.3 4.9 %collective-permute-done.6 = bf16[24,1024]{1,0:T(8,128)(2,1)S(1)} collective-permute-done((bf16[24,1024]{1,0:T(8,128)(2,1)S(1)}, bf16[24,1024]{1,0:T(8,128)(2,1)S(1)}, u32[]{:S(2)}, u32[]{:S(2)}) %collective-permute-start.6) | collective-permute-done | bytes 49184 | tf_op jit(solution)/shard_map/while/body/eval_jaxpr/ppermute | solution.py:83
  362.1 6.3 %collective-permute-done.10 = bf16[192,1024]{1,0:T(8,128)(2,1)S(1)} collective-permute-done((bf16[192,1024]{1,0:T(8,128)(2,1)S(1)}, bf16[192,1024]{1,0:T(8,128)(2,1)S(1)}, u32[]{:S(2)}, u32[]{:S(2)}) %collective-permute-start.10) | collective-permute-done | bytes 393248 | tf_op jit(solution)/shard_map/while/body/eval_jaxpr/ppermute | solution.py:83
  368.5 5.8 %collective-permute-start.11 = (bf16[384,1024]{1,0:T(8,128)(2,1)S(1)}, bf16[384,1024]{1,0:T(8,128)(2,1)}, u32[]{:S(2)}, u32[]{:S(2)}) collective-permute-start(bf16[384,1024]{1,0:T(8,128)(2,1)S(1)} %constant_dynamic-update-slice_fusion.43), channel_id=1, source_target_pairs={{0,1},{1,0},{2,3},{3,2},{4,5},{5,4},{6,7},{7,6},{8,9},{9,8},{10,11... | collective-permute-start | bytes 2359304 | tf_op jit(solution)/shard_map/while/body/eval_jaxpr/ppermute | solution.py:83
  402.6 12.7 %all-to-all-start = ((f32[256,1,4]{2,1,0:T(1,128)}), f32[256,1,4]{2,1,0:T(1,128)}, u32[]{:S(2)}, u32[]{:S(2)}) async-start(f32[256,1,4]{2,1,0:T(1,128)} %broadcast_in_dim.4), calls=%async_computation | async-start | bytes 262144 | tf_op jit(solution)/shard_map/while/body/eval_jaxpr/all_to_all | solution.py:39
  420.3 7.0 %all-to-all-done = f32[256,1,4]{2,1,0:T(1,128)} async-done(((f32[256,1,4]{2,1,0:T(1,128)}), f32[256,1,4]{2,1,0:T(1,128)}, u32[]{:S(2)}, u32[]{:S(2)}) %all-to-all-start) | async-done | bytes 4128 | tf_op jit(solution)/shard_map/while/body/eval_jaxpr/all_to_all | solution.py:39
  (344 shorter events, 269.1 us)
Async XLA Ops:
  22.0 11.9 %collective-permute-start.1 = (bf16[192,1024]{1,0:T(8,128)(2,1)S(1)}, bf16[192,1024]{1,0:T(8,128)(2,1)S(1)}, u32[]{:S(2)}, u32[]{:S(2)}) collective-permute-start(bf16[192,1024]{1,0:T(8,128)(2,1)S(1)} %dynamic-slice_convert_fusion.11), channel_id=1, source_target_pairs={{0,2},{1,3},{2,0},{3,1},{4,6},{5,7},{6,4},{7,5},{8,10},{9,11},{10,... | collective-permute-start | bytes 1179656 | tf_op jit(solution)/shard_map/while/body/eval_jaxpr/ppermute | solution.py:67
  105.8 37.9 %collective-permute-start.19 = (f32[128,256]{0,1:T(8,128)S(1)}, f32[128,256]{0,1:T(8,128)}, u32[]{:S(2)}, u32[]{:S(2)}) collective-permute-start(f32[128,256]{0,1:T(8,128)S(1)} %get-tuple-element.222), channel_id=1, source_target_pairs={{0,32},{32,0},{64,96},{96,64},{128,160},{160,128},{192,224},{224,1... | collective-permute-start | bytes 393224 | tf_op jit(solution)/shard_map/while/body/eval_jaxpr/ppermute | solution.py:83
  111.7 26.4 %all-to-all-start = ((f32[256,1,4]{2,1,0:T(1,128)}), f32[256,1,4]{2,1,0:T(1,128)}, u32[]{:S(2)}, u32[]{:S(2)}) async-start(f32[256,1,4]{2,1,0:T(1,128)} %broadcast_in_dim.4), calls=%async_computation | async-start | bytes 262144 | tf_op jit(solution)/shard_map/while/body/eval_jaxpr/all_to_all | solution.py:39
  126.1 19.5 %collective-permute-start.20 = (f32[128,256]{0,1:T(8,128)S(1)}, f32[128,256]{0,1:T(8,128)}, u32[]{:S(2)}, u32[]{:S(2)}) collective-permute-start(f32[128,256]{0,1:T(8,128)S(1)} %get-tuple-element.222), channel_id=1, source_target_pairs={{0,64},{32,96},{64,0},{96,32},{128,192},{160,224},{192,128},{224,1... | collective-permute-start | bytes 393224 | tf_op jit(solution)/shard_map/while/body/eval_jaxpr/ppermute | solution.py:83
  129.1 20.1 %collective-permute-start.21 = (f32[128,256]{0,1:T(8,128)S(1)}, f32[128,256]{0,1:T(8,128)}, u32[]{:S(2)}, u32[]{:S(2)}) collective-permute-start(f32[128,256]{0,1:T(8,128)S(1)} %get-tuple-element.222), channel_id=1, source_target_pairs={{0,96},{32,64},{64,32},{96,0},{128,224},{160,192},{192,160},{224,1... | collective-permute-start | bytes 393224 | tf_op jit(solution)/shard_map/while/body/eval_jaxpr/ppermute | solution.py:83
  130.0 20.1 %collective-permute-start.22 = (f32[128,256]{0,1:T(8,128)S(1)}, f32[128,256]{0,1:T(8,128)}, u32[]{:S(2)}, u32[]{:S(2)}) collective-permute-start(f32[128,256]{0,1:T(8,128)S(1)} %get-tuple-element.222), channel_id=1, source_target_pairs={{0,128},{32,160},{64,192},{96,224},{128,0},{160,32},{192,64},{224,... | collective-permute-start | bytes 393224 | tf_op jit(solution)/shard_map/while/body/eval_jaxpr/ppermute | solution.py:83
  131.2 19.9 %collective-permute-start.23 = (f32[128,256]{0,1:T(8,128)S(1)}, f32[128,256]{0,1:T(8,128)}, u32[]{:S(2)}, u32[]{:S(2)}) collective-permute-start(f32[128,256]{0,1:T(8,128)S(1)} %get-tuple-element.222), channel_id=1, source_target_pairs={{0,160},{32,128},{64,224},{96,192},{128,32},{160,0},{192,96},{224,... | collective-permute-start | bytes 393224 | tf_op jit(solution)/shard_map/while/body/eval_jaxpr/ppermute | solution.py:83
  170.9 11.9 %collective-permute-start.1 = (bf16[192,1024]{1,0:T(8,128)(2,1)S(1)}, bf16[192,1024]{1,0:T(8,128)(2,1)S(1)}, u32[]{:S(2)}, u32[]{:S(2)}) collective-permute-start(bf16[192,1024]{1,0:T(8,128)(2,1)S(1)} %dynamic-slice_convert_fusion.11), channel_id=1, source_target_pairs={{0,2},{1,3},{2,0},{3,1},{4,6},{5,7},{6,4},{7,5},{8,10},{9,11},{10,... | collective-permute-start | bytes 1179656 | tf_op jit(solution)/shard_map/while/body/eval_jaxpr/ppermute | solution.py:67
  184.2 9.3 %collective-permute-start.3 = (bf16[48,1024]{1,0:T(8,128)(2,1)S(1)}, bf16[48,1024]{1,0:T(8,128)(2,1)S(1)}, u32[]{:S(2)}, u32[]{:S(2)}) collective-permute-start(bf16[48,1024]{1,0:T(8,128)(2,1)S(1)} %get-tuple-element.212), channel_id=1, source_target_pairs={{0,8},{1,9},{2,10},{3,11},{4,12},{5,13},{6,14},{7,15},{8,0},{9,1},... | collective-permute-start | bytes 294920 | tf_op jit(solution)/shard_map/while/body/eval_jaxpr/ppermute | solution.py:67
  252.4 35.9 %collective-permute-start.19 = (f32[128,256]{0,1:T(8,128)S(1)}, f32[128,256]{0,1:T(8,128)}, u32[]{:S(2)}, u32[]{:S(2)}) collective-permute-start(f32[128,256]{0,1:T(8,128)S(1)} %get-tuple-element.222), channel_id=1, source_target_pairs={{0,32},{32,0},{64,96},{96,64},{128,160},{160,128},{192,224},{224,1... | collective-permute-start | bytes 393224 | tf_op jit(solution)/shard_map/while/body/eval_jaxpr/ppermute | solution.py:83
  258.1 24.7 %all-to-all-start = ((f32[256,1,4]{2,1,0:T(1,128)}), f32[256,1,4]{2,1,0:T(1,128)}, u32[]{:S(2)}, u32[]{:S(2)}) async-start(f32[256,1,4]{2,1,0:T(1,128)} %broadcast_in_dim.4), calls=%async_computation | async-start | bytes 262144 | tf_op jit(solution)/shard_map/while/body/eval_jaxpr/all_to_all | solution.py:39
  270.7 19.5 %collective-permute-start.20 = (f32[128,256]{0,1:T(8,128)S(1)}, f32[128,256]{0,1:T(8,128)}, u32[]{:S(2)}, u32[]{:S(2)}) collective-permute-start(f32[128,256]{0,1:T(8,128)S(1)} %get-tuple-element.222), channel_id=1, source_target_pairs={{0,64},{32,96},{64,0},{96,32},{128,192},{160,224},{192,128},{224,1... | collective-permute-start | bytes 393224 | tf_op jit(solution)/shard_map/while/body/eval_jaxpr/ppermute | solution.py:83
  273.7 20.1 %collective-permute-start.21 = (f32[128,256]{0,1:T(8,128)S(1)}, f32[128,256]{0,1:T(8,128)}, u32[]{:S(2)}, u32[]{:S(2)}) collective-permute-start(f32[128,256]{0,1:T(8,128)S(1)} %get-tuple-element.222), channel_id=1, source_target_pairs={{0,96},{32,64},{64,32},{96,0},{128,224},{160,192},{192,160},{224,1... | collective-permute-start | bytes 393224 | tf_op jit(solution)/shard_map/while/body/eval_jaxpr/ppermute | solution.py:83
  274.6 20.1 %collective-permute-start.22 = (f32[128,256]{0,1:T(8,128)S(1)}, f32[128,256]{0,1:T(8,128)}, u32[]{:S(2)}, u32[]{:S(2)}) collective-permute-start(f32[128,256]{0,1:T(8,128)S(1)} %get-tuple-element.222), channel_id=1, source_target_pairs={{0,128},{32,160},{64,192},{96,224},{128,0},{160,32},{192,64},{224,... | collective-permute-start | bytes 393224 | tf_op jit(solution)/shard_map/while/body/eval_jaxpr/ppermute | solution.py:83
  275.8 19.9 %collective-permute-start.23 = (f32[128,256]{0,1:T(8,128)S(1)}, f32[128,256]{0,1:T(8,128)}, u32[]{:S(2)}, u32[]{:S(2)}) collective-permute-start(f32[128,256]{0,1:T(8,128)S(1)} %get-tuple-element.222), channel_id=1, source_target_pairs={{0,160},{32,128},{64,224},{96,192},{128,32},{160,0},{192,96},{224,... | collective-permute-start | bytes 393224 | tf_op jit(solution)/shard_map/while/body/eval_jaxpr/ppermute | solution.py:83
  315.5 11.9 %collective-permute-start.1 = (bf16[192,1024]{1,0:T(8,128)(2,1)S(1)}, bf16[192,1024]{1,0:T(8,128)(2,1)S(1)}, u32[]{:S(2)}, u32[]{:S(2)}) collective-permute-start(bf16[192,1024]{1,0:T(8,128)(2,1)S(1)} %dynamic-slice_convert_fusion.11), channel_id=1, source_target_pairs={{0,2},{1,3},{2,0},{3,1},{4,6},{5,7},{6,4},{7,5},{8,10},{9,11},{10,... | collective-permute-start | bytes 1179656 | tf_op jit(solution)/shard_map/while/body/eval_jaxpr/ppermute | solution.py:67
  328.8 9.3 %collective-permute-start.3 = (bf16[48,1024]{1,0:T(8,128)(2,1)S(1)}, bf16[48,1024]{1,0:T(8,128)(2,1)S(1)}, u32[]{:S(2)}, u32[]{:S(2)}) collective-permute-start(bf16[48,1024]{1,0:T(8,128)(2,1)S(1)} %get-tuple-element.212), channel_id=1, source_target_pairs={{0,8},{1,9},{2,10},{3,11},{4,12},{5,13},{6,14},{7,15},{8,0},{9,1},... | collective-permute-start | bytes 294920 | tf_op jit(solution)/shard_map/while/body/eval_jaxpr/ppermute | solution.py:67
  329.4 8.8 %collective-permute-start.4 = (bf16[48,1024]{1,0:T(8,128)(2,1)S(1)}, bf16[48,1024]{1,0:T(8,128)(2,1)S(1)}, u32[]{:S(2)}, u32[]{:S(2)}) collective-permute-start(bf16[48,1024]{1,0:T(8,128)(2,1)S(1)} %get-tuple-element.213), channel_id=1, source_target_pairs={{0,4},{1,5},{2,6},{3,7},{4,0},{5,1},{6,2},{7,3},{8,12},{9,13},{10,... | collective-permute-start | bytes 294920 | tf_op jit(solution)/shard_map/while/body/eval_jaxpr/ppermute | solution.py:67
  396.9 35.9 %collective-permute-start.19 = (f32[128,256]{0,1:T(8,128)S(1)}, f32[128,256]{0,1:T(8,128)}, u32[]{:S(2)}, u32[]{:S(2)}) collective-permute-start(f32[128,256]{0,1:T(8,128)S(1)} %get-tuple-element.222), channel_id=1, source_target_pairs={{0,32},{32,0},{64,96},{96,64},{128,160},{160,128},{192,224},{224,1... | collective-permute-start | bytes 393224 | tf_op jit(solution)/shard_map/while/body/eval_jaxpr/ppermute | solution.py:83
  402.6 24.7 %all-to-all-start = ((f32[256,1,4]{2,1,0:T(1,128)}), f32[256,1,4]{2,1,0:T(1,128)}, u32[]{:S(2)}, u32[]{:S(2)}) async-start(f32[256,1,4]{2,1,0:T(1,128)} %broadcast_in_dim.4), calls=%async_computation | async-start | bytes 262144 | tf_op jit(solution)/shard_map/while/body/eval_jaxpr/all_to_all | solution.py:39
  415.3 19.5 %collective-permute-start.20 = (f32[128,256]{0,1:T(8,128)S(1)}, f32[128,256]{0,1:T(8,128)}, u32[]{:S(2)}, u32[]{:S(2)}) collective-permute-start(f32[128,256]{0,1:T(8,128)S(1)} %get-tuple-element.222), channel_id=1, source_target_pairs={{0,64},{32,96},{64,0},{96,32},{128,192},{160,224},{192,128},{224,1... | collective-permute-start | bytes 393224 | tf_op jit(solution)/shard_map/while/body/eval_jaxpr/ppermute | solution.py:83
  418.3 20.1 %collective-permute-start.21 = (f32[128,256]{0,1:T(8,128)S(1)}, f32[128,256]{0,1:T(8,128)}, u32[]{:S(2)}, u32[]{:S(2)}) collective-permute-start(f32[128,256]{0,1:T(8,128)S(1)} %get-tuple-element.222), channel_id=1, source_target_pairs={{0,96},{32,64},{64,32},{96,0},{128,224},{160,192},{192,160},{224,1... | collective-permute-start | bytes 393224 | tf_op jit(solution)/shard_map/while/body/eval_jaxpr/ppermute | solution.py:83
  419.2 20.1 %collective-permute-start.22 = (f32[128,256]{0,1:T(8,128)S(1)}, f32[128,256]{0,1:T(8,128)}, u32[]{:S(2)}, u32[]{:S(2)}) collective-permute-start(f32[128,256]{0,1:T(8,128)S(1)} %get-tuple-element.222), channel_id=1, source_target_pairs={{0,128},{32,160},{64,192},{96,224},{128,0},{160,32},{192,64},{224,... | collective-permute-start | bytes 393224 | tf_op jit(solution)/shard_map/while/body/eval_jaxpr/ppermute | solution.py:83
  420.3 19.9 %collective-permute-start.23 = (f32[128,256]{0,1:T(8,128)S(1)}, f32[128,256]{0,1:T(8,128)}, u32[]{:S(2)}, u32[]{:S(2)}) collective-permute-start(f32[128,256]{0,1:T(8,128)S(1)} %get-tuple-element.222), channel_id=1, source_target_pairs={{0,160},{32,128},{64,224},{96,192},{128,32},{160,0},{192,96},{224,... | collective-permute-start | bytes 393224 | tf_op jit(solution)/shard_map/while/body/eval_jaxpr/ppermute | solution.py:83
  (88 other events, 722.1 us)

commit v12 on v11

--- a/solution.py
+++ b/solution.py
@@ -53,6 +53,13 @@
     return groups
 
 
+def split_permute(value, axis, pairs):
+    if value.shape[0] < 192:
+        return lax.ppermute(value, axis, pairs)
+    upper, lower = jnp.split(value, 2, axis=0)
+    return jnp.concatenate([lax.ppermute(upper, axis, pairs), lax.ppermute(lower, axis, pairs)], 0)
+
+
 def spread_reduce(value, axis, groups, send_type):
     size = lax.axis_size(axis)
     index = lax.axis_index(axis)
@@ -64,7 +71,7 @@
         total = lax.dynamic_slice_in_dim(kept, digit * rows, rows, 0)
         for offset in range(1, width):
             send = lax.dynamic_slice_in_dim(kept, (digit ^ offset) * rows, rows, 0)
-            got = lax.ppermute(send.astype(send_type), axis, xor_pairs(size, offset << low))
+            got = split_permute(send.astype(send_type), axis, xor_pairs(size, offset << low))
             total = total + got.astype(jnp.float32)
         kept = total
     return kept
@@ -80,7 +87,7 @@
         whole = jnp.zeros((rows * width,) + chunk.shape[1:], chunk.dtype)
         whole = lax.dynamic_update_slice_in_dim(whole, chunk, digit * rows, 0)
         for offset in range(1, width):
-            got = lax.ppermute(chunk, axis, xor_pairs(size, offset << low))
+            got = split_permute(chunk, axis, xor_pairs(size, offset << low))
             whole = lax.dynamic_update_slice_in_dim(whole, got, (digit ^ offset) * rows, 0)
         chunk = whole
     return chunk

time: 454 us -> 456 us (level)
  waiting for transfers between devices: 165 us -> 159 us
  starting transfers between devices: 168 us -> 173 us
    ppermute x78 -> x90, starting transfers between devices: 128 us -> 137 us  [the longest x66 93.5 us: split_permute(): return lax.ppermute(value, axis, pairs)]
    ppermute x78 -> x90, waiting for transfers between devices: 144 us -> 138 us  [the longest x66 85.1 us: split_permute(): return lax.ppermute(value, axis, pairs)]
    dynamic_update_slice x39 -> x33, local copies, waits for them, and re-layouts: 17.6 us -> 14 us  [spread_gather(): lax.dynamic_update_slice_in_dim(whole, got, (digit ^ offset) * rows, 0)]
  transfers between devices with their start and end apart: 81 -> 93, of which waited for: 55 -> 66; matrix products, arithmetic and copies ran while one was open for 8% -> 8% of each run, Pallas kernels for 0% -> 0%
where the time goes in v12:
time: 456 us; the launch traced here: 455 us
  starting transfers between devices  173 us (38%)
  waiting for transfers between devices  159 us (35%)
  other arithmetic  44.4 us (10%)
  local copies, waits for them, and re-layouts  39.3 us (9%)
  matrix products  25.3 us (6%)
  loops' own time  13 us (3%)
    ppermute x66, starting transfers between devices, split_permute(): return lax.ppermute(value, axis, pairs)  93.5 us
    ppermute x66, waiting for transfers between devices, split_permute(): return lax.ppermute(value, axis, pairs)  85.1 us
    all_to_all x3, starting transfers between devices, scalar_sum(): lax.all_to_all(jnp.broadcast_to(values[None], (size,) + values.shape), ax...  36.1 us
    ppermute x12, starting transfers between devices, split_permute(): lax.ppermute(lower, axis, pairs)  33 us
    ppermute x12, waiting for transfers between devices, split_permute(): lax.ppermute(lower, axis, pairs)  30.9 us
    ppermute x12, waiting for transfers between devices, split_permute(): lax.ppermute(upper, axis, pairs)  22.4 us
    all_to_all x3, waiting for transfers between devices, scalar_sum(): lax.all_to_all(jnp.broadcast_to(values[None], (size,) + values.shape), ax...  20.9 us
    dynamic_update_slice x33, local copies, waits for them, and re-layouts, spread_gather(): lax.dynamic_update_slice_in_dim(whole, got, (digit ^ offset) * rows, 0)  14 us
  transfers between devices with their start and end apart: 93, of which 66 were waited for; matrix products, arithmetic and copies ran while one was open for 8% of the time, Pallas kernels for 0%

profile of v12, /device:TPU:1, one launch (start us, length us, event | category | flops | bytes accessed | tf_op | source)
XLA Modules:
  0.0 454.8 jit_solution(12844213408494767253)
XLA Ops:
  7.3 441.6 %while.15 = (s32[]{:T(128)}, f32[1024,256]{0,1:T(8,128)}, f32[1024,256]{0,1:T(8,128)}, f32[1024,256]{0,1:T(8,128)S(1)}, bf16[768,1024]{1,0:T(8,128)(2,1)}, /*ind...) while((s32[]{:T(128)}, f32[1024,256]{0,1:T(8,128)}, ...), condition=%wide.region_7.8_spmd.clone, body=%wide.region_1.7_spmd.clone.sunk | while | flops 1219331072 | bytes 112200992 | solution.py:159
  24.9 4.6 %collective-permute-done.2 = bf16[96,1024]{1,0:T(8,128)(2,1)S(1)} collective-permute-done((bf16[96,1024]{1,0:T(8,128)(2,1)S(1)}, bf16[96,1024]{1,0:T(8,128)(2,1)S(1)}, u32[]{:S(2)}, u32[]{:S(2)}) %collective-permute-start.2) | collective-permute-done | bytes 196640 | tf_op jit(solution)/shard_map/while/body/eval_jaxpr/ppermute | solution.py:60
  29.6 4.2 collective-permute-done.3
  39.4 5.5 %collective-permute-done.5 = bf16[48,1024]{1,0:T(8,128)(2,1)S(1)} collective-permute-done((bf16[48,1024]{1,0:T(8,128)(2,1)S(1)}, bf16[48,1024]{1,0:T(8,128)(2,1)S(1)}, u32[]{:S(2)}, u32[]{:S(2)}) %collective-permute-start.5) | collective-permute-done | bytes 98336 | tf_op jit(solution)/shard_map/while/body/eval_jaxpr/ppermute | solution.py:58
  45.0 5.2 %collective-permute-start.7 = (bf16[24,1024]{1,0:T(8,128)(2,1)S(1)}, bf16[24,1024]{1,0:T(8,128)(2,1)S(1)}, u32[]{:S(2)}, u32[]{:S(2)}) collective-permute-start(bf16[24,1024]{1,0:T(8,128)(2,1)S(1)} %dynamic-slice_convert_fusion.13), channel_id=1, source_target_pairs={{0,16},{1,17},{2,18},{3,19},{4,20},{5,21},{6,22},{7,23},{8,24},{9,... | collective-permute-start | bytes 147464 | tf_op jit(solution)/shard_map/while/body/eval_jaxpr/ppermute | solution.py:58
  52.1 5.2 %collective-permute-start.8 = (bf16[24,1024]{1,0:T(8,128)(2,1)S(1)}, bf16[24,1024]{1,0:T(8,128)(2,1)S(1)}, u32[]{:S(2)}, u32[]{:S(2)}) collective-permute-start(bf16[24,1024]{1,0:T(8,128)(2,1)S(1)} %get-tuple-element.235), channel_id=1, source_target_pairs={{0,16},{1,17},{2,18},{3,19},{4,20},{5,21},{6,22},{7,23},{8,24},{9,... | collective-permute-start | bytes 147464 | tf_op jit(solution)/shard_map/while/body/eval_jaxpr/ppermute | solution.py:58
  76.8 6.9 %collective-permute-start.14 = (bf16[192,1024]{1,0:T(8,128)(2,1)}, bf16[192,1024]{1,0:T(8,128)(2,1)}, u32[]{:S(2)}, u32[]{:S(2)}) collective-permute-start(bf16[192,1024]{1,0:T(8,128)(2,1)} %get-tuple-element.238), channel_id=1, source_target_pairs={{0,1},{1,0},{2,3},{3,2},{4,5},{5,4},{6,7},{7,6},{8,9},{9,8},{10,11... | collective-permute-start | bytes 1179656 | tf_op jit(solution)/shard_map/while/body/eval_jaxpr/ppermute | solution.py:60
  114.0 13.1 %all-to-all-start = ((f32[256,1,4]{2,1,0:T(1,128)}), f32[256,1,4]{2,1,0:T(1,128)}, u32[]{:S(2)}, u32[]{:S(2)}) async-start(f32[256,1,4]{2,1,0:T(1,128)} %broadcast_in_dim.4), calls=%async_computation | async-start | bytes 262144 | tf_op jit(solution)/shard_map/while/body/eval_jaxpr/all_to_all | solution.py:39
  132.1 7.0 %all-to-all-done = f32[256,1,4]{2,1,0:T(1,128)} async-done(((f32[256,1,4]{2,1,0:T(1,128)}), f32[256,1,4]{2,1,0:T(1,128)}, u32[]{:S(2)}, u32[]{:S(2)}) %all-to-all-start) | async-done | bytes 4128 | tf_op jit(solution)/shard_map/while/body/eval_jaxpr/all_to_all | solution.py:39
  175.0 4.6 %collective-permute-done.2 = bf16[96,1024]{1,0:T(8,128)(2,1)S(1)} collective-permute-done((bf16[96,1024]{1,0:T(8,128)(2,1)S(1)}, bf16[96,1024]{1,0:T(8,128)(2,1)S(1)}, u32[]{:S(2)}, u32[]{:S(2)}) %collective-permute-start.2) | collective-permute-done | bytes 196640 | tf_op jit(solution)/shard_map/while/body/eval_jaxpr/ppermute | solution.py:60
  179.7 4.2 collective-permute-done.3
  189.5 5.1 %collective-permute-done.5 = bf16[48,1024]{1,0:T(8,128)(2,1)S(1)} collective-permute-done((bf16[48,1024]{1,0:T(8,128)(2,1)S(1)}, bf16[48,1024]{1,0:T(8,128)(2,1)S(1)}, u32[]{:S(2)}, u32[]{:S(2)}) %collective-permute-start.5) | collective-permute-done | bytes 98336 | tf_op jit(solution)/shard_map/while/body/eval_jaxpr/ppermute | solution.py:58
  196.7 5.0 %collective-permute-done.7 = bf16[24,1024]{1,0:T(8,128)(2,1)S(1)} collective-permute-done((bf16[24,1024]{1,0:T(8,128)(2,1)S(1)}, bf16[24,1024]{1,0:T(8,128)(2,1)S(1)}, u32[]{:S(2)}, u32[]{:S(2)}) %collective-permute-start.7) | collective-permute-done | bytes 49184 | tf_op jit(solution)/shard_map/while/body/eval_jaxpr/ppermute | solution.py:58
  203.6 5.0 %collective-permute-done.8 = bf16[24,1024]{1,0:T(8,128)(2,1)S(1)} collective-permute-done((bf16[24,1024]{1,0:T(8,128)(2,1)S(1)}, bf16[24,1024]{1,0:T(8,128)(2,1)S(1)}, u32[]{:S(2)}, u32[]{:S(2)}) %collective-permute-start.8) | collective-permute-done | bytes 49184 | tf_op jit(solution)/shard_map/while/body/eval_jaxpr/ppermute | solution.py:58
  226.0 5.8 %collective-permute-start.14 = (bf16[192,1024]{1,0:T(8,128)(2,1)}, bf16[192,1024]{1,0:T(8,128)(2,1)}, u32[]{:S(2)}, u32[]{:S(2)}) collective-permute-start(bf16[192,1024]{1,0:T(8,128)(2,1)} %get-tuple-element.238), channel_id=1, source_target_pairs={{0,1},{1,0},{2,3},{3,2},{4,5},{5,4},{6,7},{7,6},{8,9},{9,8},{10,11... | collective-permute-start | bytes 1179656 | tf_op jit(solution)/shard_map/while/body/eval_jaxpr/ppermute | solution.py:60
  260.5 11.5 %all-to-all-start = ((f32[256,1,4]{2,1,0:T(1,128)}), f32[256,1,4]{2,1,0:T(1,128)}, u32[]{:S(2)}, u32[]{:S(2)}) async-start(f32[256,1,4]{2,1,0:T(1,128)} %broadcast_in_dim.4), calls=%async_computation | async-start | bytes 262144 | tf_op jit(solution)/shard_map/while/body/eval_jaxpr/all_to_all | solution.py:39
  277.0 7.0 %all-to-all-done = f32[256,1,4]{2,1,0:T(1,128)} async-done(((f32[256,1,4]{2,1,0:T(1,128)}), f32[256,1,4]{2,1,0:T(1,128)}, u32[]{:S(2)}, u32[]{:S(2)}) %all-to-all-start) | async-done | bytes 4128 | tf_op jit(solution)/shard_map/while/body/eval_jaxpr/all_to_all | solution.py:39
  320.0 4.6 %collective-permute-done.2 = bf16[96,1024]{1,0:T(8,128)(2,1)S(1)} collective-permute-done((bf16[96,1024]{1,0:T(8,128)(2,1)S(1)}, bf16[96,1024]{1,0:T(8,128)(2,1)S(1)}, u32[]{:S(2)}, u32[]{:S(2)}) %collective-permute-start.2) | collective-permute-done | bytes 196640 | tf_op jit(solution)/shard_map/while/body/eval_jaxpr/ppermute | solution.py:60
  334.5 5.1 %collective-permute-done.5 = bf16[48,1024]{1,0:T(8,128)(2,1)S(1)} collective-permute-done((bf16[48,1024]{1,0:T(8,128)(2,1)S(1)}, bf16[48,1024]{1,0:T(8,128)(2,1)S(1)}, u32[]{:S(2)}, u32[]{:S(2)}) %collective-permute-start.5) | collective-permute-done | bytes 98336 | tf_op jit(solution)/shard_map/while/body/eval_jaxpr/ppermute | solution.py:58
  341.6 5.0 %collective-permute-done.7 = bf16[24,1024]{1,0:T(8,128)(2,1)S(1)} collective-permute-done((bf16[24,1024]{1,0:T(8,128)(2,1)S(1)}, bf16[24,1024]{1,0:T(8,128)(2,1)S(1)}, u32[]{:S(2)}, u32[]{:S(2)}) %collective-permute-start.7) | collective-permute-done | bytes 49184 | tf_op jit(solution)/shard_map/while/body/eval_jaxpr/ppermute | solution.py:58
  348.6 5.0 %collective-permute-done.8 = bf16[24,1024]{1,0:T(8,128)(2,1)S(1)} collective-permute-done((bf16[24,1024]{1,0:T(8,128)(2,1)S(1)}, bf16[24,1024]{1,0:T(8,128)(2,1)S(1)}, u32[]{:S(2)}, u32[]{:S(2)}) %collective-permute-start.8) | collective-permute-done | bytes 49184 | tf_op jit(solution)/shard_map/while/body/eval_jaxpr/ppermute | solution.py:58
  371.0 5.8 %collective-permute-start.14 = (bf16[192,1024]{1,0:T(8,128)(2,1)}, bf16[192,1024]{1,0:T(8,128)(2,1)}, u32[]{:S(2)}, u32[]{:S(2)}) collective-permute-start(bf16[192,1024]{1,0:T(8,128)(2,1)} %get-tuple-element.238), channel_id=1, source_target_pairs={{0,1},{1,0},{2,3},{3,2},{4,5},{5,4},{6,7},{7,6},{8,9},{9,8},{10,11... | collective-permute-start | bytes 1179656 | tf_op jit(solution)/shard_map/while/body/eval_jaxpr/ppermute | solution.py:60
  405.4 11.5 %all-to-all-start = ((f32[256,1,4]{2,1,0:T(1,128)}), f32[256,1,4]{2,1,0:T(1,128)}, u32[]{:S(2)}, u32[]{:S(2)}) async-start(f32[256,1,4]{2,1,0:T(1,128)} %broadcast_in_dim.4), calls=%async_computation | async-start | bytes 262144 | tf_op jit(solution)/shard_map/while/body/eval_jaxpr/all_to_all | solution.py:39
  422.0 7.0 %all-to-all-done = f32[256,1,4]{2,1,0:T(1,128)} async-done(((f32[256,1,4]{2,1,0:T(1,128)}), f32[256,1,4]{2,1,0:T(1,128)}, u32[]{:S(2)}, u32[]{:S(2)}) %all-to-all-start) | async-done | bytes 4128 | tf_op jit(solution)/shard_map/while/body/eval_jaxpr/all_to_all | solution.py:39
  (380 shorter events, 297.0 us)
Async XLA Ops:
  23.0 10.8 %collective-permute-start.3 = (bf16[96,1024]{1,0:T(8,128)(2,1)S(1)}, bf16[96,1024]{1,0:T(8,128)(2,1)S(1)}, u32[]{:S(2)}, u32[]{:S(2)}) collective-permute-start(bf16[96,1024]{1,0:T(8,128)(2,1)S(1)} %get-tuple-element.230), channel_id=1, source_target_pairs={{0,2},{1,3},{2,0},{3,1},{4,6},{5,7},{6,4},{7,5},{8,10},{9,11},{10,... | collective-permute-start | bytes 589832 | tf_op jit(solution)/shard_map/while/body/eval_jaxpr/ppermute | solution.py:60
  97.8 8.9 %collective-permute-start.22 = (f32[128,256]{0,1:T(8,128)S(1)}, f32[128,256]{0,1:T(8,128)S(1)}, u32[]{:S(2)}, u32[]{:S(2)}) collective-permute-start(f32[128,256]{0,1:T(8,128)S(1)} %get-tuple-element.245), channel_id=1, source_target_pairs={{0,32},{32,0},{64,96},{96,64},{128,160},{160,128},{192,224},{224,1... | collective-permute-start | bytes 393224 | tf_op jit(solution)/shard_map/while/body/eval_jaxpr/ppermute | solution.py:58
  107.8 37.0 %collective-permute-start.23 = (f32[128,256]{0,1:T(8,128)S(1)}, f32[128,256]{0,1:T(8,128)}, u32[]{:S(2)}, u32[]{:S(2)}) collective-permute-start(f32[128,256]{0,1:T(8,128)S(1)} %get-tuple-element.246), channel_id=1, source_target_pairs={{0,32},{32,0},{64,96},{96,64},{128,160},{160,128},{192,224},{224,1... | collective-permute-start | bytes 393224 | tf_op jit(solution)/shard_map/while/body/eval_jaxpr/ppermute | solution.py:58
  114.0 25.1 %all-to-all-start = ((f32[256,1,4]{2,1,0:T(1,128)}), f32[256,1,4]{2,1,0:T(1,128)}, u32[]{:S(2)}, u32[]{:S(2)}) async-start(f32[256,1,4]{2,1,0:T(1,128)} %broadcast_in_dim.4), calls=%async_computation | async-start | bytes 262144 | tf_op jit(solution)/shard_map/while/body/eval_jaxpr/all_to_all | solution.py:39
  127.1 19.9 %collective-permute-start.24 = (f32[128,256]{0,1:T(8,128)S(1)}, f32[128,256]{0,1:T(8,128)}, u32[]{:S(2)}, u32[]{:S(2)}) collective-permute-start(f32[128,256]{0,1:T(8,128)S(1)} %get-tuple-element.246), channel_id=1, source_target_pairs={{0,64},{32,96},{64,0},{96,32},{128,192},{160,224},{192,128},{224,1... | collective-permute-start | bytes 393224 | tf_op jit(solution)/shard_map/while/body/eval_jaxpr/ppermute | solution.py:58
  130.0 20.3 %collective-permute-start.25 = (f32[128,256]{0,1:T(8,128)S(1)}, f32[128,256]{0,1:T(8,128)}, u32[]{:S(2)}, u32[]{:S(2)}) collective-permute-start(f32[128,256]{0,1:T(8,128)S(1)} %get-tuple-element.246), channel_id=1, source_target_pairs={{0,96},{32,64},{64,32},{96,0},{128,224},{160,192},{192,160},{224,1... | collective-permute-start | bytes 393224 | tf_op jit(solution)/shard_map/while/body/eval_jaxpr/ppermute | solution.py:58
  130.9 20.3 %collective-permute-start.26 = (f32[128,256]{0,1:T(8,128)S(1)}, f32[128,256]{0,1:T(8,128)}, u32[]{:S(2)}, u32[]{:S(2)}) collective-permute-start(f32[128,256]{0,1:T(8,128)S(1)} %get-tuple-element.246), channel_id=1, source_target_pairs={{0,128},{32,160},{64,192},{96,224},{128,0},{160,32},{192,64},{224,... | collective-permute-start | bytes 393224 | tf_op jit(solution)/shard_map/while/body/eval_jaxpr/ppermute | solution.py:58
  132.1 20.1 %collective-permute-start.27 = (f32[128,256]{0,1:T(8,128)S(1)}, f32[128,256]{0,1:T(8,128)}, u32[]{:S(2)}, u32[]{:S(2)}) collective-permute-start(f32[128,256]{0,1:T(8,128)S(1)} %get-tuple-element.246), channel_id=1, source_target_pairs={{0,160},{32,128},{64,224},{96,192},{128,32},{160,0},{192,96},{224,... | collective-permute-start | bytes 393224 | tf_op jit(solution)/shard_map/while/body/eval_jaxpr/ppermute | solution.py:58
  173.2 10.7 %collective-permute-start.3 = (bf16[96,1024]{1,0:T(8,128)(2,1)S(1)}, bf16[96,1024]{1,0:T(8,128)(2,1)S(1)}, u32[]{:S(2)}, u32[]{:S(2)}) collective-permute-start(bf16[96,1024]{1,0:T(8,128)(2,1)S(1)} %get-tuple-element.230), channel_id=1, source_target_pairs={{0,2},{1,3},{2,0},{3,1},{4,6},{5,7},{6,4},{7,5},{8,10},{9,11},{10,... | collective-permute-start | bytes 589832 | tf_op jit(solution)/shard_map/while/body/eval_jaxpr/ppermute | solution.py:60
  185.3 9.3 %collective-permute-start.5 = (bf16[48,1024]{1,0:T(8,128)(2,1)S(1)}, bf16[48,1024]{1,0:T(8,128)(2,1)S(1)}, u32[]{:S(2)}, u32[]{:S(2)}) collective-permute-start(bf16[48,1024]{1,0:T(8,128)(2,1)S(1)} %get-tuple-element.232), channel_id=1, source_target_pairs={{0,8},{1,9},{2,10},{3,11},{4,12},{5,13},{6,14},{7,15},{8,0},{9,1},... | collective-permute-start | bytes 294920 | tf_op jit(solution)/shard_map/while/body/eval_jaxpr/ppermute | solution.py:58
  254.4 35.3 %collective-permute-start.23 = (f32[128,256]{0,1:T(8,128)S(1)}, f32[128,256]{0,1:T(8,128)}, u32[]{:S(2)}, u32[]{:S(2)}) collective-permute-start(f32[128,256]{0,1:T(8,128)S(1)} %get-tuple-element.246), channel_id=1, source_target_pairs={{0,32},{32,0},{64,96},{96,64},{128,160},{160,128},{192,224},{224,1... | collective-permute-start | bytes 393224 | tf_op jit(solution)/shard_map/while/body/eval_jaxpr/ppermute | solution.py:58
  260.5 23.6 %all-to-all-start = ((f32[256,1,4]{2,1,0:T(1,128)}), f32[256,1,4]{2,1,0:T(1,128)}, u32[]{:S(2)}, u32[]{:S(2)}) async-start(f32[256,1,4]{2,1,0:T(1,128)} %broadcast_in_dim.4), calls=%async_computation | async-start | bytes 262144 | tf_op jit(solution)/shard_map/while/body/eval_jaxpr/all_to_all | solution.py:39
  272.0 19.9 %collective-permute-start.24 = (f32[128,256]{0,1:T(8,128)S(1)}, f32[128,256]{0,1:T(8,128)}, u32[]{:S(2)}, u32[]{:S(2)}) collective-permute-start(f32[128,256]{0,1:T(8,128)S(1)} %get-tuple-element.246), channel_id=1, source_target_pairs={{0,64},{32,96},{64,0},{96,32},{128,192},{160,224},{192,128},{224,1... | collective-permute-start | bytes 393224 | tf_op jit(solution)/shard_map/while/body/eval_jaxpr/ppermute | solution.py:58
  275.0 20.3 %collective-permute-start.25 = (f32[128,256]{0,1:T(8,128)S(1)}, f32[128,256]{0,1:T(8,128)}, u32[]{:S(2)}, u32[]{:S(2)}) collective-permute-start(f32[128,256]{0,1:T(8,128)S(1)} %get-tuple-element.246), channel_id=1, source_target_pairs={{0,96},{32,64},{64,32},{96,0},{128,224},{160,192},{192,160},{224,1... | collective-permute-start | bytes 393224 | tf_op jit(solution)/shard_map/while/body/eval_jaxpr/ppermute | solution.py:58
  275.8 20.3 %collective-permute-start.26 = (f32[128,256]{0,1:T(8,128)S(1)}, f32[128,256]{0,1:T(8,128)}, u32[]{:S(2)}, u32[]{:S(2)}) collective-permute-start(f32[128,256]{0,1:T(8,128)S(1)} %get-tuple-element.246), channel_id=1, source_target_pairs={{0,128},{32,160},{64,192},{96,224},{128,0},{160,32},{192,64},{224,... | collective-permute-start | bytes 393224 | tf_op jit(solution)/shard_map/while/body/eval_jaxpr/ppermute | solution.py:58
  277.0 20.1 %collective-permute-start.27 = (f32[128,256]{0,1:T(8,128)S(1)}, f32[128,256]{0,1:T(8,128)}, u32[]{:S(2)}, u32[]{:S(2)}) collective-permute-start(f32[128,256]{0,1:T(8,128)S(1)} %get-tuple-element.246), channel_id=1, source_target_pairs={{0,160},{32,128},{64,224},{96,192},{128,32},{160,0},{192,96},{224,... | collective-permute-start | bytes 393224 | tf_op jit(solution)/shard_map/while/body/eval_jaxpr/ppermute | solution.py:58
  318.1 10.7 %collective-permute-start.3 = (bf16[96,1024]{1,0:T(8,128)(2,1)S(1)}, bf16[96,1024]{1,0:T(8,128)(2,1)S(1)}, u32[]{:S(2)}, u32[]{:S(2)}) collective-permute-start(bf16[96,1024]{1,0:T(8,128)(2,1)S(1)} %get-tuple-element.230), channel_id=1, source_target_pairs={{0,2},{1,3},{2,0},{3,1},{4,6},{5,7},{6,4},{7,5},{8,10},{9,11},{10,... | collective-permute-start | bytes 589832 | tf_op jit(solution)/shard_map/while/body/eval_jaxpr/ppermute | solution.py:60
  330.3 9.3 %collective-permute-start.5 = (bf16[48,1024]{1,0:T(8,128)(2,1)S(1)}, bf16[48,1024]{1,0:T(8,128)(2,1)S(1)}, u32[]{:S(2)}, u32[]{:S(2)}) collective-permute-start(bf16[48,1024]{1,0:T(8,128)(2,1)S(1)} %get-tuple-element.232), channel_id=1, source_target_pairs={{0,8},{1,9},{2,10},{3,11},{4,12},{5,13},{6,14},{7,15},{8,0},{9,1},... | collective-permute-start | bytes 294920 | tf_op jit(solution)/shard_map/while/body/eval_jaxpr/ppermute | solution.py:58
  399.4 35.3 %collective-permute-start.23 = (f32[128,256]{0,1:T(8,128)S(1)}, f32[128,256]{0,1:T(8,128)}, u32[]{:S(2)}, u32[]{:S(2)}) collective-permute-start(f32[128,256]{0,1:T(8,128)S(1)} %get-tuple-element.246), channel_id=1, source_target_pairs={{0,32},{32,0},{64,96},{96,64},{128,160},{160,128},{192,224},{224,1... | collective-permute-start | bytes 393224 | tf_op jit(solution)/shard_map/while/body/eval_jaxpr/ppermute | solution.py:58
  405.4 23.6 %all-to-all-start = ((f32[256,1,4]{2,1,0:T(1,128)}), f32[256,1,4]{2,1,0:T(1,128)}, u32[]{:S(2)}, u32[]{:S(2)}) async-start(f32[256,1,4]{2,1,0:T(1,128)} %broadcast_in_dim.4), calls=%async_computation | async-start | bytes 262144 | tf_op jit(solution)/shard_map/while/body/eval_jaxpr/all_to_all | solution.py:39
  417.0 19.9 %collective-permute-start.24 = (f32[128,256]{0,1:T(8,128)S(1)}, f32[128,256]{0,1:T(8,128)}, u32[]{:S(2)}, u32[]{:S(2)}) collective-permute-start(f32[128,256]{0,1:T(8,128)S(1)} %get-tuple-element.246), channel_id=1, source_target_pairs={{0,64},{32,96},{64,0},{96,32},{128,192},{160,224},{192,128},{224,1... | collective-permute-start | bytes 393224 | tf_op jit(solution)/shard_map/while/body/eval_jaxpr/ppermute | solution.py:58
  419.9 20.3 %collective-permute-start.25 = (f32[128,256]{0,1:T(8,128)S(1)}, f32[128,256]{0,1:T(8,128)}, u32[]{:S(2)}, u32[]{:S(2)}) collective-permute-start(f32[128,256]{0,1:T(8,128)S(1)} %get-tuple-element.246), channel_id=1, source_target_pairs={{0,96},{32,64},{64,32},{96,0},{128,224},{160,192},{192,160},{224,1... | collective-permute-start | bytes 393224 | tf_op jit(solution)/shard_map/while/body/eval_jaxpr/ppermute | solution.py:58
  420.8 20.3 %collective-permute-start.26 = (f32[128,256]{0,1:T(8,128)S(1)}, f32[128,256]{0,1:T(8,128)}, u32[]{:S(2)}, u32[]{:S(2)}) collective-permute-start(f32[128,256]{0,1:T(8,128)S(1)} %get-tuple-element.246), channel_id=1, source_target_pairs={{0,128},{32,160},{64,192},{96,224},{128,0},{160,32},{192,64},{224,... | collective-permute-start | bytes 393224 | tf_op jit(solution)/shard_map/while/body/eval_jaxpr/ppermute | solution.py:58
  422.0 20.1 %collective-permute-start.27 = (f32[128,256]{0,1:T(8,128)S(1)}, f32[128,256]{0,1:T(8,128)}, u32[]{:S(2)}, u32[]{:S(2)}) collective-permute-start(f32[128,256]{0,1:T(8,128)S(1)} %get-tuple-element.246), channel_id=1, source_target_pairs={{0,160},{32,128},{64,224},{96,192},{128,32},{160,0},{192,96},{224,... | collective-permute-start | bytes 393224 | tf_op jit(solution)/shard_map/while/body/eval_jaxpr/ppermute | solution.py:58
  (100 other events, 771.5 us)

commit v13 on v11

--- a/solution.py
+++ b/solution.py
@@ -86,15 +86,17 @@
     return chunk
 
 
-def fisher_product(direction, residual, normed, hidden_act, slope_act, w_out, metric, width):
+def fisher_product(direction, residual, normed, hidden_act, slope_act, w_out, w_out_t, metric, width):
     tangent = direction.astype(jnp.bfloat16)
     tangent_in = tangent[:, :width]
     tangent_out_t = tangent[:, width:]
     pre_tangent = jnp.dot(normed, tangent_in, preferred_element_type=jnp.float32)
     inner_tangent = (slope_act * pre_tangent).astype(jnp.bfloat16)
-    partial_out = jnp.dot(inner_tangent, w_out, preferred_element_type=jnp.float32)
-    partial_out = partial_out + lax.dot_general(
-        hidden_act, tangent_out_t, (((1,), (1,)), ((), ())), preferred_element_type=jnp.float32
+    partial_out = lax.dot_general(
+        jnp.concatenate([inner_tangent, hidden_act], axis=1),
+        jnp.concatenate([w_out_t, tangent_out_t], axis=1),
+        (((1,), (1,)), ((), ())),
+        preferred_element_type=jnp.float32,
     )
     fsdp_groups = digit_groups(lax.axis_size("fsdp"), (1, 1, 2))
     out_chunk = spread_reduce(partial_out.astype(jnp.bfloat16), "fsdp", fsdp_groups, jnp.bfloat16)
@@ -134,12 +136,13 @@
     preact = jnp.dot(normed, w_in, preferred_element_type=jnp.float32)
     hidden_act = jax.nn.silu(preact).astype(jnp.bfloat16)
     slope_act = silu_slope(preact)
+    w_out_t = w_out.T
     residual = jnp.concatenate([grad_in, grad_out.T], axis=1)
 
     def iterate(_, carry):
         solution_now, residual, direction = carry
         fisher, sums = fisher_product(
-            direction, residual, normed, hidden_act, slope_act, w_out, metric, width
+            direction, residual, normed, hidden_act, slope_act, w_out, w_out_t, metric, width
         )
         quadratic, cross, fisher_square, norm_now = sums
         step_size = norm_now / quadratic

time: 454 us -> 455 us (level)
  starting transfers between devices: 168 us -> 156 us
  local copies, waits for them, and re-layouts: 40.3 us -> 49.1 us
  matrix products: 25.3 us -> 17.1 us
  waiting for transfers between devices: 165 us -> 173 us
    dot_general x6, matrix products: 14.8 us -> 6.94 us  [the longest x3 5.15 us: fisher_product(): jnp.dot(normed, tangent_in, preferred_element_type=jnp.float32)]
    convert_element_type x12, local copies, waits for them, and re-layouts: 0.68 us -> 6.78 us  [spread_reduce(): send.astype(send_type)]
    add x9, other arithmetic: 5.34 us -> 11.3 us  [spread_reduce(): total = total + got.astype(jnp.float32)]
    all_to_all x3, starting transfers between devices: 39.8 us -> 34.3 us  [scalar_sum(): lax.all_to_all(jnp.broadcast_to(values[None], (size,) + values.shape), ax...]
    ppermute x39, starting transfers between devices: 71.7 us -> 66.9 us  [spread_gather(): got = lax.ppermute(chunk, axis, xor_pairs(size, offset << low))]
  transfers between devices with their start and end apart: 81 -> 81, of which waited for: 55 -> 53; matrix products, arithmetic and copies ran while one was open for 8% -> 8% of each run, Pallas kernels for 0% -> 0%
where the time goes in v13:
time: 455 us; the launch traced here: 454 us
  waiting for transfers between devices  173 us (38%)
  starting transfers between devices  156 us (34%)
  local copies, waits for them, and re-layouts  49.1 us (11%)
  other arithmetic  45.4 us (10%)
  matrix products  17.1 us (4%)
  loops' own time  12.9 us (3%)
    ppermute x39, waiting for transfers between devices, spread_reduce(): lax.ppermute(send.astype(send_type), axis, xor_pairs(size, offset << low))  94.3 us
    ppermute x39, starting transfers between devices, spread_gather(): got = lax.ppermute(chunk, axis, xor_pairs(size, offset << low))  66.9 us
    ppermute x39, waiting for transfers between devices, spread_gather(): got = lax.ppermute(chunk, axis, xor_pairs(size, offset << low))  55.2 us
    ppermute x39, starting transfers between devices, spread_reduce(): lax.ppermute(send.astype(send_type), axis, xor_pairs(size, offset << low))  54.7 us
    all_to_all x3, starting transfers between devices, scalar_sum(): lax.all_to_all(jnp.broadcast_to(values[None], (size,) + values.shape), ax...  34.3 us
    all_to_all x3, waiting for transfers between devices, scalar_sum(): lax.all_to_all(jnp.broadcast_to(values[None], (size,) + values.shape), ax...  23.1 us
    dynamic_update_slice x39, local copies, waits for them, and re-layouts, spread_gather(): lax.dynamic_update_slice_in_dim(whole, got, (digit ^ offset) * rows, 0)  18.1 us
    another operation x1, loops' own time, on_device(): lax.fori_loop(0, ITERS, iterate, (jnp.zeros_like(residual), residual, res...  12.9 us
  transfers between devices with their start and end apart: 81, of which 53 were waited for; matrix products, arithmetic and copies ran while one was open for 8% of the time, Pallas kernels for 0%

profile of v13, /device:TPU:1, one launch (start us, length us, event | category | flops | bytes accessed | tf_op | source)
XLA Modules:
  0.0 453.7 jit_solution(3307912596907065519)
XLA Ops:
  9.4 438.4 %while.15 = (s32[]{:T(128)}, f32[1024,256]{0,1:T(8,128)}, f32[1024,256]{0,1:T(8,128)}, f32[1024,256]{0,1:T(8,128)S(1)}, bf16[768,1024]{1,0:T(8,128)(2,1)S(1)}, /...) while((s32[]{:T(128)}, f32[1024,256]{0,1:T(8,128)}, ...), condition=%wide.region_7.8_spmd.clone, body=%wide.region_1.7_spmd.clone.sunk | while | flops 1216250880 | bytes 98962648 | solution.py:155
  24.0 10.8 %collective-permute-done.1 = bf16[192,1024]{1,0:T(8,128)(2,1)S(1)} collective-permute-done((bf16[192,1024]{1,0:T(8,128)(2,1)S(1)}, bf16[192,1024]{1,0:T(8,128)(2,1)S(1)}, u32[]{:S(2)}, u32[]{:S(2)}) %collective-permute-start.1) | collective-permute-done | bytes 393248 | tf_op jit(solution)/shard_map/while/body/eval_jaxpr/ppermute | solution.py:67
  41.6 5.5 %collective-permute-done.3 = bf16[48,1024]{1,0:T(8,128)(2,1)S(1)} collective-permute-done((bf16[48,1024]{1,0:T(8,128)(2,1)S(1)}, bf16[48,1024]{1,0:T(8,128)(2,1)S(1)}, u32[]{:S(2)}, u32[]{:S(2)}) %collective-permute-start.3) | collective-permute-done | bytes 98336 | tf_op jit(solution)/shard_map/while/body/eval_jaxpr/ppermute | solution.py:67
  47.2 5.2 %collective-permute-start.5 = (bf16[24,1024]{1,0:T(8,128)(2,1)S(1)}, bf16[24,1024]{1,0:T(8,128)(2,1)S(1)}, u32[]{:S(2)}, u32[]{:S(2)}) collective-permute-start(bf16[24,1024]{1,0:T(8,128)(2,1)S(1)} %dynamic-slice_convert_fusion.13), channel_id=1, source_target_pairs={{0,16},{1,17},{2,18},{3,19},{4,20},{5,21},{6,22},{7,23},{8,24},{9,... | collective-permute-start | bytes 147464 | tf_op jit(solution)/shard_map/while/body/eval_jaxpr/ppermute | solution.py:67
  54.2 5.2 %collective-permute-start.6 = (bf16[24,1024]{1,0:T(8,128)(2,1)S(1)}, bf16[24,1024]{1,0:T(8,128)(2,1)S(1)}, u32[]{:S(2)}, u32[]{:S(2)}) collective-permute-start(bf16[24,1024]{1,0:T(8,128)(2,1)S(1)} %get-tuple-element.241), channel_id=1, source_target_pairs={{0,16},{1,17},{2,18},{3,19},{4,20},{5,21},{6,22},{7,23},{8,24},{9,... | collective-permute-start | bytes 147464 | tf_op jit(solution)/shard_map/while/body/eval_jaxpr/ppermute | solution.py:83
  72.0 5.9 %collective-permute-done.10 = bf16[192,1024]{1,0:T(8,128)(2,1)S(1)} collective-permute-done((bf16[192,1024]{1,0:T(8,128)(2,1)S(1)}, bf16[192,1024]{1,0:T(8,128)(2,1)S(1)}, u32[]{:S(2)}, u32[]{:S(2)}) %collective-permute-start.10) | collective-permute-done | bytes 393248 | tf_op jit(solution)/shard_map/while/body/eval_jaxpr/ppermute | solution.py:83
  77.9 6.1 %collective-permute-start.11 = (bf16[384,1024]{1,0:T(8,128)(2,1)S(1)}, bf16[384,1024]{1,0:T(8,128)(2,1)}, u32[]{:S(2)}, u32[]{:S(2)}) collective-permute-start(bf16[384,1024]{1,0:T(8,128)(2,1)S(1)} %constant_dynamic-update-slice_fusion.43), channel_id=1, source_target_pairs={{0,1},{1,0},{2,3},{3,2},{4,5},{5,4},{6,7},{7,6},{8,9},{9,8},{10,11... | collective-permute-start | bytes 2359304 | tf_op jit(solution)/shard_map/while/body/eval_jaxpr/ppermute | solution.py:83
  114.6 13.6 %all-to-all-start = ((f32[256,1,4]{2,1,0:T(1,128)}), f32[256,1,4]{2,1,0:T(1,128)S(1)}, u32[]{:S(2)}, u32[]{:S(2)}) async-start(f32[256,1,4]{2,1,0:T(1,128)} %broadcast_in_dim.4), calls=%async_computation | async-start | bytes 262144 | tf_op jit(solution)/shard_map/while/body/eval_jaxpr/all_to_all | solution.py:39
  133.3 7.7 %all-to-all-done = f32[256,1,4]{2,1,0:T(1,128)S(1)} async-done(((f32[256,1,4]{2,1,0:T(1,128)}), f32[256,1,4]{2,1,0:T(1,128)S(1)}, u32[]{:S(2)}, u32[]{:S(2)}) %all-to-all-start) | async-done | bytes 4128 | tf_op jit(solution)/shard_map/while/body/eval_jaxpr/all_to_all | solution.py:39
  173.2 10.7 %collective-permute-done.1 = bf16[192,1024]{1,0:T(8,128)(2,1)S(1)} collective-permute-done((bf16[192,1024]{1,0:T(8,128)(2,1)S(1)}, bf16[192,1024]{1,0:T(8,128)(2,1)S(1)}, u32[]{:S(2)}, u32[]{:S(2)}) %collective-permute-start.1) | collective-permute-done | bytes 393248 | tf_op jit(solution)/shard_map/while/body/eval_jaxpr/ppermute | solution.py:67
  190.7 5.1 %collective-permute-done.3 = bf16[48,1024]{1,0:T(8,128)(2,1)S(1)} collective-permute-done((bf16[48,1024]{1,0:T(8,128)(2,1)S(1)}, bf16[48,1024]{1,0:T(8,128)(2,1)S(1)}, u32[]{:S(2)}, u32[]{:S(2)}) %collective-permute-start.3) | collective-permute-done | bytes 98336 | tf_op jit(solution)/shard_map/while/body/eval_jaxpr/ppermute | solution.py:67
  197.4 5.9 %collective-permute-done.5 = bf16[24,1024]{1,0:T(8,128)(2,1)S(1)} collective-permute-done((bf16[24,1024]{1,0:T(8,128)(2,1)S(1)}, bf16[24,1024]{1,0:T(8,128)(2,1)S(1)}, u32[]{:S(2)}, u32[]{:S(2)}) %collective-permute-start.5) | collective-permute-done | bytes 49184 | tf_op jit(solution)/shard_map/while/body/eval_jaxpr/ppermute | solution.py:67
  204.4 6.0 %collective-permute-done.6 = bf16[24,1024]{1,0:T(8,128)(2,1)S(1)} collective-permute-done((bf16[24,1024]{1,0:T(8,128)(2,1)S(1)}, bf16[24,1024]{1,0:T(8,128)(2,1)S(1)}, u32[]{:S(2)}, u32[]{:S(2)}) %collective-permute-start.6) | collective-permute-done | bytes 49184 | tf_op jit(solution)/shard_map/while/body/eval_jaxpr/ppermute | solution.py:83
  218.2 7.9 %collective-permute-done.10 = bf16[192,1024]{1,0:T(8,128)(2,1)S(1)} collective-permute-done((bf16[192,1024]{1,0:T(8,128)(2,1)S(1)}, bf16[192,1024]{1,0:T(8,128)(2,1)S(1)}, u32[]{:S(2)}, u32[]{:S(2)}) %collective-permute-start.10) | collective-permute-done | bytes 393248 | tf_op jit(solution)/shard_map/while/body/eval_jaxpr/ppermute | solution.py:83
  226.1 5.9 %collective-permute-start.11 = (bf16[384,1024]{1,0:T(8,128)(2,1)S(1)}, bf16[384,1024]{1,0:T(8,128)(2,1)}, u32[]{:S(2)}, u32[]{:S(2)}) collective-permute-start(bf16[384,1024]{1,0:T(8,128)(2,1)S(1)} %constant_dynamic-update-slice_fusion.43), channel_id=1, source_target_pairs={{0,1},{1,0},{2,3},{3,2},{4,5},{5,4},{6,7},{7,6},{8,9},{9,8},{10,11... | collective-permute-start | bytes 2359304 | tf_op jit(solution)/shard_map/while/body/eval_jaxpr/ppermute | solution.py:83
  261.6 10.3 %all-to-all-start = ((f32[256,1,4]{2,1,0:T(1,128)}), f32[256,1,4]{2,1,0:T(1,128)S(1)}, u32[]{:S(2)}, u32[]{:S(2)}) async-start(f32[256,1,4]{2,1,0:T(1,128)} %broadcast_in_dim.4), calls=%async_computation | async-start | bytes 262144 | tf_op jit(solution)/shard_map/while/body/eval_jaxpr/all_to_all | solution.py:39
  277.0 7.7 %all-to-all-done = f32[256,1,4]{2,1,0:T(1,128)S(1)} async-done(((f32[256,1,4]{2,1,0:T(1,128)}), f32[256,1,4]{2,1,0:T(1,128)S(1)}, u32[]{:S(2)}, u32[]{:S(2)}) %all-to-all-start) | async-done | bytes 4128 | tf_op jit(solution)/shard_map/while/body/eval_jaxpr/all_to_all | solution.py:39
  317.2 10.7 %collective-permute-done.1 = bf16[192,1024]{1,0:T(8,128)(2,1)S(1)} collective-permute-done((bf16[192,1024]{1,0:T(8,128)(2,1)S(1)}, bf16[192,1024]{1,0:T(8,128)(2,1)S(1)}, u32[]{:S(2)}, u32[]{:S(2)}) %collective-permute-start.1) | collective-permute-done | bytes 393248 | tf_op jit(solution)/shard_map/while/body/eval_jaxpr/ppermute | solution.py:67
  341.3 5.9 %collective-permute-done.5 = bf16[24,1024]{1,0:T(8,128)(2,1)S(1)} collective-permute-done((bf16[24,1024]{1,0:T(8,128)(2,1)S(1)}, bf16[24,1024]{1,0:T(8,128)(2,1)S(1)}, u32[]{:S(2)}, u32[]{:S(2)}) %collective-permute-start.5) | collective-permute-done | bytes 49184 | tf_op jit(solution)/shard_map/while/body/eval_jaxpr/ppermute | solution.py:67
  348.3 6.0 %collective-permute-done.6 = bf16[24,1024]{1,0:T(8,128)(2,1)S(1)} collective-permute-done((bf16[24,1024]{1,0:T(8,128)(2,1)S(1)}, bf16[24,1024]{1,0:T(8,128)(2,1)S(1)}, u32[]{:S(2)}, u32[]{:S(2)}) %collective-permute-start.6) | collective-permute-done | bytes 49184 | tf_op jit(solution)/shard_map/while/body/eval_jaxpr/ppermute | solution.py:83
  362.2 7.9 %collective-permute-done.10 = bf16[192,1024]{1,0:T(8,128)(2,1)S(1)} collective-permute-done((bf16[192,1024]{1,0:T(8,128)(2,1)S(1)}, bf16[192,1024]{1,0:T(8,128)(2,1)S(1)}, u32[]{:S(2)}, u32[]{:S(2)}) %collective-permute-start.10) | collective-permute-done | bytes 393248 | tf_op jit(solution)/shard_map/while/body/eval_jaxpr/ppermute | solution.py:83
  370.1 5.9 %collective-permute-start.11 = (bf16[384,1024]{1,0:T(8,128)(2,1)S(1)}, bf16[384,1024]{1,0:T(8,128)(2,1)}, u32[]{:S(2)}, u32[]{:S(2)}) collective-permute-start(bf16[384,1024]{1,0:T(8,128)(2,1)S(1)} %constant_dynamic-update-slice_fusion.43), channel_id=1, source_target_pairs={{0,1},{1,0},{2,3},{3,2},{4,5},{5,4},{6,7},{7,6},{8,9},{9,8},{10,11... | collective-permute-start | bytes 2359304 | tf_op jit(solution)/shard_map/while/body/eval_jaxpr/ppermute | solution.py:83
  405.6 10.3 %all-to-all-start = ((f32[256,1,4]{2,1,0:T(1,128)}), f32[256,1,4]{2,1,0:T(1,128)S(1)}, u32[]{:S(2)}, u32[]{:S(2)}) async-start(f32[256,1,4]{2,1,0:T(1,128)} %broadcast_in_dim.4), calls=%async_computation | async-start | bytes 262144 | tf_op jit(solution)/shard_map/while/body/eval_jaxpr/all_to_all | solution.py:39
  420.9 7.7 %all-to-all-done = f32[256,1,4]{2,1,0:T(1,128)S(1)} async-done(((f32[256,1,4]{2,1,0:T(1,128)}), f32[256,1,4]{2,1,0:T(1,128)S(1)}, u32[]{:S(2)}, u32[]{:S(2)}) %all-to-all-start) | async-done | bytes 4128 | tf_op jit(solution)/shard_map/while/body/eval_jaxpr/all_to_all | solution.py:39
  (368 shorter events, 266.2 us)
Async XLA Ops:
  22.9 11.9 %collective-permute-start.1 = (bf16[192,1024]{1,0:T(8,128)(2,1)S(1)}, bf16[192,1024]{1,0:T(8,128)(2,1)S(1)}, u32[]{:S(2)}, u32[]{:S(2)}) collective-permute-start(bf16[192,1024]{1,0:T(8,128)(2,1)S(1)} %dynamic-slice_convert_fusion.11), channel_id=1, source_target_pairs={{0,2},{1,3},{2,0},{3,1},{4,6},{5,7},{6,4},{7,5},{8,10},{9,11},{10,... | collective-permute-start | bytes 1179656 | tf_op jit(solution)/shard_map/while/body/eval_jaxpr/ppermute | solution.py:67
  109.1 36.9 %collective-permute-start.19 = (f32[128,256]{0,1:T(8,128)S(1)}, f32[128,256]{0,1:T(8,128)S(1)}, u32[]{:S(2)}, u32[]{:S(2)}) collective-permute-start(f32[128,256]{0,1:T(8,128)S(1)} %get-tuple-element.248), channel_id=1, source_target_pairs={{0,32},{32,0},{64,96},{96,64},{128,160},{160,128},{192,224},{224,1... | collective-permute-start | bytes 393224 | tf_op jit(solution)/shard_map/while/body/eval_jaxpr/ppermute | solution.py:83
  114.6 26.4 %all-to-all-start = ((f32[256,1,4]{2,1,0:T(1,128)}), f32[256,1,4]{2,1,0:T(1,128)S(1)}, u32[]{:S(2)}, u32[]{:S(2)}) async-start(f32[256,1,4]{2,1,0:T(1,128)} %broadcast_in_dim.4), calls=%async_computation | async-start | bytes 262144 | tf_op jit(solution)/shard_map/while/body/eval_jaxpr/all_to_all | solution.py:39
  128.3 19.5 %collective-permute-start.20 = (f32[128,256]{0,1:T(8,128)S(1)}, f32[128,256]{0,1:T(8,128)S(1)}, u32[]{:S(2)}, u32[]{:S(2)}) collective-permute-start(f32[128,256]{0,1:T(8,128)S(1)} %get-tuple-element.248), channel_id=1, source_target_pairs={{0,64},{32,96},{64,0},{96,32},{128,192},{160,224},{192,128},{224,1... | collective-permute-start | bytes 393224 | tf_op jit(solution)/shard_map/while/body/eval_jaxpr/ppermute | solution.py:83
  131.3 19.7 %collective-permute-start.21 = (f32[128,256]{0,1:T(8,128)S(1)}, f32[128,256]{0,1:T(8,128)S(1)}, u32[]{:S(2)}, u32[]{:S(2)}) collective-permute-start(f32[128,256]{0,1:T(8,128)S(1)} %get-tuple-element.248), channel_id=1, source_target_pairs={{0,96},{32,64},{64,32},{96,0},{128,224},{160,192},{192,160},{224,1... | collective-permute-start | bytes 393224 | tf_op jit(solution)/shard_map/while/body/eval_jaxpr/ppermute | solution.py:83
  132.1 19.5 %collective-permute-start.22 = (f32[128,256]{0,1:T(8,128)S(1)}, f32[128,256]{0,1:T(8,128)S(1)}, u32[]{:S(2)}, u32[]{:S(2)}) collective-permute-start(f32[128,256]{0,1:T(8,128)S(1)} %get-tuple-element.248), channel_id=1, source_target_pairs={{0,128},{32,160},{64,192},{96,224},{128,0},{160,32},{192,64},{224,... | collective-permute-start | bytes 393224 | tf_op jit(solution)/shard_map/while/body/eval_jaxpr/ppermute | solution.py:83
  133.3 19.0 %collective-permute-start.23 = (f32[128,256]{0,1:T(8,128)S(1)}, f32[128,256]{0,1:T(8,128)S(1)}, u32[]{:S(2)}, u32[]{:S(2)}) collective-permute-start(f32[128,256]{0,1:T(8,128)S(1)} %get-tuple-element.248), channel_id=1, source_target_pairs={{0,160},{32,128},{64,224},{96,192},{128,32},{160,0},{192,96},{224,... | collective-permute-start | bytes 393224 | tf_op jit(solution)/shard_map/while/body/eval_jaxpr/ppermute | solution.py:83
  172.0 11.9 %collective-permute-start.1 = (bf16[192,1024]{1,0:T(8,128)(2,1)S(1)}, bf16[192,1024]{1,0:T(8,128)(2,1)S(1)}, u32[]{:S(2)}, u32[]{:S(2)}) collective-permute-start(bf16[192,1024]{1,0:T(8,128)(2,1)S(1)} %dynamic-slice_convert_fusion.11), channel_id=1, source_target_pairs={{0,2},{1,3},{2,0},{3,1},{4,6},{5,7},{6,4},{7,5},{8,10},{9,11},{10,... | collective-permute-start | bytes 1179656 | tf_op jit(solution)/shard_map/while/body/eval_jaxpr/ppermute | solution.py:67
  186.3 9.5 %collective-permute-start.3 = (bf16[48,1024]{1,0:T(8,128)(2,1)S(1)}, bf16[48,1024]{1,0:T(8,128)(2,1)S(1)}, u32[]{:S(2)}, u32[]{:S(2)}) collective-permute-start(bf16[48,1024]{1,0:T(8,128)(2,1)S(1)} %get-tuple-element.238), channel_id=1, source_target_pairs={{0,8},{1,9},{2,10},{3,11},{4,12},{5,13},{6,14},{7,15},{8,0},{9,1},... | collective-permute-start | bytes 294920 | tf_op jit(solution)/shard_map/while/body/eval_jaxpr/ppermute | solution.py:67
  241.4 8.8 %collective-permute-start.15 = (f32[128,256]{0,1:T(8,128)}, f32[128,256]{0,1:T(8,128)S(1)}, u32[]{:S(2)}, u32[]{:S(2)}) collective-permute-start(f32[128,256]{0,1:T(8,128)} %get-tuple-element.244), channel_id=1, source_target_pairs={{0,128},{32,160},{64,192},{96,224},{128,0},{160,32},{192,64},{224,... | collective-permute-start | bytes 393224 | tf_op jit(solution)/shard_map/while/body/eval_jaxpr/ppermute | solution.py:67
  255.7 33.9 %collective-permute-start.19 = (f32[128,256]{0,1:T(8,128)S(1)}, f32[128,256]{0,1:T(8,128)S(1)}, u32[]{:S(2)}, u32[]{:S(2)}) collective-permute-start(f32[128,256]{0,1:T(8,128)S(1)} %get-tuple-element.248), channel_id=1, source_target_pairs={{0,32},{32,0},{64,96},{96,64},{128,160},{160,128},{192,224},{224,1... | collective-permute-start | bytes 393224 | tf_op jit(solution)/shard_map/while/body/eval_jaxpr/ppermute | solution.py:83
  261.6 23.1 %all-to-all-start = ((f32[256,1,4]{2,1,0:T(1,128)}), f32[256,1,4]{2,1,0:T(1,128)S(1)}, u32[]{:S(2)}, u32[]{:S(2)}) async-start(f32[256,1,4]{2,1,0:T(1,128)} %broadcast_in_dim.4), calls=%async_computation | async-start | bytes 262144 | tf_op jit(solution)/shard_map/while/body/eval_jaxpr/all_to_all | solution.py:39
  271.9 19.5 %collective-permute-start.20 = (f32[128,256]{0,1:T(8,128)S(1)}, f32[128,256]{0,1:T(8,128)S(1)}, u32[]{:S(2)}, u32[]{:S(2)}) collective-permute-start(f32[128,256]{0,1:T(8,128)S(1)} %get-tuple-element.248), channel_id=1, source_target_pairs={{0,64},{32,96},{64,0},{96,32},{128,192},{160,224},{192,128},{224,1... | collective-permute-start | bytes 393224 | tf_op jit(solution)/shard_map/while/body/eval_jaxpr/ppermute | solution.py:83
  274.9 19.7 %collective-permute-start.21 = (f32[128,256]{0,1:T(8,128)S(1)}, f32[128,256]{0,1:T(8,128)S(1)}, u32[]{:S(2)}, u32[]{:S(2)}) collective-permute-start(f32[128,256]{0,1:T(8,128)S(1)} %get-tuple-element.248), channel_id=1, source_target_pairs={{0,96},{32,64},{64,32},{96,0},{128,224},{160,192},{192,160},{224,1... | collective-permute-start | bytes 393224 | tf_op jit(solution)/shard_map/while/body/eval_jaxpr/ppermute | solution.py:83
  275.8 19.5 %collective-permute-start.22 = (f32[128,256]{0,1:T(8,128)S(1)}, f32[128,256]{0,1:T(8,128)S(1)}, u32[]{:S(2)}, u32[]{:S(2)}) collective-permute-start(f32[128,256]{0,1:T(8,128)S(1)} %get-tuple-element.248), channel_id=1, source_target_pairs={{0,128},{32,160},{64,192},{96,224},{128,0},{160,32},{192,64},{224,... | collective-permute-start | bytes 393224 | tf_op jit(solution)/shard_map/while/body/eval_jaxpr/ppermute | solution.py:83
  277.0 19.0 %collective-permute-start.23 = (f32[128,256]{0,1:T(8,128)S(1)}, f32[128,256]{0,1:T(8,128)S(1)}, u32[]{:S(2)}, u32[]{:S(2)}) collective-permute-start(f32[128,256]{0,1:T(8,128)S(1)} %get-tuple-element.248), channel_id=1, source_target_pairs={{0,160},{32,128},{64,224},{96,192},{128,32},{160,0},{192,96},{224,... | collective-permute-start | bytes 393224 | tf_op jit(solution)/shard_map/while/body/eval_jaxpr/ppermute | solution.py:83
  315.9 11.9 %collective-permute-start.1 = (bf16[192,1024]{1,0:T(8,128)(2,1)S(1)}, bf16[192,1024]{1,0:T(8,128)(2,1)S(1)}, u32[]{:S(2)}, u32[]{:S(2)}) collective-permute-start(bf16[192,1024]{1,0:T(8,128)(2,1)S(1)} %dynamic-slice_convert_fusion.11), channel_id=1, source_target_pairs={{0,2},{1,3},{2,0},{3,1},{4,6},{5,7},{6,4},{7,5},{8,10},{9,11},{10,... | collective-permute-start | bytes 1179656 | tf_op jit(solution)/shard_map/while/body/eval_jaxpr/ppermute | solution.py:67
  330.2 9.5 %collective-permute-start.3 = (bf16[48,1024]{1,0:T(8,128)(2,1)S(1)}, bf16[48,1024]{1,0:T(8,128)(2,1)S(1)}, u32[]{:S(2)}, u32[]{:S(2)}) collective-permute-start(bf16[48,1024]{1,0:T(8,128)(2,1)S(1)} %get-tuple-element.238), channel_id=1, source_target_pairs={{0,8},{1,9},{2,10},{3,11},{4,12},{5,13},{6,14},{7,15},{8,0},{9,1},... | collective-permute-start | bytes 294920 | tf_op jit(solution)/shard_map/while/body/eval_jaxpr/ppermute | solution.py:67
  399.7 33.9 %collective-permute-start.19 = (f32[128,256]{0,1:T(8,128)S(1)}, f32[128,256]{0,1:T(8,128)S(1)}, u32[]{:S(2)}, u32[]{:S(2)}) collective-permute-start(f32[128,256]{0,1:T(8,128)S(1)} %get-tuple-element.248), channel_id=1, source_target_pairs={{0,32},{32,0},{64,96},{96,64},{128,160},{160,128},{192,224},{224,1... | collective-permute-start | bytes 393224 | tf_op jit(solution)/shard_map/while/body/eval_jaxpr/ppermute | solution.py:83
  405.6 23.1 %all-to-all-start = ((f32[256,1,4]{2,1,0:T(1,128)}), f32[256,1,4]{2,1,0:T(1,128)S(1)}, u32[]{:S(2)}, u32[]{:S(2)}) async-start(f32[256,1,4]{2,1,0:T(1,128)} %broadcast_in_dim.4), calls=%async_computation | async-start | bytes 262144 | tf_op jit(solution)/shard_map/while/body/eval_jaxpr/all_to_all | solution.py:39
  415.9 19.5 %collective-permute-start.20 = (f32[128,256]{0,1:T(8,128)S(1)}, f32[128,256]{0,1:T(8,128)S(1)}, u32[]{:S(2)}, u32[]{:S(2)}) collective-permute-start(f32[128,256]{0,1:T(8,128)S(1)} %get-tuple-element.248), channel_id=1, source_target_pairs={{0,64},{32,96},{64,0},{96,32},{128,192},{160,224},{192,128},{224,1... | collective-permute-start | bytes 393224 | tf_op jit(solution)/shard_map/while/body/eval_jaxpr/ppermute | solution.py:83
  418.9 19.7 %collective-permute-start.21 = (f32[128,256]{0,1:T(8,128)S(1)}, f32[128,256]{0,1:T(8,128)S(1)}, u32[]{:S(2)}, u32[]{:S(2)}) collective-permute-start(f32[128,256]{0,1:T(8,128)S(1)} %get-tuple-element.248), channel_id=1, source_target_pairs={{0,96},{32,64},{64,32},{96,0},{128,224},{160,192},{192,160},{224,1... | collective-permute-start | bytes 393224 | tf_op jit(solution)/shard_map/while/body/eval_jaxpr/ppermute | solution.py:83
  419.7 19.5 %collective-permute-start.22 = (f32[128,256]{0,1:T(8,128)S(1)}, f32[128,256]{0,1:T(8,128)S(1)}, u32[]{:S(2)}, u32[]{:S(2)}) collective-permute-start(f32[128,256]{0,1:T(8,128)S(1)} %get-tuple-element.248), channel_id=1, source_target_pairs={{0,128},{32,160},{64,192},{96,224},{128,0},{160,32},{192,64},{224,... | collective-permute-start | bytes 393224 | tf_op jit(solution)/shard_map/while/body/eval_jaxpr/ppermute | solution.py:83
  420.9 19.0 %collective-permute-start.23 = (f32[128,256]{0,1:T(8,128)S(1)}, f32[128,256]{0,1:T(8,128)S(1)}, u32[]{:S(2)}, u32[]{:S(2)}) collective-permute-start(f32[128,256]{0,1:T(8,128)S(1)} %get-tuple-element.248), channel_id=1, source_target_pairs={{0,160},{32,128},{64,224},{96,192},{128,32},{160,0},{192,96},{224,... | collective-permute-start | bytes 393224 | tf_op jit(solution)/shard_map/while/body/eval_jaxpr/ppermute | solution.py:83
  (96 other events, 578.3 us)

commit v14 on v11

--- a/solution.py
+++ b/solution.py
@@ -96,7 +96,7 @@
     partial_out = partial_out + lax.dot_general(
         hidden_act, tangent_out_t, (((1,), (1,)), ((), ())), preferred_element_type=jnp.float32
     )
-    fsdp_groups = digit_groups(lax.axis_size("fsdp"), (1, 1, 2))
+    fsdp_groups = digit_groups(lax.axis_size("fsdp"), (1, 1, 1))
     out_chunk = spread_reduce(partial_out.astype(jnp.bfloat16), "fsdp", fsdp_groups, jnp.bfloat16)
     cotangent = spread_gather((out_chunk * metric).astype(jnp.bfloat16), "fsdp", fsdp_groups)
     back_act = lax.dot_general(

time: 454 us -> 445 us (0.980)
  waiting for transfers between devices: 165 us -> 154 us
    ppermute x39, waiting for transfers between devices: 91.3 us -> 84.2 us  [spread_reduce(): lax.ppermute(send.astype(send_type), axis, xor_pairs(size, offset << low))]
  transfers between devices with their start and end apart: 81 -> 81, of which waited for: 55 -> 51; matrix products, arithmetic and copies ran while one was open for 8% -> 8% of each run, Pallas kernels for 0% -> 0%
where the time goes in v14:
time: 445 us; the launch traced here: 443 us
  starting transfers between devices  170 us (38%)
  waiting for transfers between devices  154 us (35%)
  other arithmetic  41.2 us (9%)
  local copies, waits for them, and re-layouts  40.3 us (9%)
  matrix products  25.3 us (6%)
  loops' own time  12.3 us (3%)
    ppermute x39, waiting for transfers between devices, spread_reduce(): lax.ppermute(send.astype(send_type), axis, xor_pairs(size, offset << low))  84.2 us
    ppermute x39, starting transfers between devices, spread_gather(): got = lax.ppermute(chunk, axis, xor_pairs(size, offset << low))  76.2 us
    ppermute x39, starting transfers between devices, spread_reduce(): lax.ppermute(send.astype(send_type), axis, xor_pairs(size, offset << low))  56.1 us
    ppermute x39, waiting for transfers between devices, spread_gather(): got = lax.ppermute(chunk, axis, xor_pairs(size, offset << low))  48.5 us
    all_to_all x3, starting transfers between devices, scalar_sum(): lax.all_to_all(jnp.broadcast_to(values[None], (size,) + values.shape), ax...  37.6 us
    all_to_all x3, waiting for transfers between devices, scalar_sum(): lax.all_to_all(jnp.broadcast_to(values[None], (size,) + values.shape), ax...  20.9 us
    dynamic_update_slice x39, local copies, waits for them, and re-layouts, spread_gather(): lax.dynamic_update_slice_in_dim(whole, got, (digit ^ offset) * rows, 0)  17.6 us
    another operation x1, loops' own time, on_device(): lax.fori_loop(0, ITERS, iterate, (jnp.zeros_like(residual), residual, res...  12.3 us
  transfers between devices with their start and end apart: 81, of which 51 were waited for; matrix products, arithmetic and copies ran while one was open for 8% of the time, Pallas kernels for 0%

profile of v14, /device:TPU:1, one launch (start us, length us, event | category | flops | bytes accessed | tf_op | source)
XLA Modules:
  0.0 443.1 jit_solution(6390543381817663437)
XLA Ops:
  7.2 429.9 %while.15 = (s32[]{:T(128)}, f32[1024,256]{0,1:T(8,128)}, f32[1024,256]{0,1:T(8,128)}, f32[1024,256]{0,1:T(8,128)S(1)}, bf16[768,1024]{1,0:T(8,128)(2,1)}, /*ind...) while((s32[]{:T(128)}, f32[1024,256]{0,1:T(8,128)}, ...), condition=%wide.region_7.8_spmd.clone, body=%wide.region_1.7_spmd.clone.sunk | while | flops 1215202304 | bytes 108170368 | solution.py:152
  23.1 10.8 %collective-permute-done.1 = bf16[192,1024]{1,0:T(8,128)(2,1)S(1)} collective-permute-done((bf16[192,1024]{1,0:T(8,128)(2,1)S(1)}, bf16[192,1024]{1,0:T(8,128)(2,1)S(1)}, u32[]{:S(2)}, u32[]{:S(2)}) %collective-permute-start.1) | collective-permute-done | bytes 393248 | tf_op jit(solution)/shard_map/while/body/eval_jaxpr/ppermute | solution.py:67
  34.2 5.2 %collective-permute-done.2 = bf16[96,1024]{1,0:T(8,128)(2,1)S(1)} collective-permute-done((bf16[96,1024]{1,0:T(8,128)(2,1)S(1)}, bf16[96,1024]{1,0:T(8,128)(2,1)S(1)}, u32[]{:S(2)}, u32[]{:S(2)}) %collective-permute-start.2) | collective-permute-done | bytes 196640 | tf_op jit(solution)/shard_map/while/body/eval_jaxpr/ppermute | solution.py:67
  39.5 4.4 collective-permute-start.3
  46.0 5.0 %collective-permute-done.4 = bf16[24,1024]{1,0:T(8,128)(2,1)S(1)} collective-permute-done((bf16[24,1024]{1,0:T(8,128)(2,1)S(1)}, bf16[24,1024]{1,0:T(8,128)(2,1)S(1)}, u32[]{:S(2)}, u32[]{:S(2)}) %collective-permute-start.4) | collective-permute-done | bytes 49184 | tf_op jit(solution)/shard_map/while/body/eval_jaxpr/ppermute | solution.py:67
  61.1 4.3 collective-permute-done.9
  68.4 5.3 %collective-permute-done.10 = bf16[192,1024]{1,0:T(8,128)(2,1)S(1)} collective-permute-done((bf16[192,1024]{1,0:T(8,128)(2,1)S(1)}, bf16[192,1024]{1,0:T(8,128)(2,1)S(1)}, u32[]{:S(2)}, u32[]{:S(2)}) %collective-permute-start.10) | collective-permute-done | bytes 393248 | tf_op jit(solution)/shard_map/while/body/eval_jaxpr/ppermute | solution.py:83
  73.6 7.2 %collective-permute-start.11 = (bf16[384,1024]{1,0:T(8,128)(2,1)S(1)}, bf16[384,1024]{1,0:T(8,128)(2,1)}, u32[]{:S(2)}, u32[]{:S(2)}) collective-permute-start(bf16[384,1024]{1,0:T(8,128)(2,1)S(1)} %constant_dynamic-update-slice_fusion.43), channel_id=1, source_target_pairs={{0,1},{1,0},{2,3},{3,2},{4,5},{5,4},{6,7},{7,6},{8,9},{9,8},{10,11... | collective-permute-start | bytes 2359304 | tf_op jit(solution)/shard_map/while/body/eval_jaxpr/ppermute | solution.py:83
  87.3 3.9 collective-permute-start.13
  110.6 12.3 %all-to-all-start = ((f32[256,1,4]{2,1,0:T(1,128)}), f32[256,1,4]{2,1,0:T(1,128)}, u32[]{:S(2)}, u32[]{:S(2)}) async-start(f32[256,1,4]{2,1,0:T(1,128)} %broadcast_in_dim.4), calls=%async_computation | async-start | bytes 262144 | tf_op jit(solution)/shard_map/while/body/eval_jaxpr/all_to_all | solution.py:39
  127.9 7.0 %all-to-all-done = f32[256,1,4]{2,1,0:T(1,128)} async-done(((f32[256,1,4]{2,1,0:T(1,128)}), f32[256,1,4]{2,1,0:T(1,128)}, u32[]{:S(2)}, u32[]{:S(2)}) %all-to-all-start) | async-done | bytes 4128 | tf_op jit(solution)/shard_map/while/body/eval_jaxpr/all_to_all | solution.py:39
  168.7 10.8 %collective-permute-done.1 = bf16[192,1024]{1,0:T(8,128)(2,1)S(1)} collective-permute-done((bf16[192,1024]{1,0:T(8,128)(2,1)S(1)}, bf16[192,1024]{1,0:T(8,128)(2,1)S(1)}, u32[]{:S(2)}, u32[]{:S(2)}) %collective-permute-start.1) | collective-permute-done | bytes 393248 | tf_op jit(solution)/shard_map/while/body/eval_jaxpr/ppermute | solution.py:67
  180.3 4.7 %collective-permute-done.2 = bf16[96,1024]{1,0:T(8,128)(2,1)S(1)} collective-permute-done((bf16[96,1024]{1,0:T(8,128)(2,1)S(1)}, bf16[96,1024]{1,0:T(8,128)(2,1)S(1)}, u32[]{:S(2)}, u32[]{:S(2)}) %collective-permute-start.2) | collective-permute-done | bytes 196640 | tf_op jit(solution)/shard_map/while/body/eval_jaxpr/ppermute | solution.py:67
  210.1 6.4 %collective-permute-done.10 = bf16[192,1024]{1,0:T(8,128)(2,1)S(1)} collective-permute-done((bf16[192,1024]{1,0:T(8,128)(2,1)S(1)}, bf16[192,1024]{1,0:T(8,128)(2,1)S(1)}, u32[]{:S(2)}, u32[]{:S(2)}) %collective-permute-start.10) | collective-permute-done | bytes 393248 | tf_op jit(solution)/shard_map/while/body/eval_jaxpr/ppermute | solution.py:83
  216.5 7.4 %collective-permute-start.11 = (bf16[384,1024]{1,0:T(8,128)(2,1)S(1)}, bf16[384,1024]{1,0:T(8,128)(2,1)}, u32[]{:S(2)}, u32[]{:S(2)}) collective-permute-start(bf16[384,1024]{1,0:T(8,128)(2,1)S(1)} %constant_dynamic-update-slice_fusion.43), channel_id=1, source_target_pairs={{0,1},{1,0},{2,3},{3,2},{4,5},{5,4},{6,7},{7,6},{8,9},{9,8},{10,11... | collective-permute-start | bytes 2359304 | tf_op jit(solution)/shard_map/while/body/eval_jaxpr/ppermute | solution.py:83
  251.7 12.6 %all-to-all-start = ((f32[256,1,4]{2,1,0:T(1,128)}), f32[256,1,4]{2,1,0:T(1,128)}, u32[]{:S(2)}, u32[]{:S(2)}) async-start(f32[256,1,4]{2,1,0:T(1,128)} %broadcast_in_dim.4), calls=%async_computation | async-start | bytes 262144 | tf_op jit(solution)/shard_map/while/body/eval_jaxpr/all_to_all | solution.py:39
  269.4 7.0 %all-to-all-done = f32[256,1,4]{2,1,0:T(1,128)} async-done(((f32[256,1,4]{2,1,0:T(1,128)}), f32[256,1,4]{2,1,0:T(1,128)}, u32[]{:S(2)}, u32[]{:S(2)}) %all-to-all-start) | async-done | bytes 4128 | tf_op jit(solution)/shard_map/while/body/eval_jaxpr/all_to_all | solution.py:39
  310.2 10.8 %collective-permute-done.1 = bf16[192,1024]{1,0:T(8,128)(2,1)S(1)} collective-permute-done((bf16[192,1024]{1,0:T(8,128)(2,1)S(1)}, bf16[192,1024]{1,0:T(8,128)(2,1)S(1)}, u32[]{:S(2)}, u32[]{:S(2)}) %collective-permute-start.1) | collective-permute-done | bytes 393248 | tf_op jit(solution)/shard_map/while/body/eval_jaxpr/ppermute | solution.py:67
  321.8 4.7 %collective-permute-done.2 = bf16[96,1024]{1,0:T(8,128)(2,1)S(1)} collective-permute-done((bf16[96,1024]{1,0:T(8,128)(2,1)S(1)}, bf16[96,1024]{1,0:T(8,128)(2,1)S(1)}, u32[]{:S(2)}, u32[]{:S(2)}) %collective-permute-start.2) | collective-permute-done | bytes 196640 | tf_op jit(solution)/shard_map/while/body/eval_jaxpr/ppermute | solution.py:67
  327.2 3.7 collective-permute-start.4
  351.6 6.4 %collective-permute-done.10 = bf16[192,1024]{1,0:T(8,128)(2,1)S(1)} collective-permute-done((bf16[192,1024]{1,0:T(8,128)(2,1)S(1)}, bf16[192,1024]{1,0:T(8,128)(2,1)S(1)}, u32[]{:S(2)}, u32[]{:S(2)}) %collective-permute-start.10) | collective-permute-done | bytes 393248 | tf_op jit(solution)/shard_map/while/body/eval_jaxpr/ppermute | solution.py:83
  358.0 7.4 %collective-permute-start.11 = (bf16[384,1024]{1,0:T(8,128)(2,1)S(1)}, bf16[384,1024]{1,0:T(8,128)(2,1)}, u32[]{:S(2)}, u32[]{:S(2)}) collective-permute-start(bf16[384,1024]{1,0:T(8,128)(2,1)S(1)} %constant_dynamic-update-slice_fusion.43), channel_id=1, source_target_pairs={{0,1},{1,0},{2,3},{3,2},{4,5},{5,4},{6,7},{7,6},{8,9},{9,8},{10,11... | collective-permute-start | bytes 2359304 | tf_op jit(solution)/shard_map/while/body/eval_jaxpr/ppermute | solution.py:83
  393.2 12.6 %all-to-all-start = ((f32[256,1,4]{2,1,0:T(1,128)}), f32[256,1,4]{2,1,0:T(1,128)}, u32[]{:S(2)}, u32[]{:S(2)}) async-start(f32[256,1,4]{2,1,0:T(1,128)} %broadcast_in_dim.4), calls=%async_computation | async-start | bytes 262144 | tf_op jit(solution)/shard_map/while/body/eval_jaxpr/all_to_all | solution.py:39
  410.9 7.0 %all-to-all-done = f32[256,1,4]{2,1,0:T(1,128)} async-done(((f32[256,1,4]{2,1,0:T(1,128)}), f32[256,1,4]{2,1,0:T(1,128)}, u32[]{:S(2)}, u32[]{:S(2)}) %all-to-all-start) | async-done | bytes 4128 | tf_op jit(solution)/shard_map/while/body/eval_jaxpr/all_to_all | solution.py:39
  (344 shorter events, 263.4 us)
Async XLA Ops:
  22.0 11.9 %collective-permute-start.1 = (bf16[192,1024]{1,0:T(8,128)(2,1)S(1)}, bf16[192,1024]{1,0:T(8,128)(2,1)S(1)}, u32[]{:S(2)}, u32[]{:S(2)}) collective-permute-start(bf16[192,1024]{1,0:T(8,128)(2,1)S(1)} %dynamic-slice_convert_fusion.11), channel_id=1, source_target_pairs={{0,2},{1,3},{2,0},{3,1},{4,6},{5,7},{6,4},{7,5},{8,10},{9,11},{10,... | collective-permute-start | bytes 1179656 | tf_op jit(solution)/shard_map/while/body/eval_jaxpr/ppermute | solution.py:67
  73.6 9.2 %collective-permute-start.11 = (bf16[384,1024]{1,0:T(8,128)(2,1)S(1)}, bf16[384,1024]{1,0:T(8,128)(2,1)}, u32[]{:S(2)}, u32[]{:S(2)}) collective-permute-start(bf16[384,1024]{1,0:T(8,128)(2,1)S(1)} %constant_dynamic-update-slice_fusion.43), channel_id=1, source_target_pairs={{0,1},{1,0},{2,3},{3,2},{4,5},{5,4},{6,7},{7,6},{8,9},{9,8},{10,11... | collective-permute-start | bytes 2359304 | tf_op jit(solution)/shard_map/while/body/eval_jaxpr/ppermute | solution.py:83
  104.7 35.8 %collective-permute-start.19 = (f32[128,256]{0,1:T(8,128)S(1)}, f32[128,256]{0,1:T(8,128)}, u32[]{:S(2)}, u32[]{:S(2)}) collective-permute-start(f32[128,256]{0,1:T(8,128)S(1)} %get-tuple-element.222), channel_id=1, source_target_pairs={{0,32},{32,0},{64,96},{96,64},{128,160},{160,128},{192,224},{224,1... | collective-permute-start | bytes 393224 | tf_op jit(solution)/shard_map/while/body/eval_jaxpr/ppermute | solution.py:83
  110.6 24.3 %all-to-all-start = ((f32[256,1,4]{2,1,0:T(1,128)}), f32[256,1,4]{2,1,0:T(1,128)}, u32[]{:S(2)}, u32[]{:S(2)}) async-start(f32[256,1,4]{2,1,0:T(1,128)} %broadcast_in_dim.4), calls=%async_computation | async-start | bytes 262144 | tf_op jit(solution)/shard_map/while/body/eval_jaxpr/all_to_all | solution.py:39
  122.9 19.5 %collective-permute-start.20 = (f32[128,256]{0,1:T(8,128)S(1)}, f32[128,256]{0,1:T(8,128)}, u32[]{:S(2)}, u32[]{:S(2)}) collective-permute-start(f32[128,256]{0,1:T(8,128)S(1)} %get-tuple-element.222), channel_id=1, source_target_pairs={{0,64},{32,96},{64,0},{96,32},{128,192},{160,224},{192,128},{224,1... | collective-permute-start | bytes 393224 | tf_op jit(solution)/shard_map/while/body/eval_jaxpr/ppermute | solution.py:83
  125.9 20.1 %collective-permute-start.21 = (f32[128,256]{0,1:T(8,128)S(1)}, f32[128,256]{0,1:T(8,128)}, u32[]{:S(2)}, u32[]{:S(2)}) collective-permute-start(f32[128,256]{0,1:T(8,128)S(1)} %get-tuple-element.222), channel_id=1, source_target_pairs={{0,96},{32,64},{64,32},{96,0},{128,224},{160,192},{192,160},{224,1... | collective-permute-start | bytes 393224 | tf_op jit(solution)/shard_map/while/body/eval_jaxpr/ppermute | solution.py:83
  126.7 20.1 %collective-permute-start.22 = (f32[128,256]{0,1:T(8,128)S(1)}, f32[128,256]{0,1:T(8,128)}, u32[]{:S(2)}, u32[]{:S(2)}) collective-permute-start(f32[128,256]{0,1:T(8,128)S(1)} %get-tuple-element.222), channel_id=1, source_target_pairs={{0,128},{32,160},{64,192},{96,224},{128,0},{160,32},{192,64},{224,... | collective-permute-start | bytes 393224 | tf_op jit(solution)/shard_map/while/body/eval_jaxpr/ppermute | solution.py:83
  127.9 19.9 %collective-permute-start.23 = (f32[128,256]{0,1:T(8,128)S(1)}, f32[128,256]{0,1:T(8,128)}, u32[]{:S(2)}, u32[]{:S(2)}) collective-permute-start(f32[128,256]{0,1:T(8,128)S(1)} %get-tuple-element.222), channel_id=1, source_target_pairs={{0,160},{32,128},{64,224},{96,192},{128,32},{160,0},{192,96},{224,... | collective-permute-start | bytes 393224 | tf_op jit(solution)/shard_map/while/body/eval_jaxpr/ppermute | solution.py:83
  167.6 11.9 %collective-permute-start.1 = (bf16[192,1024]{1,0:T(8,128)(2,1)S(1)}, bf16[192,1024]{1,0:T(8,128)(2,1)S(1)}, u32[]{:S(2)}, u32[]{:S(2)}) collective-permute-start(bf16[192,1024]{1,0:T(8,128)(2,1)S(1)} %dynamic-slice_convert_fusion.11), channel_id=1, source_target_pairs={{0,2},{1,3},{2,0},{3,1},{4,6},{5,7},{6,4},{7,5},{8,10},{9,11},{10,... | collective-permute-start | bytes 1179656 | tf_op jit(solution)/shard_map/while/body/eval_jaxpr/ppermute | solution.py:67
  216.5 9.4 %collective-permute-start.11 = (bf16[384,1024]{1,0:T(8,128)(2,1)S(1)}, bf16[384,1024]{1,0:T(8,128)(2,1)}, u32[]{:S(2)}, u32[]{:S(2)}) collective-permute-start(bf16[384,1024]{1,0:T(8,128)(2,1)S(1)} %constant_dynamic-update-slice_fusion.43), channel_id=1, source_target_pairs={{0,1},{1,0},{2,3},{3,2},{4,5},{5,4},{6,7},{7,6},{8,9},{9,8},{10,11... | collective-permute-start | bytes 2359304 | tf_op jit(solution)/shard_map/while/body/eval_jaxpr/ppermute | solution.py:83
  246.2 35.7 %collective-permute-start.19 = (f32[128,256]{0,1:T(8,128)S(1)}, f32[128,256]{0,1:T(8,128)}, u32[]{:S(2)}, u32[]{:S(2)}) collective-permute-start(f32[128,256]{0,1:T(8,128)S(1)} %get-tuple-element.222), channel_id=1, source_target_pairs={{0,32},{32,0},{64,96},{96,64},{128,160},{160,128},{192,224},{224,1... | collective-permute-start | bytes 393224 | tf_op jit(solution)/shard_map/while/body/eval_jaxpr/ppermute | solution.py:83
  251.7 24.6 %all-to-all-start = ((f32[256,1,4]{2,1,0:T(1,128)}), f32[256,1,4]{2,1,0:T(1,128)}, u32[]{:S(2)}, u32[]{:S(2)}) async-start(f32[256,1,4]{2,1,0:T(1,128)} %broadcast_in_dim.4), calls=%async_computation | async-start | bytes 262144 | tf_op jit(solution)/shard_map/while/body/eval_jaxpr/all_to_all | solution.py:39
  264.4 19.5 %collective-permute-start.20 = (f32[128,256]{0,1:T(8,128)S(1)}, f32[128,256]{0,1:T(8,128)}, u32[]{:S(2)}, u32[]{:S(2)}) collective-permute-start(f32[128,256]{0,1:T(8,128)S(1)} %get-tuple-element.222), channel_id=1, source_target_pairs={{0,64},{32,96},{64,0},{96,32},{128,192},{160,224},{192,128},{224,1... | collective-permute-start | bytes 393224 | tf_op jit(solution)/shard_map/while/body/eval_jaxpr/ppermute | solution.py:83
  267.3 20.1 %collective-permute-start.21 = (f32[128,256]{0,1:T(8,128)S(1)}, f32[128,256]{0,1:T(8,128)}, u32[]{:S(2)}, u32[]{:S(2)}) collective-permute-start(f32[128,256]{0,1:T(8,128)S(1)} %get-tuple-element.222), channel_id=1, source_target_pairs={{0,96},{32,64},{64,32},{96,0},{128,224},{160,192},{192,160},{224,1... | collective-permute-start | bytes 393224 | tf_op jit(solution)/shard_map/while/body/eval_jaxpr/ppermute | solution.py:83
  268.2 20.1 %collective-permute-start.22 = (f32[128,256]{0,1:T(8,128)S(1)}, f32[128,256]{0,1:T(8,128)}, u32[]{:S(2)}, u32[]{:S(2)}) collective-permute-start(f32[128,256]{0,1:T(8,128)S(1)} %get-tuple-element.222), channel_id=1, source_target_pairs={{0,128},{32,160},{64,192},{96,224},{128,0},{160,32},{192,64},{224,... | collective-permute-start | bytes 393224 | tf_op jit(solution)/shard_map/while/body/eval_jaxpr/ppermute | solution.py:83
  269.4 19.9 %collective-permute-start.23 = (f32[128,256]{0,1:T(8,128)S(1)}, f32[128,256]{0,1:T(8,128)}, u32[]{:S(2)}, u32[]{:S(2)}) collective-permute-start(f32[128,256]{0,1:T(8,128)S(1)} %get-tuple-element.222), channel_id=1, source_target_pairs={{0,160},{32,128},{64,224},{96,192},{128,32},{160,0},{192,96},{224,... | collective-permute-start | bytes 393224 | tf_op jit(solution)/shard_map/while/body/eval_jaxpr/ppermute | solution.py:83
  309.1 11.9 %collective-permute-start.1 = (bf16[192,1024]{1,0:T(8,128)(2,1)S(1)}, bf16[192,1024]{1,0:T(8,128)(2,1)S(1)}, u32[]{:S(2)}, u32[]{:S(2)}) collective-permute-start(bf16[192,1024]{1,0:T(8,128)(2,1)S(1)} %dynamic-slice_convert_fusion.11), channel_id=1, source_target_pairs={{0,2},{1,3},{2,0},{3,1},{4,6},{5,7},{6,4},{7,5},{8,10},{9,11},{10,... | collective-permute-start | bytes 1179656 | tf_op jit(solution)/shard_map/while/body/eval_jaxpr/ppermute | solution.py:67
  358.0 9.4 %collective-permute-start.11 = (bf16[384,1024]{1,0:T(8,128)(2,1)S(1)}, bf16[384,1024]{1,0:T(8,128)(2,1)}, u32[]{:S(2)}, u32[]{:S(2)}) collective-permute-start(bf16[384,1024]{1,0:T(8,128)(2,1)S(1)} %constant_dynamic-update-slice_fusion.43), channel_id=1, source_target_pairs={{0,1},{1,0},{2,3},{3,2},{4,5},{5,4},{6,7},{7,6},{8,9},{9,8},{10,11... | collective-permute-start | bytes 2359304 | tf_op jit(solution)/shard_map/while/body/eval_jaxpr/ppermute | solution.py:83
  387.7 35.7 %collective-permute-start.19 = (f32[128,256]{0,1:T(8,128)S(1)}, f32[128,256]{0,1:T(8,128)}, u32[]{:S(2)}, u32[]{:S(2)}) collective-permute-start(f32[128,256]{0,1:T(8,128)S(1)} %get-tuple-element.222), channel_id=1, source_target_pairs={{0,32},{32,0},{64,96},{96,64},{128,160},{160,128},{192,224},{224,1... | collective-permute-start | bytes 393224 | tf_op jit(solution)/shard_map/while/body/eval_jaxpr/ppermute | solution.py:83
  393.2 24.7 %all-to-all-start = ((f32[256,1,4]{2,1,0:T(1,128)}), f32[256,1,4]{2,1,0:T(1,128)}, u32[]{:S(2)}, u32[]{:S(2)}) async-start(f32[256,1,4]{2,1,0:T(1,128)} %broadcast_in_dim.4), calls=%async_computation | async-start | bytes 262144 | tf_op jit(solution)/shard_map/while/body/eval_jaxpr/all_to_all | solution.py:39
  405.8 19.5 %collective-permute-start.20 = (f32[128,256]{0,1:T(8,128)S(1)}, f32[128,256]{0,1:T(8,128)}, u32[]{:S(2)}, u32[]{:S(2)}) collective-permute-start(f32[128,256]{0,1:T(8,128)S(1)} %get-tuple-element.222), channel_id=1, source_target_pairs={{0,64},{32,96},{64,0},{96,32},{128,192},{160,224},{192,128},{224,1... | collective-permute-start | bytes 393224 | tf_op jit(solution)/shard_map/while/body/eval_jaxpr/ppermute | solution.py:83
  408.8 20.1 %collective-permute-start.21 = (f32[128,256]{0,1:T(8,128)S(1)}, f32[128,256]{0,1:T(8,128)}, u32[]{:S(2)}, u32[]{:S(2)}) collective-permute-start(f32[128,256]{0,1:T(8,128)S(1)} %get-tuple-element.222), channel_id=1, source_target_pairs={{0,96},{32,64},{64,32},{96,0},{128,224},{160,192},{192,160},{224,1... | collective-permute-start | bytes 393224 | tf_op jit(solution)/shard_map/while/body/eval_jaxpr/ppermute | solution.py:83
  409.7 20.1 %collective-permute-start.22 = (f32[128,256]{0,1:T(8,128)S(1)}, f32[128,256]{0,1:T(8,128)}, u32[]{:S(2)}, u32[]{:S(2)}) collective-permute-start(f32[128,256]{0,1:T(8,128)S(1)} %get-tuple-element.222), channel_id=1, source_target_pairs={{0,128},{32,160},{64,192},{96,224},{128,0},{160,32},{192,64},{224,... | collective-permute-start | bytes 393224 | tf_op jit(solution)/shard_map/while/body/eval_jaxpr/ppermute | solution.py:83
  410.9 19.9 %collective-permute-start.23 = (f32[128,256]{0,1:T(8,128)S(1)}, f32[128,256]{0,1:T(8,128)}, u32[]{:S(2)}, u32[]{:S(2)}) collective-permute-start(f32[128,256]{0,1:T(8,128)S(1)} %get-tuple-element.222), channel_id=1, source_target_pairs={{0,160},{32,128},{64,224},{96,192},{128,32},{160,0},{192,96},{224,... | collective-permute-start | bytes 393224 | tf_op jit(solution)/shard_map/while/body/eval_jaxpr/ppermute | solution.py:83
  (88 other events, 704.8 us)

commit v15 on v14

--- a/solution.py
+++ b/solution.py
@@ -96,7 +96,7 @@
     partial_out = partial_out + lax.dot_general(
         hidden_act, tangent_out_t, (((1,), (1,)), ((), ())), preferred_element_type=jnp.float32
     )
-    fsdp_groups = digit_groups(lax.axis_size("fsdp"), (1, 1, 1))
+    fsdp_groups = digit_groups(lax.axis_size("fsdp"), (1, 1, 1, 1))
     out_chunk = spread_reduce(partial_out.astype(jnp.bfloat16), "fsdp", fsdp_groups, jnp.bfloat16)
     cotangent = spread_gather((out_chunk * metric).astype(jnp.bfloat16), "fsdp", fsdp_groups)
     back_act = lax.dot_general(

time: 445 us -> 469 us (1.054)
  waiting for transfers between devices: 154 us -> 191 us
  starting transfers between devices: 170 us -> 157 us
    ppermute x39 -> x36, waiting for transfers between devices: 48.5 us -> 72.9 us  [spread_gather(): got = lax.ppermute(chunk, axis, xor_pairs(size, offset << low))]
    ppermute x39 -> x36, waiting for transfers between devices: 84.2 us -> 97.3 us  [spread_reduce(): lax.ppermute(send.astype(send_type), axis, xor_pairs(size, offset << low))]
    ppermute x39 -> x36, starting transfers between devices: 76.2 us -> 66.5 us  [spread_gather(): got = lax.ppermute(chunk, axis, xor_pairs(size, offset << low))]
    ppermute x39 -> x36, starting transfers between devices: 56.1 us -> 50.3 us  [spread_reduce(): lax.ppermute(send.astype(send_type), axis, xor_pairs(size, offset << low))]
    dynamic_update_slice x39 -> x36, local copies, waits for them, and re-layouts: 17.6 us -> 17.6 us  [spread_gather(): lax.dynamic_update_slice_in_dim(whole, got, (digit ^ offset) * rows, 0)]
  transfers between devices with their start and end apart: 81 -> 75, of which waited for: 51 -> 53; matrix products, arithmetic and copies ran while one was open for 8% -> 8% of each run, Pallas kernels for 0% -> 0%
where the time goes in v15:
time: 469 us; the launch traced here: 468 us
  waiting for transfers between devices  191 us (41%)
  starting transfers between devices  157 us (33%)
  other arithmetic  40.5 us (9%)
  local copies, waits for them, and re-layouts  40.3 us (9%)
  matrix products  25.3 us (5%)
  loops' own time  12.9 us (3%)
    ppermute x36, waiting for transfers between devices, spread_reduce(): lax.ppermute(send.astype(send_type), axis, xor_pairs(size, offset << low))  97.3 us
    ppermute x36, waiting for transfers between devices, spread_gather(): got = lax.ppermute(chunk, axis, xor_pairs(size, offset << low))  72.9 us
    ppermute x36, starting transfers between devices, spread_gather(): got = lax.ppermute(chunk, axis, xor_pairs(size, offset << low))  66.5 us
    ppermute x36, starting transfers between devices, spread_reduce(): lax.ppermute(send.astype(send_type), axis, xor_pairs(size, offset << low))  50.3 us
    all_to_all x3, starting transfers between devices, scalar_sum(): lax.all_to_all(jnp.broadcast_to(values[None], (size,) + values.shape), ax...  39.8 us
    all_to_all x3, waiting for transfers between devices, scalar_sum(): lax.all_to_all(jnp.broadcast_to(values[None], (size,) + values.shape), ax...  20.9 us
    dynamic_update_slice x36, local copies, waits for them, and re-layouts, spread_gather(): lax.dynamic_update_slice_in_dim(whole, got, (digit ^ offset) * rows, 0)  17.6 us
    another operation x1, loops' own time, on_device(): lax.fori_loop(0, ITERS, iterate, (jnp.zeros_like(residual), residual, res...  12.9 us
  transfers between devices with their start and end apart: 75, of which 53 were waited for; matrix products, arithmetic and copies ran while one was open for 8% of the time, Pallas kernels for 0%

profile of v15, /device:TPU:1, one launch (start us, length us, event | category | flops | bytes accessed | tf_op | source)
XLA Modules:
  0.0 467.6 jit_solution(15298567368721306493)
XLA Ops:
  7.2 454.4 %while.15 = (s32[]{:T(128)}, f32[1024,256]{0,1:T(8,128)}, f32[1024,256]{0,1:T(8,128)}, f32[1024,256]{0,1:T(8,128)S(1)}, bf16[768,1024]{1,0:T(8,128)(2,1)}, /*ind...) while((s32[]{:T(128)}, f32[1024,256]{0,1:T(8,128)}, ...), condition=%wide.region_7.8_spmd.clone, body=%wide.region_1.7_spmd.clone.sunk | while | flops 1215202304 | bytes 108858440 | solution.py:152
  23.1 10.8 %collective-permute-done.1 = bf16[192,1024]{1,0:T(8,128)(2,1)S(1)} collective-permute-done((bf16[192,1024]{1,0:T(8,128)(2,1)S(1)}, bf16[192,1024]{1,0:T(8,128)(2,1)S(1)}, u32[]{:S(2)}, u32[]{:S(2)}) %collective-permute-start.1) | collective-permute-done | bytes 393248 | tf_op jit(solution)/shard_map/while/body/eval_jaxpr/ppermute | solution.py:67
  59.7 5.9 %collective-permute-done.6 = bf16[48,1024]{1,0:T(8,128)(2,1)S(1)} collective-permute-done((bf16[48,1024]{1,0:T(8,128)(2,1)S(1)}, bf16[48,1024]{1,0:T(8,128)(2,1)S(1)}, u32[]{:S(2)}, u32[]{:S(2)}) %collective-permute-start.6) | collective-permute-done | bytes 98336 | tf_op jit(solution)/shard_map/while/body/eval_jaxpr/ppermute | solution.py:83
  65.8 5.5 %collective-permute-done.7 = bf16[96,1024]{1,0:T(8,128)(2,1)S(1)} collective-permute-done((bf16[96,1024]{1,0:T(8,128)(2,1)S(1)}, bf16[96,1024]{1,0:T(8,128)(2,1)S(1)}, u32[]{:S(2)}, u32[]{:S(2)}) %collective-permute-start.7) | collective-permute-done | bytes 196640 | tf_op jit(solution)/shard_map/while/body/eval_jaxpr/ppermute | solution.py:83
  79.6 6.7 %collective-permute-start.9 = (bf16[384,1024]{1,0:T(8,128)(2,1)S(1)}, bf16[384,1024]{1,0:T(8,128)(2,1)}, u32[]{:S(2)}, u32[]{:S(2)}) collective-permute-start(bf16[384,1024]{1,0:T(8,128)(2,1)S(1)} %constant_dynamic-update-slice_fusion.43), channel_id=1, source_target_pairs={{0,1},{1,0},{2,3},{3,2},{4,5},{5,4},{6,7},{7,6},{8,9},{9,8},{10,11... | collective-permute-start | bytes 2359304 | tf_op jit(solution)/shard_map/while/body/eval_jaxpr/ppermute | solution.py:83
  115.9 14.8 %all-to-all-start = ((f32[256,1,4]{2,1,0:T(1,128)}), f32[256,1,4]{2,1,0:T(1,128)}, u32[]{:S(2)}, u32[]{:S(2)}) async-start(f32[256,1,4]{2,1,0:T(1,128)} %broadcast_in_dim.4), calls=%async_computation | async-start | bytes 262144 | tf_op jit(solution)/shard_map/while/body/eval_jaxpr/all_to_all | solution.py:39
  135.7 7.0 %all-to-all-done = f32[256,1,4]{2,1,0:T(1,128)} async-done(((f32[256,1,4]{2,1,0:T(1,128)}), f32[256,1,4]{2,1,0:T(1,128)}, u32[]{:S(2)}, u32[]{:S(2)}) %all-to-all-start) | async-done | bytes 4128 | tf_op jit(solution)/shard_map/while/body/eval_jaxpr/all_to_all | solution.py:39
  176.8 10.7 %collective-permute-done.1 = bf16[192,1024]{1,0:T(8,128)(2,1)S(1)} collective-permute-done((bf16[192,1024]{1,0:T(8,128)(2,1)S(1)}, bf16[192,1024]{1,0:T(8,128)(2,1)S(1)}, u32[]{:S(2)}, u32[]{:S(2)}) %collective-permute-start.1) | collective-permute-done | bytes 393248 | tf_op jit(solution)/shard_map/while/body/eval_jaxpr/ppermute | solution.py:67
  200.2 5.3 %collective-permute-done.4 = bf16[24,1024]{1,0:T(8,128)(2,1)S(1)} collective-permute-done((bf16[24,1024]{1,0:T(8,128)(2,1)S(1)}, bf16[24,1024]{1,0:T(8,128)(2,1)S(1)}, u32[]{:S(2)}, u32[]{:S(2)}) %collective-permute-start.4) | collective-permute-done | bytes 49184 | tf_op jit(solution)/shard_map/while/body/eval_jaxpr/ppermute | solution.py:67
  207.2 5.3 %collective-permute-done.5 = bf16[24,1024]{1,0:T(8,128)(2,1)S(1)} collective-permute-done((bf16[24,1024]{1,0:T(8,128)(2,1)S(1)}, bf16[24,1024]{1,0:T(8,128)(2,1)S(1)}, u32[]{:S(2)}, u32[]{:S(2)}) %collective-permute-start.5) | collective-permute-done | bytes 49184 | tf_op jit(solution)/shard_map/while/body/eval_jaxpr/ppermute | solution.py:83
  212.7 5.4 %collective-permute-done.6 = bf16[48,1024]{1,0:T(8,128)(2,1)S(1)} collective-permute-done((bf16[48,1024]{1,0:T(8,128)(2,1)S(1)}, bf16[48,1024]{1,0:T(8,128)(2,1)S(1)}, u32[]{:S(2)}, u32[]{:S(2)}) %collective-permute-start.6) | collective-permute-done | bytes 98336 | tf_op jit(solution)/shard_map/while/body/eval_jaxpr/ppermute | solution.py:83
  218.2 5.5 %collective-permute-done.7 = bf16[96,1024]{1,0:T(8,128)(2,1)S(1)} collective-permute-done((bf16[96,1024]{1,0:T(8,128)(2,1)S(1)}, bf16[96,1024]{1,0:T(8,128)(2,1)S(1)}, u32[]{:S(2)}, u32[]{:S(2)}) %collective-permute-start.7) | collective-permute-done | bytes 196640 | tf_op jit(solution)/shard_map/while/body/eval_jaxpr/ppermute | solution.py:83
  225.4 6.5 %collective-permute-done.8 = bf16[192,1024]{1,0:T(8,128)(2,1)S(1)} collective-permute-done((bf16[192,1024]{1,0:T(8,128)(2,1)S(1)}, bf16[192,1024]{1,0:T(8,128)(2,1)S(1)}, u32[]{:S(2)}, u32[]{:S(2)}) %collective-permute-start.8) | collective-permute-done | bytes 393248 | tf_op jit(solution)/shard_map/while/body/eval_jaxpr/ppermute | solution.py:83
  232.0 7.8 %collective-permute-start.9 = (bf16[384,1024]{1,0:T(8,128)(2,1)S(1)}, bf16[384,1024]{1,0:T(8,128)(2,1)}, u32[]{:S(2)}, u32[]{:S(2)}) collective-permute-start(bf16[384,1024]{1,0:T(8,128)(2,1)S(1)} %constant_dynamic-update-slice_fusion.43), channel_id=1, source_target_pairs={{0,1},{1,0},{2,3},{3,2},{4,5},{5,4},{6,7},{7,6},{8,9},{9,8},{10,11... | collective-permute-start | bytes 2359304 | tf_op jit(solution)/shard_map/while/body/eval_jaxpr/ppermute | solution.py:83
  267.9 12.5 %all-to-all-start = ((f32[256,1,4]{2,1,0:T(1,128)}), f32[256,1,4]{2,1,0:T(1,128)}, u32[]{:S(2)}, u32[]{:S(2)}) async-start(f32[256,1,4]{2,1,0:T(1,128)} %broadcast_in_dim.4), calls=%async_computation | async-start | bytes 262144 | tf_op jit(solution)/shard_map/while/body/eval_jaxpr/all_to_all | solution.py:39
  285.5 7.0 %all-to-all-done = f32[256,1,4]{2,1,0:T(1,128)} async-done(((f32[256,1,4]{2,1,0:T(1,128)}), f32[256,1,4]{2,1,0:T(1,128)}, u32[]{:S(2)}, u32[]{:S(2)}) %all-to-all-start) | async-done | bytes 4128 | tf_op jit(solution)/shard_map/while/body/eval_jaxpr/all_to_all | solution.py:39
  326.5 10.7 %collective-permute-done.1 = bf16[192,1024]{1,0:T(8,128)(2,1)S(1)} collective-permute-done((bf16[192,1024]{1,0:T(8,128)(2,1)S(1)}, bf16[192,1024]{1,0:T(8,128)(2,1)S(1)}, u32[]{:S(2)}, u32[]{:S(2)}) %collective-permute-start.1) | collective-permute-done | bytes 393248 | tf_op jit(solution)/shard_map/while/body/eval_jaxpr/ppermute | solution.py:67
  356.9 5.3 %collective-permute-done.5 = bf16[24,1024]{1,0:T(8,128)(2,1)S(1)} collective-permute-done((bf16[24,1024]{1,0:T(8,128)(2,1)S(1)}, bf16[24,1024]{1,0:T(8,128)(2,1)S(1)}, u32[]{:S(2)}, u32[]{:S(2)}) %collective-permute-start.5) | collective-permute-done | bytes 49184 | tf_op jit(solution)/shard_map/while/body/eval_jaxpr/ppermute | solution.py:83
  362.4 5.4 %collective-permute-done.6 = bf16[48,1024]{1,0:T(8,128)(2,1)S(1)} collective-permute-done((bf16[48,1024]{1,0:T(8,128)(2,1)S(1)}, bf16[48,1024]{1,0:T(8,128)(2,1)S(1)}, u32[]{:S(2)}, u32[]{:S(2)}) %collective-permute-start.6) | collective-permute-done | bytes 98336 | tf_op jit(solution)/shard_map/while/body/eval_jaxpr/ppermute | solution.py:83
  368.0 5.5 %collective-permute-done.7 = bf16[96,1024]{1,0:T(8,128)(2,1)S(1)} collective-permute-done((bf16[96,1024]{1,0:T(8,128)(2,1)S(1)}, bf16[96,1024]{1,0:T(8,128)(2,1)S(1)}, u32[]{:S(2)}, u32[]{:S(2)}) %collective-permute-start.7) | collective-permute-done | bytes 196640 | tf_op jit(solution)/shard_map/while/body/eval_jaxpr/ppermute | solution.py:83
  375.2 6.5 %collective-permute-done.8 = bf16[192,1024]{1,0:T(8,128)(2,1)S(1)} collective-permute-done((bf16[192,1024]{1,0:T(8,128)(2,1)S(1)}, bf16[192,1024]{1,0:T(8,128)(2,1)S(1)}, u32[]{:S(2)}, u32[]{:S(2)}) %collective-permute-start.8) | collective-permute-done | bytes 393248 | tf_op jit(solution)/shard_map/while/body/eval_jaxpr/ppermute | solution.py:83
  381.7 7.8 %collective-permute-start.9 = (bf16[384,1024]{1,0:T(8,128)(2,1)S(1)}, bf16[384,1024]{1,0:T(8,128)(2,1)}, u32[]{:S(2)}, u32[]{:S(2)}) collective-permute-start(bf16[384,1024]{1,0:T(8,128)(2,1)S(1)} %constant_dynamic-update-slice_fusion.43), channel_id=1, source_target_pairs={{0,1},{1,0},{2,3},{3,2},{4,5},{5,4},{6,7},{7,6},{8,9},{9,8},{10,11... | collective-permute-start | bytes 2359304 | tf_op jit(solution)/shard_map/while/body/eval_jaxpr/ppermute | solution.py:83
  417.7 12.5 %all-to-all-start = ((f32[256,1,4]{2,1,0:T(1,128)}), f32[256,1,4]{2,1,0:T(1,128)}, u32[]{:S(2)}, u32[]{:S(2)}) async-start(f32[256,1,4]{2,1,0:T(1,128)} %broadcast_in_dim.4), calls=%async_computation | async-start | bytes 262144 | tf_op jit(solution)/shard_map/while/body/eval_jaxpr/all_to_all | solution.py:39
  435.2 7.0 %all-to-all-done = f32[256,1,4]{2,1,0:T(1,128)} async-done(((f32[256,1,4]{2,1,0:T(1,128)}), f32[256,1,4]{2,1,0:T(1,128)}, u32[]{:S(2)}, u32[]{:S(2)}) %all-to-all-start) | async-done | bytes 4128 | tf_op jit(solution)/shard_map/while/body/eval_jaxpr/all_to_all | solution.py:39
  (341 shorter events, 276.7 us)
Async XLA Ops:
  22.0 11.9 %collective-permute-start.1 = (bf16[192,1024]{1,0:T(8,128)(2,1)S(1)}, bf16[192,1024]{1,0:T(8,128)(2,1)S(1)}, u32[]{:S(2)}, u32[]{:S(2)}) collective-permute-start(bf16[192,1024]{1,0:T(8,128)(2,1)S(1)} %dynamic-slice_convert_fusion.11), channel_id=1, source_target_pairs={{0,2},{1,3},{2,0},{3,1},{4,6},{5,7},{6,4},{7,5},{8,10},{9,11},{10,... | collective-permute-start | bytes 1179656 | tf_op jit(solution)/shard_map/while/body/eval_jaxpr/ppermute | solution.py:67
  79.6 8.8 %collective-permute-start.9 = (bf16[384,1024]{1,0:T(8,128)(2,1)S(1)}, bf16[384,1024]{1,0:T(8,128)(2,1)}, u32[]{:S(2)}, u32[]{:S(2)}) collective-permute-start(bf16[384,1024]{1,0:T(8,128)(2,1)S(1)} %constant_dynamic-update-slice_fusion.43), channel_id=1, source_target_pairs={{0,1},{1,0},{2,3},{3,2},{4,5},{5,4},{6,7},{7,6},{8,9},{9,8},{10,11... | collective-permute-start | bytes 2359304 | tf_op jit(solution)/shard_map/while/body/eval_jaxpr/ppermute | solution.py:83
  110.1 38.3 %collective-permute-start.17 = (f32[128,256]{0,1:T(8,128)S(1)}, f32[128,256]{0,1:T(8,128)}, u32[]{:S(2)}, u32[]{:S(2)}) collective-permute-start(f32[128,256]{0,1:T(8,128)S(1)} %get-tuple-element.213), channel_id=1, source_target_pairs={{0,32},{32,0},{64,96},{96,64},{128,160},{160,128},{192,224},{224,1... | collective-permute-start | bytes 393224 | tf_op jit(solution)/shard_map/while/body/eval_jaxpr/ppermute | solution.py:83
  115.9 26.8 %all-to-all-start = ((f32[256,1,4]{2,1,0:T(1,128)}), f32[256,1,4]{2,1,0:T(1,128)}, u32[]{:S(2)}, u32[]{:S(2)}) async-start(f32[256,1,4]{2,1,0:T(1,128)} %broadcast_in_dim.4), calls=%async_computation | async-start | bytes 262144 | tf_op jit(solution)/shard_map/while/body/eval_jaxpr/all_to_all | solution.py:39
  130.7 19.6 %collective-permute-start.18 = (f32[128,256]{0,1:T(8,128)S(1)}, f32[128,256]{0,1:T(8,128)}, u32[]{:S(2)}, u32[]{:S(2)}) collective-permute-start(f32[128,256]{0,1:T(8,128)S(1)} %get-tuple-element.213), channel_id=1, source_target_pairs={{0,64},{32,96},{64,0},{96,32},{128,192},{160,224},{192,128},{224,1... | collective-permute-start | bytes 393224 | tf_op jit(solution)/shard_map/while/body/eval_jaxpr/ppermute | solution.py:83
  133.7 20.4 %collective-permute-start.19 = (f32[128,256]{0,1:T(8,128)S(1)}, f32[128,256]{0,1:T(8,128)}, u32[]{:S(2)}, u32[]{:S(2)}) collective-permute-start(f32[128,256]{0,1:T(8,128)S(1)} %get-tuple-element.213), channel_id=1, source_target_pairs={{0,96},{32,64},{64,32},{96,0},{128,224},{160,192},{192,160},{224,1... | collective-permute-start | bytes 393224 | tf_op jit(solution)/shard_map/while/body/eval_jaxpr/ppermute | solution.py:83
  134.6 20.4 %collective-permute-start.20 = (f32[128,256]{0,1:T(8,128)S(1)}, f32[128,256]{0,1:T(8,128)}, u32[]{:S(2)}, u32[]{:S(2)}) collective-permute-start(f32[128,256]{0,1:T(8,128)S(1)} %get-tuple-element.213), channel_id=1, source_target_pairs={{0,128},{32,160},{64,192},{96,224},{128,0},{160,32},{192,64},{224,... | collective-permute-start | bytes 393224 | tf_op jit(solution)/shard_map/while/body/eval_jaxpr/ppermute | solution.py:83
  135.7 20.1 %collective-permute-start.21 = (f32[128,256]{0,1:T(8,128)S(1)}, f32[128,256]{0,1:T(8,128)}, u32[]{:S(2)}, u32[]{:S(2)}) collective-permute-start(f32[128,256]{0,1:T(8,128)S(1)} %get-tuple-element.213), channel_id=1, source_target_pairs={{0,160},{32,128},{64,224},{96,192},{128,32},{160,0},{192,96},{224,... | collective-permute-start | bytes 393224 | tf_op jit(solution)/shard_map/while/body/eval_jaxpr/ppermute | solution.py:83
  175.6 11.9 %collective-permute-start.1 = (bf16[192,1024]{1,0:T(8,128)(2,1)S(1)}, bf16[192,1024]{1,0:T(8,128)(2,1)S(1)}, u32[]{:S(2)}, u32[]{:S(2)}) collective-permute-start(bf16[192,1024]{1,0:T(8,128)(2,1)S(1)} %dynamic-slice_convert_fusion.11), channel_id=1, source_target_pairs={{0,2},{1,3},{2,0},{3,1},{4,6},{5,7},{6,4},{7,5},{8,10},{9,11},{10,... | collective-permute-start | bytes 1179656 | tf_op jit(solution)/shard_map/while/body/eval_jaxpr/ppermute | solution.py:67
  232.0 9.9 %collective-permute-start.9 = (bf16[384,1024]{1,0:T(8,128)(2,1)S(1)}, bf16[384,1024]{1,0:T(8,128)(2,1)}, u32[]{:S(2)}, u32[]{:S(2)}) collective-permute-start(bf16[384,1024]{1,0:T(8,128)(2,1)S(1)} %constant_dynamic-update-slice_fusion.43), channel_id=1, source_target_pairs={{0,1},{1,0},{2,3},{3,2},{4,5},{5,4},{6,7},{7,6},{8,9},{9,8},{10,11... | collective-permute-start | bytes 2359304 | tf_op jit(solution)/shard_map/while/body/eval_jaxpr/ppermute | solution.py:83
  262.2 35.9 %collective-permute-start.17 = (f32[128,256]{0,1:T(8,128)S(1)}, f32[128,256]{0,1:T(8,128)}, u32[]{:S(2)}, u32[]{:S(2)}) collective-permute-start(f32[128,256]{0,1:T(8,128)S(1)} %get-tuple-element.213), channel_id=1, source_target_pairs={{0,32},{32,0},{64,96},{96,64},{128,160},{160,128},{192,224},{224,1... | collective-permute-start | bytes 393224 | tf_op jit(solution)/shard_map/while/body/eval_jaxpr/ppermute | solution.py:83
  267.9 24.5 %all-to-all-start = ((f32[256,1,4]{2,1,0:T(1,128)}), f32[256,1,4]{2,1,0:T(1,128)}, u32[]{:S(2)}, u32[]{:S(2)}) async-start(f32[256,1,4]{2,1,0:T(1,128)} %broadcast_in_dim.4), calls=%async_computation | async-start | bytes 262144 | tf_op jit(solution)/shard_map/while/body/eval_jaxpr/all_to_all | solution.py:39
  280.5 19.6 %collective-permute-start.18 = (f32[128,256]{0,1:T(8,128)S(1)}, f32[128,256]{0,1:T(8,128)}, u32[]{:S(2)}, u32[]{:S(2)}) collective-permute-start(f32[128,256]{0,1:T(8,128)S(1)} %get-tuple-element.213), channel_id=1, source_target_pairs={{0,64},{32,96},{64,0},{96,32},{128,192},{160,224},{192,128},{224,1... | collective-permute-start | bytes 393224 | tf_op jit(solution)/shard_map/while/body/eval_jaxpr/ppermute | solution.py:83
  283.4 20.4 %collective-permute-start.19 = (f32[128,256]{0,1:T(8,128)S(1)}, f32[128,256]{0,1:T(8,128)}, u32[]{:S(2)}, u32[]{:S(2)}) collective-permute-start(f32[128,256]{0,1:T(8,128)S(1)} %get-tuple-element.213), channel_id=1, source_target_pairs={{0,96},{32,64},{64,32},{96,0},{128,224},{160,192},{192,160},{224,1... | collective-permute-start | bytes 393224 | tf_op jit(solution)/shard_map/while/body/eval_jaxpr/ppermute | solution.py:83
  284.3 20.4 %collective-permute-start.20 = (f32[128,256]{0,1:T(8,128)S(1)}, f32[128,256]{0,1:T(8,128)}, u32[]{:S(2)}, u32[]{:S(2)}) collective-permute-start(f32[128,256]{0,1:T(8,128)S(1)} %get-tuple-element.213), channel_id=1, source_target_pairs={{0,128},{32,160},{64,192},{96,224},{128,0},{160,32},{192,64},{224,... | collective-permute-start | bytes 393224 | tf_op jit(solution)/shard_map/while/body/eval_jaxpr/ppermute | solution.py:83
  285.5 20.1 %collective-permute-start.21 = (f32[128,256]{0,1:T(8,128)S(1)}, f32[128,256]{0,1:T(8,128)}, u32[]{:S(2)}, u32[]{:S(2)}) collective-permute-start(f32[128,256]{0,1:T(8,128)S(1)} %get-tuple-element.213), channel_id=1, source_target_pairs={{0,160},{32,128},{64,224},{96,192},{128,32},{160,0},{192,96},{224,... | collective-permute-start | bytes 393224 | tf_op jit(solution)/shard_map/while/body/eval_jaxpr/ppermute | solution.py:83
  325.3 11.9 %collective-permute-start.1 = (bf16[192,1024]{1,0:T(8,128)(2,1)S(1)}, bf16[192,1024]{1,0:T(8,128)(2,1)S(1)}, u32[]{:S(2)}, u32[]{:S(2)}) collective-permute-start(bf16[192,1024]{1,0:T(8,128)(2,1)S(1)} %dynamic-slice_convert_fusion.11), channel_id=1, source_target_pairs={{0,2},{1,3},{2,0},{3,1},{4,6},{5,7},{6,4},{7,5},{8,10},{9,11},{10,... | collective-permute-start | bytes 1179656 | tf_op jit(solution)/shard_map/while/body/eval_jaxpr/ppermute | solution.py:67
  381.7 9.9 %collective-permute-start.9 = (bf16[384,1024]{1,0:T(8,128)(2,1)S(1)}, bf16[384,1024]{1,0:T(8,128)(2,1)}, u32[]{:S(2)}, u32[]{:S(2)}) collective-permute-start(bf16[384,1024]{1,0:T(8,128)(2,1)S(1)} %constant_dynamic-update-slice_fusion.43), channel_id=1, source_target_pairs={{0,1},{1,0},{2,3},{3,2},{4,5},{5,4},{6,7},{7,6},{8,9},{9,8},{10,11... | collective-permute-start | bytes 2359304 | tf_op jit(solution)/shard_map/while/body/eval_jaxpr/ppermute | solution.py:83
  412.0 35.9 %collective-permute-start.17 = (f32[128,256]{0,1:T(8,128)S(1)}, f32[128,256]{0,1:T(8,128)}, u32[]{:S(2)}, u32[]{:S(2)}) collective-permute-start(f32[128,256]{0,1:T(8,128)S(1)} %get-tuple-element.213), channel_id=1, source_target_pairs={{0,32},{32,0},{64,96},{96,64},{128,160},{160,128},{192,224},{224,1... | collective-permute-start | bytes 393224 | tf_op jit(solution)/shard_map/while/body/eval_jaxpr/ppermute | solution.py:83
  417.7 24.5 %all-to-all-start = ((f32[256,1,4]{2,1,0:T(1,128)}), f32[256,1,4]{2,1,0:T(1,128)}, u32[]{:S(2)}, u32[]{:S(2)}) async-start(f32[256,1,4]{2,1,0:T(1,128)} %broadcast_in_dim.4), calls=%async_computation | async-start | bytes 262144 | tf_op jit(solution)/shard_map/while/body/eval_jaxpr/all_to_all | solution.py:39
  430.2 19.6 %collective-permute-start.18 = (f32[128,256]{0,1:T(8,128)S(1)}, f32[128,256]{0,1:T(8,128)}, u32[]{:S(2)}, u32[]{:S(2)}) collective-permute-start(f32[128,256]{0,1:T(8,128)S(1)} %get-tuple-element.213), channel_id=1, source_target_pairs={{0,64},{32,96},{64,0},{96,32},{128,192},{160,224},{192,128},{224,1... | collective-permute-start | bytes 393224 | tf_op jit(solution)/shard_map/while/body/eval_jaxpr/ppermute | solution.py:83
  433.1 20.4 %collective-permute-start.19 = (f32[128,256]{0,1:T(8,128)S(1)}, f32[128,256]{0,1:T(8,128)}, u32[]{:S(2)}, u32[]{:S(2)}) collective-permute-start(f32[128,256]{0,1:T(8,128)S(1)} %get-tuple-element.213), channel_id=1, source_target_pairs={{0,96},{32,64},{64,32},{96,0},{128,224},{160,192},{192,160},{224,1... | collective-permute-start | bytes 393224 | tf_op jit(solution)/shard_map/while/body/eval_jaxpr/ppermute | solution.py:83
  434.0 20.4 %collective-permute-start.20 = (f32[128,256]{0,1:T(8,128)S(1)}, f32[128,256]{0,1:T(8,128)}, u32[]{:S(2)}, u32[]{:S(2)}) collective-permute-start(f32[128,256]{0,1:T(8,128)S(1)} %get-tuple-element.213), channel_id=1, source_target_pairs={{0,128},{32,160},{64,192},{96,224},{128,0},{160,32},{192,64},{224,... | collective-permute-start | bytes 393224 | tf_op jit(solution)/shard_map/while/body/eval_jaxpr/ppermute | solution.py:83
  435.2 20.1 %collective-permute-start.21 = (f32[128,256]{0,1:T(8,128)S(1)}, f32[128,256]{0,1:T(8,128)}, u32[]{:S(2)}, u32[]{:S(2)}) collective-permute-start(f32[128,256]{0,1:T(8,128)S(1)} %get-tuple-element.213), channel_id=1, source_target_pairs={{0,160},{32,128},{64,224},{96,192},{128,32},{160,0},{192,96},{224,... | collective-permute-start | bytes 393224 | tf_op jit(solution)/shard_map/while/body/eval_jaxpr/ppermute | solution.py:83
  (82 other events, 680.6 us)
